TPU v7x, 32 devices: a whole 2x2x4 slice. The times are simulated.
32 devices in a mesh: dp: 4 (over y, x), seq: 8 (over z, core).
Axes of the slice: x: 2, y: 2, z: 4, core: 2. Of those that a mesh axis runs over, the one named last changes fastest.
Arguments:
- asking_vectors_matrix: bfloat16 [4, 1024, 2048], P('dp', 'seq'), may hold values from -6 to 6
- matched_keys_matrix: bfloat16 [4, 1024, 2048], P('dp', 'seq'), may hold values from -6 to 6
- carried_vectors_matrix: bfloat16 [4, 1024, 2048], P('dp', 'seq'), may hold values from -6 to 6
- upstream_cotangent: bfloat16 [4, 1024, 2048], P('dp', 'seq'), may hold values from -6 to 6
- w_out: bfloat16 [2048, 2048], P('seq'), may hold values from -0.125 to 0.125
- panel_entry_offsets: int32 [4, 9], P('dp'), may hold values from 0 to 32, as said below
- rightward_panel_per_entry: int32 [4, 32], P('dp'), may hold values from 0 to 7, as said below
Outputs:
- layer_out: bfloat16 [4, 1024, 2048], P('dp', 'seq')
- q_grad: bfloat16 [4, 1024, 2048], P('dp', 'seq')
- k_grad: bfloat16 [4, 1024, 2048], P('dp', 'seq')
- v_grad: bfloat16 [4, 1024, 2048], P('dp', 'seq')
- w_out_grad: float32 [2048, 2048], P('seq')
Inputs may be any that keep to these rules, and one draw needn't show every extreme that they name: panel_entry_offsets[b, 0] is 0 and panel_entry_offsets never falls along a row; tile row r owns slots panel_entry_offsets[b, r] to panel_entry_offsets[b, r + 1] - 1, 1 to 8 of them, and its own tile r is among its blocks; in every subgraph one tile row holds all 8 tiles; panel_entry_offsets[b, 8], the used slots, lies between 16 and 32 and equals 32 for at least one subgraph. `rightward_panel_per_entry`: the slots of a tile row hold distinct column tiles in rising order; slots from panel_entry_offsets[b, 8] on hold arbitrary tile numbers that take no part.
All inputs are finite; a program needn't handle non-finite values.
Results may differ from a plain program's by a relative error of at most 0.034.
Values may be sent and summed in bfloat16 or wider, within the bound.
No kernel may reach another device: no remote copies, remote signals or barrier semaphores. Data moves between devices by JAX's collectives and lax.ppermute only.
A program may use at most 128 MiB of HBM per device.

v0:
```python
import math

import jax
import jax.numpy as jnp
from jax import lax
from jax.sharding import PartitionSpec as P

H = 16
HD = 128


def entry_tables(starts, columns):
    tile_count = starts.shape[0] - 1
    slot_count = columns.shape[0]
    slot_index = jnp.arange(slot_count, dtype=jnp.int32)
    entry_row = jnp.sum((starts[1:][None, :] <= slot_index[:, None]).astype(jnp.int32), axis=1)
    in_use = entry_row < tile_count
    safe_row = jnp.minimum(entry_row, tile_count - 1)
    target_col = jnp.where(in_use, columns, tile_count)
    return (safe_row, in_use, target_col, columns, tile_count)


def row_sum(values, safe_row, tile_count):
    return jax.ops.segment_sum(values, safe_row, num_segments=tile_count, indices_are_sorted=True)


def col_sum(values, target_col, tile_count):
    return jax.ops.segment_sum(values, target_col, num_segments=tile_count + 1)[:tile_count]


def attend_forward(query_rows, key_rows, value_rows, tables):
    safe_row, in_use, target_col, columns, tile_count = tables
    tile_size = query_rows.shape[0] // tile_count
    head_depth = query_rows.shape[1]
    factor = 1.0 / math.sqrt(head_depth)
    q_blocks = query_rows.reshape(tile_count, tile_size, head_depth)[safe_row]
    k_blocks = key_rows.reshape(tile_count, tile_size, head_depth)[columns]
    v_blocks = value_rows.reshape(tile_count, tile_size, head_depth)[columns]
    scores = (
        jnp.einsum("eid,ejd->eij", q_blocks, k_blocks, preferred_element_type=jnp.float32) * factor
    )
    block_max = jnp.where(in_use[:, None], jnp.max(scores, axis=2), -jnp.inf)
    row_max = jax.ops.segment_max(
        block_max, safe_row, num_segments=tile_count, indices_are_sorted=True
    )
    expd = jnp.where(in_use[:, None, None], jnp.exp(scores - row_max[safe_row][:, :, None]), 0.0)
    row_total = row_sum(jnp.sum(expd, axis=2), safe_row, tile_count)
    expd_low = expd.astype(jnp.bfloat16)
    weighted = jnp.einsum("eij,ejd->eid", expd_low, v_blocks, preferred_element_type=jnp.float32)
    summed = row_sum(weighted, safe_row, tile_count)
    attended = (
        (summed / row_total[:, :, None])
        .reshape(tile_count * tile_size, head_depth)
        .astype(jnp.bfloat16)
    )
    return (attended, row_max, row_total)


def attend_backward(
    query_rows, key_rows, value_rows, attended, grad_rows, row_max, row_total, tables
):
    safe_row, in_use, target_col, columns, tile_count = tables
    tile_size = query_rows.shape[0] // tile_count
    head_depth = query_rows.shape[1]
    factor = 1.0 / math.sqrt(head_depth)
    q_blocks = query_rows.reshape(tile_count, tile_size, head_depth)[safe_row]
    k_blocks = key_rows.reshape(tile_count, tile_size, head_depth)[columns]
    v_blocks = value_rows.reshape(tile_count, tile_size, head_depth)[columns]
    g_blocks = grad_rows.reshape(tile_count, tile_size, head_depth)[safe_row]
    scores = (
        jnp.einsum("eid,ejd->eij", q_blocks, k_blocks, preferred_element_type=jnp.float32) * factor
    )
    prob = jnp.where(
        in_use[:, None, None],
        jnp.exp(scores - row_max[safe_row][:, :, None]) / row_total[safe_row][:, :, None],
        0.0,
    )
    prob_low = prob.astype(jnp.bfloat16)
    v_terms = jnp.einsum("eij,eid->ejd", prob_low, g_blocks, preferred_element_type=jnp.float32)
    v_sum = col_sum(v_terms, target_col, tile_count)
    prob_grad = jnp.einsum("eid,ejd->eij", g_blocks, v_blocks, preferred_element_type=jnp.float32)
    delta = jnp.sum(attended.astype(jnp.float32) * grad_rows.astype(jnp.float32), axis=1).reshape(
        tile_count, tile_size
    )
    score_grad = (prob * (prob_grad - delta[safe_row][:, :, None]) * factor).astype(jnp.bfloat16)
    q_terms = jnp.einsum("eij,ejd->eid", score_grad, k_blocks, preferred_element_type=jnp.float32)
    q_sum = row_sum(q_terms, safe_row, tile_count)
    k_terms = jnp.einsum("eij,eid->ejd", score_grad, q_blocks, preferred_element_type=jnp.float32)
    k_sum = col_sum(k_terms, target_col, tile_count)
    node_count = tile_count * tile_size
    return (
        q_sum.reshape(node_count, head_depth).astype(jnp.bfloat16),
        k_sum.reshape(node_count, head_depth).astype(jnp.bfloat16),
        v_sum.reshape(node_count, head_depth).astype(jnp.bfloat16),
    )


def shards(
    asking_vectors_matrix,
    matched_keys_matrix,
    carried_vectors_matrix,
    upstream_cotangent,
    w_out,
    panel_entry_offsets,
    rightward_panel_per_entry,
):
    nodes_here = asking_vectors_matrix.shape[1]
    width = asking_vectors_matrix.shape[2]

    def head_rows(values):
        return values.reshape(nodes_here, H, HD)

    def node_rows(values):
        return values.transpose(1, 0, 2).reshape(nodes_here, width)[None]

    q_heads, k_heads, v_heads = (
        lax.all_to_all(
            head_rows(asking_vectors_matrix[0]), "seq", split_axis=1, concat_axis=0, tiled=True
        ),
        lax.all_to_all(
            head_rows(matched_keys_matrix[0]), "seq", split_axis=1, concat_axis=0, tiled=True
        ),
        lax.all_to_all(
            head_rows(carried_vectors_matrix[0]), "seq", split_axis=1, concat_axis=0, tiled=True
        ),
    )
    local_heads = q_heads.shape[1]
    tables = entry_tables(panel_entry_offsets[0], rightward_panel_per_entry[0])

    def pick(values, which):
        return lax.dynamic_index_in_dim(values, which, 1, keepdims=False)

    def forward_one(which):
        return attend_forward(
            pick(q_heads, which), pick(k_heads, which), pick(v_heads, which), tables
        )

    head_outputs, max_stack, total_stack = lax.map(
        forward_one, jnp.arange(local_heads, dtype=jnp.int32)
    )
    returned = lax.all_to_all(head_outputs, "seq", split_axis=1, concat_axis=0, tiled=True)
    attended = returned.transpose(1, 0, 2).reshape(nodes_here, width)
    grad_here = upstream_cotangent[0]
    shard_piece = lax.all_gather(w_out, "seq", axis=0, tiled=True)
    columns_here = attended
    layer_acc = jnp.dot(columns_here, shard_piece, preferred_element_type=jnp.float32)
    back_part = lax.dot_general(
        grad_here, shard_piece, (((1,), (1,)), ((), ())), preferred_element_type=jnp.float32
    )
    layer_out = layer_acc.astype(jnp.bfloat16)[None]
    attended_grad = back_part.astype(jnp.bfloat16).reshape(nodes_here, H, HD)
    grad_heads = lax.all_to_all(attended_grad, "seq", split_axis=1, concat_axis=0, tiled=True)

    def backward_one(which):
        return attend_backward(
            pick(q_heads, which),
            pick(k_heads, which),
            pick(v_heads, which),
            head_outputs[which],
            pick(grad_heads, which),
            max_stack[which],
            total_stack[which],
            tables,
        )

    q_local, k_local, v_local = lax.map(backward_one, jnp.arange(local_heads, dtype=jnp.int32))
    q_back, k_back, v_back = (
        lax.all_to_all(q_local, "seq", split_axis=1, concat_axis=0, tiled=True),
        lax.all_to_all(k_local, "seq", split_axis=1, concat_axis=0, tiled=True),
        lax.all_to_all(v_local, "seq", split_axis=1, concat_axis=0, tiled=True),
    )
    columns_here = attended
    summed_rows = lax.psum_scatter(
        lax.dot_general(
            columns_here, grad_here, (((0,), (0,)), ((), ())), preferred_element_type=jnp.float32
        ).astype(jnp.bfloat16),
        "seq",
        scatter_dimension=0,
        tiled=True,
    )
    w_out_grad = lax.psum(summed_rows, "dp").astype(jnp.float32) / lax.axis_size("dp")
    return (layer_out, node_rows(q_back), node_rows(k_back), node_rows(v_back), w_out_grad)


def solution(mesh):
    return jax.shard_map(
        shards,
        mesh=mesh,
        in_specs=(
            P("dp", "seq", None),
            P("dp", "seq", None),
            P("dp", "seq", None),
            P("dp", "seq", None),
            P("seq", None),
            P("dp", None),
            P("dp", None),
        ),
        out_specs=(
            P("dp", "seq", None),
            P("dp", "seq", None),
            P("dp", "seq", None),
            P("dp", "seq", None),
            P("seq", None),
        ),
        check_vma=False,
    )
```

profile of v0, /device:TPU:0, one launch (start us, length us, event | category | flops | bytes accessed | tf_op | source)
XLA Modules:
  0.0 399.9 jit_solution(10691402979172913246)
XLA Ops:
  7.9 2.1 copy.130
  10.0 6.3 %all-to-all-start = ((bf16[128,16,128]{0,2,1:T(8,128)(2,1)}), bf16[128,16,128]{0,2,1:T(8,128)(2,1)S(1)}, u32[]{:S(2)}, u32[]{:S(2)}) async-start(bf16[128,16,128]{0,2,1:T(8,128)(2,1)} %bitcast.29), calls=%async_computation | async-start | bytes 1048576 | tf_op jit(solution)/shard_map/all_to_all | solution.py:117
  17.4 23.6 %all-to-all-done = bf16[128,16,128]{0,2,1:T(8,128)(2,1)S(1)} async-done(((bf16[128,16,128]{0,2,1:T(8,128)(2,1)}), bf16[128,16,128]{0,2,1:T(8,128)(2,1)S(1)}, u32[]{:S(2)}, u32[]{:S(2)}) %all-to-all-start) | async-done | bytes 524320 | tf_op jit(solution)/shard_map/all_to_all | solution.py:117
  41.0 5.9 %all-to-all-start.1 = ((bf16[128,16,128]{0,2,1:T(8,128)(2,1)}), bf16[128,16,128]{0,2,1:T(8,128)(2,1)S(1)}, u32[]{:S(2)}, u32[]{:S(2)}) async-start(bf16[128,16,128]{0,2,1:T(8,128)(2,1)} %bitcast.34), calls=%async_computation.1 | async-start | bytes 1048576 | tf_op jit(solution)/shard_map/all_to_all | solution.py:120
  47.9 28.8 %all-to-all-done.1 = bf16[128,16,128]{0,2,1:T(8,128)(2,1)S(1)} async-done(((bf16[128,16,128]{0,2,1:T(8,128)(2,1)}), bf16[128,16,128]{0,2,1:T(8,128)(2,1)S(1)}, u32[]{:S(2)}, u32[]{:S(2)}) %all-to-all-start.1) | async-done | bytes 524320 | tf_op jit(solution)/shard_map/all_to_all | solution.py:120
  76.7 3.5 all-to-all-start.2
  82.5 26.3 %all-to-all-done.2 = bf16[128,16,128]{0,2,1:T(8,128)(2,1)S(1)} async-done(((bf16[128,16,128]{0,2,1:T(8,128)(2,1)}), bf16[128,16,128]{0,2,1:T(8,128)(2,1)S(1)}, u32[]{:S(2)}, u32[]{:S(2)}) %all-to-all-start.2) | async-done | bytes 524320 | tf_op jit(solution)/shard_map/all_to_all | solution.py:123
  110.7 49.0 %while.28 = (s32[]{:T(128)}, bf16[2,1024,128]{2,1,0:T(8,128)(2,1)}, f32[2,8,128]{2,1,0:T(8,128)S(1)}, f32[2,8,128]{2,1,0:T(8,128)S(1)}, s32[32]{0:T(128)S(1)}, /...) while((s32[]{:T(128)}, bf16[2,1024,128]{2,1,0:T(8,128)(2,1)}, ...), condition=%wide.region_7.8_spmd, body=%wide.region_1.7_spmd.sunk | while | flops 274471104 | bytes 27679912 | solution.py:138
  114.2 1.7 gather_fusion
  121.2 2.4 multiply_reduce_fusion.2
  125.0 3.3 fusion.82
  128.3 4.7 %scatter_fusion = f32[8,128,128]{2,1,0:T(8,128)S(1)} fusion(f32[8,128,128]{2,1,0:T(8,128)S(1)} %broadcast.203, s32[32]{0:T(128)S(1)} %get-tuple-element.438, f32[32,128,128]{2,1,0:T(8,128)} %fusion.82), kind=kCustom, calls=%fused_computation.12.clone.1 | custom fusion | flops 524288 | bytes 6291584 | tf_op jit(solution)/shard_map/while/body/eval_jaxpr/scatter-add | solution.py:24
  138.7 1.7 gather_fusion
  145.7 2.4 multiply_reduce_fusion.2
  149.5 3.3 fusion.82
  152.8 4.7 %scatter_fusion = f32[8,128,128]{2,1,0:T(8,128)S(1)} fusion(f32[8,128,128]{2,1,0:T(8,128)S(1)} %broadcast.203, s32[32]{0:T(128)S(1)} %get-tuple-element.438, f32[32,128,128]{2,1,0:T(8,128)} %fusion.82), kind=kCustom, calls=%fused_computation.12.clone.1 | custom fusion | flops 524288 | bytes 6291584 | tf_op jit(solution)/shard_map/while/body/eval_jaxpr/scatter-add | solution.py:24
  161.3 17.8 %all_to_all.144 = bf16[2,1024,128]{2,0,1:T(2,128)(2,1)S(1)} all-to-all(bf16[2,1024,128]{2,0,1:T(2,128)(2,1)S(1)} %copy.139), channel_id=1, replica_groups=mesh['dp'=4,'seq'=8] {'seq'}, dimensions={1} | all-to-all | bytes 1048576 | tf_op jit(solution)/shard_map/all_to_all | solution.py:141
  179.4 5.6 %convolution_convert_fusion = bf16[2048,2048]{1,0:T(8,128)(2,1)} fusion(bf16[128,2048]{0,1:T(8,128)(2,1)S(1)} %bitcast.219, bf16[1,128,2048]{2,1,0:T(8,128)(2,1)S(1)} %copy-done), kind=kOutput, calls=%fused_computation.71 | convolution fusion | flops 1077936128 | bytes 9437184 | tf_op jit(solution)/shard_map/dot_general | solution.py:174
  185.1 6.3 %fusion.25 = bf16[16,16,8,128]{3,2,1,0:T(8,128)(2,1)S(1)} fusion(bf16[2048,2048]{1,0:T(8,128)(2,1)} %all-gather.2.cloned.1.call-done, bf16[1,128,2048]{2,1,0:T(8,128)(2,1)S(1)} %copy-done), kind=kOutput, calls=%fused_computation.76 | convolution fusion | flops 1074003968 | bytes 9437184 | tf_op jit(solution)/shard_map/dot_general | solution.py:147
  192.3 3.7 all-to-all-start.4
  196.0 23.8 %all-to-all-done.4 = bf16[128,16,128]{2,0,1:T(8,128)(2,1)S(1)} async-done(((bf16[128,16,128]{2,0,1:T(8,128)(2,1)}), bf16[128,16,128]{2,0,1:T(8,128)(2,1)S(1)}, u32[]{:S(2)}, u32[]{:S(2)}) %all-to-all-start.4) | async-done | bytes 524320 | tf_op jit(solution)/shard_map/all_to_all | solution.py:152
  222.9 85.0 %while.29 = (s32[]{:T(128)}, bf16[2,1024,128]{2,1,0:T(8,128)(2,1)}, bf16[2,1024,128]{2,1,0:T(8,128)(2,1)}, bf16[2,1024,128]{2,1,0:T(8,128)(2,1)}, s32[32]{0:T(12...) while((s32[]{:T(128)}, bf16[2,1024,128]{2,1,0:T(8,128)(2,1)}, ...), condition=%wide.region_13.14_spmd, body=%wide.region_8.13_spmd.sunk | while | flops 678036672 | bytes 82360864 | solution.py:166
  230.3 2.8 divide_select_fusion.2
  237.5 3.4 multiply_convert_fusion.2
  240.9 1.8 fusion.97
  242.8 4.7 %scatter_fusion.1 = f32[8,128,128]{2,1,0:T(8,128)S(1)} fusion(f32[8,128,128]{2,1,0:T(8,128)S(1)} %broadcast.214, s32[32]{0:T(128)S(1)} %get-tuple-element.494, f32[32,128,128]{2,1,0:T(8,128)} %fusion.97), kind=kCustom, calls=%fused_computation.14.clone.1 | custom fusion | flops 524288 | bytes 6291584 | tf_op jit(solution)/shard_map/while/body/eval_jaxpr/scatter-add | solution.py:24
  248.2 3.5 fusion.98
  251.7 4.7 %scatter_fusion.2 = f32[9,128,128]{2,1,0:T(8,128)S(1)} fusion(f32[9,128,128]{2,1,0:T(8,128)S(1)} %broadcast.215.clone, s32[32]{0:T(128)S(1)} %get-tuple-element.505, f32[32,128,128]{2,1,0:T(8,128)} %fusion.98), kind=kCustom, calls=%fused_computation.16.clone.1 | custom fusion | flops 524288 | bytes 6291584 | tf_op jit(solution)/shard_map/while/body/eval_jaxpr/scatter-add | solution.py:28
  256.5 3.1 fusion.99
  259.6 4.7 %scatter_fusion.3 = f32[9,128,128]{2,1,0:T(8,128)S(1)} fusion(f32[9,128,128]{2,1,0:T(8,128)S(1)} %broadcast.215.clone.1, s32[32]{0:T(128)S(1)} %get-tuple-element.505, f32[32,128,128]{2,1,0:T(8,128)} %fusion.99), kind=kCustom, calls=%fused_computation.15.clone.1 | custom fusion | flops 524288 | bytes 6291584 | tf_op jit(solution)/shard_map/while/body/eval_jaxpr/scatter-add | solution.py:28
  272.9 2.8 divide_select_fusion.2
  280.1 3.4 multiply_convert_fusion.2
  283.5 1.8 fusion.97
  285.3 4.7 %scatter_fusion.1 = f32[8,128,128]{2,1,0:T(8,128)S(1)} fusion(f32[8,128,128]{2,1,0:T(8,128)S(1)} %broadcast.214, s32[32]{0:T(128)S(1)} %get-tuple-element.494, f32[32,128,128]{2,1,0:T(8,128)} %fusion.97), kind=kCustom, calls=%fused_computation.14.clone.1 | custom fusion | flops 524288 | bytes 6291584 | tf_op jit(solution)/shard_map/while/body/eval_jaxpr/scatter-add | solution.py:24
  290.8 3.4 fusion.98
  294.3 4.7 %scatter_fusion.2 = f32[9,128,128]{2,1,0:T(8,128)S(1)} fusion(f32[9,128,128]{2,1,0:T(8,128)S(1)} %broadcast.215.clone, s32[32]{0:T(128)S(1)} %get-tuple-element.505, f32[32,128,128]{2,1,0:T(8,128)} %fusion.98), kind=kCustom, calls=%fused_computation.16.clone.1 | custom fusion | flops 524288 | bytes 6291584 | tf_op jit(solution)/shard_map/while/body/eval_jaxpr/scatter-add | solution.py:28
  299.0 3.1 fusion.99
  302.1 4.7 %scatter_fusion.3 = f32[9,128,128]{2,1,0:T(8,128)S(1)} fusion(f32[9,128,128]{2,1,0:T(8,128)S(1)} %broadcast.215.clone.1, s32[32]{0:T(128)S(1)} %get-tuple-element.505, f32[32,128,128]{2,1,0:T(8,128)} %fusion.99), kind=kCustom, calls=%fused_computation.15.clone.1 | custom fusion | flops 524288 | bytes 6291584 | tf_op jit(solution)/shard_map/while/body/eval_jaxpr/scatter-add | solution.py:28
  307.9 2.4 copy.145
  310.4 3.6 all-to-all-start.5
  315.3 13.9 %all-to-all-done.5 = bf16[2,1024,128]{2,0,1:T(2,128)(2,1)S(1)} async-done(((bf16[2,1024,128]{2,0,1:T(2,128)(2,1)}), bf16[2,1024,128]{2,0,1:T(2,128)(2,1)S(1)}, u32[]{:S(2)}, u32[]{:S(2)}) %all-to-all-start.5) | async-done | bytes 524320 | tf_op jit(solution)/shard_map/all_to_all | solution.py:168
  329.3 3.5 all-to-all-start.6
  334.9 13.2 %all-to-all-done.6 = bf16[2,1024,128]{2,0,1:T(2,128)(2,1)S(1)} async-done(((bf16[2,1024,128]{2,0,1:T(2,128)(2,1)}), bf16[2,1024,128]{2,0,1:T(2,128)(2,1)S(1)}, u32[]{:S(2)}, u32[]{:S(2)}) %all-to-all-start.6) | async-done | bytes 524320 | tf_op jit(solution)/shard_map/all_to_all | solution.py:169
  348.1 3.7 all-to-all-start.7
  351.8 5.5 %fusion.24 = bf16[1,128,2048]{2,1,0:T(8,128)(2,1)} fusion(bf16[128,2048]{0,1:T(8,128)(2,1)S(1)} %bitcast.220, bf16[2048,2048]{1,0:T(8,128)(2,1)} %all-gather.2.cloned.1.call-done), kind=kOutput, calls=%fused_computation.74 | convolution fusion | flops 1074003968 | bytes 9437184 | tf_op jit(solution)/shard_map/dot_general | solution.py:146
  360.1 6.7 %all-to-all-done.7 = bf16[2,1024,128]{2,0,1:T(2,128)(2,1)S(1)} async-done(((bf16[2,1024,128]{2,0,1:T(2,128)(2,1)}), bf16[2,1024,128]{2,0,1:T(2,128)(2,1)S(1)}, u32[]{:S(2)}, u32[]{:S(2)}) %all-to-all-start.7) | async-done | bytes 524320 | tf_op jit(solution)/shard_map/all_to_all | solution.py:170
  368.3 22.3 %all-reduce.2.cloned.1.call-done = bf16[256,2048]{1,0:T(8,128)(2,1)} async-done(((bf16[256,2048]{1,0:T(8,128)(2,1)}), bf16[256,2048]{1,0:T(8,128)(2,1)}) %all-reduce.2.cloned.1.call-update) | async-done | bytes 1048592 | tf_op jit(solution)/shard_map/psum | solution.py:181
  390.6 2.8 convert_multiply_fusion.1
  (189 shorter events, 64.8 us)
Async XLA Ops:
  7.2 172.3 %copy-start = (bf16[1,128,2048]{2,1,0:T(8,128)(2,1)S(1)}, bf16[1,128,2048]{2,1,0:T(8,128)(2,1)}, u32[]{:S(2)}) copy-start(bf16[1,128,2048]{2,1,0:T(8,128)(2,1)} %param.14) | copy-start | bytes 1572868
  7.2 9.2 %copy-start.14 = (bf16[1,128,2048]{2,1,0:T(8,128)(2,1)S(1)}, bf16[1,128,2048]{2,1,0:T(8,128)(2,1)}, u32[]{:S(2)}) copy-start(bf16[1,128,2048]{2,1,0:T(8,128)(2,1)} %param.12) | copy-start | bytes 1572868
  7.2 177.9 %all-gather.2.cloned.1.call-start = ((), (), s32[]{:S(2)}) async-start(), calls=%async_computation.9 | async-start | bytes 9437184 | tf_op jit(solution)/shard_map/all_gather | solution.py:144
  7.9 39.0 %copy-start.15 = (bf16[1,128,2048]{2,1,0:T(8,128)(2,1)S(1)}, bf16[1,128,2048]{2,1,0:T(8,128)(2,1)}, u32[]{:S(2)}) copy-start(bf16[1,128,2048]{2,1,0:T(8,128)(2,1)} %param.13) | copy-start | bytes 1572868
  10.0 30.9 %all-to-all-start = ((bf16[128,16,128]{0,2,1:T(8,128)(2,1)}), bf16[128,16,128]{0,2,1:T(8,128)(2,1)S(1)}, u32[]{:S(2)}, u32[]{:S(2)}) async-start(bf16[128,16,128]{0,2,1:T(8,128)(2,1)} %bitcast.29), calls=%async_computation | async-start | bytes 1048576 | tf_op jit(solution)/shard_map/all_to_all | solution.py:117
  16.4 63.9 %copy-start.17 = (s32[1,9]{1,0:T(1,128)S(1)}, s32[1,9]{1,0:T(1,128)}, u32[]{:S(2)}) copy-start(s32[1,9]{1,0:T(1,128)} %param.16) | copy-start | bytes 112
  16.4 64.1 %copy-start.16 = (s32[1,32]{1,0:T(1,128)S(1)}, s32[1,32]{1,0:T(1,128)}, u32[]{:S(2)}) copy-start(s32[1,32]{1,0:T(1,128)} %param.17) | copy-start | bytes 388
  41.0 35.7 %all-to-all-start.1 = ((bf16[128,16,128]{0,2,1:T(8,128)(2,1)}), bf16[128,16,128]{0,2,1:T(8,128)(2,1)S(1)}, u32[]{:S(2)}, u32[]{:S(2)}) async-start(bf16[128,16,128]{0,2,1:T(8,128)(2,1)} %bitcast.34), calls=%async_computation.1 | async-start | bytes 1048576 | tf_op jit(solution)/shard_map/all_to_all | solution.py:120
  76.7 32.1 %all-to-all-start.2 = ((bf16[128,16,128]{0,2,1:T(8,128)(2,1)}), bf16[128,16,128]{0,2,1:T(8,128)(2,1)S(1)}, u32[]{:S(2)}, u32[]{:S(2)}) async-start(bf16[128,16,128]{0,2,1:T(8,128)(2,1)} %bitcast.40), calls=%async_computation.2 | async-start | bytes 1048576 | tf_op jit(solution)/shard_map/all_to_all | solution.py:123
  80.2 252.6 %reduce-scatter.2.cloned.1.call-start = ((), (), s32[]{:S(2)}) async-start(), calls=%async_computation.10 | async-start | bytes 9437184 | tf_op jit(solution)/shard_map/reduce_scatter | solution.py:173
  179.4 5.6 %copy-start.6 = (bf16[128,16,128]{0,2,1:T(8,128)(2,1)}, bf16[128,16,128]{0,2,1:T(8,128)(2,1)S(1)}, u32[]{:S(2)}) copy-start(bf16[128,16,128]{0,2,1:T(8,128)(2,1)S(1)} %copy.142) | copy-start | bytes 1572868
  192.3 27.4 %all-to-all-start.4 = ((bf16[128,16,128]{2,0,1:T(8,128)(2,1)}), bf16[128,16,128]{2,0,1:T(8,128)(2,1)S(1)}, u32[]{:S(2)}, u32[]{:S(2)}) async-start(bf16[128,16,128]{2,0,1:T(8,128)(2,1)} %bitcast.129), calls=%async_computation.4 | async-start | bytes 1048576 | tf_op jit(solution)/shard_map/all_to_all | solution.py:152
  227.2 6.0 %copy-start.2 = (bf16[32,128,128]{2,1,0:T(8,128)(2,1)}, bf16[32,128,128]{2,1,0:T(8,128)(2,1)S(1)}, u32[]{:S(2)}) copy-start(bf16[32,128,128]{2,1,0:T(8,128)(2,1)S(1)} %gather_fusion.4) | copy-start | bytes 3145732 | tf_op jit(solution)/shard_map/while
  229.1 4.0 %copy-start.3 = (bf16[32,128,128]{2,1,0:T(8,128)(2,1)}, bf16[32,128,128]{2,1,0:T(8,128)(2,1)S(1)}, u32[]{:S(2)}) copy-start(bf16[32,128,128]{2,1,0:T(8,128)(2,1)S(1)} %gather_fusion.5) | copy-start | bytes 3145732 | tf_op jit(solution)/shard_map/while
  233.3 3.4 copy-start.5
  237.5 3.4 copy-start.4
  259.6 4.8 %copy-start.8 = (bf16[2,1024,128]{2,1,0:T(8,128)(2,1)S(1)}, bf16[2,1024,128]{2,1,0:T(8,128)(2,1)}, u32[]{:S(2)}) copy-start(bf16[2,1024,128]{2,1,0:T(8,128)(2,1)} %get-tuple-element.472) | copy-start | bytes 1572868 | tf_op jit(solution)/shard_map/while
  259.6 4.8 %copy-start.11 = (bf16[2,1024,128]{2,1,0:T(8,128)(2,1)S(1)}, bf16[2,1024,128]{2,1,0:T(8,128)(2,1)}, u32[]{:S(2)}) copy-start(bf16[2,1024,128]{2,1,0:T(8,128)(2,1)} %get-tuple-element.473) | copy-start | bytes 1572868 | tf_op jit(solution)/shard_map/while
  264.5 0.8 copy-start.9
  264.5 1.0 copy-start.12
  269.8 6.0 %copy-start.2 = (bf16[32,128,128]{2,1,0:T(8,128)(2,1)}, bf16[32,128,128]{2,1,0:T(8,128)(2,1)S(1)}, u32[]{:S(2)}) copy-start(bf16[32,128,128]{2,1,0:T(8,128)(2,1)S(1)} %gather_fusion.4) | copy-start | bytes 3145732 | tf_op jit(solution)/shard_map/while
  271.7 4.0 %copy-start.3 = (bf16[32,128,128]{2,1,0:T(8,128)(2,1)}, bf16[32,128,128]{2,1,0:T(8,128)(2,1)S(1)}, u32[]{:S(2)}) copy-start(bf16[32,128,128]{2,1,0:T(8,128)(2,1)S(1)} %gather_fusion.5) | copy-start | bytes 3145732 | tf_op jit(solution)/shard_map/while
  275.9 3.4 copy-start.5
  280.1 3.4 copy-start.4
  302.1 4.7 %copy-start.8 = (bf16[2,1024,128]{2,1,0:T(8,128)(2,1)S(1)}, bf16[2,1024,128]{2,1,0:T(8,128)(2,1)}, u32[]{:S(2)}) copy-start(bf16[2,1024,128]{2,1,0:T(8,128)(2,1)} %get-tuple-element.472) | copy-start | bytes 1572868 | tf_op jit(solution)/shard_map/while
  302.1 4.7 %copy-start.11 = (bf16[2,1024,128]{2,1,0:T(8,128)(2,1)S(1)}, bf16[2,1024,128]{2,1,0:T(8,128)(2,1)}, u32[]{:S(2)}) copy-start(bf16[2,1024,128]{2,1,0:T(8,128)(2,1)} %get-tuple-element.473) | copy-start | bytes 1572868 | tf_op jit(solution)/shard_map/while
  306.9 0.8 copy-start.9
  306.9 1.0 copy-start.12
  307.9 6.1 %copy-start.10 = (bf16[2,1024,128]{2,1,0:T(8,128)(2,1)S(1)}, bf16[2,1024,128]{2,1,0:T(8,128)(2,1)}, u32[]{:S(2)}) copy-start(bf16[2,1024,128]{2,1,0:T(8,128)(2,1)} %get-tuple-element.152) | copy-start | bytes 1572868
  310.4 23.2 %copy-start.13 = (bf16[2,1024,128]{2,1,0:T(8,128)(2,1)S(1)}, bf16[2,1024,128]{2,1,0:T(8,128)(2,1)}, u32[]{:S(2)}) copy-start(bf16[2,1024,128]{2,1,0:T(8,128)(2,1)} %get-tuple-element.153) | copy-start | bytes 1572868
  310.4 18.9 %all-to-all-start.5 = ((bf16[2,1024,128]{2,0,1:T(2,128)(2,1)}), bf16[2,1024,128]{2,0,1:T(2,128)(2,1)S(1)}, u32[]{:S(2)}, u32[]{:S(2)}) async-start(bf16[2,1024,128]{2,0,1:T(2,128)(2,1)} %copy.145), calls=%async_computation.5 | async-start | bytes 1048576 | tf_op jit(solution)/shard_map/all_to_all | solution.py:168
  315.3 36.4 %copy-start.7 = (bf16[128,16,128]{0,2,1:T(8,128)(2,1)S(1)}, bf16[128,16,128]{0,2,1:T(8,128)(2,1)}, u32[]{:S(2)}) copy-start(bf16[128,16,128]{0,2,1:T(8,128)(2,1)} %copy-done.6) | copy-start | bytes 1572868
  329.3 18.8 %all-to-all-start.6 = ((bf16[2,1024,128]{2,0,1:T(2,128)(2,1)}), bf16[2,1024,128]{2,0,1:T(2,128)(2,1)S(1)}, u32[]{:S(2)}, u32[]{:S(2)}) async-start(bf16[2,1024,128]{2,0,1:T(2,128)(2,1)} %copy.149), calls=%async_computation.6 | async-start | bytes 1048576 | tf_op jit(solution)/shard_map/all_to_all | solution.py:169
  332.8 57.8 %all-reduce.2.cloned.1.call-start = ((), (), s32[]{:S(2)}) async-start(), calls=%async_computation.11 | async-start | bytes 2097152 | tf_op jit(solution)/shard_map/psum | solution.py:181
  348.1 18.8 %all-to-all-start.7 = ((bf16[2,1024,128]{2,0,1:T(2,128)(2,1)}), bf16[2,1024,128]{2,0,1:T(2,128)(2,1)S(1)}, u32[]{:S(2)}, u32[]{:S(2)}) async-start(bf16[2,1024,128]{2,0,1:T(2,128)(2,1)} %copy.153), calls=%async_computation.7 | async-start | bytes 1048576 | tf_op jit(solution)/shard_map/all_to_all | solution.py:170
  367.2 26.1 %copy-start.1 = (bf16[1,128,2048]{2,1,0:T(8,128)(2,1)S(1)}, bf16[1,128,2048]{2,1,0:T(8,128)(2,1)}, u32[]{:S(2)}) copy-start(bf16[1,128,2048]{2,1,0:T(8,128)(2,1)} %param.14) | copy-start | bytes 1572868
Sparse Core Ops, SparseCore 0:
  9.6 113.8 all-gather.1
  185.2 96.8 reduce-scatter.1
  336.7 53.8 all-reduce.1
where the time goes:
time: 402 us; the launch traced here: 400 us
  waiting for transfers between devices  160 us (40%)
  local copies, waits for them, and re-layouts  66.1 us (16%)
  matrix products  57.9 us (14%)
  other arithmetic  45.3 us (11%)
  starting transfers between devices  30.4 us (8%)
  blocking collectives  17.8 us (4%)
  between operations  14 us (3%)
  loops' own time  8.46 us (2%)
    all_to_all x1, waiting for transfers between devices, shards(): lax.all_to_all(head_rows(matched_keys_matrix[0]), 'seq', split_axis=1, co...  28.8 us
    all_to_all x1, waiting for transfers between devices, shards(): lax.all_to_all(head_rows(carried_vectors_matrix[0]), 'seq', split_axis=1,...  26.3 us
    all_to_all x1, waiting for transfers between devices, shards(): lax.all_to_all(attended_grad, 'seq', split_axis=1, concat_axis=0, tiled=T...  23.8 us
    all_to_all x1, waiting for transfers between devices, shards(): lax.all_to_all(head_rows(asking_vectors_matrix[0]), 'seq', split_axis=1,...  23.6 us
    psum x1, waiting for transfers between devices, shards(): lax.psum(summed_rows, 'dp').astype(jnp.float32) / lax.axis_size('dp')  22.3 us
    scatter-add x6, other arithmetic, row_sum(): jax.ops.segment_sum(values, safe_row, num_segments=tile_count, indices_ar...  20.2 us
    scatter-add x4, other arithmetic, col_sum(): jax.ops.segment_sum(values, target_col, num_segments=tile_count + 1)  18.7 us
    all_to_all x1, blocking collectives, shards(): lax.all_to_all(head_outputs, 'seq', split_axis=1, concat_axis=0, tiled=True)  17.8 us
  transfers between devices with their start and end apart: 10, of which 8 were waited for; matrix products, arithmetic and copies ran while one was open for 41% of the time, Pallas kernels for 0%

commit v1 on v0

v1 whole, which is shorter than its diff:
```python
import math

import jax
import jax.numpy as jnp
from jax import lax
from jax.sharding import PartitionSpec as P

H = 16
HD = 128


def tile_mask(starts, columns, nodes):
    tile_count = starts.shape[0] - 1
    slot_count = columns.shape[0]
    tile_size = nodes // tile_count
    slot_index = jnp.arange(slot_count, dtype=jnp.int32)
    entry_row = jnp.sum((starts[1:][None, :] <= slot_index[:, None]).astype(jnp.int32), axis=1)
    tile_ids = jnp.arange(tile_count, dtype=jnp.int32)
    row_hot = (entry_row[:, None] == tile_ids[None, :]).astype(jnp.int32)
    col_hot = (columns[:, None] == tile_ids[None, :]).astype(jnp.int32)
    pairs = jnp.einsum("er,ec->rc", row_hot, col_hot) > 0
    full = jnp.broadcast_to(
        pairs[:, None, :, None], (tile_count, tile_size, tile_count, tile_size)
    )
    return full.reshape(nodes, nodes)


def attend(q, k, v, g, allowed):
    factor = 1.0 / math.sqrt(q.shape[-1])
    scores = jnp.einsum("ihd,jhd->hij", q, k, preferred_element_type=jnp.float32) * factor
    masked = jnp.where(allowed[None], scores, -jnp.inf)
    row_max = jnp.max(masked, axis=2, keepdims=True)
    expd = jnp.where(allowed[None], jnp.exp(scores - row_max), 0.0)
    row_total = jnp.sum(expd, axis=2, keepdims=True)
    weighted = jnp.einsum(
        "hij,jhd->ihd", expd.astype(jnp.bfloat16), v, preferred_element_type=jnp.float32
    )
    totals = jnp.transpose(row_total[:, :, 0])[:, :, None]
    attended = (weighted / totals).astype(jnp.bfloat16)
    return attended, expd, row_total


def attend_back(q, k, v, g, attended, expd, row_total):
    factor = 1.0 / math.sqrt(q.shape[-1])
    prob = expd / row_total
    prob_low = prob.astype(jnp.bfloat16)
    v_grad = jnp.einsum("hij,ihd->jhd", prob_low, g, preferred_element_type=jnp.float32)
    prob_grad = jnp.einsum("ihd,jhd->hij", g, v, preferred_element_type=jnp.float32)
    delta = jnp.sum(attended.astype(jnp.float32) * g.astype(jnp.float32), axis=2)
    delta = jnp.transpose(delta)[:, :, None]
    score_grad = (prob * (prob_grad - delta) * factor).astype(jnp.bfloat16)
    q_grad = jnp.einsum("hij,jhd->ihd", score_grad, k, preferred_element_type=jnp.float32)
    k_grad = jnp.einsum("hij,ihd->jhd", score_grad, q, preferred_element_type=jnp.float32)
    return (
        q_grad.astype(jnp.bfloat16),
        k_grad.astype(jnp.bfloat16),
        v_grad.astype(jnp.bfloat16),
    )


def shards(
    asking_vectors_matrix,
    matched_keys_matrix,
    carried_vectors_matrix,
    upstream_cotangent,
    w_out,
    panel_entry_offsets,
    rightward_panel_per_entry,
):
    nodes_here = asking_vectors_matrix.shape[1]
    width = asking_vectors_matrix.shape[2]
    n_seq = lax.axis_size("seq")
    nodes = nodes_here * n_seq

    grad_here = upstream_cotangent[0]
    grad_full = lax.all_gather(grad_here, "seq", axis=0, tiled=True)
    w_full = lax.all_gather(w_out, "seq", axis=0, tiled=True)

    stacked = jnp.stack(
        [asking_vectors_matrix[0], matched_keys_matrix[0], carried_vectors_matrix[0]]
    ).reshape(3, nodes_here, H, HD)
    heads = lax.all_to_all(stacked, "seq", split_axis=2, concat_axis=1, tiled=True)
    q_heads, k_heads, v_heads = heads[0], heads[1], heads[2]
    local_heads = q_heads.shape[1]

    allowed = tile_mask(panel_entry_offsets[0], rightward_panel_per_entry[0], nodes)

    g_flat = lax.dot_general(
        grad_full, w_out, (((1,), (1,)), ((), ())), preferred_element_type=jnp.float32
    ).astype(jnp.bfloat16)
    g_heads = g_flat.reshape(nodes, local_heads, HD)

    attended, expd, row_total = attend(q_heads, k_heads, v_heads, g_heads, allowed)

    returned = lax.all_to_all(attended, "seq", split_axis=0, concat_axis=1, tiled=True)
    attended_nodes = returned.reshape(nodes_here, width)
    layer_out = jnp.dot(attended_nodes, w_full, preferred_element_type=jnp.float32)
    layer_out = layer_out.astype(jnp.bfloat16)[None]

    att_blocks = attended.reshape(n_seq, nodes_here, local_heads * HD)
    grad_blocks = grad_full.reshape(n_seq, nodes_here, width)
    terms = jnp.einsum(
        "bnf,bnk->bfk", att_blocks, grad_blocks, preferred_element_type=jnp.float32
    ).astype(jnp.bfloat16)
    w_rows = jnp.sum(terms.astype(jnp.float32), axis=0)
    batch = asking_vectors_matrix.shape[0] * lax.axis_size("dp")
    w_out_grad = lax.psum(w_rows, "dp") / batch

    q_g, k_g, v_g = attend_back(q_heads, k_heads, v_heads, g_heads, attended, expd, row_total)
    grads = jnp.stack([q_g, k_g, v_g])
    back = lax.all_to_all(grads, "seq", split_axis=1, concat_axis=2, tiled=True)
    back = back.reshape(3, 1, nodes_here, width)
    return (layer_out, back[0], back[1], back[2], w_out_grad)


def solution(mesh):
    return jax.shard_map(
        shards,
        mesh=mesh,
        in_specs=(
            P("dp", "seq", None),
            P("dp", "seq", None),
            P("dp", "seq", None),
            P("dp", "seq", None),
            P("seq", None),
            P("dp", None),
            P("dp", None),
        ),
        out_specs=(
            P("dp", "seq", None),
            P("dp", "seq", None),
            P("dp", "seq", None),
            P("dp", "seq", None),
            P("seq", None),
        ),
        check_vma=False,
    )
```

time: 402 us -> 277 us (0.69)
  local copies, waits for them, and re-layouts: 66.1 us -> 19.5 us
  other arithmetic: 45.3 us -> 3.58 us
  waiting for transfers between devices: 160 us -> 189 us
  matrix products: 57.9 us -> 36.1 us
  blocking collectives: 17.8 us -> 0 us
  starting transfers between devices: 30.4 us -> 14.8 us
  loops' own time: 8.46 us -> 0 us
    all_gather x1 -> x2, waiting for transfers between devices: 0.02 us -> 74.8 us  [the longest x1 74.8 us: shards(): w_full = lax.all_gather(w_out, 'seq', axis=0, tiled=True)]
    all_to_all x7 -> x3, waiting for transfers between devices: 136 us -> 69.3 us  [the longest x1 69.1 us: shards(): lax.all_to_all(stacked, 'seq', split_axis=2, concat_axis=1, tiled=True)]
    scatter-add x10 -> x0, other arithmetic: 38.9 us -> none  [the longest x6 20.2 us: row_sum(): jax.ops.segment_sum(values, safe_row, num_segments=tile_count, indices_ar...]
    dot_general x17 -> x9, matrix products: 57.9 us -> 28.9 us  [the longest x1 5.46 us: shards(): jnp.dot(attended_nodes, w_full, preferred_element_type=jnp.float32)]
    gather x22 -> x0, local copies, waits for them, and re-layouts: 22.5 us -> none  [the longest x2 3.49 us: attend_forward(): v_blocks = value_rows.reshape(tile_count, tile_size, head_depth)[columns]]
    psum x1, waiting for transfers between devices: 22.3 us -> 43.1 us  [shards(): w_out_grad = lax.psum(w_rows, 'dp') / batch]
    all_to_all x1 -> x0, blocking collectives: 17.8 us -> none  [shards(): lax.all_to_all(head_outputs, 'seq', split_axis=1, concat_axis=0, tiled=True)]
    all_to_all x7 -> x3, starting transfers between devices: 30.2 us -> 14.7 us  [the longest x1 6.33 us: shards(): lax.all_to_all(stacked, 'seq', split_axis=2, concat_axis=1, tiled=True)]
  transfers between devices with their start and end apart: 10 -> 6, of which waited for: 8 -> 4; matrix products, arithmetic and copies ran while one was open for 41% -> 15% of each run, Pallas kernels for 0% -> 0%
where the time goes in v1:
time: 277 us; the launch traced here: 276 us
  waiting for transfers between devices  189 us (68%)
  matrix products  36.1 us (13%)
  local copies, waits for them, and re-layouts  19.5 us (7%)
  starting transfers between devices  14.8 us (5%)
  between operations  14 us (5%)
  other arithmetic  3.58 us (1%)
    all_gather x1, waiting for transfers between devices, shards(): w_full = lax.all_gather(w_out, 'seq', axis=0, tiled=True)  74.8 us
    all_to_all x1, waiting for transfers between devices, shards(): lax.all_to_all(stacked, 'seq', split_axis=2, concat_axis=1, tiled=True)  69.1 us
    psum x1, waiting for transfers between devices, shards(): w_out_grad = lax.psum(w_rows, 'dp') / batch  43.1 us
    sub x1, matrix products, attend(): expd = jnp.where(allowed[None], jnp.exp(scores - row_max), 0.0)  7.15 us
    all_to_all x1, starting transfers between devices, shards(): lax.all_to_all(stacked, 'seq', split_axis=2, concat_axis=1, tiled=True)  6.33 us
    unnamed x17, local copies, waits for them, and re-layouts  5.75 us
  transfers between devices with their start and end apart: 6, of which 4 were waited for; matrix products, arithmetic and copies ran while one was open for 15% of the time, Pallas kernels for 0%

profile of v1, /device:TPU:0, one launch (start us, length us, event | category | flops | bytes accessed | tf_op | source)
XLA Modules:
  0.0 276.4 jit_solution(7157705828374576800)
XLA Ops:
  7.2 0.7 all-gather.6.cloned.1.call-update
  7.9 1.3 copy.117
  9.2 1.3 copy.118
  10.5 1.3 copy.119
  11.9 0.2 pad_maximum_fusion
  12.1 1.2 copy.120
  13.3 6.3 %all-to-all-start = ((bf16[3,128,16,128]{1,3,0,2:T(8,128)(2,1)}), bf16[3,128,16,128]{1,3,0,2:T(8,128)(2,1)S(1)}, u32[]{:S(2)}, u32[]{:S(2)}) async-start(bf16[3,128,16,128]{1,3,0,2:T(8,128)(2,1)} %copy.120), calls=%async_computation | async-start | bytes 3145728 | tf_op jit(solution)/shard_map/all_to_all | solution.py:82
  19.7 0.1 slice_bitcast_fusion
  19.8 0.1 convert_reduce_fusion.1
  19.9 0.3 convolution_compare_fusion
  20.1 0.1 copy.123
  20.2 0.3 broadcast_in_dim.38
  20.5 1.5 copy.157
  22.0 69.1 %all-to-all-done = bf16[3,128,16,128]{1,3,0,2:T(8,128)(2,1)S(1)} async-done(((bf16[3,128,16,128]{1,3,0,2:T(8,128)(2,1)}), bf16[3,128,16,128]{1,3,0,2:T(8,128)(2,1)S(1)}, u32[]{:S(2)}, u32[]{:S(2)}) %all-to-all-start) | async-done | bytes 1572896 | tf_op jit(solution)/shard_map/all_to_all | solution.py:82
  91.2 0.9 copy.121
  92.1 0.1 fusion.43
  92.3 0.3 copy.122
  92.6 0.2 squeeze.22
  92.9 7.1 %fusion.44 = (f32[2,1024]{1,0:T(2,128)S(1)}, f32[2,1024,1024]{1,2,0:T(8,128)}) fusion(pred[1024,1024]{0,1:T(8,128)(4,1)} %bitcast.89, bf16[1024,2,128]{2,0,1:T(8,128)(2,1)S(1)} %bitcast.86, bf16[1024,2,128]{2,0,1:T(8,128)(2,1)S(1)} %bitcast.82), kind=kOutput, calls=%fused_computation.48 | convolution fusion | flops 1086325760 | bytes 10493952 | tf_op jit(solution)/shard_map/sub | solution.py:33
  100.0 3.5 %fusion.27 = bf16[1024,256]{0,1:T(8,128)(2,1)S(1)} fusion(bf16[256,2048]{1,0:T(8,128)(2,1)S(1)} %copy-done, bf16[1,1024,2048]{2,1,0:T(8,128)(2,1)} %all-gather.6.cloned.1.call-done), kind=kOutput, calls=%fused_computation.28 | convolution fusion | flops 1074003968 | bytes 5767168 | tf_op jit(solution)/shard_map/dot_general | solution.py:88
  103.5 4.5 %multiply_reduce_fusion = (f32[1024,2]{0,1:T(2,128)S(1)}, bf16[1024,2,128]{0,2,1:T(8,128)(2,1)S(1)}) fusion(bf16[1024,256]{0,1:T(8,128)(2,1)S(1)} %fusion.27, f32[1024,2]{0,1:T(2,128)S(1)} %bitcast.93, bf16[1024,2,128]{0,2,1:T(8,128)(2,1)S(1)} %squeeze.22, f32[2,1024,1024]{1,2,0:T(8,128)} %get-tuple-element.12), kind=kOutput, calls=%fused_computation.34 | convolution fusion | flops 540538880 | bytes 9977856 | tf_op jit(solution)/shard_map/hij,jhd->ihd/dot_general | solution.py:35
  108.0 0.1 copy.153
  108.1 0.2 copy-done.3
  108.3 3.6 %convert_reduce_fusion = f32[256,2048]{1,0:T(8,128)} fusion(bf16[8,128,2048]{2,1,0:T(8,128)(2,1)S(1)} %bitcast.95, bf16[8,128,256]{1,0,2:T(8,128)(2,1)S(1)} %bitcast.92), kind=kOutput, calls=%fused_computation.1 | convolution fusion | flops 1085800448 | bytes 6815744 | tf_op jit(solution)/shard_map/bnf,bnk->bfk/dot_general | solution.py:102
  112.0 0.7 all-gather.4.cloned.1.call-update
  112.7 1.1 copy.127
  113.8 3.7 %all-to-all-start.1 = ((bf16[1024,2,128]{2,1,0:T(2,128)(2,1)}), bf16[1024,2,128]{2,1,0:T(2,128)(2,1)S(1)}, u32[]{:S(2)}, u32[]{:S(2)}) async-start(bf16[1024,2,128]{2,1,0:T(2,128)(2,1)} %copy.127), calls=%async_computation.1 | async-start | bytes 1048576 | tf_op jit(solution)/shard_map/all_to_all | solution.py:95
  117.5 4.3 %multiply_convert_fusion = bf16[2,1024,1024]{1,2,0:T(8,128)(2,1)S(1)} fusion(f32[2,1024]{1,0:T(2,128)S(1)} %bitcast.94, f32[2,1024,1024]{1,2,0:T(8,128)} %get-tuple-element.12, f32[2,1024]{1,0:T(2,128)S(1)} %get-tuple-element.11, bf16[1024,2,128]{0,2,1:T(8,128)(2,1)S(1)} %bitcast.90, bf16[1024,2,128]{0,2,1:T(8,128)(2,1)S(1)} %squeeze.22), kind=kOutput, calls=%fused_computation.2 | convolution fusion | flops 547356672 | bytes 13647872 | tf_op jit(solution)/shard_map/ihd,jhd->hij/dot_general | solution.py:48
  121.8 0.8 fusion.30
  122.6 1.6 fusion.31
  124.2 5.0 %fusion.32 = bf16[1,1024,2,128]{1,3,2,0:T(8,128)(2,1)S(1)} fusion(bf16[1024,2,128]{0,2,1:T(8,128)(2,1)S(1)} %bitcast.91, f32[2,1024,1024]{1,2,0:T(8,128)} %get-tuple-element.12, f32[2,1024]{1,0:T(2,128)S(1)} %get-tuple-element.11), kind=kOutput, calls=%fused_computation.31 | convolution fusion | flops 541327360 | bytes 9445376 | tf_op jit(solution)/shard_map/hij,ihd->jhd/dot_general | solution.py:47
  129.2 0.2 pad_maximum_fusion.1
  129.4 3.0 %copy.138 = bf16[3,1024,2,128]{3,2,0,1:T(2,128)(2,1)} copy(bf16[3,1024,2,128]{1,3,2,0:T(8,128)(2,1)S(1)} %pad_maximum_fusion.1) | data formatting | bytes 3145728 | tf_op jit(solution)/shard_map/stack | solution.py:110
  132.4 0.2 all-to-all-done.1
  132.6 4.6 %all-to-all-start.2 = ((bf16[3,1024,2,128]{3,2,0,1:T(2,128)(2,1)}), bf16[3,1024,2,128]{3,2,0,1:T(2,128)(2,1)S(1)}, u32[]{:S(2)}, u32[]{:S(2)}) async-start(bf16[3,1024,2,128]{3,2,0,1:T(2,128)(2,1)} %copy.138), calls=%async_computation.2 | async-start | bytes 3145728 | tf_op jit(solution)/shard_map/all_to_all | solution.py:111
  137.2 0.1 copy.128
  137.3 0.3 copy.129
  137.6 43.1 %all-reduce.2.cloned.1.call-done = f32[256,2048]{1,0:T(8,128)} async-done(((f32[256,2048]{1,0:T(8,128)}), f32[256,2048]{1,0:T(8,128)}) %all-reduce.2.cloned.1.call-update) | async-done | bytes 2097168 | tf_op jit(solution)/shard_map/psum | solution.py:107
  180.7 3.1 %broadcast_multiply_fusion = f32[256,2048]{1,0:T(8,128)} fusion(f32[256,2048]{1,0:T(8,128)} %all-reduce.2.cloned.1.call-done), kind=kLoop, calls=%fused_computation.33 | loop fusion | flops 524288 | bytes 4194304 | tf_op jit(solution)/shard_map/div | solution.py:107
  183.8 1.2 fusion.42
  185.0 0.4 copy.139
  185.4 1.2 squeeze.26
  186.6 0.4 copy.140
  186.9 1.2 squeeze.27
  188.1 0.4 copy.141
  188.5 1.2 squeeze.28
  189.7 74.8 %all-gather.4.cloned.1.call-done = bf16[2048,2048]{1,0:T(8,128)(2,1)} async-done(((bf16[256,2048]{1,0:T(8,128)(2,1)}), bf16[2048,2048]{1,0:T(8,128)(2,1)}) %all-gather.4.cloned.1.call-update) | async-done | bytes 8388624 | tf_op jit(solution)/shard_map/all_gather | solution.py:77
  264.5 5.5 %fusion.14 = bf16[1,128,2048]{2,1,0:T(8,128)(2,1)} fusion(bf16[128,2048]{0,1:T(8,128)(2,1)S(1)} %bitcast.84, bf16[2048,2048]{1,0:T(8,128)(2,1)} %all-gather.4.cloned.1.call-done), kind=kOutput, calls=%fused_computation.19 | convolution fusion | flops 1074003968 | bytes 9437184 | tf_op jit(solution)/shard_map/dot_general | solution.py:97
  (19 shorter events, 0.2 us)
Async XLA Ops:
  7.2 92.9 %all-gather.6.cloned.1.call-start = ((), (), s32[]{:S(2)}) async-start(), calls=%async_computation.5 | async-start | bytes 4718592 | tf_op jit(solution)/shard_map/all_gather | solution.py:76
  11.9 7.8 %copy-start.4 = (s32[1,9]{1,0:T(1,128)S(1)}, s32[1,9]{1,0:T(1,128)}, u32[]{:S(2)}) copy-start(s32[1,9]{1,0:T(1,128)} %param.12) | copy-start | bytes 112
  11.9 8.0 %copy-start.5 = (s32[1,32]{1,0:T(1,128)S(1)}, s32[1,32]{1,0:T(1,128)}, u32[]{:S(2)}) copy-start(s32[1,32]{1,0:T(1,128)} %param.13) | copy-start | bytes 388
  13.3 77.9 %all-to-all-start = ((bf16[3,128,16,128]{1,3,0,2:T(8,128)(2,1)}), bf16[3,128,16,128]{1,3,0,2:T(8,128)(2,1)S(1)}, u32[]{:S(2)}, u32[]{:S(2)}) async-start(bf16[3,128,16,128]{1,3,0,2:T(8,128)(2,1)} %copy.120), calls=%async_computation | async-start | bytes 3145728 | tf_op jit(solution)/shard_map/all_to_all | solution.py:82
  19.6 161.0 %all-reduce.2.cloned.1.call-start = ((), (), s32[]{:S(2)}) async-start(), calls=%async_computation.4 | async-start | bytes 4194304 | tf_op jit(solution)/shard_map/psum | solution.py:107
  92.9 7.2 %copy-start = (bf16[256,2048]{1,0:T(8,128)(2,1)S(1)}, bf16[256,2048]{1,0:T(8,128)(2,1)}, u32[]{:S(2)}) copy-start(bf16[256,2048]{1,0:T(8,128)(2,1)} %param.11) | copy-start | bytes 3145732
  103.5 4.5 %copy-start.1 = (bf16[1024,256]{0,1:T(8,128)(2,1)}, bf16[1024,256]{0,1:T(8,128)(2,1)S(1)}, u32[]{:S(2)}) copy-start(bf16[1024,256]{0,1:T(8,128)(2,1)S(1)} %fusion.27) | copy-start | bytes 1572868
  103.5 4.8 %copy-start.3 = (bf16[1,1024,2048]{2,1,0:T(8,128)(2,1)S(1)}, bf16[1,1024,2048]{2,1,0:T(8,128)(2,1)}, u32[]{:S(2)}) copy-start(bf16[1,1024,2048]{2,1,0:T(8,128)(2,1)} %all-gather.6.cloned.1.call-done) | copy-start | bytes 12582916
  111.9 5.6 %copy-start.2 = (bf16[1024,256]{0,1:T(8,128)(2,1)S(1)}, bf16[1024,256]{0,1:T(8,128)(2,1)}, u32[]{:S(2)}) copy-start(bf16[1024,256]{0,1:T(8,128)(2,1)} %copy-done.1) | copy-start | bytes 1572868
  111.9 152.5 %all-gather.4.cloned.1.call-start = ((), (), s32[]{:S(2)}) async-start(), calls=%async_computation.3 | async-start | bytes 9437184 | tf_op jit(solution)/shard_map/all_gather | solution.py:77
  113.8 18.8 %all-to-all-start.1 = ((bf16[1024,2,128]{2,1,0:T(2,128)(2,1)}), bf16[1024,2,128]{2,1,0:T(2,128)(2,1)S(1)}, u32[]{:S(2)}, u32[]{:S(2)}) async-start(bf16[1024,2,128]{2,1,0:T(2,128)(2,1)} %copy.127), calls=%async_computation.1 | async-start | bytes 1048576 | tf_op jit(solution)/shard_map/all_to_all | solution.py:95
  132.6 51.2 %all-to-all-start.2 = ((bf16[3,1024,2,128]{3,2,0,1:T(2,128)(2,1)}), bf16[3,1024,2,128]{3,2,0,1:T(2,128)(2,1)S(1)}, u32[]{:S(2)}, u32[]{:S(2)}) async-start(bf16[3,1024,2,128]{3,2,0,1:T(2,128)(2,1)} %copy.138), calls=%async_computation.2 | async-start | bytes 3145728 | tf_op jit(solution)/shard_map/all_to_all | solution.py:111
Sparse Core Ops, SparseCore 0:
  9.6 83.0 all-gather.5
  112.1 68.5 all-reduce.1
  182.4 82.0 all-gather.3

commit v2 on v1

--- a/solution.py
+++ b/solution.py
@@ -58,6 +58,18 @@
     )
 
 
+def dp_sum(values):
+    n_dp = lax.axis_size("dp")
+    if n_dp & (n_dp - 1):
+        return lax.psum(values, "dp")
+    step = 1
+    while step < n_dp:
+        pairs = [(i, i ^ step) for i in range(n_dp)]
+        values = values + lax.ppermute(values, "dp", pairs)
+        step *= 2
+    return values
+
+
 def shards(
     asking_vectors_matrix,
     matched_keys_matrix,
@@ -74,7 +86,6 @@
 
     grad_here = upstream_cotangent[0]
     grad_full = lax.all_gather(grad_here, "seq", axis=0, tiled=True)
-    w_full = lax.all_gather(w_out, "seq", axis=0, tiled=True)
 
     stacked = jnp.stack(
         [asking_vectors_matrix[0], matched_keys_matrix[0], carried_vectors_matrix[0]]
@@ -85,26 +96,28 @@
 
     allowed = tile_mask(panel_entry_offsets[0], rightward_panel_per_entry[0], nodes)
 
+    attended, expd, row_total = attend(q_heads, k_heads, v_heads, None, allowed)
+    att_flat = attended.reshape(nodes, local_heads * HD)
+
+    partial = jnp.dot(att_flat, w_out, preferred_element_type=jnp.float32)
+    layer_out = lax.psum_scatter(
+        partial.astype(jnp.bfloat16), "seq", scatter_dimension=0, tiled=True
+    )[None]
+
     g_flat = lax.dot_general(
         grad_full, w_out, (((1,), (1,)), ((), ())), preferred_element_type=jnp.float32
     ).astype(jnp.bfloat16)
     g_heads = g_flat.reshape(nodes, local_heads, HD)
 
-    attended, expd, row_total = attend(q_heads, k_heads, v_heads, g_heads, allowed)
-
-    returned = lax.all_to_all(attended, "seq", split_axis=0, concat_axis=1, tiled=True)
-    attended_nodes = returned.reshape(nodes_here, width)
-    layer_out = jnp.dot(attended_nodes, w_full, preferred_element_type=jnp.float32)
-    layer_out = layer_out.astype(jnp.bfloat16)[None]
-
-    att_blocks = attended.reshape(n_seq, nodes_here, local_heads * HD)
+    att_blocks = att_flat.reshape(n_seq, nodes_here, local_heads * HD)
     grad_blocks = grad_full.reshape(n_seq, nodes_here, width)
     terms = jnp.einsum(
         "bnf,bnk->bfk", att_blocks, grad_blocks, preferred_element_type=jnp.float32
     ).astype(jnp.bfloat16)
     w_rows = jnp.sum(terms.astype(jnp.float32), axis=0)
+    w_rows = dp_sum(w_rows)
     batch = asking_vectors_matrix.shape[0] * lax.axis_size("dp")
-    w_out_grad = lax.psum(w_rows, "dp") / batch
+    w_out_grad = w_rows / batch
 
     q_g, k_g, v_g = attend_back(q_heads, k_heads, v_heads, g_heads, attended, expd, row_total)
     grads = jnp.stack([q_g, k_g, v_g])

time: 277 us -> 227 us (0.82)
  waiting for transfers between devices: 189 us -> 128 us
  local copies, waits for them, and re-layouts: 19.5 us -> 29.9 us
    all_gather x1 -> x0, waiting for transfers between devices: 74.8 us -> none  [shards(): w_full = lax.all_gather(w_out, 'seq', axis=0, tiled=True)]
    psum x1 -> x0, waiting for transfers between devices: 43.1 us -> none  [shards(): w_out_grad = lax.psum(w_rows, 'dp') / batch]
    ppermute x0 -> x2, waiting for transfers between devices: none -> 35.8 us  [dp_sum(): values = values + lax.ppermute(values, 'dp', pairs)]
    all_to_all x1, waiting for transfers between devices: 0.01 us -> 22.7 us  [shards(): back = lax.all_to_all(grads, 'seq', split_axis=1, concat_axis=2, tiled=True)]
    slice x4, local copies, waits for them, and re-layouts: 2.3 us -> 9.21 us  [shards(): return (layer_out, back[0], back[1], back[2], w_out_grad)]
    all_to_all x1 -> x0, starting transfers between devices: 3.71 us -> none  [shards(): lax.all_to_all(attended, 'seq', split_axis=0, concat_axis=1, tiled=True)]
    dot_general x1, matrix products: 4.99 us -> 1.53 us  [attend_back(): jnp.einsum('hij,ihd->jhd', prob_low, g, preferred_element_type=jnp.float32)]
    squeeze x3, local copies, waits for them, and re-layouts: 3.54 us -> 6.65 us  [shards(): return (layer_out, back[0], back[1], back[2], w_out_grad)]
  transfers between devices with their start and end apart: 6 -> 6, of which waited for: 4 -> 4; matrix products, arithmetic and copies ran while one was open for 15% -> 26% of each run, Pallas kernels for 0% -> 0%
where the time goes in v2:
time: 227 us; the launch traced here: 226 us
  waiting for transfers between devices  128 us (56%)
  matrix products  33.4 us (15%)
  local copies, waits for them, and re-layouts  29.9 us (13%)
  between operations  14.3 us (6%)
  starting transfers between devices  14 us (6%)
  other arithmetic  6.13 us (3%)
    all_to_all x1, waiting for transfers between devices, shards(): lax.all_to_all(stacked, 'seq', split_axis=2, concat_axis=1, tiled=True)  69 us
    ppermute x2, waiting for transfers between devices, dp_sum(): values = values + lax.ppermute(values, 'dp', pairs)  35.8 us
    all_to_all x1, waiting for transfers between devices, shards(): back = lax.all_to_all(grads, 'seq', split_axis=1, concat_axis=2, tiled=True)  22.7 us
    slice x4, local copies, waits for them, and re-layouts, shards(): return (layer_out, back[0], back[1], back[2], w_out_grad)  9.21 us
    sub x1, matrix products, attend(): expd = jnp.where(allowed[None], jnp.exp(scores - row_max), 0.0)  7.3 us
    squeeze x3, local copies, waits for them, and re-layouts, shards(): return (layer_out, back[0], back[1], back[2], w_out_grad)  6.65 us
    all_to_all x1, starting transfers between devices, shards(): lax.all_to_all(stacked, 'seq', split_axis=2, concat_axis=1, tiled=True)  6.33 us
    dot_general x1, matrix products, shards(): jnp.einsum('bnf,bnk->bfk', att_blocks, grad_blocks, preferred_element_typ...  6.1 us
  transfers between devices with their start and end apart: 6, of which 4 were waited for; matrix products, arithmetic and copies ran while one was open for 26% of the time, Pallas kernels for 0%

profile of v2, /device:TPU:0, one launch (start us, length us, event | category | flops | bytes accessed | tf_op | source)
XLA Modules:
  0.0 225.9 jit_solution(9730390199058051251)
XLA Ops:
  7.2 0.0 all-gather.3.cloned.1.call-start
  7.2 0.7 all-gather.3.cloned.1.call-update
  7.9 1.3 copy.88
  9.2 1.3 copy.89
  10.6 1.3 copy.90
  11.9 0.2 pad_maximum_fusion
  12.1 1.2 copy.91
  13.3 6.3 %all-to-all-start = ((bf16[3,128,16,128]{1,3,0,2:T(8,128)(2,1)}), bf16[3,128,16,128]{1,3,0,2:T(8,128)(2,1)S(1)}, u32[]{:S(2)}, u32[]{:S(2)}) async-start(bf16[3,128,16,128]{1,3,0,2:T(8,128)(2,1)} %copy.91), calls=%async_computation | async-start | bytes 3145728 | tf_op jit(solution)/shard_map/all_to_all | solution.py:93
  19.6 0.0 reduce-scatter.2.cloned.1.call-start
  19.7 0.1 slice_bitcast_fusion
  19.8 0.1 convert_reduce_fusion.1
  19.9 0.3 convolution_compare_fusion
  20.1 0.1 copy.94
  20.2 0.3 broadcast_in_dim.38
  20.6 1.6 copy.125
  22.1 69.0 %all-to-all-done = bf16[3,128,16,128]{1,3,0,2:T(8,128)(2,1)S(1)} async-done(((bf16[3,128,16,128]{1,3,0,2:T(8,128)(2,1)}), bf16[3,128,16,128]{1,3,0,2:T(8,128)(2,1)S(1)}, u32[]{:S(2)}, u32[]{:S(2)}) %all-to-all-start) | async-done | bytes 1572896 | tf_op jit(solution)/shard_map/all_to_all | solution.py:93
  91.2 1.6 copy.92
  92.7 1.5 fusion.42
  94.3 0.3 copy.93
  94.6 0.2 squeeze.22
  94.9 7.3 %fusion.43 = (f32[2,1024]{1,0:T(2,128)S(1)}, f32[2,1024,1024]{1,2,0:T(8,128)}) fusion(pred[1024,1024]{0,1:T(8,128)(4,1)} %bitcast.85, bf16[1024,2,128]{2,0,1:T(8,128)(2,1)S(1)} %bitcast.83, bf16[1024,2,128]{2,0,1:T(8,128)(2,1)S(1)} %bitcast.80), kind=kOutput, calls=%fused_computation.47 | convolution fusion | flops 1086325760 | bytes 10493952 | tf_op jit(solution)/shard_map/sub | solution.py:33
  102.2 3.5 %fusion.26 = bf16[1024,256]{0,1:T(8,128)(2,1)S(1)} fusion(bf16[256,2048]{1,0:T(8,128)(2,1)S(1)} %copy-done, bf16[1,1024,2048]{2,1,0:T(8,128)(2,1)} %all-gather.3.cloned.1.call-done), kind=kOutput, calls=%fused_computation.28 | convolution fusion | flops 1074003968 | bytes 5767168 | tf_op jit(solution)/shard_map/dot_general | solution.py:107
  105.7 4.4 %multiply_reduce_fusion = (f32[1024,2]{0,1:T(2,128)S(1)}, bf16[1024,2,128]{0,2,1:T(8,128)(2,1)S(1)}) fusion(bf16[1024,256]{0,1:T(8,128)(2,1)S(1)} %fusion.26, f32[1024,2]{0,1:T(2,128)S(1)} %bitcast.89, bf16[1024,2,128]{0,2,1:T(8,128)(2,1)S(1)} %squeeze.22, f32[2,1024,1024]{1,2,0:T(8,128)} %get-tuple-element.12), kind=kOutput, calls=%fused_computation.33 | convolution fusion | flops 540538880 | bytes 9977856 | tf_op jit(solution)/shard_map/hij,jhd->ihd/dot_general | solution.py:35
  110.1 3.3 %convolution_convert_fusion = bf16[1024,2048]{1,0:T(8,128)(2,1)} fusion(bf16[1024,256]{0,1:T(8,128)(2,1)S(1)} %bitcast.76, bf16[256,2048]{1,0:T(8,128)(2,1)S(1)} %copy-done), kind=kOutput, calls=%fused_computation.18 | convolution fusion | flops 1075838976 | bytes 5767168 | tf_op jit(solution)/shard_map/dot_general | solution.py:102
  113.3 0.0 reduce-scatter.2.cloned.1.call-update
  113.4 0.1 copy.121
  113.5 6.1 %convert_reduce_fusion = f32[256,2048]{1,0:T(8,128)} fusion(bf16[8,128,2048]{2,1,0:T(8,128)(2,1)} %bitcast.91, bf16[8,128,256]{1,0,2:T(8,128)(2,1)S(1)} %bitcast.88), kind=kOutput, calls=%fused_computation.1 | convolution fusion | flops 1085800448 | bytes 6815744 | tf_op jit(solution)/shard_map/bnf,bnk->bfk/dot_general | solution.py:114
  119.6 1.5 collective-permute-start
  121.1 4.7 %multiply_convert_fusion = bf16[2,1024,1024]{1,2,0:T(8,128)(2,1)S(1)} fusion(f32[2,1024]{1,0:T(2,128)S(1)} %bitcast.90, f32[2,1024,1024]{1,2,0:T(8,128)} %get-tuple-element.12, f32[2,1024]{1,0:T(2,128)S(1)} %get-tuple-element.11, bf16[1024,2,128]{0,2,1:T(8,128)(2,1)S(1)} %bitcast.86, bf16[1024,2,128]{0,2,1:T(8,128)(2,1)S(1)} %squeeze.22), kind=kOutput, calls=%fused_computation.2 | convolution fusion | flops 547356672 | bytes 13647872 | tf_op jit(solution)/shard_map/ihd,jhd->hij/dot_general | solution.py:48
  125.8 0.8 fusion.29
  126.6 1.5 fusion.30
  128.2 1.5 fusion.31
  129.8 0.2 pad_maximum_fusion.1
  129.9 3.0 %copy.106 = bf16[3,1024,2,128]{3,2,0,1:T(2,128)(2,1)} copy(bf16[3,1024,2,128]{1,3,2,0:T(8,128)(2,1)S(1)} %pad_maximum_fusion.1) | data formatting | bytes 3145728 | tf_op jit(solution)/shard_map/stack | solution.py:123
  132.9 4.5 %all-to-all-start.1 = ((bf16[3,1024,2,128]{3,2,0,1:T(2,128)(2,1)}), bf16[3,1024,2,128]{3,2,0,1:T(2,128)(2,1)}, u32[]{:S(2)}, u32[]{:S(2)}) async-start(bf16[3,1024,2,128]{3,2,0,1:T(2,128)(2,1)} %copy.106), calls=%async_computation.2 | async-start | bytes 3145728 | tf_op jit(solution)/shard_map/all_to_all | solution.py:124
  137.4 29.6 %collective-permute-done = f32[256,2048]{1,0:T(8,128)} collective-permute-done((f32[256,2048]{1,0:T(8,128)}, f32[256,2048]{1,0:T(8,128)}, u32[]{:S(2)}, u32[]{:S(2)}) %collective-permute-start) | collective-permute-done | bytes 2097184 | tf_op jit(solution)/shard_map/ppermute | solution.py:68
  167.0 2.5 %add.8 = f32[256,2048]{1,0:T(8,128)S(1)} add(f32[256,2048]{1,0:T(8,128)} %convert_reduce_fusion, f32[256,2048]{1,0:T(8,128)} %collective-permute-done) | non-fusion elementwise | flops 524288 | bytes 6291456 | tf_op jit(solution)/shard_map/add | solution.py:68
  169.5 1.6 collective-permute-start.1
  171.1 22.7 %all-to-all-done.1 = bf16[3,1024,2,128]{3,2,0,1:T(2,128)(2,1)} async-done(((bf16[3,1024,2,128]{3,2,0,1:T(2,128)(2,1)}), bf16[3,1024,2,128]{3,2,0,1:T(2,128)(2,1)}, u32[]{:S(2)}, u32[]{:S(2)}) %all-to-all-start.1) | async-done | bytes 1572896 | tf_op jit(solution)/shard_map/all_to_all | solution.py:124
  193.8 3.7 %fusion.41 = (bf16[1,128,8,2,128]{4,3,0,1,2:T(2,128)(2,1)}, bf16[1,128,8,2,128]{4,3,0,1,2:T(2,128)(2,1)}, bf16[1,128,8,2,128]{4,3,0,1,2:T(2,128)(2,1)S(1)}) fusion(bf16[3,128,8,2,128]{4,3,0,1,2:T(2,128)(2,1)} %bitcast.22), kind=kLoop, calls=%fused_computation.45 | loop fusion | bytes 3145728 | tf_op jit(solution)/shard_map/slice | solution.py:126
  197.5 1.2 copy.107
  198.6 2.2 squeeze.26
  200.8 2.2 copy.108
  203.0 2.2 squeeze.27
  205.2 2.2 copy.109
  207.4 2.2 squeeze.28
  209.7 6.2 %collective-permute-done.1 = f32[256,2048]{1,0:T(8,128)} collective-permute-done((f32[256,2048]{1,0:T(8,128)S(1)}, f32[256,2048]{1,0:T(8,128)}, u32[]{:S(2)}, u32[]{:S(2)}) %collective-permute-start.1) | collective-permute-done | bytes 2097184 | tf_op jit(solution)/shard_map/ppermute | solution.py:68
  215.9 3.2 %add_multiply_fusion = f32[256,2048]{1,0:T(8,128)} fusion(f32[256,2048]{1,0:T(8,128)S(1)} %add.8, f32[256,2048]{1,0:T(8,128)} %collective-permute-done.1), kind=kLoop, calls=%fused_computation.19 | loop fusion | flops 1048576 | bytes 6291456 | tf_op jit(solution)/shard_map/div | solution.py:120
  (19 shorter events, 0.1 us)
Async XLA Ops:
  7.2 95.0 %copy-start = (bf16[256,2048]{1,0:T(8,128)(2,1)S(1)}, bf16[256,2048]{1,0:T(8,128)(2,1)}, u32[]{:S(2)}) copy-start(bf16[256,2048]{1,0:T(8,128)(2,1)} %param.11) | copy-start | bytes 3145732
  7.2 95.0 %all-gather.3.cloned.1.call-start = ((), (), s32[]{:S(2)}) async-start(), calls=%async_computation.4 | async-start | bytes 4718592 | tf_op jit(solution)/shard_map/all_gather | solution.py:88
  11.9 7.8 %copy-start.3 = (s32[1,9]{1,0:T(1,128)S(1)}, s32[1,9]{1,0:T(1,128)}, u32[]{:S(2)}) copy-start(s32[1,9]{1,0:T(1,128)} %param.12) | copy-start | bytes 112
  11.9 8.0 %copy-start.4 = (s32[1,32]{1,0:T(1,128)S(1)}, s32[1,32]{1,0:T(1,128)}, u32[]{:S(2)}) copy-start(s32[1,32]{1,0:T(1,128)} %param.13) | copy-start | bytes 388
  13.3 77.9 %all-to-all-start = ((bf16[3,128,16,128]{1,3,0,2:T(8,128)(2,1)}), bf16[3,128,16,128]{1,3,0,2:T(8,128)(2,1)S(1)}, u32[]{:S(2)}, u32[]{:S(2)}) async-start(bf16[3,128,16,128]{1,3,0,2:T(8,128)(2,1)} %copy.91), calls=%async_computation | async-start | bytes 3145728 | tf_op jit(solution)/shard_map/all_to_all | solution.py:93
  19.6 199.4 %reduce-scatter.2.cloned.1.call-start = ((), (), s32[]{:S(2)}) async-start(), calls=%async_computation.3 | async-start | bytes 4718592 | tf_op jit(solution)/shard_map/reduce_scatter | solution.py:103
  105.6 4.4 %copy-start.1 = (bf16[1024,256]{0,1:T(8,128)(2,1)}, bf16[1024,256]{0,1:T(8,128)(2,1)S(1)}, u32[]{:S(2)}) copy-start(bf16[1024,256]{0,1:T(8,128)(2,1)S(1)} %fusion.26) | copy-start | bytes 1572868
  113.5 7.6 %copy-start.2 = (bf16[1024,256]{0,1:T(8,128)(2,1)S(1)}, bf16[1024,256]{0,1:T(8,128)(2,1)}, u32[]{:S(2)}) copy-start(bf16[1024,256]{0,1:T(8,128)(2,1)} %copy-done.1) | copy-start | bytes 1572868
  113.5 14.7 %slice-start = ((s8[8388608]{0:T(1024)(128)(4,1)}), s8[4194304]{0:T(1024)(128)(4,1)S(1)}, s32[]{:S(2)}) async-start(s8[8388608]{0:T(1024)(128)(4,1)} %bitcast.74), calls=%async_computation.5 | async-start | bytes 8388608
  119.6 47.4 %collective-permute-start = (f32[256,2048]{1,0:T(8,128)}, f32[256,2048]{1,0:T(8,128)}, u32[]{:S(2)}, u32[]{:S(2)}) collective-permute-start(f32[256,2048]{1,0:T(8,128)} %convert_reduce_fusion), channel_id=1, source_target_pairs={{0,8},{8,0},{16,24},{24,16},{1,9},{9,1},{17,25},{25,17},{2,10},{10... | collective-permute-start | bytes 6291464 | tf_op jit(solution)/shard_map/ppermute | solution.py:68
  121.1 7.1 %slice-start.1 = ((s8[8388608]{0:T(1024)(128)(4,1)}), s8[4194304]{0:T(1024)(128)(4,1)S(1)}, s32[]{:S(2)}) async-start(s8[8388608]{0:T(1024)(128)(4,1)} %bitcast.74), calls=%async_computation.6 | async-start | bytes 8388608
  132.9 60.9 %all-to-all-start.1 = ((bf16[3,1024,2,128]{3,2,0,1:T(2,128)(2,1)}), bf16[3,1024,2,128]{3,2,0,1:T(2,128)(2,1)}, u32[]{:S(2)}, u32[]{:S(2)}) async-start(bf16[3,1024,2,128]{3,2,0,1:T(2,128)(2,1)} %copy.106), calls=%async_computation.2 | async-start | bytes 3145728 | tf_op jit(solution)/shard_map/all_to_all | solution.py:124
  169.5 46.4 %collective-permute-start.1 = (f32[256,2048]{1,0:T(8,128)S(1)}, f32[256,2048]{1,0:T(8,128)}, u32[]{:S(2)}, u32[]{:S(2)}) collective-permute-start(f32[256,2048]{1,0:T(8,128)S(1)} %add.8), channel_id=1, source_target_pairs={{0,16},{8,24},{16,0},{24,8},{1,17},{9,25},{17,1},{25,9},{2,18},{10... | collective-permute-start | bytes 6291464 | tf_op jit(solution)/shard_map/ppermute | solution.py:68
Sparse Core Ops, SparseCore 0:
  9.6 83.0 all-gather.2
  113.5 65.6 reduce-scatter.1

commit v3 on v2

--- a/solution.py
+++ b/solution.py
@@ -70,6 +70,44 @@
     return values
 
 
+def seq_reduce_scatter(partial):
+    n = lax.axis_size("seq")
+    rows = partial.shape[0] // n
+    if n % 2:
+        return lax.psum_scatter(partial, "seq", scatter_dimension=0, tiled=True)
+    chips = n // 2
+    s = lax.axis_index("seq")
+    core = s % 2
+    z = s // 2
+    halves = partial.reshape(chips, 2, rows, partial.shape[1])
+    mine = jnp.where(core == 0, halves[:, 0], halves[:, 1])
+    other = jnp.where(core == 0, halves[:, 1], halves[:, 0])
+    got = lax.ppermute(other.astype(jnp.bfloat16), "seq", [(i, i ^ 1) for i in range(n)])
+    chip = mine + got.astype(jnp.float32)
+    own = lax.dynamic_index_in_dim(chip, z, 0, keepdims=False)
+    right = [(i, i + 2) for i in range(n - 2)]
+    left = [(i, i - 2) for i in range(2, n)]
+    recv_r = None
+    recv_l = None
+    for step in range(1, chips):
+        d_r = jnp.clip(z + chips - step, 0, chips - 1)
+        d_l = jnp.clip(z - chips + step, 0, chips - 1)
+        acc_r = lax.dynamic_index_in_dim(chip, d_r, 0, keepdims=False)
+        acc_l = lax.dynamic_index_in_dim(chip, d_l, 0, keepdims=False)
+        if recv_r is not None:
+            ok_r = (step >= z + 1) & (z >= 1)
+            ok_l = (step >= chips - z) & (z <= chips - 2)
+            acc_r = acc_r + jnp.where(ok_r, recv_r.astype(jnp.float32), 0.0)
+            acc_l = acc_l + jnp.where(ok_l, recv_l.astype(jnp.float32), 0.0)
+        recv_r = lax.ppermute(acc_r.astype(jnp.bfloat16), "seq", right)
+        recv_l = lax.ppermute(acc_l.astype(jnp.bfloat16), "seq", left)
+    total = own
+    if recv_r is not None:
+        total = total + jnp.where(z >= 1, recv_r.astype(jnp.float32), 0.0)
+        total = total + jnp.where(z <= chips - 2, recv_l.astype(jnp.float32), 0.0)
+    return total
+
+
 def shards(
     asking_vectors_matrix,
     matched_keys_matrix,
@@ -100,9 +138,7 @@
     att_flat = attended.reshape(nodes, local_heads * HD)
 
     partial = jnp.dot(att_flat, w_out, preferred_element_type=jnp.float32)
-    layer_out = lax.psum_scatter(
-        partial.astype(jnp.bfloat16), "seq", scatter_dimension=0, tiled=True
-    )[None]
+    layer_out = seq_reduce_scatter(partial).astype(jnp.bfloat16)[None]
 
     g_flat = lax.dot_general(
         grad_full, w_out, (((1,), (1,)), ((), ())), preferred_element_type=jnp.float32

time: 227 us -> 247 us (1.088)
  starting transfers between devices: 14 us -> 37.4 us
  other arithmetic: 6.13 us -> 21.9 us
  waiting for transfers between devices: 128 us -> 114 us
  matrix products: 33.4 us -> 28.3 us
    ppermute x0 -> x7, starting transfers between devices: none -> 23.7 us  [the longest x3 19.8 us: seq_reduce_scatter(): recv_r = lax.ppermute(acc_r.astype(jnp.bfloat16), 'seq', right)]
    all_to_all x1, waiting for transfers between devices: 22.7 us -> 0.01 us  [shards(): back = lax.all_to_all(grads, 'seq', split_axis=1, concat_axis=2, tiled=True)]
    ppermute x0 -> x7, waiting for transfers between devices: none -> 21.5 us  [the longest x3 12.2 us: seq_reduce_scatter(): recv_r = lax.ppermute(acc_r.astype(jnp.bfloat16), 'seq', right)]
    ppermute x2, waiting for transfers between devices: 35.8 us -> 22.7 us  [dp_sum(): values = values + lax.ppermute(values, 'dp', pairs)]
    convert_element_type x0 -> x4, other arithmetic: none -> 7.91 us  [the longest x2 4.62 us: seq_reduce_scatter(): recv_r = lax.ppermute(acc_r.astype(jnp.bfloat16), 'seq', right)]
    add x0 -> x1, other arithmetic: none -> 5.57 us  [seq_reduce_scatter(): chip = mine + got.astype(jnp.float32)]
    unnamed x19 -> x33, local copies, waits for them, and re-layouts: 5.65 us -> 11 us
    dot_general x1, matrix products: 1.53 us -> 5.93 us  [attend_back(): jnp.einsum('hij,ihd->jhd', prob_low, g, preferred_element_type=jnp.float32)]
  transfers between devices with their start and end apart: 6 -> 12, of which waited for: 4 -> 8; matrix products, arithmetic and copies ran while one was open for 26% -> 23% of each run, Pallas kernels for 0% -> 0%
where the time goes in v3:
time: 247 us; the launch traced here: 246 us
  waiting for transfers between devices  114 us (46%)
  starting transfers between devices  37.4 us (15%)
  local copies, waits for them, and re-layouts  29.9 us (12%)
  matrix products  28.3 us (11%)
  other arithmetic  21.9 us (9%)
  between operations  14.4 us (6%)
    all_to_all x1, waiting for transfers between devices, shards(): lax.all_to_all(stacked, 'seq', split_axis=2, concat_axis=1, tiled=True)  69.1 us
    ppermute x2, waiting for transfers between devices, dp_sum(): values = values + lax.ppermute(values, 'dp', pairs)  22.7 us
    ppermute x3, starting transfers between devices, seq_reduce_scatter(): recv_r = lax.ppermute(acc_r.astype(jnp.bfloat16), 'seq', right)  19.8 us
    ppermute x3, waiting for transfers between devices, seq_reduce_scatter(): recv_r = lax.ppermute(acc_r.astype(jnp.bfloat16), 'seq', right)  12.2 us
    unnamed x33, local copies, waits for them, and re-layouts  11 us
    ppermute x3, waiting for transfers between devices, seq_reduce_scatter(): recv_l = lax.ppermute(acc_l.astype(jnp.bfloat16), 'seq', left)  9.25 us
    sub x1, matrix products, attend(): expd = jnp.where(allowed[None], jnp.exp(scores - row_max), 0.0)  7.07 us
    all_to_all x1, starting transfers between devices, shards(): lax.all_to_all(stacked, 'seq', split_axis=2, concat_axis=1, tiled=True)  6.33 us
  transfers between devices with their start and end apart: 12, of which 8 were waited for; matrix products, arithmetic and copies ran while one was open for 23% of the time, Pallas kernels for 0%

profile of v3, /device:TPU:0, one launch (start us, length us, event | category | flops | bytes accessed | tf_op | source)
XLA Modules:
  0.0 245.9 jit_solution(16097202645838312487)
XLA Ops:
  7.9 1.3 copy.108
  9.2 1.3 copy.109
  10.6 1.3 copy.110
  12.1 1.2 copy.111
  13.3 6.3 %all-to-all-start = ((bf16[3,128,16,128]{1,3,0,2:T(8,128)(2,1)}), bf16[3,128,16,128]{1,3,0,2:T(8,128)(2,1)S(1)}, u32[]{:S(2)}, u32[]{:S(2)}) async-start(bf16[3,128,16,128]{1,3,0,2:T(8,128)(2,1)} %copy.111), calls=%async_computation | async-start | bytes 3145728 | tf_op jit(solution)/shard_map/all_to_all | solution.py:131
  20.5 1.5 copy.154
  22.0 69.1 %all-to-all-done = bf16[3,128,16,128]{1,3,0,2:T(8,128)(2,1)S(1)} async-done(((bf16[3,128,16,128]{1,3,0,2:T(8,128)(2,1)}), bf16[3,128,16,128]{1,3,0,2:T(8,128)(2,1)S(1)}, u32[]{:S(2)}, u32[]{:S(2)}) %all-to-all-start) | async-done | bytes 1572896 | tf_op jit(solution)/shard_map/all_to_all | solution.py:131
  91.2 1.6 copy.112
  92.7 1.5 fusion.57
  94.9 7.1 %fusion.58 = (f32[2,1024]{1,0:T(2,128)S(1)}, f32[2,1024,1024]{1,2,0:T(8,128)}) fusion(pred[1024,1024]{0,1:T(8,128)(4,1)} %bitcast.139, bf16[1024,2,128]{2,0,1:T(8,128)(2,1)S(1)} %bitcast.137, bf16[1024,2,128]{2,0,1:T(8,128)(2,1)S(1)} %bitcast.134), kind=kOutput, calls=%fused_computation.70 | convolution fusion | flops 1086325760 | bytes 10493952 | tf_op jit(solution)/shard_map/sub | solution.py:33
  102.0 3.6 %fusion.29 = bf16[1024,256]{0,1:T(8,128)(2,1)S(1)} fusion(bf16[256,2048]{1,0:T(8,128)(2,1)S(1)} %copy-done, bf16[1,1024,2048]{2,1,0:T(8,128)(2,1)} %all-gather.3.cloned.1.call-done), kind=kOutput, calls=%fused_computation.32 | convolution fusion | flops 1074003968 | bytes 5767168 | tf_op jit(solution)/shard_map/dot_general | solution.py:143
  105.6 5.9 %fusion.34 = bf16[1,1024,2,128]{1,3,2,0:T(8,128)(2,1)} fusion(bf16[1024,2,128]{0,2,1:T(8,128)(2,1)S(1)} %bitcast.140, f32[2,1024,1024]{1,2,0:T(8,128)} %get-tuple-element.16, f32[2,1024]{1,0:T(2,128)S(1)} %get-tuple-element.15), kind=kOutput, calls=%fused_computation.35 | convolution fusion | flops 541327360 | bytes 9445376 | tf_op jit(solution)/shard_map/hij,ihd->jhd/dot_general | solution.py:47
  111.6 0.9 multiply_reduce_fusion
  112.5 1.2 dot_general.35
  113.8 2.5 %fusion.37 = f32[4,2,128,2048]{3,2,1,0:T(8,128)S(1)} fusion(bf16[256,2048]{1,0:T(8,128)(2,1)S(1)} %copy-done, bf16[4,2,128,256]{2,1,0,3:T(2,128)(2,1)} %dot_general.35), kind=kOutput, calls=%fused_computation.37 | convolution fusion | flops 1073741824 | bytes 9961472 | tf_op jit(solution)/shard_map/dot_general | solution.py:140
  116.3 3.3 %copy-done.2 = f32[4,2,128,2048]{3,2,1,0:T(8,128)} copy-done((f32[4,2,128,2048]{3,2,1,0:T(8,128)}, f32[4,2,128,2048]{3,2,1,0:T(8,128)S(1)}, u32[]{:S(2)}) %copy-start.2) | copy-done | bytes 8388632
  119.5 1.7 fusion.16
  121.2 3.6 %convert_reduce_fusion = f32[256,2048]{1,0:T(8,128)} fusion(bf16[8,128,2048]{2,1,0:T(8,128)(2,1)S(1)} %bitcast.145, bf16[8,128,256]{1,0,2:T(8,128)(2,1)S(1)} %bitcast.142), kind=kOutput, calls=%fused_computation.1 | convolution fusion | flops 1085800448 | bytes 6815744 | tf_op jit(solution)/shard_map/bnf,bnk->bfk/dot_general | solution.py:150
  124.9 1.5 collective-permute-start.7
  126.4 2.0 multiply_convert_fusion
  128.4 1.5 fusion.33
  131.2 3.0 %copy.131 = bf16[3,1024,2,128]{3,2,0,1:T(2,128)(2,1)} copy(bf16[3,1024,2,128]{1,3,2,0:T(8,128)(2,1)S(1)} %pad_maximum_fusion.1) | data formatting | bytes 3145728 | tf_op jit(solution)/shard_map/stack | solution.py:159
  134.2 4.3 %all-to-all-start.1 = ((bf16[3,1024,2,128]{3,2,0,1:T(2,128)(2,1)}), bf16[3,1024,2,128]{3,2,0,1:T(2,128)(2,1)}, u32[]{:S(2)}, u32[]{:S(2)}) async-start(bf16[3,1024,2,128]{3,2,0,1:T(2,128)(2,1)} %copy.131), calls=%async_computation.1 | async-start | bytes 3145728 | tf_op jit(solution)/shard_map/all_to_all | solution.py:160
  138.5 5.6 %fusion.6 = f32[4,128,2048]{2,1,0:T(8,128)S(1)} fusion(bf16[4,128,2048]{2,1,0:T(8,128)(2,1)} %collective-permute-done, f32[4,2,128,2048]{3,2,1,0:T(8,128)} %copy-done.2, pred[]{:T(512)S(6)} %eq.34), kind=kLoop, calls=%fused_computation.9 | loop fusion | flops 3145728 | bytes 14680065 | tf_op jit(solution)/shard_map/add | solution.py:86
  144.1 1.9 copy-done.3
  146.2 4.6 %collective-permute-start.1 = (bf16[128,2048]{1,0:T(8,128)(2,1)S(1)}, bf16[128,2048]{1,0:T(8,128)(2,1)}, u32[]{:S(2)}, u32[]{:S(2)}) collective-permute-start(bf16[128,2048]{1,0:T(8,128)(2,1)S(1)} %get-tuple-element.7), channel_id=1, source_target_pairs={{0,2},{1,3},{2,4},{3,5},{4,6},{5,7},{8,10},{9,11},{10,12},{11,13},... | collective-permute-start | bytes 1572872 | tf_op jit(solution)/shard_map/ppermute | solution.py:102
  150.8 22.4 %collective-permute-done.7 = f32[256,2048]{1,0:T(8,128)} collective-permute-done((f32[256,2048]{1,0:T(8,128)}, f32[256,2048]{1,0:T(8,128)}, u32[]{:S(2)}, u32[]{:S(2)}) %collective-permute-start.7) | collective-permute-done | bytes 2097184 | tf_op jit(solution)/shard_map/ppermute | solution.py:68
  173.2 2.5 %add.84 = f32[256,2048]{1,0:T(8,128)S(1)} add(f32[256,2048]{1,0:T(8,128)} %convert_reduce_fusion, f32[256,2048]{1,0:T(8,128)} %collective-permute-done.7) | non-fusion elementwise | flops 524288 | bytes 6291456 | tf_op jit(solution)/shard_map/add | solution.py:68
  175.7 1.6 collective-permute-start.8
  177.3 1.3 collective-permute-start.4
  178.6 1.5 fusion.41
  180.1 10.1 %collective-permute-start.2 = (bf16[128,2048]{1,0:T(8,128)(2,1)S(1)}, bf16[128,2048]{1,0:T(8,128)(2,1)}, u32[]{:S(2)}, u32[]{:S(2)}) collective-permute-start(bf16[128,2048]{1,0:T(8,128)(2,1)S(1)} %fusion.41), channel_id=1, source_target_pairs={{0,2},{1,3},{2,4},{3,5},{4,6},{5,7},{8,10},{9,11},{10,12},{11,13},... | collective-permute-start | bytes 1572872 | tf_op jit(solution)/shard_map/ppermute | solution.py:102
  190.2 2.3 collective-permute-done.4
  192.5 8.2 %collective-permute-done.2 = bf16[128,2048]{1,0:T(8,128)(2,1)} collective-permute-done((bf16[128,2048]{1,0:T(8,128)(2,1)S(1)}, bf16[128,2048]{1,0:T(8,128)(2,1)}, u32[]{:S(2)}, u32[]{:S(2)}) %collective-permute-start.2) | collective-permute-done | bytes 524320 | tf_op jit(solution)/shard_map/ppermute | solution.py:102
  200.8 3.1 %fusion.42 = (bf16[128,2048]{1,0:T(8,128)(2,1)}, bf16[128,2048]{1,0:T(8,128)(2,1)}) fusion(bf16[128,2048]{1,0:T(8,128)(2,1)} %collective-permute-done.2, f32[4,128,2048]{2,1,0:T(8,128)} %copy-done.3, s32[]{:T(128)S(6)} %min.19, pred[]{:T(512)S(6)} %and.25, bf16[128,2048]{1,0:T(8,128)(2,1)} %collective-permute-done.4, pred[]{:T(512)S(6)} %and.28, s32[]{:T(128)S(6)} %min.23), kind=kLoop, calls=%fused_computation.46 | loop fusion | flops 2097152 | bytes 4194314 | tf_op jit(solution)/shard_map/convert_element_type | solution.py:102
  203.9 1.3 collective-permute-start.5
  205.2 3.5 %fusion.56 = (bf16[1,128,8,2,128]{4,3,0,1,2:T(2,128)(2,1)S(1)}, bf16[1,128,8,2,128]{4,3,0,1,2:T(2,128)(2,1)}, bf16[1,128,8,2,128]{4,3,0,1,2:T(2,128)(2,1)S(1)}) fusion(bf16[3,128,8,2,128]{4,3,0,1,2:T(2,128)(2,1)} %bitcast.35), kind=kLoop, calls=%fused_computation.68 | loop fusion | bytes 3145728 | tf_op jit(solution)/shard_map/slice | solution.py:162
  209.0 1.2 squeeze.55
  210.2 1.4 copy.133
  211.6 1.2 squeeze.54
  213.1 1.2 squeeze.53
  214.3 5.1 %collective-permute-start.3 = (bf16[128,2048]{1,0:T(8,128)(2,1)}, bf16[128,2048]{1,0:T(8,128)(2,1)S(1)}, u32[]{:S(2)}, u32[]{:S(2)}) collective-permute-start(bf16[128,2048]{1,0:T(8,128)(2,1)} %get-tuple-element.5), channel_id=1, source_target_pairs={{0,2},{1,3},{2,4},{3,5},{4,6},{5,7},{8,10},{9,11},{10,12},{11,13},... | collective-permute-start | bytes 1572872 | tf_op jit(solution)/shard_map/ppermute | solution.py:102
  220.0 1.6 fusion.40
  221.6 1.3 collective-permute-start.6
  223.1 3.2 %add_multiply_fusion = f32[256,2048]{1,0:T(8,128)} fusion(f32[256,2048]{1,0:T(8,128)S(1)} %add.84, f32[256,2048]{1,0:T(8,128)} %collective-permute-done.8), kind=kLoop, calls=%fused_computation.23 | loop fusion | flops 1048576 | bytes 6291456 | tf_op jit(solution)/shard_map/div | solution.py:156
  226.3 4.0 %collective-permute-done.3 = bf16[128,2048]{1,0:T(8,128)(2,1)S(1)} collective-permute-done((bf16[128,2048]{1,0:T(8,128)(2,1)}, bf16[128,2048]{1,0:T(8,128)(2,1)S(1)}, u32[]{:S(2)}, u32[]{:S(2)}) %collective-permute-start.3) | collective-permute-done | bytes 524320 | tf_op jit(solution)/shard_map/ppermute | solution.py:102
  230.3 6.4 %collective-permute-done.6 = bf16[128,2048]{1,0:T(8,128)(2,1)S(1)} collective-permute-done((bf16[128,2048]{1,0:T(8,128)(2,1)S(1)}, bf16[128,2048]{1,0:T(8,128)(2,1)S(1)}, u32[]{:S(2)}, u32[]{:S(2)}) %collective-permute-start.6) | collective-permute-done | bytes 524320 | tf_op jit(solution)/shard_map/ppermute | solution.py:103
  236.7 2.3 fusion.49
  (53 shorter events, 5.3 us)
Async XLA Ops:
  7.2 94.8 %copy-start = (bf16[256,2048]{1,0:T(8,128)(2,1)S(1)}, bf16[256,2048]{1,0:T(8,128)(2,1)}, u32[]{:S(2)}) copy-start(bf16[256,2048]{1,0:T(8,128)(2,1)} %param.11) | copy-start | bytes 3145732
  7.2 94.8 %all-gather.3.cloned.1.call-start = ((), (), s32[]{:S(2)}) async-start(), calls=%async_computation.2 | async-start | bytes 4718592 | tf_op jit(solution)/shard_map/all_gather | solution.py:126
  11.9 7.8 %copy-start.8 = (s32[1,9]{1,0:T(1,128)S(1)}, s32[1,9]{1,0:T(1,128)}, u32[]{:S(2)}) copy-start(s32[1,9]{1,0:T(1,128)} %param.12) | copy-start | bytes 112
  11.9 7.9 %copy-start.9 = (s32[1,32]{1,0:T(1,128)S(1)}, s32[1,32]{1,0:T(1,128)}, u32[]{:S(2)}) copy-start(s32[1,32]{1,0:T(1,128)} %param.13) | copy-start | bytes 388
  13.3 77.9 %all-to-all-start = ((bf16[3,128,16,128]{1,3,0,2:T(8,128)(2,1)}), bf16[3,128,16,128]{1,3,0,2:T(8,128)(2,1)S(1)}, u32[]{:S(2)}, u32[]{:S(2)}) async-start(bf16[3,128,16,128]{1,3,0,2:T(8,128)(2,1)} %copy.111), calls=%async_computation | async-start | bytes 3145728 | tf_op jit(solution)/shard_map/all_to_all | solution.py:131
  102.0 9.6 %slice-start = ((s8[8388608]{0:T(1024)(128)(4,1)}), s8[4194304]{0:T(1024)(128)(4,1)S(1)}, s32[]{:S(2)}) async-start(s8[8388608]{0:T(1024)(128)(4,1)} %bitcast.127), calls=%async_computation.3 | async-start | bytes 8388608
  105.6 6.0 %copy-start.4 = (bf16[1024,256]{0,1:T(8,128)(2,1)}, bf16[1024,256]{0,1:T(8,128)(2,1)S(1)}, u32[]{:S(2)}) copy-start(bf16[1024,256]{0,1:T(8,128)(2,1)S(1)} %fusion.29) | copy-start | bytes 1572868
  105.6 6.0 %slice-start.1 = ((s8[8388608]{0:T(1024)(128)(4,1)}), s8[4194304]{0:T(1024)(128)(4,1)S(1)}, s32[]{:S(2)}) async-start(s8[8388608]{0:T(1024)(128)(4,1)} %bitcast.127), calls=%async_computation.4 | async-start | bytes 8388608
  113.7 7.5 %copy-start.7 = (bf16[1,1024,2048]{2,1,0:T(8,128)(2,1)S(1)}, bf16[1,1024,2048]{2,1,0:T(8,128)(2,1)}, u32[]{:S(2)}) copy-start(bf16[1,1024,2048]{2,1,0:T(8,128)(2,1)} %all-gather.3.cloned.1.call-done) | copy-start | bytes 12582916
  116.2 3.3 %copy-start.2 = (f32[4,2,128,2048]{3,2,1,0:T(8,128)}, f32[4,2,128,2048]{3,2,1,0:T(8,128)S(1)}, u32[]{:S(2)}) copy-start(f32[4,2,128,2048]{3,2,1,0:T(8,128)S(1)} %fusion.37) | copy-start | bytes 25165828
  119.5 6.8 %slice-start.2 = ((s8[8388608]{0:T(1024)(128)(4,1)}), s8[4194304]{0:T(1024)(128)(4,1)S(1)}, s32[]{:S(2)}) async-start(s8[8388608]{0:T(1024)(128)(4,1)} %bitcast.129), calls=%async_computation.5 | async-start | bytes 8388608
  121.2 17.3 %collective-permute-start = (bf16[4,128,2048]{2,1,0:T(8,128)(2,1)}, bf16[4,128,2048]{2,1,0:T(8,128)(2,1)}, u32[]{:S(2)}, u32[]{:S(2)}) collective-permute-start(bf16[4,128,2048]{2,1,0:T(8,128)(2,1)} %fusion.16), channel_id=1, source_target_pairs={{0,1},{1,0},{2,3},{3,2},{4,5},{5,4},{6,7},{7,6},{8,9},{9,8},{10,11... | collective-permute-start | bytes 6291464 | tf_op jit(solution)/shard_map/ppermute | solution.py:85
  121.2 5.1 %slice-start.3 = ((s8[8388608]{0:T(1024)(128)(4,1)}), s8[4194304]{0:T(1024)(128)(4,1)S(1)}, s32[]{:S(2)}) async-start(s8[8388608]{0:T(1024)(128)(4,1)} %bitcast.129), calls=%async_computation.6 | async-start | bytes 8388608
  121.2 5.1 %copy-start.5 = (bf16[1024,256]{0,1:T(8,128)(2,1)S(1)}, bf16[1024,256]{0,1:T(8,128)(2,1)}, u32[]{:S(2)}) copy-start(bf16[1024,256]{0,1:T(8,128)(2,1)} %copy-done.4) | copy-start | bytes 1572868
  124.9 48.4 %collective-permute-start.7 = (f32[256,2048]{1,0:T(8,128)}, f32[256,2048]{1,0:T(8,128)}, u32[]{:S(2)}, u32[]{:S(2)}) collective-permute-start(f32[256,2048]{1,0:T(8,128)} %convert_reduce_fusion), channel_id=1, source_target_pairs={{0,8},{8,0},{16,24},{24,16},{1,9},{9,1},{17,25},{25,17},{2,10},{10... | collective-permute-start | bytes 6291464 | tf_op jit(solution)/shard_map/ppermute | solution.py:68
  129.9 1.0 copy-start.6
  134.2 71.0 %all-to-all-start.1 = ((bf16[3,1024,2,128]{3,2,0,1:T(2,128)(2,1)}), bf16[3,1024,2,128]{3,2,0,1:T(2,128)(2,1)}, u32[]{:S(2)}, u32[]{:S(2)}) async-start(bf16[3,1024,2,128]{3,2,0,1:T(2,128)(2,1)} %copy.131), calls=%async_computation.1 | async-start | bytes 3145728 | tf_op jit(solution)/shard_map/all_to_all | solution.py:160
  144.1 1.9 copy-start.3
  146.2 32.4 %collective-permute-start.1 = (bf16[128,2048]{1,0:T(8,128)(2,1)S(1)}, bf16[128,2048]{1,0:T(8,128)(2,1)}, u32[]{:S(2)}, u32[]{:S(2)}) collective-permute-start(bf16[128,2048]{1,0:T(8,128)(2,1)S(1)} %get-tuple-element.7), channel_id=1, source_target_pairs={{0,2},{1,3},{2,4},{3,5},{4,6},{5,7},{8,10},{9,11},{10,12},{11,13},... | collective-permute-start | bytes 1572872 | tf_op jit(solution)/shard_map/ppermute | solution.py:102
  175.7 47.4 %collective-permute-start.8 = (f32[256,2048]{1,0:T(8,128)S(1)}, f32[256,2048]{1,0:T(8,128)}, u32[]{:S(2)}, u32[]{:S(2)}) collective-permute-start(f32[256,2048]{1,0:T(8,128)S(1)} %add.84), channel_id=1, source_target_pairs={{0,16},{8,24},{16,0},{24,8},{1,17},{9,25},{17,1},{25,9},{2,18},{10... | collective-permute-start | bytes 6291464 | tf_op jit(solution)/shard_map/ppermute | solution.py:68
  177.3 15.3 %collective-permute-start.4 = (bf16[128,2048]{1,0:T(8,128)(2,1)S(1)}, bf16[128,2048]{1,0:T(8,128)(2,1)}, u32[]{:S(2)}, u32[]{:S(2)}) collective-permute-start(bf16[128,2048]{1,0:T(8,128)(2,1)S(1)} %get-tuple-element.8), channel_id=1, source_target_pairs={{2,0},{3,1},{4,2},{5,3},{6,4},{7,5},{10,8},{11,9},{12,10},{13,11},... | collective-permute-start | bytes 1572872 | tf_op jit(solution)/shard_map/ppermute | solution.py:103
  180.1 20.7 %collective-permute-start.2 = (bf16[128,2048]{1,0:T(8,128)(2,1)S(1)}, bf16[128,2048]{1,0:T(8,128)(2,1)}, u32[]{:S(2)}, u32[]{:S(2)}) collective-permute-start(bf16[128,2048]{1,0:T(8,128)(2,1)S(1)} %fusion.41), channel_id=1, source_target_pairs={{0,2},{1,3},{2,4},{3,5},{4,6},{5,7},{8,10},{9,11},{10,12},{11,13},... | collective-permute-start | bytes 1572872 | tf_op jit(solution)/shard_map/ppermute | solution.py:102
  203.9 16.1 %collective-permute-start.5 = (bf16[128,2048]{1,0:T(8,128)(2,1)}, bf16[128,2048]{1,0:T(8,128)(2,1)}, u32[]{:S(2)}, u32[]{:S(2)}) collective-permute-start(bf16[128,2048]{1,0:T(8,128)(2,1)} %get-tuple-element.6), channel_id=1, source_target_pairs={{2,0},{3,1},{4,2},{5,3},{6,4},{7,5},{10,8},{11,9},{12,10},{13,11},... | collective-permute-start | bytes 1572872 | tf_op jit(solution)/shard_map/ppermute | solution.py:103
  214.3 16.0 %collective-permute-start.3 = (bf16[128,2048]{1,0:T(8,128)(2,1)}, bf16[128,2048]{1,0:T(8,128)(2,1)S(1)}, u32[]{:S(2)}, u32[]{:S(2)}) collective-permute-start(bf16[128,2048]{1,0:T(8,128)(2,1)} %get-tuple-element.5), channel_id=1, source_target_pairs={{0,2},{1,3},{2,4},{3,5},{4,6},{5,7},{8,10},{9,11},{10,12},{11,13},... | collective-permute-start | bytes 1572872 | tf_op jit(solution)/shard_map/ppermute | solution.py:102
  220.0 19.0 %copy-start.1 = (bf16[256,2048]{1,0:T(8,128)(2,1)S(1)}, bf16[256,2048]{1,0:T(8,128)(2,1)}, u32[]{:S(2)}) copy-start(bf16[256,2048]{1,0:T(8,128)(2,1)} %param.11) | copy-start | bytes 3145732
  221.6 15.2 %collective-permute-start.6 = (bf16[128,2048]{1,0:T(8,128)(2,1)S(1)}, bf16[128,2048]{1,0:T(8,128)(2,1)S(1)}, u32[]{:S(2)}, u32[]{:S(2)}) collective-permute-start(bf16[128,2048]{1,0:T(8,128)(2,1)S(1)} %fusion.40), channel_id=1, source_target_pairs={{2,0},{3,1},{4,2},{5,3},{6,4},{7,5},{10,8},{11,9},{12,10},{13,11},... | collective-permute-start | bytes 1572872 | tf_op jit(solution)/shard_map/ppermute | solution.py:103
Sparse Core Ops, SparseCore 0:
  9.6 83.0 all-gather.2

commit v4 on v2

--- a/solution.py
+++ b/solution.py
@@ -25,18 +25,15 @@
     return full.reshape(nodes, nodes)
 
 
-def attend(q, k, v, g, allowed):
+def attend(q, k, v, allowed):
     factor = 1.0 / math.sqrt(q.shape[-1])
-    scores = jnp.einsum("ihd,jhd->hij", q, k, preferred_element_type=jnp.float32) * factor
-    masked = jnp.where(allowed[None], scores, -jnp.inf)
-    row_max = jnp.max(masked, axis=2, keepdims=True)
-    expd = jnp.where(allowed[None], jnp.exp(scores - row_max), 0.0)
-    row_total = jnp.sum(expd, axis=2, keepdims=True)
-    weighted = jnp.einsum(
-        "hij,jhd->ihd", expd.astype(jnp.bfloat16), v, preferred_element_type=jnp.float32
-    )
-    totals = jnp.transpose(row_total[:, :, 0])[:, :, None]
-    attended = (weighted / totals).astype(jnp.bfloat16)
+    scores = jnp.dot(q, k.T, preferred_element_type=jnp.float32) * factor
+    masked = jnp.where(allowed, scores, -jnp.inf)
+    row_max = jnp.max(masked, axis=1, keepdims=True)
+    expd = jnp.where(allowed, jnp.exp(scores - row_max), 0.0)
+    row_total = jnp.sum(expd, axis=1, keepdims=True)
+    weighted = jnp.dot(expd.astype(jnp.bfloat16), v, preferred_element_type=jnp.float32)
+    attended = (weighted / row_total).astype(jnp.bfloat16)
     return attended, expd, row_total
 
 
@@ -44,13 +41,14 @@
     factor = 1.0 / math.sqrt(q.shape[-1])
     prob = expd / row_total
     prob_low = prob.astype(jnp.bfloat16)
-    v_grad = jnp.einsum("hij,ihd->jhd", prob_low, g, preferred_element_type=jnp.float32)
-    prob_grad = jnp.einsum("ihd,jhd->hij", g, v, preferred_element_type=jnp.float32)
-    delta = jnp.sum(attended.astype(jnp.float32) * g.astype(jnp.float32), axis=2)
-    delta = jnp.transpose(delta)[:, :, None]
+    v_grad = jnp.dot(prob_low.T, g, preferred_element_type=jnp.float32)
+    prob_grad = jnp.dot(g, v.T, preferred_element_type=jnp.float32)
+    delta = jnp.sum(
+        attended.astype(jnp.float32) * g.astype(jnp.float32), axis=1, keepdims=True
+    )
     score_grad = (prob * (prob_grad - delta) * factor).astype(jnp.bfloat16)
-    q_grad = jnp.einsum("hij,jhd->ihd", score_grad, k, preferred_element_type=jnp.float32)
-    k_grad = jnp.einsum("hij,ihd->jhd", score_grad, q, preferred_element_type=jnp.float32)
+    q_grad = jnp.dot(score_grad, k, preferred_element_type=jnp.float32)
+    k_grad = jnp.dot(score_grad.T, q, preferred_element_type=jnp.float32)
     return (
         q_grad.astype(jnp.bfloat16),
         k_grad.astype(jnp.bfloat16),
@@ -87,17 +85,33 @@
     grad_here = upstream_cotangent[0]
     grad_full = lax.all_gather(grad_here, "seq", axis=0, tiled=True)
 
+    groups = n_seq
+    group_width = width // groups
+    local_heads = group_width // HD
+
+    def to_groups(values):
+        return values.reshape(nodes_here, groups, group_width).transpose(1, 0, 2)
+
     stacked = jnp.stack(
-        [asking_vectors_matrix[0], matched_keys_matrix[0], carried_vectors_matrix[0]]
-    ).reshape(3, nodes_here, H, HD)
-    heads = lax.all_to_all(stacked, "seq", split_axis=2, concat_axis=1, tiled=True)
-    q_heads, k_heads, v_heads = heads[0], heads[1], heads[2]
-    local_heads = q_heads.shape[1]
+        [
+            to_groups(asking_vectors_matrix[0]),
+            to_groups(matched_keys_matrix[0]),
+            to_groups(carried_vectors_matrix[0]),
+        ]
+    )
+    heads = lax.all_to_all(stacked, "seq", split_axis=1, concat_axis=1, tiled=True)
+    heads = heads.reshape(3, nodes, group_width)
 
     allowed = tile_mask(panel_entry_offsets[0], rightward_panel_per_entry[0], nodes)
 
-    attended, expd, row_total = attend(q_heads, k_heads, v_heads, None, allowed)
-    att_flat = attended.reshape(nodes, local_heads * HD)
+    def head_cols(values, h):
+        return values[:, h * HD : (h + 1) * HD]
+
+    fwd = [
+        attend(head_cols(heads[0], h), head_cols(heads[1], h), head_cols(heads[2], h), allowed)
+        for h in range(local_heads)
+    ]
+    att_flat = jnp.concatenate([f[0] for f in fwd], axis=1)
 
     partial = jnp.dot(att_flat, w_out, preferred_element_type=jnp.float32)
     layer_out = lax.psum_scatter(
@@ -107,8 +121,6 @@
     g_flat = lax.dot_general(
         grad_full, w_out, (((1,), (1,)), ((), ())), preferred_element_type=jnp.float32
     ).astype(jnp.bfloat16)
-    g_heads = g_flat.reshape(nodes, local_heads, HD)
-
     att_blocks = att_flat.reshape(n_seq, nodes_here, local_heads * HD)
     grad_blocks = grad_full.reshape(n_seq, nodes_here, width)
     terms = jnp.einsum(
@@ -119,10 +131,24 @@
     batch = asking_vectors_matrix.shape[0] * lax.axis_size("dp")
     w_out_grad = w_rows / batch
 
-    q_g, k_g, v_g = attend_back(q_heads, k_heads, v_heads, g_heads, attended, expd, row_total)
-    grads = jnp.stack([q_g, k_g, v_g])
-    back = lax.all_to_all(grads, "seq", split_axis=1, concat_axis=2, tiled=True)
-    back = back.reshape(3, 1, nodes_here, width)
+    bwd = [
+        attend_back(
+            head_cols(heads[0], h),
+            head_cols(heads[1], h),
+            head_cols(heads[2], h),
+            head_cols(g_flat, h),
+            fwd[h][0],
+            fwd[h][1],
+            fwd[h][2],
+        )
+        for h in range(local_heads)
+    ]
+    grads = jnp.stack(
+        [jnp.concatenate([b[i] for b in bwd], axis=1).reshape(groups, nodes_here, group_width)
+         for i in range(3)]
+    )
+    back = lax.all_to_all(grads, "seq", split_axis=1, concat_axis=1, tiled=True)
+    back = back.transpose(0, 2, 1, 3).reshape(3, 1, nodes_here, width)
     return (layer_out, back[0], back[1], back[2], w_out_grad)
 
 

time: 227 us -> 225 us (level)
  local copies, waits for them, and re-layouts: 29.9 us -> 22.4 us
  waiting for transfers between devices: 128 us -> 133 us
  other arithmetic: 6.13 us -> 9.92 us
  matrix products: 33.4 us -> 30.9 us
    unnamed x19 -> x40, local copies, waits for them, and re-layouts: 5.65 us -> 16.8 us
    all_to_all x2, waiting for transfers between devices: 91.7 us -> 99.3 us  [the longest x1 71 us: shards(): lax.all_to_all(stacked, 'seq', split_axis=1, concat_axis=1, tiled=True)]
    sub x1 -> x0, matrix products: 7.3 us -> none  [attend(): expd = jnp.where(allowed[None], jnp.exp(scores - row_max), 0.0)]
    squeeze x4 -> x0, local copies, waits for them, and re-layouts: 6.87 us -> none  [the longest x3 6.65 us: shards(): return (layer_out, back[0], back[1], back[2], w_out_grad)]
    slice x4 -> x1, local copies, waits for them, and re-layouts: 9.21 us -> 2.53 us  [shards(): return (layer_out, back[0], back[1], back[2], w_out_grad)]
    dot_general x5 -> x12, matrix products: 13 us -> 17.8 us  [the longest x2 6.32 us: attend_back(): prob_grad = jnp.dot(g, v.T, preferred_element_type=jnp.float32)]
    ppermute x2, waiting for transfers between devices: 35.8 us -> 32.9 us  [dp_sum(): values = values + lax.ppermute(values, 'dp', pairs)]
    reduce_sum x0 -> x1, other arithmetic: none -> 2.42 us  [attend(): row_total = jnp.sum(expd, axis=1, keepdims=True)]
  transfers between devices with their start and end apart: 6 -> 6, of which waited for: 4 -> 4; matrix products, arithmetic and copies ran while one was open for 26% -> 21% of each run, Pallas kernels for 0% -> 0%
where the time goes in v4:
time: 225 us; the launch traced here: 224 us
  waiting for transfers between devices  133 us (59%)
  matrix products  30.9 us (14%)
  local copies, waits for them, and re-layouts  22.4 us (10%)
  between operations  14.5 us (6%)
  starting transfers between devices  13.8 us (6%)
  other arithmetic  9.92 us (4%)
    all_to_all x1, waiting for transfers between devices, shards(): lax.all_to_all(stacked, 'seq', split_axis=1, concat_axis=1, tiled=True)  71 us
    ppermute x2, waiting for transfers between devices, dp_sum(): values = values + lax.ppermute(values, 'dp', pairs)  32.9 us
    all_to_all x1, waiting for transfers between devices, shards(): back = lax.all_to_all(grads, 'seq', split_axis=1, concat_axis=1, tiled=True)  28.3 us
    unnamed x40, local copies, waits for them, and re-layouts  16.8 us
    all_to_all x1, starting transfers between devices, shards(): lax.all_to_all(stacked, 'seq', split_axis=1, concat_axis=1, tiled=True)  6.33 us
    dot_general x2, matrix products, attend_back(): prob_grad = jnp.dot(g, v.T, preferred_element_type=jnp.float32)  6.32 us
    dot_general x1, matrix products, shards(): jnp.einsum('bnf,bnk->bfk', att_blocks, grad_blocks, preferred_element_typ...  6.04 us
  transfers between devices with their start and end apart: 6, of which 4 were waited for; matrix products, arithmetic and copies ran while one was open for 21% of the time, Pallas kernels for 0%

profile of v4, /device:TPU:0, one launch (start us, length us, event | category | flops | bytes accessed | tf_op | source)
XLA Modules:
  0.0 224.5 jit_solution(7513062520037611335)
XLA Ops:
  7.2 0.7 all-gather.3.cloned.1.call-update
  7.9 1.3 copy.59
  9.2 1.3 copy.57
  10.6 1.3 copy.58
  11.9 0.2 pad_maximum_fusion
  12.1 1.2 copy.60
  13.3 6.3 %all-to-all-start = ((bf16[3,8,128,256]{2,3,0,1:T(8,128)(2,1)}), bf16[3,8,128,256]{2,3,0,1:T(8,128)(2,1)S(1)}, u32[]{:S(2)}, u32[]{:S(2)}) async-start(bf16[3,8,128,256]{2,3,0,1:T(8,128)(2,1)} %copy.60), calls=%async_computation | async-start | bytes 3145728 | tf_op jit(solution)/shard_map/all_to_all | solution.py:102
  19.9 0.3 convolution_compare_fusion
  20.2 71.0 %all-to-all-done = bf16[3,8,128,256]{2,3,0,1:T(8,128)(2,1)S(1)} async-done(((bf16[3,8,128,256]{2,3,0,1:T(8,128)(2,1)}), bf16[3,8,128,256]{2,3,0,1:T(8,128)(2,1)S(1)}, u32[]{:S(2)}, u32[]{:S(2)}) %all-to-all-start) | async-done | bytes 1572896 | tf_op jit(solution)/shard_map/all_to_all | solution.py:102
  91.2 1.1 fusion.58
  92.3 1.2 copy.75
  93.5 1.2 copy.76
  94.8 1.0 copy.77
  95.8 0.7 fusion.37
  96.5 0.3 broadcast_in_dim.13
  96.9 2.5 %select_reduce_fusion.1 = (f32[1024]{0:T(1024)S(1)}, f32[1024]{0:T(1024)S(1)}, f32[1024,1024]{0,1:T(8,128)S(1)}) fusion(pred[128,8,8,128]{3,2,1,0:T(8,128)(4,1)S(1)} %bitcast.95, f32[1024,1024]{0,1:T(8,128)S(1)} %fusion.37, bf16[1024,256]{1,0:T(8,128)(2,1)} %bitcast.117, bf16[1024,256]{1,0:T(8,128)(2,1)S(1)} %bitcast.104), kind=kOutput, calls=%fused_computation.8 | convolution fusion | flops 274724864 | bytes 9969664 | tf_op jit(solution)/shard_map/dot_general | solution.py:30
  99.4 2.4 %fusion.55 = (f32[1024]{0:T(1024)S(1)}, f32[1024]{0:T(1024)S(1)}) fusion(f32[1024]{0:T(1024)S(1)} %get-tuple-element.17, f32[1024,1024]{0,1:T(8,128)S(1)} %get-tuple-element.27, pred[128,8,8,128]{3,2,1,0:T(8,128)(4,1)S(1)} %bitcast.96, f32[1024]{0:T(1024)S(1)} %get-tuple-element.18, f32[1024,1024]{0,1:T(8,128)S(1)} %fusion.37), kind=kLoop, calls=%fused_computation.70 | loop fusion | flops 8386560 | bytes 9453568 | tf_op jit(solution)/shard_map/reduce_sum | solution.py:34
  101.9 1.2 fusion.25
  103.2 3.6 %fusion.10 = bf16[1024,256]{0,1:T(8,128)(2,1)S(1)} fusion(bf16[256,2048]{1,0:T(8,128)(2,1)S(1)} %copy-done, bf16[1,1024,2048]{2,1,0:T(8,128)(2,1)} %all-gather.3.cloned.1.call-done), kind=kOutput, calls=%fused_computation.23 | convolution fusion | flops 1074003968 | bytes 5767168 | tf_op jit(solution)/shard_map/dot_general | solution.py:121
  106.8 1.3 multiply_reduce_fusion.1
  108.1 0.7 copy-done.9
  108.8 3.2 %convolution_convert_fusion = bf16[1024,2048]{1,0:T(8,128)(2,1)} fusion(bf16[256,2048]{1,0:T(8,128)(2,1)S(1)} %copy-done, bf16[1024,128]{0,1:T(8,128)(2,1)S(1)} %fusion.25, bf16[1024,128]{0,1:T(8,128)(2,1)S(1)} %get-tuple-element.28), kind=kOutput, calls=%fused_computation.9 | convolution fusion | flops 1076887552 | bytes 5767168 | tf_op jit(solution)/shard_map/dot_general | solution.py:116
  112.1 6.0 %convert_reduce_fusion = f32[256,2048]{1,0:T(8,128)} fusion(bf16[8,128,2048]{2,1,0:T(8,128)(2,1)} %bitcast.124, bf16[1024,128]{0,1:T(8,128)(2,1)S(1)} %fusion.25, bf16[1024,128]{0,1:T(8,128)(2,1)} %copy-done.9), kind=kOutput, calls=%fused_computation | convolution fusion | flops 1086849024 | bytes 6815744 | tf_op jit(solution)/shard_map/bnf,bnk->bfk/dot_general | solution.py:126
  118.1 1.5 collective-permute-start
  119.7 4.1 %multiply_convert_fusion.1 = bf16[1024,1024]{0,1:T(8,128)(2,1)S(1)} fusion(f32[1024]{0:T(1024)S(1)} %get-tuple-element.19, f32[1024]{0:T(1024)S(1)} %get-tuple-element.15, bf16[1024,256]{1,0:T(8,128)(2,1)S(1)} %bitcast.122, bf16[1024,256]{0,1:T(8,128)(2,1)} %copy-done.12, f32[1024]{0:T(1024)S(1)} %get-tuple-element.17, f32[1024,1024]{0,1:T(8,128)} %copy-done.3, ...), kind=kOutput, calls=%fused_computation.4 | convolution fusion | flops 276824064 | bytes 7876608 | tf_op jit(solution)/shard_map/dot_general | solution.py:45
  123.8 0.5 convolution_convert_fusion.4
  124.3 1.7 copy-done.2
  126.0 2.2 multiply_convert_fusion
  128.2 0.5 convolution_convert_fusion.3
  128.8 0.8 convolution_convert_fusion.2
  129.6 0.8 convolution_convert_fusion.1
  130.5 0.5 copy-done.5
  131.0 1.5 fusion.19
  132.6 0.1 copy.80
  132.7 0.1 copy.81
  132.9 1.5 fusion.22
  134.7 1.4 pad_maximum_fusion.1
  136.1 4.3 %all-to-all-start.1 = ((bf16[3,8,128,256]{2,3,0,1:T(8,128)(2,1)}), bf16[3,8,128,256]{2,3,0,1:T(8,128)(2,1)}, u32[]{:S(2)}, u32[]{:S(2)}) async-start(bf16[3,8,128,256]{2,3,0,1:T(8,128)(2,1)} %pad_maximum_fusion.1), calls=%async_computation.2 | async-start | bytes 3145728 | tf_op jit(solution)/shard_map/all_to_all | solution.py:150
  140.4 25.2 %collective-permute-done = f32[256,2048]{1,0:T(8,128)} collective-permute-done((f32[256,2048]{1,0:T(8,128)}, f32[256,2048]{1,0:T(8,128)}, u32[]{:S(2)}, u32[]{:S(2)}) %collective-permute-start) | collective-permute-done | bytes 2097184 | tf_op jit(solution)/shard_map/ppermute | solution.py:66
  165.5 2.5 %add.8 = f32[256,2048]{1,0:T(8,128)S(1)} add(f32[256,2048]{1,0:T(8,128)} %convert_reduce_fusion, f32[256,2048]{1,0:T(8,128)} %collective-permute-done) | non-fusion elementwise | flops 524288 | bytes 6291456 | tf_op jit(solution)/shard_map/add | solution.py:66
  168.1 1.6 collective-permute-start.1
  169.6 28.3 %all-to-all-done.1 = bf16[3,8,128,256]{2,3,0,1:T(8,128)(2,1)} async-done(((bf16[3,8,128,256]{2,3,0,1:T(8,128)(2,1)}), bf16[3,8,128,256]{2,3,0,1:T(8,128)(2,1)}, u32[]{:S(2)}, u32[]{:S(2)}) %all-to-all-start.1) | async-done | bytes 1572896 | tf_op jit(solution)/shard_map/all_to_all | solution.py:150
  198.0 2.5 %fusion.57 = (bf16[1,128,8,256]{1,3,0,2:T(8,128)(2,1)}, bf16[1,128,8,256]{1,3,0,2:T(8,128)(2,1)}, bf16[1,128,8,256]{1,3,0,2:T(8,128)(2,1)}) fusion(bf16[3,128,8,256]{1,3,0,2:T(8,128)(2,1)} %bitcast.16), kind=kLoop, calls=%fused_computation.72 | loop fusion | bytes 3145728 | tf_op jit(solution)/shard_map/slice | solution.py:152
  200.5 2.0 copy.70
  202.5 2.0 copy.71
  204.6 2.0 copy.72
  206.6 7.8 %collective-permute-done.1 = f32[256,2048]{1,0:T(8,128)} collective-permute-done((f32[256,2048]{1,0:T(8,128)S(1)}, f32[256,2048]{1,0:T(8,128)}, u32[]{:S(2)}, u32[]{:S(2)}) %collective-permute-start.1) | collective-permute-done | bytes 2097184 | tf_op jit(solution)/shard_map/ppermute | solution.py:66
  214.4 3.2 %add_multiply_fusion = f32[256,2048]{1,0:T(8,128)} fusion(f32[256,2048]{1,0:T(8,128)S(1)} %add.8, f32[256,2048]{1,0:T(8,128)} %collective-permute-done.1), kind=kLoop, calls=%fused_computation.10 | loop fusion | flops 1048576 | bytes 6291456 | tf_op jit(solution)/shard_map/div | solution.py:132
  (40 shorter events, 0.8 us)
Async XLA Ops:
  7.2 96.0 %copy-start = (bf16[256,2048]{1,0:T(8,128)(2,1)S(1)}, bf16[256,2048]{1,0:T(8,128)(2,1)}, u32[]{:S(2)}) copy-start(bf16[256,2048]{1,0:T(8,128)(2,1)} %param.11) | copy-start | bytes 3145732
  7.2 96.0 %all-gather.3.cloned.1.call-start = ((), (), s32[]{:S(2)}) async-start(), calls=%async_computation.4 | async-start | bytes 4718592 | tf_op jit(solution)/shard_map/all_gather | solution.py:86
  11.9 7.8 %copy-start.10 = (s32[1,9]{1,0:T(1,128)S(1)}, s32[1,9]{1,0:T(1,128)}, u32[]{:S(2)}) copy-start(s32[1,9]{1,0:T(1,128)} %param.12) | copy-start | bytes 112
  11.9 8.0 %copy-start.11 = (s32[1,32]{1,0:T(1,128)S(1)}, s32[1,32]{1,0:T(1,128)}, u32[]{:S(2)}) copy-start(s32[1,32]{1,0:T(1,128)} %param.13) | copy-start | bytes 388
  13.3 77.9 %all-to-all-start = ((bf16[3,8,128,256]{2,3,0,1:T(8,128)(2,1)}), bf16[3,8,128,256]{2,3,0,1:T(8,128)(2,1)S(1)}, u32[]{:S(2)}, u32[]{:S(2)}) async-start(bf16[3,8,128,256]{2,3,0,1:T(8,128)(2,1)} %copy.60), calls=%async_computation | async-start | bytes 3145728 | tf_op jit(solution)/shard_map/all_to_all | solution.py:102
  19.7 198.0 %reduce-scatter.2.cloned.1.call-start = ((), (), s32[]{:S(2)}) async-start(), calls=%async_computation.3 | async-start | bytes 4718592 | tf_op jit(solution)/shard_map/reduce_scatter | solution.py:117
  94.8 1.0 copy-start.6
  96.5 5.4 %copy-start.1 = (f32[1024,1024]{0,1:T(8,128)}, f32[1024,1024]{0,1:T(8,128)S(1)}, u32[]{:S(2)}) copy-start(f32[1024,1024]{0,1:T(8,128)S(1)} %fusion.37) | copy-start | bytes 12582916
  99.4 2.5 %copy-start.3 = (f32[1024,1024]{0,1:T(8,128)}, f32[1024,1024]{0,1:T(8,128)S(1)}, u32[]{:S(2)}) copy-start(f32[1024,1024]{0,1:T(8,128)S(1)} %get-tuple-element.27) | copy-start | bytes 12582916
  99.4 2.5 %copy-start.8 = (bf16[1,8,128,256]{3,2,1,0:T(8,128)(2,1)S(1)}, bf16[1,8,128,256]{3,2,1,0:T(8,128)(2,1)}, u32[]{:S(2)}) copy-start(bf16[1,8,128,256]{3,2,1,0:T(8,128)(2,1)} %copy.77) | copy-start | bytes 1572868
  103.2 3.6 %copy-start.4 = (f32[1024,1024]{0,1:T(8,128)S(1)}, f32[1024,1024]{0,1:T(8,128)}, u32[]{:S(2)}) copy-start(f32[1024,1024]{0,1:T(8,128)} %copy-done.3) | copy-start | bytes 12582916
  106.8 1.3 copy-start.12
  108.1 0.7 copy-start.9
  118.1 47.4 %collective-permute-start = (f32[256,2048]{1,0:T(8,128)}, f32[256,2048]{1,0:T(8,128)}, u32[]{:S(2)}, u32[]{:S(2)}) collective-permute-start(f32[256,2048]{1,0:T(8,128)} %convert_reduce_fusion), channel_id=1, source_target_pairs={{0,8},{8,0},{16,24},{24,16},{1,9},{9,1},{17,25},{25,17},{2,10},{10... | collective-permute-start | bytes 6291464 | tf_op jit(solution)/shard_map/ppermute | solution.py:66
  119.6 4.1 %copy-start.7 = (bf16[1,8,128,256]{3,2,1,0:T(8,128)(2,1)S(1)}, bf16[1,8,128,256]{3,2,1,0:T(8,128)(2,1)}, u32[]{:S(2)}) copy-start(bf16[1,8,128,256]{3,2,1,0:T(8,128)(2,1)} %copy-done.6) | copy-start | bytes 1572868
  119.6 4.6 %copy-start.13 = (bf16[1024,256]{0,1:T(8,128)(2,1)S(1)}, bf16[1024,256]{0,1:T(8,128)(2,1)}, u32[]{:S(2)}) copy-start(bf16[1024,256]{0,1:T(8,128)(2,1)} %copy-done.12) | copy-start | bytes 1572868
  123.8 2.2 copy-start.2
  128.7 2.2 %copy-start.5 = (f32[1024,1024]{0,1:T(8,128)S(1)}, f32[1024,1024]{0,1:T(8,128)}, u32[]{:S(2)}) copy-start(f32[1024,1024]{0,1:T(8,128)} %copy-done.3) | copy-start | bytes 12582916
  136.1 61.9 %all-to-all-start.1 = ((bf16[3,8,128,256]{2,3,0,1:T(8,128)(2,1)}), bf16[3,8,128,256]{2,3,0,1:T(8,128)(2,1)}, u32[]{:S(2)}, u32[]{:S(2)}) async-start(bf16[3,8,128,256]{2,3,0,1:T(8,128)(2,1)} %pad_maximum_fusion.1), calls=%async_computation.2 | async-start | bytes 3145728 | tf_op jit(solution)/shard_map/all_to_all | solution.py:150
  168.1 46.3 %collective-permute-start.1 = (f32[256,2048]{1,0:T(8,128)S(1)}, f32[256,2048]{1,0:T(8,128)}, u32[]{:S(2)}, u32[]{:S(2)}) collective-permute-start(f32[256,2048]{1,0:T(8,128)S(1)} %add.8), channel_id=1, source_target_pairs={{0,16},{8,24},{16,0},{24,8},{1,17},{9,25},{17,1},{25,9},{2,18},{10... | collective-permute-start | bytes 6291464 | tf_op jit(solution)/shard_map/ppermute | solution.py:66
Sparse Core Ops, SparseCore 0:
  9.6 83.0 all-gather.2
  119.8 67.2 reduce-scatter.1

commit v5 on v4

--- a/solution.py
+++ b/solution.py
@@ -66,6 +66,36 @@
         values = values + lax.ppermute(values, "dp", pairs)
         step *= 2
     return values
+
+
+def line_gather(x):
+    n = lax.axis_size("seq")
+    chips = n // 2
+    s = lax.axis_index("seq")
+    core = s % 2
+    z = s // 2
+    right = [(i, i + 2) for i in range(n - 2)]
+    left = [(i, i - 2) for i in range(2, n)]
+    before = []
+    after = []
+    r = x
+    l = x
+    for step in range(1, chips):
+        r = lax.ppermute(r, "seq", right)
+        l = lax.ppermute(l, "seq", left)
+        before.append(r)
+        after.append(l)
+    rel = jnp.stack(before[::-1] + [x] + after)
+    mine = lax.dynamic_slice_in_dim(rel, chips - 1 - z, chips, axis=0)
+    other = lax.ppermute(mine, "seq", [(i, i ^ 1) for i in range(n)])
+    return mine, other, core
+
+
+def pair_rows(first, second, core):
+    pair = jnp.where(
+        core == 0, jnp.stack([first, second], axis=1), jnp.stack([second, first], axis=1)
+    )
+    return pair
 
 
 def shards(
@@ -83,7 +113,7 @@
     nodes = nodes_here * n_seq
 
     grad_here = upstream_cotangent[0]
-    grad_full = lax.all_gather(grad_here, "seq", axis=0, tiled=True)
+    up_mine, up_other, core = line_gather(grad_here)
 
     groups = n_seq
     group_width = width // groups
@@ -118,15 +148,25 @@
         partial.astype(jnp.bfloat16), "seq", scatter_dimension=0, tiled=True
     )[None]
 
-    g_flat = lax.dot_general(
-        grad_full, w_out, (((1,), (1,)), ((), ())), preferred_element_type=jnp.float32
-    ).astype(jnp.bfloat16)
-    att_blocks = att_flat.reshape(n_seq, nodes_here, local_heads * HD)
-    grad_blocks = grad_full.reshape(n_seq, nodes_here, width)
-    terms = jnp.einsum(
-        "bnf,bnk->bfk", att_blocks, grad_blocks, preferred_element_type=jnp.float32
-    ).astype(jnp.bfloat16)
-    w_rows = jnp.sum(terms.astype(jnp.float32), axis=0)
+    def times_w(values):
+        return lax.dot_general(
+            values, w_out, (((2,), (1,)), ((), ())), preferred_element_type=jnp.float32
+        ).astype(jnp.bfloat16)
+
+    g_flat = pair_rows(times_w(up_mine), times_w(up_other), core).reshape(nodes, group_width)
+
+    att4 = att_flat.reshape(n_seq // 2, 2, nodes_here, group_width)
+    att_mine = jnp.where(core == 0, att4[:, 0], att4[:, 1])
+    att_other = jnp.where(core == 0, att4[:, 1], att4[:, 0])
+
+    def block_terms(att_part, up_part):
+        return jnp.einsum(
+            "bnf,bnk->bfk", att_part, up_part, preferred_element_type=jnp.float32
+        ).astype(jnp.bfloat16)
+
+    w_rows = jnp.sum(block_terms(att_mine, up_mine).astype(jnp.float32), axis=0) + jnp.sum(
+        block_terms(att_other, up_other).astype(jnp.float32), axis=0
+    )
     w_rows = dp_sum(w_rows)
     batch = asking_vectors_matrix.shape[0] * lax.axis_size("dp")
     w_out_grad = w_rows / batch

time: 225 us -> 259 us (1.15)
  starting transfers between devices: 13.8 us -> 32 us
  local copies, waits for them, and re-layouts: 22.4 us -> 35.5 us
    all_to_all x1, waiting for transfers between devices: 71 us -> 0.01 us  [shards(): lax.all_to_all(stacked, 'seq', split_axis=1, concat_axis=1, tiled=True)]
    ppermute x0 -> x7, waiting for transfers between devices: none -> 60.6 us  [the longest x3 51.3 us: line_gather(): l = lax.ppermute(l, 'seq', left)]
    ppermute x0 -> x7, starting transfers between devices: none -> 20.3 us  [the longest x3 16.4 us: line_gather(): r = lax.ppermute(r, 'seq', right)]
    ppermute x2, waiting for transfers between devices: 32.9 us -> 53.1 us  [dp_sum(): values = values + lax.ppermute(values, 'dp', pairs)]
    all_to_all x1, waiting for transfers between devices: 28.3 us -> 17.5 us  [shards(): back = lax.all_to_all(grads, 'seq', split_axis=1, concat_axis=1, tiled=True)]
    dot_general x2, matrix products: 3.06 us -> 8.59 us  [attend_back(): v_grad = jnp.dot(prob_low.T, g, preferred_element_type=jnp.float32)]
    unnamed x40 -> x74, local copies, waits for them, and re-layouts: 16.8 us -> 22.2 us
    select_n x0 -> x2, local copies, waits for them, and re-layouts: none -> 4.21 us  [pair_rows(): jnp.where(core == 0, jnp.stack([first, second], axis=1), jnp.stack([secon...]
  transfers between devices with their start and end apart: 6 -> 12, of which waited for: 4 -> 6; matrix products, arithmetic and copies ran while one was open for 21% -> 23% of each run, Pallas kernels for 0% -> 0%
where the time goes in v5:
time: 259 us; the launch traced here: 257 us
  waiting for transfers between devices  131 us (51%)
  local copies, waits for them, and re-layouts  35.5 us (14%)
  matrix products  32.5 us (13%)
  starting transfers between devices  32 us (12%)
  between operations  14.7 us (6%)
  other arithmetic  11.3 us (4%)
    ppermute x2, waiting for transfers between devices, dp_sum(): values = values + lax.ppermute(values, 'dp', pairs)  53.1 us
    ppermute x3, waiting for transfers between devices, line_gather(): l = lax.ppermute(l, 'seq', left)  51.3 us
    unnamed x74, local copies, waits for them, and re-layouts  22.2 us
    all_to_all x1, waiting for transfers between devices, shards(): back = lax.all_to_all(grads, 'seq', split_axis=1, concat_axis=1, tiled=True)  17.5 us
    ppermute x3, starting transfers between devices, line_gather(): r = lax.ppermute(r, 'seq', right)  16.4 us
    ppermute x3, waiting for transfers between devices, line_gather(): r = lax.ppermute(r, 'seq', right)  9.37 us
    dot_general x2, matrix products, attend_back(): v_grad = jnp.dot(prob_low.T, g, preferred_element_type=jnp.float32)  8.59 us
  transfers between devices with their start and end apart: 12, of which 6 were waited for; matrix products, arithmetic and copies ran while one was open for 23% of the time, Pallas kernels for 0%

profile of v5, /device:TPU:0, one launch (start us, length us, event | category | flops | bytes accessed | tf_op | source)
XLA Modules:
  0.0 257.3 jit_solution(11738661293988624675)
XLA Ops:
  7.2 5.9 %collective-permute-start = (bf16[128,2048]{1,0:T(8,128)(2,1)}, bf16[128,2048]{1,0:T(8,128)(2,1)}, u32[]{:S(2)}, u32[]{:S(2)}) collective-permute-start(bf16[128,2048]{1,0:T(8,128)(2,1)} %bitcast.141), channel_id=1, source_target_pairs={{0,2},{1,3},{2,4},{3,5},{4,6},{5,7},{8,10},{9,11},{10,12},{11,13},... | collective-permute-start | bytes 1572872 | tf_op jit(solution)/shard_map/ppermute | solution.py:84
  13.1 1.3 collective-permute-start.3
  14.4 9.4 %collective-permute-done = bf16[128,2048]{1,0:T(8,128)(2,1)} collective-permute-done((bf16[128,2048]{1,0:T(8,128)(2,1)}, bf16[128,2048]{1,0:T(8,128)(2,1)}, u32[]{:S(2)}, u32[]{:S(2)}) %collective-permute-start) | collective-permute-done | bytes 524320 | tf_op jit(solution)/shard_map/ppermute | solution.py:84
  23.7 5.2 %collective-permute-start.1 = (bf16[128,2048]{1,0:T(8,128)(2,1)}, bf16[128,2048]{1,0:T(8,128)(2,1)}, u32[]{:S(2)}, u32[]{:S(2)}) collective-permute-start(bf16[128,2048]{1,0:T(8,128)(2,1)} %collective-permute-done), channel_id=1, source_target_pairs={{0,2},{1,3},{2,4},{3,5},{4,6},{5,7},{8,10},{9,11},{10,12},{11,13},... | collective-permute-start | bytes 1572872 | tf_op jit(solution)/shard_map/ppermute | solution.py:84
  28.9 1.3 copy.65
  30.2 1.3 copy.66
  31.5 1.3 copy.67
  33.1 1.2 copy.68
  34.3 4.3 %all-to-all-start = ((bf16[3,8,128,256]{2,3,0,1:T(8,128)(2,1)}), bf16[3,8,128,256]{2,3,0,1:T(8,128)(2,1)}, u32[]{:S(2)}, u32[]{:S(2)}) async-start(bf16[3,8,128,256]{2,3,0,1:T(8,128)(2,1)} %copy.68), calls=%async_computation | async-start | bytes 3145728 | tf_op jit(solution)/shard_map/all_to_all | solution.py:132
  38.7 1.3 collective-permute-start.4
  40.0 5.4 %collective-permute-start.2 = (bf16[128,2048]{1,0:T(8,128)(2,1)}, bf16[128,2048]{1,0:T(8,128)(2,1)}, u32[]{:S(2)}, u32[]{:S(2)}) collective-permute-start(bf16[128,2048]{1,0:T(8,128)(2,1)} %collective-permute-done.1), channel_id=1, source_target_pairs={{0,2},{1,3},{2,4},{3,5},{4,6},{5,7},{8,10},{9,11},{10,12},{11,13},... | collective-permute-start | bytes 1572872 | tf_op jit(solution)/shard_map/ppermute | solution.py:84
  45.9 32.4 %collective-permute-done.4 = bf16[128,2048]{1,0:T(8,128)(2,1)S(1)} collective-permute-done((bf16[128,2048]{1,0:T(8,128)(2,1)S(1)}, bf16[128,2048]{1,0:T(8,128)(2,1)S(1)}, u32[]{:S(2)}, u32[]{:S(2)}) %collective-permute-start.4) | collective-permute-done | bytes 524320 | tf_op jit(solution)/shard_map/ppermute | solution.py:85
  78.3 1.3 collective-permute-start.5
  80.6 1.1 bitcast_dynamic-update-slice_fusion.4
  82.9 18.9 %collective-permute-done.5 = bf16[128,2048]{1,0:T(8,128)(2,1)S(1)} collective-permute-done((bf16[128,2048]{1,0:T(8,128)(2,1)S(1)}, bf16[128,2048]{1,0:T(8,128)(2,1)S(1)}, u32[]{:S(2)}, u32[]{:S(2)}) %collective-permute-start.5) | collective-permute-done | bytes 524320 | tf_op jit(solution)/shard_map/ppermute | solution.py:85
  102.1 1.5 fusion.26
  103.6 2.5 fusion.63
  106.1 2.0 copy.87
  108.1 2.0 copy.86
  110.2 2.0 copy.85
  112.2 1.8 fusion.39
  114.4 1.3 select_reduce_fusion.1
  115.8 2.1 fusion.60
  117.9 1.2 fusion.20
  119.2 2.3 fusion.27
  122.4 2.0 copy.72
  124.4 2.2 select_n.66
  126.6 4.8 %fusion.14 = bf16[1024,128]{0,1:T(8,128)(2,1)} fusion(f32[1024]{0:T(1024)S(1)} %get-tuple-element.15, bf16[1024,256]{0,1:T(8,128)(2,1)} %select_n.66, f32[1024,1024]{0,1:T(8,128)} %copy-done.8, f32[1024]{0:T(1024)S(1)} %get-tuple-element.17, pred[128,8,8,128]{3,2,1,0:T(8,128)(4,1)} %bitcast.119), kind=kOutput, calls=%fused_computation.24 | convolution fusion | flops 273809408 | bytes 5775360 | tf_op jit(solution)/shard_map/dot_general | solution.py:44
  131.5 1.2 multiply_reduce_fusion.1
  133.4 3.2 %convolution_convert_fusion = bf16[1024,2048]{1,0:T(8,128)(2,1)} fusion(bf16[256,2048]{1,0:T(8,128)(2,1)S(1)} %copy-done, bf16[1024,128]{0,1:T(8,128)(2,1)S(1)} %fusion.20, bf16[1024,128]{0,1:T(8,128)(2,1)S(1)} %get-tuple-element.30), kind=kOutput, calls=%fused_computation.8 | convolution fusion | flops 1076887552 | bytes 5767168 | tf_op jit(solution)/shard_map/dot_general | solution.py:146
  136.7 1.2 copy-done.6
  137.9 3.7 %fusion.17 = bf16[1024,128]{0,1:T(8,128)(2,1)S(1)} fusion(f32[1024]{0:T(1024)S(1)} %get-tuple-element.16, bf16[1024,256]{0,1:T(8,128)(2,1)} %select_n.66, f32[1024,1024]{0,1:T(8,128)} %copy-done.2, f32[1024]{0:T(1024)S(1)} %get-tuple-element.18, pred[128,8,8,128]{3,2,1,0:T(8,128)(4,1)S(1)} %bitcast.121), kind=kOutput, calls=%fused_computation.25 | convolution fusion | flops 273809408 | bytes 5775360 | tf_op jit(solution)/shard_map/dot_general | solution.py:44
  143.8 1.2 convert_reduce_fusion.1
  145.0 3.0 %convert_reduce_fusion = f32[256,2048]{1,0:T(8,128)S(1)} fusion(bf16[4,128,2048]{2,1,0:T(8,128)(2,1)} %collective-permute-done.6, pred[]{:T(512)S(6)} %eq.42, bf16[4,1,128,256]{2,1,0,3:T(2,128)(2,1)S(1)} %get-tuple-element.28, bf16[4,1,128,256]{2,1,0,3:T(2,128)(2,1)S(1)} %get-tuple-element.27), kind=kOutput, calls=%fused_computation | convolution fusion | flops 542769152 | bytes 4718593 | tf_op jit(solution)/shard_map/bnf,bnk->bfk/dot_general | solution.py:163
  148.3 1.5 collective-permute-start.7
  150.9 1.9 multiply_convert_fusion.1
  153.7 2.3 multiply_convert_fusion
  158.6 1.4 pad_maximum_fusion.1
  159.9 4.3 %all-to-all-start.1 = ((bf16[3,8,128,256]{2,3,0,1:T(8,128)(2,1)}), bf16[3,8,128,256]{2,3,0,1:T(8,128)(2,1)}, u32[]{:S(2)}, u32[]{:S(2)}) async-start(bf16[3,8,128,256]{2,3,0,1:T(8,128)(2,1)} %pad_maximum_fusion.1), calls=%async_computation.2 | async-start | bytes 3145728 | tf_op jit(solution)/shard_map/all_to_all | solution.py:190
  164.2 32.3 %collective-permute-done.7 = f32[256,2048]{1,0:T(8,128)} collective-permute-done((f32[256,2048]{1,0:T(8,128)S(1)}, f32[256,2048]{1,0:T(8,128)}, u32[]{:S(2)}, u32[]{:S(2)}) %collective-permute-start.7) | collective-permute-done | bytes 2097184 | tf_op jit(solution)/shard_map/ppermute | solution.py:66
  196.5 3.2 %add.23 = f32[256,2048]{1,0:T(8,128)} add(f32[256,2048]{1,0:T(8,128)S(1)} %add.22, f32[256,2048]{1,0:T(8,128)} %collective-permute-done.7) | non-fusion elementwise | flops 524288 | bytes 6291456 | tf_op jit(solution)/shard_map/add | solution.py:66
  199.7 1.5 collective-permute-start.8
  201.2 17.5 %all-to-all-done.1 = bf16[3,8,128,256]{2,3,0,1:T(8,128)(2,1)} async-done(((bf16[3,8,128,256]{2,3,0,1:T(8,128)(2,1)}), bf16[3,8,128,256]{2,3,0,1:T(8,128)(2,1)}, u32[]{:S(2)}, u32[]{:S(2)}) %all-to-all-start.1) | async-done | bytes 1572896 | tf_op jit(solution)/shard_map/all_to_all | solution.py:190
  218.8 2.5 fusion.62
  222.3 2.1 copy.81
  224.4 2.0 copy.80
  226.4 20.8 %collective-permute-done.8 = f32[256,2048]{1,0:T(8,128)S(1)} collective-permute-done((f32[256,2048]{1,0:T(8,128)}, f32[256,2048]{1,0:T(8,128)S(1)}, u32[]{:S(2)}, u32[]{:S(2)}) %collective-permute-start.8) | collective-permute-done | bytes 2097184 | tf_op jit(solution)/shard_map/ppermute | solution.py:66
  247.2 3.2 %add_multiply_fusion = f32[256,2048]{1,0:T(8,128)} fusion(f32[256,2048]{1,0:T(8,128)} %add.23, f32[256,2048]{1,0:T(8,128)S(1)} %collective-permute-done.8), kind=kLoop, calls=%fused_computation.9 | loop fusion | flops 1048576 | bytes 6291456 | tf_op jit(solution)/shard_map/div | solution.py:172
  (96 shorter events, 13.0 us)
Async XLA Ops:
  7.2 94.9 %copy-start = (bf16[256,2048]{1,0:T(8,128)(2,1)S(1)}, bf16[256,2048]{1,0:T(8,128)(2,1)}, u32[]{:S(2)}) copy-start(bf16[256,2048]{1,0:T(8,128)(2,1)} %param.11) | copy-start | bytes 3145732
  7.2 16.6 %collective-permute-start = (bf16[128,2048]{1,0:T(8,128)(2,1)}, bf16[128,2048]{1,0:T(8,128)(2,1)}, u32[]{:S(2)}, u32[]{:S(2)}) collective-permute-start(bf16[128,2048]{1,0:T(8,128)(2,1)} %bitcast.141), channel_id=1, source_target_pairs={{0,2},{1,3},{2,4},{3,5},{4,6},{5,7},{8,10},{9,11},{10,12},{11,13},... | collective-permute-start | bytes 1572872 | tf_op jit(solution)/shard_map/ppermute | solution.py:84
  13.1 25.6 %collective-permute-start.3 = (bf16[128,2048]{1,0:T(8,128)(2,1)}, bf16[128,2048]{1,0:T(8,128)(2,1)S(1)}, u32[]{:S(2)}, u32[]{:S(2)}) collective-permute-start(bf16[128,2048]{1,0:T(8,128)(2,1)} %bitcast.142), channel_id=1, source_target_pairs={{2,0},{3,1},{4,2},{5,3},{6,4},{7,5},{10,8},{11,9},{12,10},{13,11},... | collective-permute-start | bytes 1572872 | tf_op jit(solution)/shard_map/ppermute | solution.py:85
  23.7 16.3 %collective-permute-start.1 = (bf16[128,2048]{1,0:T(8,128)(2,1)}, bf16[128,2048]{1,0:T(8,128)(2,1)}, u32[]{:S(2)}, u32[]{:S(2)}) collective-permute-start(bf16[128,2048]{1,0:T(8,128)(2,1)} %collective-permute-done), channel_id=1, source_target_pairs={{0,2},{1,3},{2,4},{3,5},{4,6},{5,7},{8,10},{9,11},{10,12},{11,13},... | collective-permute-start | bytes 1572872 | tf_op jit(solution)/shard_map/ppermute | solution.py:84
  32.9 12.5 %copy-start.26 = (s32[1,9]{1,0:T(1,128)S(1)}, s32[1,9]{1,0:T(1,128)}, u32[]{:S(2)}) copy-start(s32[1,9]{1,0:T(1,128)} %param.12) | copy-start | bytes 112
  32.9 12.7 %copy-start.27 = (s32[1,32]{1,0:T(1,128)S(1)}, s32[1,32]{1,0:T(1,128)}, u32[]{:S(2)}) copy-start(s32[1,32]{1,0:T(1,128)} %param.13) | copy-start | bytes 388
  33.1 49.7 %copy-start.18 = (bf16[1,128,2048]{2,1,0:T(8,128)(2,1)S(1)}, bf16[1,128,2048]{2,1,0:T(8,128)(2,1)}, u32[]{:S(2)}) copy-start(bf16[1,128,2048]{2,1,0:T(8,128)(2,1)} %param.10) | copy-start | bytes 1572868
  34.3 69.2 %all-to-all-start = ((bf16[3,8,128,256]{2,3,0,1:T(8,128)(2,1)}), bf16[3,8,128,256]{2,3,0,1:T(8,128)(2,1)}, u32[]{:S(2)}, u32[]{:S(2)}) async-start(bf16[3,8,128,256]{2,3,0,1:T(8,128)(2,1)} %copy.68), calls=%async_computation | async-start | bytes 3145728 | tf_op jit(solution)/shard_map/all_to_all | solution.py:132
  38.6 211.8 %reduce-scatter.2.cloned.1.call-start = ((), (), s32[]{:S(2)}) async-start(), calls=%async_computation.3 | async-start | bytes 4718592 | tf_op jit(solution)/shard_map/reduce_scatter | solution.py:147
  38.7 39.5 %collective-permute-start.4 = (bf16[128,2048]{1,0:T(8,128)(2,1)S(1)}, bf16[128,2048]{1,0:T(8,128)(2,1)S(1)}, u32[]{:S(2)}, u32[]{:S(2)}) collective-permute-start(bf16[128,2048]{1,0:T(8,128)(2,1)S(1)} %collective-permute-done.3), channel_id=1, source_target_pairs={{2,0},{3,1},{4,2},{5,3},{6,4},{7,5},{10,8},{11,9},{12,10},{13,11},... | collective-permute-start | bytes 1572872 | tf_op jit(solution)/shard_map/ppermute | solution.py:85
  40.0 39.5 %collective-permute-start.2 = (bf16[128,2048]{1,0:T(8,128)(2,1)}, bf16[128,2048]{1,0:T(8,128)(2,1)}, u32[]{:S(2)}, u32[]{:S(2)}) collective-permute-start(bf16[128,2048]{1,0:T(8,128)(2,1)} %collective-permute-done.1), channel_id=1, source_target_pairs={{0,2},{1,3},{2,4},{3,5},{4,6},{5,7},{8,10},{9,11},{10,12},{11,13},... | collective-permute-start | bytes 1572872 | tf_op jit(solution)/shard_map/ppermute | solution.py:84
  78.3 23.6 %collective-permute-start.5 = (bf16[128,2048]{1,0:T(8,128)(2,1)S(1)}, bf16[128,2048]{1,0:T(8,128)(2,1)S(1)}, u32[]{:S(2)}, u32[]{:S(2)}) collective-permute-start(bf16[128,2048]{1,0:T(8,128)(2,1)S(1)} %collective-permute-done.4), channel_id=1, source_target_pairs={{2,0},{3,1},{4,2},{5,3},{6,4},{7,5},{10,8},{11,9},{12,10},{13,11},... | collective-permute-start | bytes 1572872 | tf_op jit(solution)/shard_map/ppermute | solution.py:85
  102.0 17.2 %collective-permute-start.6 = (bf16[4,128,2048]{2,1,0:T(8,128)(2,1)S(1)}, bf16[4,128,2048]{2,1,0:T(8,128)(2,1)}, u32[]{:S(2)}, u32[]{:S(2)}) collective-permute-start(bf16[4,128,2048]{2,1,0:T(8,128)(2,1)S(1)} %constant_dynamic-slice_fusion), channel_id=1, source_target_pairs={{0,1},{1,0},{2,3},{3,2},{4,5},{5,4},{6,7},{7,6},{8,9},{9,8},{10,11... | collective-permute-start | bytes 6291464 | tf_op jit(solution)/shard_map/ppermute | solution.py:90
  112.2 2.2 copy-start.11
  112.2 2.2 copy-start.14
  114.1 3.8 %copy-start.2 = (f32[1024,1024]{0,1:T(8,128)}, f32[1024,1024]{0,1:T(8,128)S(1)}, u32[]{:S(2)}) copy-start(f32[1024,1024]{0,1:T(8,128)S(1)} %fusion.39) | copy-start | bytes 12582916
  114.4 3.5 %copy-start.4 = (pred[8,128,8,128]{1,0,3,2:T(8,128)(4,1)}, pred[8,128,8,128]{1,0,3,2:T(8,128)(4,1)S(1)}, u32[]{:S(2)}) copy-start(pred[8,128,8,128]{1,0,3,2:T(8,128)(4,1)S(1)} %broadcast_in_dim.13) | copy-start | bytes 3145732
  115.8 2.1 copy-start.8
  115.8 2.2 copy-start.19
  117.9 3.6 %copy-start.24 = (bf16[4,1,128,256]{3,2,0,1:T(8,128)(2,1)S(1)}, bf16[4,1,128,256]{3,2,0,1:T(8,128)(2,1)}, u32[]{:S(2)}) copy-start(bf16[4,1,128,256]{3,2,0,1:T(8,128)(2,1)} %fusion.26) | copy-start | bytes 786436
  126.6 4.9 %copy-start.5 = (pred[8,128,8,128]{1,0,3,2:T(8,128)(4,1)S(1)}, pred[8,128,8,128]{1,0,3,2:T(8,128)(4,1)}, u32[]{:S(2)}) copy-start(pred[8,128,8,128]{1,0,3,2:T(8,128)(4,1)} %copy-done.4) | copy-start | bytes 3145732
  126.6 4.9 %copy-start.9 = (f32[1024,1024]{0,1:T(8,128)S(1)}, f32[1024,1024]{0,1:T(8,128)}, u32[]{:S(2)}) copy-start(f32[1024,1024]{0,1:T(8,128)} %copy-done.8) | copy-start | bytes 12582916
  126.6 4.9 %copy-start.20 = (bf16[1,8,128,256]{3,2,1,0:T(8,128)(2,1)S(1)}, bf16[1,8,128,256]{3,2,1,0:T(8,128)(2,1)}, u32[]{:S(2)}) copy-start(bf16[1,8,128,256]{3,2,1,0:T(8,128)(2,1)} %copy.87) | copy-start | bytes 1572868
  126.6 4.9 %copy-start.22 = (bf16[1024,256]{0,1:T(8,128)(2,1)S(1)}, bf16[1024,256]{0,1:T(8,128)(2,1)}, u32[]{:S(2)}) copy-start(bf16[1024,256]{0,1:T(8,128)(2,1)} %select_n.66) | copy-start | bytes 1572868
  132.7 0.7 copy-start.16
  136.6 1.2 copy-start.6
  137.9 3.8 %copy-start.25 = (bf16[1024,128]{0,1:T(8,128)(2,1)S(1)}, bf16[1024,128]{0,1:T(8,128)(2,1)}, u32[]{:S(2)}) copy-start(bf16[1024,128]{0,1:T(8,128)(2,1)} %fusion.14) | copy-start | bytes 786436
  137.9 4.8 %copy-start.17 = (bf16[1024,128]{0,1:T(8,128)(2,1)S(1)}, bf16[1024,128]{0,1:T(8,128)(2,1)}, u32[]{:S(2)}) copy-start(bf16[1024,128]{0,1:T(8,128)(2,1)} %copy-done.16) | copy-start | bytes 786436
  148.0 1.8 copy-start.7
  148.0 2.6 copy-start.10
  148.0 2.7 %copy-start.21 = (bf16[1,8,128,256]{3,2,1,0:T(8,128)(2,1)S(1)}, bf16[1,8,128,256]{3,2,1,0:T(8,128)(2,1)}, u32[]{:S(2)}) copy-start(bf16[1,8,128,256]{3,2,1,0:T(8,128)(2,1)} %copy.87) | copy-start | bytes 1572868
  148.0 2.8 %copy-start.23 = (bf16[1024,256]{0,1:T(8,128)(2,1)S(1)}, bf16[1024,256]{0,1:T(8,128)(2,1)}, u32[]{:S(2)}) copy-start(bf16[1024,256]{0,1:T(8,128)(2,1)} %select_n.66) | copy-start | bytes 1572868
  148.3 48.2 %collective-permute-start.7 = (f32[256,2048]{1,0:T(8,128)S(1)}, f32[256,2048]{1,0:T(8,128)}, u32[]{:S(2)}, u32[]{:S(2)}) collective-permute-start(f32[256,2048]{1,0:T(8,128)S(1)} %add.22), channel_id=1, source_target_pairs={{0,8},{8,0},{16,24},{24,16},{1,9},{9,1},{17,25},{25,17},{2,10},{10... | collective-permute-start | bytes 6291464 | tf_op jit(solution)/shard_map/ppermute | solution.py:66
  150.9 1.9 copy-start.12
  150.9 2.8 %copy-start.3 = (f32[1024,1024]{0,1:T(8,128)S(1)}, f32[1024,1024]{0,1:T(8,128)}, u32[]{:S(2)}) copy-start(f32[1024,1024]{0,1:T(8,128)} %copy-done.2) | copy-start | bytes 12582916
  155.9 1.1 copy-start.15
  157.5 1.1 copy-start.13
  159.9 58.9 %all-to-all-start.1 = ((bf16[3,8,128,256]{2,3,0,1:T(8,128)(2,1)}), bf16[3,8,128,256]{2,3,0,1:T(8,128)(2,1)}, u32[]{:S(2)}, u32[]{:S(2)}) async-start(bf16[3,8,128,256]{2,3,0,1:T(8,128)(2,1)} %pad_maximum_fusion.1), calls=%async_computation.2 | async-start | bytes 3145728 | tf_op jit(solution)/shard_map/all_to_all | solution.py:190
  199.7 47.5 %collective-permute-start.8 = (f32[256,2048]{1,0:T(8,128)}, f32[256,2048]{1,0:T(8,128)S(1)}, u32[]{:S(2)}, u32[]{:S(2)}) collective-permute-start(f32[256,2048]{1,0:T(8,128)} %add.23), channel_id=1, source_target_pairs={{0,16},{8,24},{16,0},{24,8},{1,17},{9,25},{17,1},{25,9},{2,18},{10... | collective-permute-start | bytes 6291464 | tf_op jit(solution)/shard_map/ppermute | solution.py:66
  222.3 28.1 %copy-start.1 = (bf16[256,2048]{1,0:T(8,128)(2,1)S(1)}, bf16[256,2048]{1,0:T(8,128)(2,1)}, u32[]{:S(2)}) copy-start(bf16[256,2048]{1,0:T(8,128)(2,1)} %param.11) | copy-start | bytes 3145732
Sparse Core Ops, SparseCore 0:
  136.8 64.0 reduce-scatter.1

commit v6 on v4

--- a/solution.py
+++ b/solution.py
@@ -66,6 +66,35 @@
         values = values + lax.ppermute(values, "dp", pairs)
         step *= 2
     return values
+
+
+def chip_layer_out(att_flat, w_out):
+    n = lax.axis_size("seq")
+    rows = att_flat.shape[0] // n
+    chips = n // 2
+    s = lax.axis_index("seq")
+    core = s % 2
+    z = s // 2
+    sibling = [(i, i ^ 1) for i in range(n)]
+    att_sib = lax.ppermute(att_flat, "seq", sibling)
+    w_sib = lax.ppermute(w_out, "seq", sibling)
+
+    def parity_rows(values):
+        quads = values.reshape(chips, 2, rows, values.shape[1])
+        return jnp.where(core == 0, quads[:, 0], quads[:, 1])
+
+    att_chip = jnp.concatenate([parity_rows(att_flat), parity_rows(att_sib)], axis=2)
+    w_chip = jnp.concatenate([w_out, w_sib], axis=0)
+    chip_partial = lax.dot_general(
+        att_chip, w_chip, (((2,), (0,)), ((), ())), preferred_element_type=jnp.float32
+    )
+    total = lax.dynamic_index_in_dim(chip_partial, z, 0, keepdims=False)
+    sent = chip_partial.astype(jnp.bfloat16)
+    for k in range(1, chips):
+        pairs = [(i, ((i // 2 + k) % chips) * 2 + i % 2) for i in range(n)]
+        piece = lax.dynamic_index_in_dim(sent, (z + k) % chips, 0, keepdims=False)
+        total = total + lax.ppermute(piece, "seq", pairs).astype(jnp.float32)
+    return total
 
 
 def shards(
@@ -113,10 +142,7 @@
     ]
     att_flat = jnp.concatenate([f[0] for f in fwd], axis=1)
 
-    partial = jnp.dot(att_flat, w_out, preferred_element_type=jnp.float32)
-    layer_out = lax.psum_scatter(
-        partial.astype(jnp.bfloat16), "seq", scatter_dimension=0, tiled=True
-    )[None]
+    layer_out = chip_layer_out(att_flat, w_out).astype(jnp.bfloat16)[None]
 
     g_flat = lax.dot_general(
         grad_full, w_out, (((1,), (1,)), ((), ())), preferred_element_type=jnp.float32

time: 225 us -> 238 us (1.058)
  the two profiles are of different devices: /device:TPU:0 before, /device:TPU:8 now
where the time goes in v6:
time: 238 us; the launch traced here: 237 us
  waiting for transfers between devices  135 us (57%)
  local copies, waits for them, and re-layouts  26.4 us (11%)
  matrix products  25.1 us (11%)
  starting transfers between devices  22.3 us (9%)
  between operations  14.5 us (6%)
  other arithmetic  13.5 us (6%)
    all_to_all x1, waiting for transfers between devices, shards(): lax.all_to_all(stacked, 'seq', split_axis=1, concat_axis=1, tiled=True)  67.4 us
    ppermute x3, waiting for transfers between devices, chip_layer_out(): total = total + lax.ppermute(piece, 'seq', pairs).astype(jnp.float32)  43.2 us
    ppermute x2, waiting for transfers between devices, dp_sum(): values = values + lax.ppermute(values, 'dp', pairs)  23.8 us
    unnamed x46, local copies, waits for them, and re-layouts  16.1 us
    all_to_all x1, starting transfers between devices, shards(): back = lax.all_to_all(grads, 'seq', split_axis=1, concat_axis=1, tiled=True)  7.65 us
    ppermute x3, starting transfers between devices, chip_layer_out(): total = total + lax.ppermute(piece, 'seq', pairs).astype(jnp.float32)  5.41 us
    all_to_all x1, starting transfers between devices, shards(): lax.all_to_all(stacked, 'seq', split_axis=1, concat_axis=1, tiled=True)  5.32 us
  transfers between devices with their start and end apart: 10, of which 5 were waited for; matrix products, arithmetic and copies ran while one was open for 19% of the time, Pallas kernels for 0%

profile of v6, /device:TPU:8, one launch (start us, length us, event | category | flops | bytes accessed | tf_op | source)
XLA Modules:
  0.0 236.9 jit_solution(3467364240547550284)
XLA Ops:
  7.9 1.3 copy.75
  9.2 1.3 copy.73
  10.5 1.3 copy.74
  12.1 1.2 copy.76
  13.3 5.3 %all-to-all-start = ((bf16[3,8,128,256]{2,3,0,1:T(8,128)(2,1)}), bf16[3,8,128,256]{2,3,0,1:T(8,128)(2,1)S(1)}, u32[]{:S(2)}, u32[]{:S(2)}) async-start(bf16[3,8,128,256]{2,3,0,1:T(8,128)(2,1)} %copy.76), calls=%async_computation | async-start | bytes 3145728 | tf_op jit(solution)/shard_map/all_to_all | solution.py:131
  19.1 67.4 %all-to-all-done = bf16[3,8,128,256]{2,3,0,1:T(8,128)(2,1)S(1)} async-done(((bf16[3,8,128,256]{2,3,0,1:T(8,128)(2,1)}), bf16[3,8,128,256]{2,3,0,1:T(8,128)(2,1)S(1)}, u32[]{:S(2)}, u32[]{:S(2)}) %all-to-all-start) | async-done | bytes 1572896 | tf_op jit(solution)/shard_map/all_to_all | solution.py:131
  87.2 1.0 copy.97
  88.2 0.7 fusion.46
  89.2 1.3 select_reduce_fusion.1
  90.6 2.2 fusion.65
  92.9 1.2 fusion.28
  94.2 3.6 %fusion.13 = bf16[1024,256]{0,1:T(8,128)(2,1)S(1)} fusion(bf16[256,2048]{1,0:T(8,128)(2,1)S(1)} %copy-done.6, bf16[1,1024,2048]{2,1,0:T(8,128)(2,1)} %all-gather.3.cloned.1.call-done), kind=kOutput, calls=%fused_computation.26 | convolution fusion | flops 1074003968 | bytes 5767168 | tf_op jit(solution)/shard_map/dot_general | solution.py:147
  97.8 1.3 multiply_reduce_fusion.1
  99.1 2.0 multiply_convert_fusion.1
  101.7 0.8 convolution_convert_fusion.1
  102.5 0.8 copy-done.1
  103.4 2.1 multiply_convert_fusion
  106.0 0.8 convolution_convert_fusion
  106.9 1.5 fusion.22
  108.4 0.9 fusion.64
  109.3 2.3 convert_reduce_fusion
  111.7 1.7 collective-permute-start.5
  113.8 1.5 fusion.25
  115.6 1.4 pad_maximum_fusion.1
  117.0 7.7 %all-to-all-start.1 = ((bf16[3,8,128,256]{2,3,0,1:T(8,128)(2,1)}), bf16[3,8,128,256]{2,3,0,1:T(8,128)(2,1)}, u32[]{:S(2)}, u32[]{:S(2)}) async-start(bf16[3,8,128,256]{2,3,0,1:T(8,128)(2,1)} %pad_maximum_fusion.1), calls=%async_computation.1 | async-start | bytes 3145728 | tf_op jit(solution)/shard_map/all_to_all | solution.py:176
  125.5 1.7 fusion.69
  127.2 1.2 copy.98
  128.4 1.9 copy.99
  130.3 1.4 reshape.56
  131.7 1.5 fusion.70
  133.2 1.3 copy.100
  134.5 1.1 copy.101
  135.6 23.8 %collective-permute-done.5 = f32[256,2048]{1,0:T(8,128)} collective-permute-done((f32[256,2048]{1,0:T(8,128)S(1)}, f32[256,2048]{1,0:T(8,128)}, u32[]{:S(2)}, u32[]{:S(2)}) %collective-permute-start.5) | collective-permute-done | bytes 2097184 | tf_op jit(solution)/shard_map/ppermute | solution.py:66
  159.4 2.5 %add.66 = f32[256,2048]{1,0:T(8,128)S(1)} add(f32[256,2048]{1,0:T(8,128)} %copy-done.4, f32[256,2048]{1,0:T(8,128)} %collective-permute-done.5) | non-fusion elementwise | flops 524288 | bytes 6291456 | tf_op jit(solution)/shard_map/add | solution.py:66
  161.9 1.7 collective-permute-start.6
  163.7 4.5 %fusion.71 = (bf16[4,128,2048]{2,1,0:T(8,128)(2,1)S(1)}, f32[4,128,2048]{2,1,0:T(8,128)}) fusion(bf16[256,2048]{1,0:T(8,128)(2,1)} %collective-permute-done.1, bf16[256,2048]{1,0:T(8,128)(2,1)S(1)} %copy-done.7, bf16[4,128,256]{2,1,0:T(8,128)(2,1)S(1)} %get-tuple-element.40, bf16[4,128,256]{2,1,0:T(8,128)(2,1)S(1)} %get-tuple-element.41), kind=kOutput, calls=%fused_computation.92 | convolution fusion | flops 1080033280 | bytes 8912896 | tf_op jit(solution)/shard_map/dot_general | solution.py:88
  168.2 0.9 dynamic-slice_bitcast_fusion.2
  169.1 1.1 collective-permute-start.2
  170.2 4.3 %collective-permute-start.3 = (bf16[128,2048]{1,0:T(8,128)(2,1)S(1)}, bf16[128,2048]{1,0:T(8,128)(2,1)}, u32[]{:S(2)}, u32[]{:S(2)}) collective-permute-start(bf16[128,2048]{1,0:T(8,128)(2,1)S(1)} %get-tuple-element.23), channel_id=1, source_target_pairs={{0,4},{1,5},{2,6},{3,7},{4,0},{5,1},{6,2},{7,3},{8,12},{9,13},{10,... | collective-permute-start | bytes 1572872 | tf_op jit(solution)/shard_map/ppermute | solution.py:96
  174.5 30.9 %collective-permute-done.2 = bf16[128,2048]{1,0:T(8,128)(2,1)} collective-permute-done((bf16[128,2048]{1,0:T(8,128)(2,1)}, bf16[128,2048]{1,0:T(8,128)(2,1)}, u32[]{:S(2)}, u32[]{:S(2)}) %collective-permute-start.2) | collective-permute-done | bytes 524320 | tf_op jit(solution)/shard_map/ppermute | solution.py:96
  205.4 8.4 %collective-permute-done.3 = bf16[128,2048]{1,0:T(8,128)(2,1)} collective-permute-done((bf16[128,2048]{1,0:T(8,128)(2,1)S(1)}, bf16[128,2048]{1,0:T(8,128)(2,1)}, u32[]{:S(2)}, u32[]{:S(2)}) %collective-permute-start.3) | collective-permute-done | bytes 524320 | tf_op jit(solution)/shard_map/ppermute | solution.py:96
  213.8 4.0 %collective-permute-done.4 = bf16[128,2048]{1,0:T(8,128)(2,1)} collective-permute-done((bf16[128,2048]{1,0:T(8,128)(2,1)S(1)}, bf16[128,2048]{1,0:T(8,128)(2,1)}, u32[]{:S(2)}, u32[]{:S(2)}) %collective-permute-start.4) | collective-permute-done | bytes 524320 | tf_op jit(solution)/shard_map/ppermute | solution.py:96
  217.8 2.8 %fusion.37 = bf16[1,128,2048]{2,1,0:T(8,128)(2,1)} fusion(bf16[128,2048]{1,0:T(8,128)(2,1)} %collective-permute-done.4, bf16[128,2048]{1,0:T(8,128)(2,1)} %collective-permute-done.3, bf16[128,2048]{1,0:T(8,128)(2,1)} %collective-permute-done.2, f32[4,128,2048]{2,1,0:T(8,128)} %get-tuple-element.38, s32[]{:T(128)S(6)} %select_n.79), kind=kLoop, calls=%fused_computation.42 | loop fusion | flops 1835008 | bytes 3145732 | tf_op jit(solution)/shard_map/broadcast_in_dim | solution.py:145
  220.6 2.3 fusion.67
  222.8 2.0 copy.90
  224.9 1.0 copy.91
  225.9 1.0 copy.92
  226.9 3.2 %add_multiply_fusion = f32[256,2048]{1,0:T(8,128)} fusion(f32[256,2048]{1,0:T(8,128)S(1)} %add.66, f32[256,2048]{1,0:T(8,128)} %collective-permute-done.6), kind=kLoop, calls=%fused_computation.13 | loop fusion | flops 1048576 | bytes 6291456 | tf_op jit(solution)/shard_map/div | solution.py:158
  (61 shorter events, 5.0 us)
Async XLA Ops:
  7.2 87.0 %all-gather.3.cloned.1.call-start = ((), (), s32[]{:S(2)}) async-start(), calls=%async_computation.2 | async-start | bytes 4718592 | tf_op jit(solution)/shard_map/all_gather | solution.py:115
  11.9 6.8 %copy-start.13 = (s32[1,9]{1,0:T(1,128)S(1)}, s32[1,9]{1,0:T(1,128)}, u32[]{:S(2)}) copy-start(s32[1,9]{1,0:T(1,128)} %param.12) | copy-start | bytes 112
  11.9 6.9 %copy-start.14 = (s32[1,32]{1,0:T(1,128)S(1)}, s32[1,32]{1,0:T(1,128)}, u32[]{:S(2)}) copy-start(s32[1,32]{1,0:T(1,128)} %param.13) | copy-start | bytes 388
  13.3 73.2 %all-to-all-start = ((bf16[3,8,128,256]{2,3,0,1:T(8,128)(2,1)}), bf16[3,8,128,256]{2,3,0,1:T(8,128)(2,1)S(1)}, u32[]{:S(2)}, u32[]{:S(2)}) async-start(bf16[3,8,128,256]{2,3,0,1:T(8,128)(2,1)} %copy.76), calls=%async_computation | async-start | bytes 3145728 | tf_op jit(solution)/shard_map/all_to_all | solution.py:131
  88.9 4.0 %copy-start = (f32[1024,1024]{0,1:T(8,128)}, f32[1024,1024]{0,1:T(8,128)S(1)}, u32[]{:S(2)}) copy-start(f32[1024,1024]{0,1:T(8,128)S(1)} %fusion.46) | copy-start | bytes 12582916
  90.6 2.3 copy-start.2
  90.6 2.3 copy-start.10
  92.9 1.3 copy-start.6
  94.2 3.6 %copy-start.3 = (f32[1024,1024]{0,1:T(8,128)S(1)}, f32[1024,1024]{0,1:T(8,128)}, u32[]{:S(2)}) copy-start(f32[1024,1024]{0,1:T(8,128)} %copy-done.2) | copy-start | bytes 12582916
  94.2 3.6 %copy-start.11 = (bf16[1,8,128,256]{3,2,1,0:T(8,128)(2,1)S(1)}, bf16[1,8,128,256]{3,2,1,0:T(8,128)(2,1)}, u32[]{:S(2)}) copy-start(bf16[1,8,128,256]{3,2,1,0:T(8,128)(2,1)} %copy.97) | copy-start | bytes 1572868
  101.2 2.2 copy-start.1
  106.9 2.5 %copy-start.12 = (bf16[1,1024,2048]{2,1,0:T(8,128)(2,1)S(1)}, bf16[1,1024,2048]{2,1,0:T(8,128)(2,1)}, u32[]{:S(2)}) copy-start(bf16[1,1024,2048]{2,1,0:T(8,128)(2,1)} %all-gather.3.cloned.1.call-done) | copy-start | bytes 12582916
  111.6 3.7 %copy-start.4 = (f32[256,2048]{1,0:T(8,128)}, f32[256,2048]{1,0:T(8,128)S(1)}, u32[]{:S(2)}) copy-start(f32[256,2048]{1,0:T(8,128)S(1)} %convert_reduce_fusion) | copy-start | bytes 6291460
  111.7 47.8 %collective-permute-start.5 = (f32[256,2048]{1,0:T(8,128)S(1)}, f32[256,2048]{1,0:T(8,128)}, u32[]{:S(2)}, u32[]{:S(2)}) collective-permute-start(f32[256,2048]{1,0:T(8,128)S(1)} %convert_reduce_fusion), channel_id=1, source_target_pairs={{0,8},{8,0},{16,24},{24,16},{1,9},{9,1},{17,25},{25,17},{2,10},{10... | collective-permute-start | bytes 6291464 | tf_op jit(solution)/shard_map/ppermute | solution.py:66
  115.4 9.3 %copy-start.5 = (bf16[1024,256]{0,1:T(8,128)(2,1)S(1)}, bf16[1024,256]{0,1:T(8,128)(2,1)}, u32[]{:S(2)}) copy-start(bf16[1024,256]{0,1:T(8,128)(2,1)} %get-tuple-element.31) | copy-start | bytes 1572868
  117.0 103.6 %all-to-all-start.1 = ((bf16[3,8,128,256]{2,3,0,1:T(8,128)(2,1)}), bf16[3,8,128,256]{2,3,0,1:T(8,128)(2,1)}, u32[]{:S(2)}, u32[]{:S(2)}) async-start(bf16[3,8,128,256]{2,3,0,1:T(8,128)(2,1)} %pad_maximum_fusion.1), calls=%async_computation.1 | async-start | bytes 3145728 | tf_op jit(solution)/shard_map/all_to_all | solution.py:176
  124.6 5.7 %collective-permute-start = (bf16[1024,256]{0,1:T(8,128)(2,1)S(1)}, bf16[1024,256]{0,1:T(8,128)(2,1)}, u32[]{:S(2)}, u32[]{:S(2)}) collective-permute-start(bf16[1024,256]{0,1:T(8,128)(2,1)S(1)} %copy-done.5), channel_id=1, source_target_pairs={{0,1},{1,0},{2,3},{3,2},{4,5},{5,4},{6,7},{7,6},{8,9},{9,8},{10,11... | collective-permute-start | bytes 1572872 | tf_op jit(solution)/shard_map/ppermute | solution.py:79
  124.8 38.9 %collective-permute-start.1 = (bf16[256,2048]{1,0:T(8,128)(2,1)}, bf16[256,2048]{1,0:T(8,128)(2,1)}, u32[]{:S(2)}, u32[]{:S(2)}) collective-permute-start(bf16[256,2048]{1,0:T(8,128)(2,1)} %param.11), channel_id=1, source_target_pairs={{0,1},{1,0},{2,3},{3,2},{4,5},{5,4},{6,7},{7,6},{8,9},{9,8},{10,11... | collective-permute-start | bytes 3145736 | tf_op jit(solution)/shard_map/ppermute | solution.py:80
  133.2 30.4 %copy-start.8 = (bf16[4,1,128,256]{3,2,0,1:T(8,128)(2,1)S(1)}, bf16[4,1,128,256]{3,2,0,1:T(8,128)(2,1)}, u32[]{:S(2)}) copy-start(bf16[4,1,128,256]{3,2,0,1:T(8,128)(2,1)} %copy.99) | copy-start | bytes 786436
  135.6 28.0 %copy-start.9 = (bf16[4,1,128,256]{3,2,0,1:T(8,128)(2,1)S(1)}, bf16[4,1,128,256]{3,2,0,1:T(8,128)(2,1)}, u32[]{:S(2)}) copy-start(bf16[4,1,128,256]{3,2,0,1:T(8,128)(2,1)} %copy.101) | copy-start | bytes 786436
  135.6 28.0 %copy-start.7 = (bf16[256,2048]{1,0:T(8,128)(2,1)S(1)}, bf16[256,2048]{1,0:T(8,128)(2,1)}, u32[]{:S(2)}) copy-start(bf16[256,2048]{1,0:T(8,128)(2,1)} %param.11) | copy-start | bytes 3145732
  161.9 65.0 %collective-permute-start.6 = (f32[256,2048]{1,0:T(8,128)S(1)}, f32[256,2048]{1,0:T(8,128)}, u32[]{:S(2)}, u32[]{:S(2)}) collective-permute-start(f32[256,2048]{1,0:T(8,128)S(1)} %add.66), channel_id=1, source_target_pairs={{0,16},{8,24},{16,0},{24,8},{1,17},{9,25},{17,1},{25,9},{2,18},{10... | collective-permute-start | bytes 6291464 | tf_op jit(solution)/shard_map/ppermute | solution.py:66
  169.1 36.3 %collective-permute-start.2 = (bf16[128,2048]{1,0:T(8,128)(2,1)}, bf16[128,2048]{1,0:T(8,128)(2,1)}, u32[]{:S(2)}, u32[]{:S(2)}) collective-permute-start(bf16[128,2048]{1,0:T(8,128)(2,1)} %get-tuple-element.21), channel_id=1, source_target_pairs={{0,2},{1,3},{2,4},{3,5},{4,6},{5,7},{6,0},{7,1},{8,10},{9,11},{10,... | collective-permute-start | bytes 1572872 | tf_op jit(solution)/shard_map/ppermute | solution.py:96
  170.2 43.5 %collective-permute-start.3 = (bf16[128,2048]{1,0:T(8,128)(2,1)S(1)}, bf16[128,2048]{1,0:T(8,128)(2,1)}, u32[]{:S(2)}, u32[]{:S(2)}) collective-permute-start(bf16[128,2048]{1,0:T(8,128)(2,1)S(1)} %get-tuple-element.23), channel_id=1, source_target_pairs={{0,4},{1,5},{2,6},{3,7},{4,0},{5,1},{6,2},{7,3},{8,12},{9,13},{10,... | collective-permute-start | bytes 1572872 | tf_op jit(solution)/shard_map/ppermute | solution.py:96
  174.5 43.3 %collective-permute-start.4 = (bf16[128,2048]{1,0:T(8,128)(2,1)S(1)}, bf16[128,2048]{1,0:T(8,128)(2,1)}, u32[]{:S(2)}, u32[]{:S(2)}) collective-permute-start(bf16[128,2048]{1,0:T(8,128)(2,1)S(1)} %get-tuple-element.22), channel_id=1, source_target_pairs={{0,6},{1,7},{2,0},{3,1},{4,2},{5,3},{6,4},{7,5},{8,14},{9,15},{10,... | collective-permute-start | bytes 1572872 | tf_op jit(solution)/shard_map/ppermute | solution.py:96
Sparse Core Ops, SparseCore 0:
  9.6 76.9 all-gather.2

commit v7 on v6

--- a/solution.py
+++ b/solution.py
@@ -54,18 +54,6 @@
         k_grad.astype(jnp.bfloat16),
         v_grad.astype(jnp.bfloat16),
     )
-
-
-def dp_sum(values):
-    n_dp = lax.axis_size("dp")
-    if n_dp & (n_dp - 1):
-        return lax.psum(values, "dp")
-    step = 1
-    while step < n_dp:
-        pairs = [(i, i ^ step) for i in range(n_dp)]
-        values = values + lax.ppermute(values, "dp", pairs)
-        step *= 2
-    return values
 
 
 def chip_layer_out(att_flat, w_out):
@@ -153,7 +141,7 @@
         "bnf,bnk->bfk", att_blocks, grad_blocks, preferred_element_type=jnp.float32
     ).astype(jnp.bfloat16)
     w_rows = jnp.sum(terms.astype(jnp.float32), axis=0)
-    w_rows = dp_sum(w_rows)
+    w_rows = lax.psum(w_rows.astype(jnp.bfloat16), "dp").astype(jnp.float32)
     batch = asking_vectors_matrix.shape[0] * lax.axis_size("dp")
     w_out_grad = w_rows / batch
 

time: 238 us -> 221 us (0.929)
  the two profiles are of different devices: /device:TPU:8 before, /device:TPU:0 now
where the time goes in v7:
time: 221 us
  waiting for transfers between devices  128 us (58%)
  matrix products  32 us (14%)
  local copies, waits for them, and re-layouts  18.5 us (8%)
  starting transfers between devices  15.4 us (7%)
  between operations  14.5 us (7%)
  other arithmetic  12.6 us (6%)
    all_to_all x1, waiting for transfers between devices, shards(): lax.all_to_all(stacked, 'seq', split_axis=1, concat_axis=1, tiled=True)  70.5 us
    psum x1, waiting for transfers between devices, shards(): w_rows = lax.psum(w_rows.astype(jnp.bfloat16), 'dp').astype(jnp.float32)  36.3 us
    ppermute x3, waiting for transfers between devices, chip_layer_out(): total = total + lax.ppermute(piece, 'seq', pairs).astype(jnp.float32)  20.2 us
    unnamed x38, local copies, waits for them, and re-layouts  12 us
    all_to_all x1, starting transfers between devices, shards(): lax.all_to_all(stacked, 'seq', split_axis=1, concat_axis=1, tiled=True)  6.33 us
    dot_general x1, matrix products, shards(): jnp.einsum('bnf,bnk->bfk', att_blocks, grad_blocks, preferred_element_typ...  5.71 us
    ppermute x3, starting transfers between devices, chip_layer_out(): total = total + lax.ppermute(piece, 'seq', pairs).astype(jnp.float32)  4.87 us
    dot_general x1, matrix products, chip_layer_out(): lax.dot_general(att_chip, w_chip, (((2,), (0,)), ((), ())), preferred_ele...  4.75 us
  transfers between devices with their start and end apart: 9, of which 3 were waited for; matrix products, arithmetic and copies ran while one was open for 27% of the time, Pallas kernels for 0%

profile of v7, /device:TPU:0, one launch (start us, length us, event | category | flops | bytes accessed | tf_op | source)
XLA Modules:
  0.0 220.7 jit_solution(16444093942752190734)
XLA Ops:
  7.2 0.7 all-gather.3.cloned.1.call-update
  7.9 1.3 copy.73
  9.2 1.3 copy.74
  10.5 1.3 copy.75
  12.1 1.2 copy.76
  13.3 6.3 %all-to-all-start = ((bf16[3,8,128,256]{2,3,0,1:T(8,128)(2,1)}), bf16[3,8,128,256]{2,3,0,1:T(8,128)(2,1)S(1)}, u32[]{:S(2)}, u32[]{:S(2)}) async-start(bf16[3,8,128,256]{2,3,0,1:T(8,128)(2,1)} %copy.76), calls=%async_computation | async-start | bytes 3145728 | tf_op jit(solution)/shard_map/all_to_all | solution.py:119
  19.6 0.5 collective-permute-start.1
  20.7 70.5 %all-to-all-done = bf16[3,8,128,256]{2,3,0,1:T(8,128)(2,1)S(1)} async-done(((bf16[3,8,128,256]{2,3,0,1:T(8,128)(2,1)}), bf16[3,8,128,256]{2,3,0,1:T(8,128)(2,1)S(1)}, u32[]{:S(2)}, u32[]{:S(2)}) %all-to-all-start) | async-done | bytes 1572896 | tf_op jit(solution)/shard_map/all_to_all | solution.py:119
  91.3 1.0 copy.97
  92.8 0.7 fusion.46
  93.8 1.3 select_reduce_fusion.1
  95.2 2.2 %fusion.65 = (f32[1024]{0:T(1024)S(1)}, f32[1024]{0:T(1024)S(1)}) fusion(f32[1024]{0:T(1024)S(1)} %get-tuple-element.17, f32[1024,1024]{0,1:T(8,128)S(1)} %get-tuple-element.36, pred[128,8,8,128]{3,2,1,0:T(8,128)(4,1)S(1)} %bitcast.124, f32[1024]{0:T(1024)S(1)} %get-tuple-element.18, f32[1024,1024]{0,1:T(8,128)S(1)} %fusion.46), kind=kLoop, calls=%fused_computation.86 | loop fusion | flops 8386560 | bytes 9453568 | tf_op jit(solution)/shard_map/reduce_sum | solution.py:34
  97.5 1.2 fusion.28
  98.8 3.9 %fusion.13 = bf16[1024,256]{0,1:T(8,128)(2,1)S(1)} fusion(bf16[256,2048]{1,0:T(8,128)(2,1)} %param.11, bf16[1,1024,2048]{2,1,0:T(8,128)(2,1)} %all-gather.3.cloned.1.call-done), kind=kOutput, calls=%fused_computation.26 | convolution fusion | flops 1074003968 | bytes 5767168 | tf_op jit(solution)/shard_map/dot_general | solution.py:135
  102.7 2.2 %fusion.25 = bf16[1024,128]{0,1:T(8,128)(2,1)} fusion(f32[1024]{0:T(1024)S(1)} %get-tuple-element.16, bf16[1024,256]{0,1:T(8,128)(2,1)S(1)} %fusion.13, f32[1024,1024]{0,1:T(8,128)S(1)} %copy-done.1, f32[1024]{0:T(1024)S(1)} %get-tuple-element.18, pred[128,8,8,128]{3,2,1,0:T(8,128)(4,1)S(1)} %bitcast.126), kind=kOutput, calls=%fused_computation.30 | convolution fusion | flops 273809408 | bytes 5775360 | tf_op jit(solution)/shard_map/dot_general | solution.py:44
  105.0 2.2 %fusion.22 = bf16[1024,128]{0,1:T(8,128)(2,1)} fusion(f32[1024]{0:T(1024)S(1)} %get-tuple-element.15, bf16[1024,256]{0,1:T(8,128)(2,1)S(1)} %fusion.13, f32[1024,1024]{0,1:T(8,128)S(1)} %copy-done.3, f32[1024]{0:T(1024)S(1)} %get-tuple-element.17, pred[128,8,8,128]{3,2,1,0:T(8,128)(4,1)S(1)} %bitcast.127), kind=kOutput, calls=%fused_computation.29 | convolution fusion | flops 273809408 | bytes 5775360 | tf_op jit(solution)/shard_map/dot_general | solution.py:44
  107.2 1.3 multiply_reduce_fusion.1
  108.5 2.2 %multiply_convert_fusion.1 = bf16[1024,1024]{0,1:T(8,128)(2,1)S(1)} fusion(f32[1024]{0:T(1024)S(1)} %get-tuple-element.19, f32[1024]{0:T(1024)S(1)} %get-tuple-element.15, bf16[1024,256]{1,0:T(8,128)(2,1)S(1)} %bitcast.150, bf16[1024,256]{0,1:T(8,128)(2,1)S(1)} %fusion.13, f32[1024]{0:T(1024)S(1)} %get-tuple-element.17, f32[1024,1024]{0,1:T(8,128)S(1)} %copy-done.3, ...), kind=kOutput, calls=%fused_computation.4 | convolution fusion | flops 276824064 | bytes 7876608 | tf_op jit(solution)/shard_map/dot_general | solution.py:45
  110.7 0.8 convolution_convert_fusion.1
  111.6 1.2 convolution_convert_fusion.3
  112.8 2.0 multiply_convert_fusion
  114.8 1.2 convolution_convert_fusion.2
  116.0 0.8 convolution_convert_fusion
  117.1 0.4 reshape.55
  117.5 1.0 maximum_bitcast_fusion.4
  118.9 1.0 maximum_bitcast_fusion.2
  120.1 1.3 pad_maximum_fusion.1
  121.4 3.6 %all-to-all-start.1 = ((bf16[3,8,128,256]{2,3,0,1:T(8,128)(2,1)}), bf16[3,8,128,256]{2,3,0,1:T(8,128)(2,1)S(1)}, u32[]{:S(2)}, u32[]{:S(2)}) async-start(bf16[3,8,128,256]{2,3,0,1:T(8,128)(2,1)} %pad_maximum_fusion.1), calls=%async_computation.1 | async-start | bytes 3145728 | tf_op jit(solution)/shard_map/all_to_all | solution.py:164
  125.1 5.7 %convert_reduce_fusion = bf16[256,2048]{1,0:T(8,128)(2,1)} fusion(bf16[8,128,2048]{2,1,0:T(8,128)(2,1)} %bitcast.152, bf16[32,8,8,128]{3,2,1,0:T(8,128)(2,1)S(1)} %get-tuple-element.30), kind=kOutput, calls=%fused_computation | convolution fusion | flops 1081606144 | bytes 5767168 | tf_op jit(solution)/shard_map/bnf,bnk->bfk/dot_general | solution.py:140
  130.8 1.5 fusion.69
  132.3 1.2 copy.99
  133.6 1.1 copy.98
  134.7 1.4 reshape.56
  136.1 0.7 fusion.70
  136.8 0.5 copy.101
  137.3 0.5 copy.100
  137.8 1.0 select_bitcast_fusion
  138.8 4.8 %fusion.71 = (bf16[4,128,2048]{2,1,0:T(8,128)(2,1)S(1)}, f32[4,128,2048]{2,1,0:T(8,128)}) fusion(bf16[256,2048]{1,0:T(8,128)(2,1)} %collective-permute-done.1, bf16[256,2048]{1,0:T(8,128)(2,1)} %param.11, bf16[4,128,256]{2,1,0:T(8,128)(2,1)S(1)} %get-tuple-element.40, bf16[4,128,256]{2,1,0:T(8,128)(2,1)S(1)} %get-tuple-element.41), kind=kOutput, calls=%fused_computation.92 | convolution fusion | flops 1080033280 | bytes 8912896 | tf_op jit(solution)/shard_map/dot_general | solution.py:76
  143.8 1.9 collective-permute-start.2
  145.7 1.9 collective-permute-start.4
  147.6 1.0 collective-permute-start.3
  148.6 36.3 %all-reduce.2.cloned.1.call-done = bf16[256,2048]{1,0:T(8,128)(2,1)} async-done(((bf16[256,2048]{1,0:T(8,128)(2,1)}), bf16[256,2048]{1,0:T(8,128)(2,1)}) %all-reduce.2.cloned.1.call-update) | async-done | bytes 1048592 | tf_op jit(solution)/shard_map/psum | solution.py:144
  184.9 2.8 %convert_multiply_fusion = f32[256,2048]{1,0:T(8,128)} fusion(bf16[256,2048]{1,0:T(8,128)(2,1)} %all-reduce.2.cloned.1.call-done), kind=kLoop, calls=%fused_computation.13 | loop fusion | flops 1048576 | bytes 3145728 | tf_op jit(solution)/shard_map/div | solution.py:146
  187.7 20.2 %collective-permute-done.3 = bf16[128,2048]{1,0:T(8,128)(2,1)} collective-permute-done((bf16[128,2048]{1,0:T(8,128)(2,1)S(1)}, bf16[128,2048]{1,0:T(8,128)(2,1)}, u32[]{:S(2)}, u32[]{:S(2)}) %collective-permute-start.3) | collective-permute-done | bytes 524320 | tf_op jit(solution)/shard_map/ppermute | solution.py:84
  207.9 2.8 %fusion.37 = bf16[1,128,2048]{2,1,0:T(8,128)(2,1)} fusion(bf16[128,2048]{1,0:T(8,128)(2,1)} %collective-permute-done.4, bf16[128,2048]{1,0:T(8,128)(2,1)} %collective-permute-done.3, bf16[128,2048]{1,0:T(8,128)(2,1)} %collective-permute-done.2, f32[4,128,2048]{2,1,0:T(8,128)} %get-tuple-element.38, s32[]{:T(128)S(6)} %select_n.79), kind=kLoop, calls=%fused_computation.42 | loop fusion | flops 1835008 | bytes 3145732 | tf_op jit(solution)/shard_map/broadcast_in_dim | solution.py:133
  210.8 1.0 copy.92
  211.8 1.0 copy.91
  212.8 1.0 copy.90
  (51 shorter events, 2.9 us)
Async XLA Ops:
  7.2 91.6 %all-gather.3.cloned.1.call-start = ((), (), s32[]{:S(2)}) async-start(), calls=%async_computation.3 | async-start | bytes 4718592 | tf_op jit(solution)/shard_map/all_gather | solution.py:103
  11.9 8.3 %copy-start.9 = (s32[1,9]{1,0:T(1,128)S(1)}, s32[1,9]{1,0:T(1,128)}, u32[]{:S(2)}) copy-start(s32[1,9]{1,0:T(1,128)} %param.12) | copy-start | bytes 112
  11.9 8.4 %copy-start.10 = (s32[1,32]{1,0:T(1,128)S(1)}, s32[1,32]{1,0:T(1,128)}, u32[]{:S(2)}) copy-start(s32[1,32]{1,0:T(1,128)} %param.13) | copy-start | bytes 388
  13.3 77.9 %all-to-all-start = ((bf16[3,8,128,256]{2,3,0,1:T(8,128)(2,1)}), bf16[3,8,128,256]{2,3,0,1:T(8,128)(2,1)S(1)}, u32[]{:S(2)}, u32[]{:S(2)}) async-start(bf16[3,8,128,256]{2,3,0,1:T(8,128)(2,1)} %copy.76), calls=%async_computation | async-start | bytes 3145728 | tf_op jit(solution)/shard_map/all_to_all | solution.py:119
  19.6 119.2 %collective-permute-start.1 = (bf16[256,2048]{1,0:T(8,128)(2,1)}, bf16[256,2048]{1,0:T(8,128)(2,1)}, u32[]{:S(2)}, u32[]{:S(2)}) collective-permute-start(bf16[256,2048]{1,0:T(8,128)(2,1)} %param.11), channel_id=1, source_target_pairs={{0,1},{1,0},{2,3},{3,2},{4,5},{5,4},{6,7},{7,6},{8,9},{9,8},{10,11... | collective-permute-start | bytes 3145736 | tf_op jit(solution)/shard_map/ppermute | solution.py:68
  93.5 4.0 %copy-start = (f32[1024,1024]{0,1:T(8,128)}, f32[1024,1024]{0,1:T(8,128)S(1)}, u32[]{:S(2)}) copy-start(f32[1024,1024]{0,1:T(8,128)S(1)} %fusion.46) | copy-start | bytes 12582916
  95.2 2.3 %copy-start.2 = (f32[1024,1024]{0,1:T(8,128)}, f32[1024,1024]{0,1:T(8,128)S(1)}, u32[]{:S(2)}) copy-start(f32[1024,1024]{0,1:T(8,128)S(1)} %get-tuple-element.36) | copy-start | bytes 12582916
  95.2 2.3 %copy-start.4 = (bf16[1,8,128,256]{3,2,1,0:T(8,128)(2,1)S(1)}, bf16[1,8,128,256]{3,2,1,0:T(8,128)(2,1)}, u32[]{:S(2)}) copy-start(bf16[1,8,128,256]{3,2,1,0:T(8,128)(2,1)} %copy.97) | copy-start | bytes 1572868
  98.7 8.5 %copy-start.7 = (bf16[1024,128]{0,1:T(8,128)(2,1)}, bf16[1024,128]{0,1:T(8,128)(2,1)S(1)}, u32[]{:S(2)}) copy-start(bf16[1024,128]{0,1:T(8,128)(2,1)S(1)} %fusion.28) | copy-start | bytes 786436
  98.8 3.9 %copy-start.1 = (f32[1024,1024]{0,1:T(8,128)S(1)}, f32[1024,1024]{0,1:T(8,128)}, u32[]{:S(2)}) copy-start(f32[1024,1024]{0,1:T(8,128)} %copy-done) | copy-start | bytes 12582916
  102.7 2.2 %copy-start.3 = (f32[1024,1024]{0,1:T(8,128)S(1)}, f32[1024,1024]{0,1:T(8,128)}, u32[]{:S(2)}) copy-start(f32[1024,1024]{0,1:T(8,128)} %copy-done.2) | copy-start | bytes 12582916
  114.8 2.1 copy-start.8
  114.8 2.7 %copy-start.6 = (bf16[1024,128]{0,1:T(8,128)(2,1)S(1)}, bf16[1024,128]{0,1:T(8,128)(2,1)}, u32[]{:S(2)}) copy-start(bf16[1024,128]{0,1:T(8,128)(2,1)} %fusion.25) | copy-start | bytes 786436
  116.9 2.1 copy-start.5
  117.4 17.3 %collective-permute-start = (bf16[1024,256]{0,1:T(8,128)(2,1)S(1)}, bf16[1024,256]{0,1:T(8,128)(2,1)}, u32[]{:S(2)}, u32[]{:S(2)}) collective-permute-start(bf16[1024,256]{0,1:T(8,128)(2,1)S(1)} %get-tuple-element.31), channel_id=1, source_target_pairs={{0,1},{1,0},{2,3},{3,2},{4,5},{5,4},{6,7},{7,6},{8,9},{9,8},{10,11... | collective-permute-start | bytes 1572872 | tf_op jit(solution)/shard_map/ppermute | solution.py:67
  121.4 89.2 %all-to-all-start.1 = ((bf16[3,8,128,256]{2,3,0,1:T(8,128)(2,1)}), bf16[3,8,128,256]{2,3,0,1:T(8,128)(2,1)S(1)}, u32[]{:S(2)}, u32[]{:S(2)}) async-start(bf16[3,8,128,256]{2,3,0,1:T(8,128)(2,1)} %pad_maximum_fusion.1), calls=%async_computation.1 | async-start | bytes 3145728 | tf_op jit(solution)/shard_map/all_to_all | solution.py:164
  125.0 59.8 %all-reduce.2.cloned.1.call-start = ((), (), s32[]{:S(2)}) async-start(), calls=%async_computation.2 | async-start | bytes 2097152 | tf_op jit(solution)/shard_map/psum | solution.py:144
  143.8 43.9 %collective-permute-start.2 = (bf16[128,2048]{1,0:T(8,128)(2,1)S(1)}, bf16[128,2048]{1,0:T(8,128)(2,1)}, u32[]{:S(2)}, u32[]{:S(2)}) collective-permute-start(bf16[128,2048]{1,0:T(8,128)(2,1)S(1)} %get-tuple-element.21), channel_id=1, source_target_pairs={{0,2},{1,3},{2,4},{3,5},{4,6},{5,7},{6,0},{7,1},{8,10},{9,11},{10,... | collective-permute-start | bytes 1572872 | tf_op jit(solution)/shard_map/ppermute | solution.py:84
  145.7 42.0 %collective-permute-start.4 = (bf16[128,2048]{1,0:T(8,128)(2,1)S(1)}, bf16[128,2048]{1,0:T(8,128)(2,1)}, u32[]{:S(2)}, u32[]{:S(2)}) collective-permute-start(bf16[128,2048]{1,0:T(8,128)(2,1)S(1)} %get-tuple-element.22), channel_id=1, source_target_pairs={{0,6},{1,7},{2,0},{3,1},{4,2},{5,3},{6,4},{7,5},{8,14},{9,15},{10,... | collective-permute-start | bytes 1572872 | tf_op jit(solution)/shard_map/ppermute | solution.py:84
  147.6 60.2 %collective-permute-start.3 = (bf16[128,2048]{1,0:T(8,128)(2,1)S(1)}, bf16[128,2048]{1,0:T(8,128)(2,1)}, u32[]{:S(2)}, u32[]{:S(2)}) collective-permute-start(bf16[128,2048]{1,0:T(8,128)(2,1)S(1)} %get-tuple-element.23), channel_id=1, source_target_pairs={{0,4},{1,5},{2,6},{3,7},{4,0},{5,1},{6,2},{7,3},{8,12},{9,13},{10,... | collective-permute-start | bytes 1572872 | tf_op jit(solution)/shard_map/ppermute | solution.py:84
Sparse Core Ops, SparseCore 0:
  9.6 83.0 all-gather.2
  130.9 53.8 all-reduce.1

commit v8 on v7

--- a/solution.py
+++ b/solution.py
@@ -53,6 +53,29 @@
         q_grad.astype(jnp.bfloat16),
         k_grad.astype(jnp.bfloat16),
         v_grad.astype(jnp.bfloat16),
+    )
+
+
+def chip_gather(x):
+    n = lax.axis_size("seq")
+    chips = n // 2
+    s = lax.axis_index("seq")
+    core = s % 2
+    z = s // 2
+    pieces = [x]
+    for k in range(1, chips):
+        pairs = [(i, ((i // 2 + k) % chips) * 2 + i % 2) for i in range(n)]
+        pieces.append(lax.ppermute(x, "seq", pairs))
+    by_shift = jnp.stack(pieces)
+    order = (z - jnp.arange(chips, dtype=jnp.int32)) % chips
+    mine = jnp.take(by_shift, order, axis=0)
+    other = lax.ppermute(mine, "seq", [(i, i ^ 1) for i in range(n)])
+    return mine, other, core
+
+
+def pair_rows(first, second, core):
+    return jnp.where(
+        core == 0, jnp.stack([first, second], axis=1), jnp.stack([second, first], axis=1)
     )
 
 
@@ -100,7 +123,7 @@
     nodes = nodes_here * n_seq
 
     grad_here = upstream_cotangent[0]
-    grad_full = lax.all_gather(grad_here, "seq", axis=0, tiled=True)
+    up_mine, up_other, core = chip_gather(grad_here)
 
     groups = n_seq
     group_width = width // groups
@@ -132,15 +155,25 @@
 
     layer_out = chip_layer_out(att_flat, w_out).astype(jnp.bfloat16)[None]
 
-    g_flat = lax.dot_general(
-        grad_full, w_out, (((1,), (1,)), ((), ())), preferred_element_type=jnp.float32
-    ).astype(jnp.bfloat16)
-    att_blocks = att_flat.reshape(n_seq, nodes_here, local_heads * HD)
-    grad_blocks = grad_full.reshape(n_seq, nodes_here, width)
-    terms = jnp.einsum(
-        "bnf,bnk->bfk", att_blocks, grad_blocks, preferred_element_type=jnp.float32
-    ).astype(jnp.bfloat16)
-    w_rows = jnp.sum(terms.astype(jnp.float32), axis=0)
+    def times_w(values):
+        return lax.dot_general(
+            values, w_out, (((2,), (1,)), ((), ())), preferred_element_type=jnp.float32
+        ).astype(jnp.bfloat16)
+
+    g_flat = pair_rows(times_w(up_mine), times_w(up_other), core).reshape(nodes, group_width)
+
+    att4 = att_flat.reshape(n_seq // 2, 2, nodes_here, group_width)
+    att_mine = jnp.where(core == 0, att4[:, 0], att4[:, 1])
+    att_other = jnp.where(core == 0, att4[:, 1], att4[:, 0])
+
+    def block_terms(att_part, up_part):
+        return jnp.einsum(
+            "bnf,bnk->bfk", att_part, up_part, preferred_element_type=jnp.float32
+        ).astype(jnp.bfloat16)
+
+    w_rows = jnp.sum(block_terms(att_mine, up_mine).astype(jnp.float32), axis=0) + jnp.sum(
+        block_terms(att_other, up_other).astype(jnp.float32), axis=0
+    )
     w_rows = lax.psum(w_rows.astype(jnp.bfloat16), "dp").astype(jnp.float32)
     batch = asking_vectors_matrix.shape[0] * lax.axis_size("dp")
     w_out_grad = w_rows / batch

time: 221 us -> 233 us (1.054)
  the two profiles are of different devices: /device:TPU:0 before, /device:TPU:14 now
where the time goes in v8:
time: 233 us; the launch traced here: 232 us
  waiting for transfers between devices  117 us (50%)
  matrix products  34.5 us (15%)
  local copies, waits for them, and re-layouts  29.1 us (12%)
  starting transfers between devices  22.3 us (10%)
  other arithmetic  14.7 us (6%)
  between operations  14.5 us (6%)
    ppermute x3, waiting for transfers between devices, chip_layer_out(): total = total + lax.ppermute(piece, 'seq', pairs).astype(jnp.float32)  64.3 us
    ppermute x3, waiting for transfers between devices, chip_gather(): pieces.append(lax.ppermute(x, 'seq', pairs))  50 us
    unnamed x40, local copies, waits for them, and re-layouts  15.3 us
    all_to_all x1, starting transfers between devices, shards(): back = lax.all_to_all(grads, 'seq', split_axis=1, concat_axis=1, tiled=True)  6.82 us
    dot_general x2, matrix products, block_terms(): jnp.einsum('bnf,bnk->bfk', att_part, up_part, preferred_element_type=jnp....  5.61 us
    all_to_all x1, starting transfers between devices, shards(): lax.all_to_all(stacked, 'seq', split_axis=1, concat_axis=1, tiled=True)  5.53 us
    dot_general x1, matrix products, chip_layer_out(): lax.dot_general(att_chip, w_chip, (((2,), (0,)), ((), ())), preferred_ele...  4.75 us
    ppermute x3, starting transfers between devices, chip_gather(): pieces.append(lax.ppermute(x, 'seq', pairs))  4.67 us
  transfers between devices with their start and end apart: 12, of which 7 were waited for; matrix products, arithmetic and copies ran while one was open for 32% of the time, Pallas kernels for 0%

profile of v8, /device:TPU:14, one launch (start us, length us, event | category | flops | bytes accessed | tf_op | source)
XLA Modules:
  0.0 232.2 jit_solution(15814271421486179087)
XLA Ops:
  7.2 1.6 collective-permute-start.5
  8.8 1.2 collective-permute-start.6
  10.0 1.8 collective-permute-start.7
  11.8 1.3 copy.83
  13.1 1.3 copy.81
  14.5 1.3 copy.82
  16.0 1.2 copy.84
  17.2 5.5 %all-to-all-start = ((bf16[3,8,128,256]{2,3,0,1:T(8,128)(2,1)}), bf16[3,8,128,256]{2,3,0,1:T(8,128)(2,1)}, u32[]{:S(2)}, u32[]{:S(2)}) async-start(bf16[3,8,128,256]{2,3,0,1:T(8,128)(2,1)} %copy.84), calls=%async_computation | async-start | bytes 3145728 | tf_op jit(solution)/shard_map/all_to_all | solution.py:142
  22.8 27.2 %collective-permute-done.5 = bf16[128,2048]{1,0:T(8,128)(2,1)S(1)} collective-permute-done((bf16[128,2048]{1,0:T(8,128)(2,1)}, bf16[128,2048]{1,0:T(8,128)(2,1)S(1)}, u32[]{:S(2)}, u32[]{:S(2)}) %collective-permute-start.5) | collective-permute-done | bytes 524320 | tf_op jit(solution)/shard_map/ppermute | solution.py:68
  50.0 22.0 %collective-permute-done.6 = bf16[128,2048]{1,0:T(8,128)(2,1)S(1)} collective-permute-done((bf16[128,2048]{1,0:T(8,128)(2,1)}, bf16[128,2048]{1,0:T(8,128)(2,1)S(1)}, u32[]{:S(2)}, u32[]{:S(2)}) %collective-permute-start.6) | collective-permute-done | bytes 524320 | tf_op jit(solution)/shard_map/ppermute | solution.py:68
  72.8 1.5 pad_maximum_fusion
  74.3 2.0 gather_fusion
  76.3 1.9 broadcast_select_fusion
  79.3 2.0 fusion.29
  81.2 2.8 %collective-permute-done.8 = bf16[4,128,2048]{2,1,0:T(8,128)(2,1)} collective-permute-done((bf16[4,128,2048]{2,1,0:T(8,128)(2,1)S(1)}, bf16[4,128,2048]{2,1,0:T(8,128)(2,1)}, u32[]{:S(2)}, u32[]{:S(2)}) %collective-permute-start.8) | collective-permute-done | bytes 2097184 | tf_op jit(solution)/shard_map/ppermute | solution.py:72
  84.0 2.6 %fusion.30 = bf16[4,1,128,256]{3,2,0,1:T(8,128)(2,1)S(1)} fusion(bf16[4,128,2048]{2,1,0:T(8,128)(2,1)} %collective-permute-done.8, bf16[256,2048]{1,0:T(8,128)(2,1)} %param.11), kind=kOutput, calls=%fused_computation.42 | convolution fusion | flops 537001984 | bytes 3407872 | tf_op jit(solution)/shard_map/dot_general | solution.py:159
  88.4 2.5 %fusion.70 = (bf16[1,8,128,256]{2,3,0,1:T(8,128)(2,1)S(1)}, bf16[1,8,128,256]{2,3,0,1:T(8,128)(2,1)}, bf16[1,8,128,256]{2,3,0,1:T(8,128)(2,1)}) fusion(bf16[3,8,128,256]{2,3,0,1:T(8,128)(2,1)} %all-to-all-done), kind=kLoop, calls=%fused_computation.111 | loop fusion | bytes 3145728 | tf_op jit(solution)/shard_map/slice | solution.py:151
  90.8 1.2 copy.107
  92.1 2.0 copy.108
  95.1 1.7 fusion.46
  97.2 1.3 select_reduce_fusion.1
  98.6 2.1 fusion.67
  100.7 1.2 fusion.23
  101.9 1.2 multiply_reduce_fusion.1
  103.2 2.0 multiply_convert_fusion.1
  106.4 1.5 convolution_convert_fusion.1
  107.9 2.0 multiply_convert_fusion
  111.1 1.6 convolution_convert_fusion
  112.6 2.2 fusion.17
  114.8 2.2 fusion.20
  117.6 1.7 fusion.71
  119.3 1.2 copy.110
  120.5 1.2 copy.111
  121.8 2.6 %convert_reduce_fusion.1 = f32[256,2048]{1,0:T(8,128)} fusion(bf16[4,128,256]{2,1,0:T(8,128)(2,1)S(1)} %select_bitcast_fusion.1, bf16[4,128,2048]{2,1,0:T(8,128)(2,1)S(1)} %broadcast_select_fusion), kind=kOutput, calls=%fused_computation.2 | convolution fusion | flops 542638080 | bytes 4456448 | tf_op jit(solution)/shard_map/bnf,bnk->bfk/dot_general | solution.py:170
  126.2 1.3 pad_maximum_fusion.2
  127.6 6.8 %all-to-all-start.1 = ((bf16[3,8,128,256]{2,3,0,1:T(8,128)(2,1)}), bf16[3,8,128,256]{2,3,0,1:T(8,128)(2,1)}, u32[]{:S(2)}, u32[]{:S(2)}) async-start(bf16[3,8,128,256]{2,3,0,1:T(8,128)(2,1)} %pad_maximum_fusion.2), calls=%async_computation.1 | async-start | bytes 3145728 | tf_op jit(solution)/shard_map/all_to_all | solution.py:197
  134.4 3.0 %convert_reduce_fusion = f32[256,2048]{1,0:T(8,128)S(1)} fusion(bf16[4,128,2048]{2,1,0:T(8,128)(2,1)} %collective-permute-done.8, bf16[4,1,128,256]{3,2,0,1:T(8,128)(2,1)S(1)} %copy.111, bf16[4,1,128,256]{3,2,0,1:T(8,128)(2,1)S(1)} %copy.110, pred[]{:T(512)S(6)} %eq.43), kind=kOutput, calls=%fused_computation.1 | convolution fusion | flops 542769152 | bytes 4718593 | tf_op jit(solution)/shard_map/bnf,bnk->bfk/dot_general | solution.py:170
  137.4 1.2 add_convert_fusion
  138.7 1.4 reshape.112
  142.1 4.7 %fusion.73 = (bf16[4,128,2048]{2,1,0:T(8,128)(2,1)S(1)}, f32[4,128,2048]{2,1,0:T(8,128)}) fusion(bf16[256,2048]{1,0:T(8,128)(2,1)} %collective-permute-done.1, bf16[256,2048]{1,0:T(8,128)(2,1)} %param.11, bf16[4,128,256]{2,1,0:T(8,128)(2,1)S(1)} %select_bitcast_fusion, bf16[4,128,256]{2,1,0:T(8,128)(2,1)S(1)} %select_bitcast_fusion.1), kind=kOutput, calls=%fused_computation.114 | convolution fusion | flops 1080033280 | bytes 8912896 | tf_op jit(solution)/shard_map/dot_general | solution.py:99
  147.0 1.5 collective-permute-start.2
  149.6 1.9 collective-permute-start.4
  151.5 51.0 %collective-permute-done.2 = bf16[128,2048]{1,0:T(8,128)(2,1)S(1)} collective-permute-done((bf16[128,2048]{1,0:T(8,128)(2,1)S(1)}, bf16[128,2048]{1,0:T(8,128)(2,1)S(1)}, u32[]{:S(2)}, u32[]{:S(2)}) %collective-permute-start.2) | collective-permute-done | bytes 524320 | tf_op jit(solution)/shard_map/ppermute | solution.py:107
  202.4 11.2 %collective-permute-done.3 = bf16[128,2048]{1,0:T(8,128)(2,1)S(1)} collective-permute-done((bf16[128,2048]{1,0:T(8,128)(2,1)S(1)}, bf16[128,2048]{1,0:T(8,128)(2,1)S(1)}, u32[]{:S(2)}, u32[]{:S(2)}) %collective-permute-start.3) | collective-permute-done | bytes 524320 | tf_op jit(solution)/shard_map/ppermute | solution.py:107
  213.7 2.1 collective-permute-done.4
  215.8 2.3 fusion.36
  218.1 2.8 %convert_multiply_fusion = f32[256,2048]{1,0:T(8,128)} fusion(bf16[256,2048]{1,0:T(8,128)(2,1)} %all-reduce.2.cloned.1.call-done), kind=kLoop, calls=%fused_computation.14 | loop fusion | flops 1048576 | bytes 3145728 | tf_op jit(solution)/shard_map/div | solution.py:179
  220.9 1.5 fusion.69
  (71 shorter events, 16.1 us)
Async XLA Ops:
  7.2 42.9 %collective-permute-start.5 = (bf16[128,2048]{1,0:T(8,128)(2,1)}, bf16[128,2048]{1,0:T(8,128)(2,1)S(1)}, u32[]{:S(2)}, u32[]{:S(2)}) collective-permute-start(bf16[128,2048]{1,0:T(8,128)(2,1)} %bitcast.163), channel_id=1, source_target_pairs={{0,2},{1,3},{2,4},{3,5},{4,6},{5,7},{6,0},{7,1},{8,10},{9,11},{10,... | collective-permute-start | bytes 1572872 | tf_op jit(solution)/shard_map/ppermute | solution.py:68
  8.8 63.2 %collective-permute-start.6 = (bf16[128,2048]{1,0:T(8,128)(2,1)}, bf16[128,2048]{1,0:T(8,128)(2,1)S(1)}, u32[]{:S(2)}, u32[]{:S(2)}) collective-permute-start(bf16[128,2048]{1,0:T(8,128)(2,1)} %bitcast.164), channel_id=1, source_target_pairs={{0,4},{1,5},{2,6},{3,7},{4,0},{5,1},{6,2},{7,3},{8,12},{9,13},{10,... | collective-permute-start | bytes 1572872 | tf_op jit(solution)/shard_map/ppermute | solution.py:68
  10.0 62.8 %collective-permute-start.7 = (bf16[128,2048]{1,0:T(8,128)(2,1)}, bf16[128,2048]{1,0:T(8,128)(2,1)}, u32[]{:S(2)}, u32[]{:S(2)}) collective-permute-start(bf16[128,2048]{1,0:T(8,128)(2,1)} %bitcast.165), channel_id=1, source_target_pairs={{0,6},{1,7},{2,0},{3,1},{4,2},{5,3},{6,4},{7,5},{8,14},{9,15},{10,... | collective-permute-start | bytes 1572872 | tf_op jit(solution)/shard_map/ppermute | solution.py:68
  15.8 57.0 %copy-start.6 = (bf16[1,128,2048]{2,1,0:T(8,128)(2,1)S(1)}, bf16[1,128,2048]{2,1,0:T(8,128)(2,1)}, u32[]{:S(2)}) copy-start(bf16[1,128,2048]{2,1,0:T(8,128)(2,1)} %param.10) | copy-start | bytes 1572868
  17.2 71.1 %all-to-all-start = ((bf16[3,8,128,256]{2,3,0,1:T(8,128)(2,1)}), bf16[3,8,128,256]{2,3,0,1:T(8,128)(2,1)}, u32[]{:S(2)}, u32[]{:S(2)}) async-start(bf16[3,8,128,256]{2,3,0,1:T(8,128)(2,1)} %copy.84), calls=%async_computation | async-start | bytes 3145728 | tf_op jit(solution)/shard_map/all_to_all | solution.py:142
  72.0 0.8 copy-start.7
  74.3 4.5 %copy-start.10 = (s32[1,9]{1,0:T(1,128)S(1)}, s32[1,9]{1,0:T(1,128)}, u32[]{:S(2)}) copy-start(s32[1,9]{1,0:T(1,128)} %param.12) | copy-start | bytes 112
  74.3 4.6 %copy-start.11 = (s32[1,32]{1,0:T(1,128)S(1)}, s32[1,32]{1,0:T(1,128)}, u32[]{:S(2)}) copy-start(s32[1,32]{1,0:T(1,128)} %param.13) | copy-start | bytes 388
  78.2 5.9 %collective-permute-start.8 = (bf16[4,128,2048]{2,1,0:T(8,128)(2,1)S(1)}, bf16[4,128,2048]{2,1,0:T(8,128)(2,1)}, u32[]{:S(2)}, u32[]{:S(2)}) collective-permute-start(bf16[4,128,2048]{2,1,0:T(8,128)(2,1)S(1)} %broadcast_select_fusion), channel_id=1, source_target_pairs={{0,1},{1,0},{2,3},{3,2},{4,5},{5,4},{6,7},{7,6},{8,9},{9,8},{10,11... | collective-permute-start | bytes 6291464 | tf_op jit(solution)/shard_map/ppermute | solution.py:72
  78.3 63.8 %collective-permute-start.1 = (bf16[256,2048]{1,0:T(8,128)(2,1)}, bf16[256,2048]{1,0:T(8,128)(2,1)}, u32[]{:S(2)}, u32[]{:S(2)}) collective-permute-start(bf16[256,2048]{1,0:T(8,128)(2,1)} %param.11), channel_id=1, source_target_pairs={{0,1},{1,0},{2,3},{3,2},{4,5},{5,4},{6,7},{7,6},{8,9},{9,8},{10,11... | collective-permute-start | bytes 3145736 | tf_op jit(solution)/shard_map/ppermute | solution.py:91
  95.1 2.1 copy-start.1
  98.6 2.1 copy-start.5
  100.7 1.2 copy-start.4
  117.4 21.3 %collective-permute-start = (bf16[1024,256]{0,1:T(8,128)(2,1)S(1)}, bf16[1024,256]{0,1:T(8,128)(2,1)}, u32[]{:S(2)}, u32[]{:S(2)}) collective-permute-start(bf16[1024,256]{0,1:T(8,128)(2,1)S(1)} %pad_maximum_fusion.3), channel_id=1, source_target_pairs={{0,1},{1,0},{2,3},{3,2},{4,5},{5,4},{6,7},{7,6},{8,9},{9,8},{10,11... | collective-permute-start | bytes 1572872 | tf_op jit(solution)/shard_map/ppermute | solution.py:90
  121.8 4.0 %copy-start.2 = (bf16[1024,128]{0,1:T(8,128)(2,1)S(1)}, bf16[1024,128]{0,1:T(8,128)(2,1)}, u32[]{:S(2)}) copy-start(bf16[1024,128]{0,1:T(8,128)(2,1)} %convolution_convert_fusion.1) | copy-start | bytes 786436
  121.8 4.0 %copy-start.3 = (bf16[1024,128]{0,1:T(8,128)(2,1)S(1)}, bf16[1024,128]{0,1:T(8,128)(2,1)}, u32[]{:S(2)}) copy-start(bf16[1024,128]{0,1:T(8,128)(2,1)} %convolution_convert_fusion) | copy-start | bytes 786436
  124.4 1.6 copy-start.8
  124.4 1.6 copy-start.9
  127.6 9.8 %copy-start = (f32[256,2048]{1,0:T(8,128)S(1)}, f32[256,2048]{1,0:T(8,128)}, u32[]{:S(2)}) copy-start(f32[256,2048]{1,0:T(8,128)} %convert_reduce_fusion.1) | copy-start | bytes 6291460
  127.6 93.3 %all-to-all-start.1 = ((bf16[3,8,128,256]{2,3,0,1:T(8,128)(2,1)}), bf16[3,8,128,256]{2,3,0,1:T(8,128)(2,1)}, u32[]{:S(2)}, u32[]{:S(2)}) async-start(bf16[3,8,128,256]{2,3,0,1:T(8,128)(2,1)} %pad_maximum_fusion.2), calls=%async_computation.1 | async-start | bytes 3145728 | tf_op jit(solution)/shard_map/all_to_all | solution.py:197
  134.4 83.7 %all-reduce.2.cloned.1.call-start = ((), (), s32[]{:S(2)}) async-start(), calls=%async_computation.2 | async-start | bytes 2097152 | tf_op jit(solution)/shard_map/psum | solution.py:177
  147.0 55.5 %collective-permute-start.2 = (bf16[128,2048]{1,0:T(8,128)(2,1)S(1)}, bf16[128,2048]{1,0:T(8,128)(2,1)S(1)}, u32[]{:S(2)}, u32[]{:S(2)}) collective-permute-start(bf16[128,2048]{1,0:T(8,128)(2,1)S(1)} %get-tuple-element.21), channel_id=1, source_target_pairs={{0,2},{1,3},{2,4},{3,5},{4,6},{5,7},{6,0},{7,1},{8,10},{9,11},{10,... | collective-permute-start | bytes 1572872 | tf_op jit(solution)/shard_map/ppermute | solution.py:107
  148.5 65.1 %collective-permute-start.3 = (bf16[128,2048]{1,0:T(8,128)(2,1)S(1)}, bf16[128,2048]{1,0:T(8,128)(2,1)S(1)}, u32[]{:S(2)}, u32[]{:S(2)}) collective-permute-start(bf16[128,2048]{1,0:T(8,128)(2,1)S(1)} %get-tuple-element.23), channel_id=1, source_target_pairs={{0,4},{1,5},{2,6},{3,7},{4,0},{5,1},{6,2},{7,3},{8,12},{9,13},{10,... | collective-permute-start | bytes 1572872 | tf_op jit(solution)/shard_map/ppermute | solution.py:107
  149.6 66.2 %collective-permute-start.4 = (bf16[128,2048]{1,0:T(8,128)(2,1)S(1)}, bf16[128,2048]{1,0:T(8,128)(2,1)S(1)}, u32[]{:S(2)}, u32[]{:S(2)}) collective-permute-start(bf16[128,2048]{1,0:T(8,128)(2,1)S(1)} %get-tuple-element.22), channel_id=1, source_target_pairs={{0,6},{1,7},{2,0},{3,1},{4,2},{5,3},{6,4},{7,5},{8,14},{9,15},{10,... | collective-permute-start | bytes 1572872 | tf_op jit(solution)/shard_map/ppermute | solution.py:107
Sparse Core Ops, SparseCore 0:
  138.9 52.5 all-reduce.1

commit v9 on v8

--- a/solution.py
+++ b/solution.py
@@ -62,13 +62,19 @@
     s = lax.axis_index("seq")
     core = s % 2
     z = s // 2
-    pieces = [x]
-    for k in range(1, chips):
-        pairs = [(i, ((i // 2 + k) % chips) * 2 + i % 2) for i in range(n)]
-        pieces.append(lax.ppermute(x, "seq", pairs))
-    by_shift = jnp.stack(pieces)
-    order = (z - jnp.arange(chips, dtype=jnp.int32)) % chips
-    mine = jnp.take(by_shift, order, axis=0)
+    right = [(i, i + 2) for i in range(n - 2)]
+    left = [(i, i - 2) for i in range(2, n)]
+    before = []
+    after = []
+    r = x
+    l = x
+    for step in range(1, chips):
+        r = lax.ppermute(r, "seq", right)
+        l = lax.ppermute(l, "seq", left)
+        before.append(r)
+        after.append(l)
+    rel = jnp.stack(before[::-1] + [x] + after)
+    mine = lax.dynamic_slice_in_dim(rel, chips - 1 - z, chips, axis=0)
     other = lax.ppermute(mine, "seq", [(i, i ^ 1) for i in range(n)])
     return mine, other, core
 
@@ -99,12 +105,27 @@
     chip_partial = lax.dot_general(
         att_chip, w_chip, (((2,), (0,)), ((), ())), preferred_element_type=jnp.float32
     )
-    total = lax.dynamic_index_in_dim(chip_partial, z, 0, keepdims=False)
-    sent = chip_partial.astype(jnp.bfloat16)
-    for k in range(1, chips):
-        pairs = [(i, ((i // 2 + k) % chips) * 2 + i % 2) for i in range(n)]
-        piece = lax.dynamic_index_in_dim(sent, (z + k) % chips, 0, keepdims=False)
-        total = total + lax.ppermute(piece, "seq", pairs).astype(jnp.float32)
+    own = lax.dynamic_index_in_dim(chip_partial, z, 0, keepdims=False)
+    right = [(i, i + 2) for i in range(n - 2)]
+    left = [(i, i - 2) for i in range(2, n)]
+    recv_r = None
+    recv_l = None
+    for step in range(1, chips):
+        d_r = jnp.clip(z + chips - step, 0, chips - 1)
+        d_l = jnp.clip(z - chips + step, 0, chips - 1)
+        acc_r = lax.dynamic_index_in_dim(chip_partial, d_r, 0, keepdims=False)
+        acc_l = lax.dynamic_index_in_dim(chip_partial, d_l, 0, keepdims=False)
+        if recv_r is not None:
+            ok_r = (step >= z + 1) & (z >= 1)
+            ok_l = (step >= chips - z) & (z <= chips - 2)
+            acc_r = acc_r + jnp.where(ok_r, recv_r.astype(jnp.float32), 0.0)
+            acc_l = acc_l + jnp.where(ok_l, recv_l.astype(jnp.float32), 0.0)
+        recv_r = lax.ppermute(acc_r.astype(jnp.bfloat16), "seq", right)
+        recv_l = lax.ppermute(acc_l.astype(jnp.bfloat16), "seq", left)
+    total = own
+    if recv_r is not None:
+        total = total + jnp.where(z >= 1, recv_r.astype(jnp.float32), 0.0)
+        total = total + jnp.where(z <= chips - 2, recv_l.astype(jnp.float32), 0.0)
     return total
 
 

time: 233 us -> 276 us (1.18)
  the two profiles are of different devices: /device:TPU:14 before, /device:TPU:0 now
where the time goes in v9:
time: 276 us; the launch traced here: 274 us
  waiting for transfers between devices  115 us (42%)
  starting transfers between devices  51.3 us (19%)
  local copies, waits for them, and re-layouts  38.1 us (14%)
  matrix products  36.3 us (13%)
  other arithmetic  18.8 us (7%)
  between operations  14.7 us (5%)
    ppermute x3, waiting for transfers between devices, chip_gather(): l = lax.ppermute(l, 'seq', left)  54.8 us
    ppermute x3, waiting for transfers between devices, chip_layer_out(): recv_l = lax.ppermute(acc_l.astype(jnp.bfloat16), 'seq', left)  47.4 us
    ppermute x3, starting transfers between devices, chip_layer_out(): recv_r = lax.ppermute(acc_r.astype(jnp.bfloat16), 'seq', right)  20.1 us
    unnamed x68, local copies, waits for them, and re-layouts  18.3 us
    ppermute x3, starting transfers between devices, chip_gather(): r = lax.ppermute(r, 'seq', right)  13.8 us
    ppermute x3, waiting for transfers between devices, chip_gather(): r = lax.ppermute(r, 'seq', right)  10.2 us
  transfers between devices with their start and end apart: 18, of which 8 were waited for; matrix products, arithmetic and copies ran while one was open for 30% of the time, Pallas kernels for 0%

profile of v9, /device:TPU:0, one launch (start us, length us, event | category | flops | bytes accessed | tf_op | source)
XLA Modules:
  0.0 274.4 jit_solution(9134969421398094017)
XLA Ops:
  7.2 5.0 %collective-permute-start.8 = (bf16[128,2048]{1,0:T(8,128)(2,1)}, bf16[128,2048]{1,0:T(8,128)(2,1)S(1)}, u32[]{:S(2)}, u32[]{:S(2)}) collective-permute-start(bf16[128,2048]{1,0:T(8,128)(2,1)} %bitcast.176), channel_id=1, source_target_pairs={{0,2},{1,3},{2,4},{3,5},{4,6},{5,7},{8,10},{9,11},{10,12},{11,13},... | collective-permute-start | bytes 1572872 | tf_op jit(solution)/shard_map/ppermute | solution.py:72
  13.4 10.1 %collective-permute-done.8 = bf16[128,2048]{1,0:T(8,128)(2,1)S(1)} collective-permute-done((bf16[128,2048]{1,0:T(8,128)(2,1)}, bf16[128,2048]{1,0:T(8,128)(2,1)S(1)}, u32[]{:S(2)}, u32[]{:S(2)}) %collective-permute-start.8) | collective-permute-done | bytes 524320 | tf_op jit(solution)/shard_map/ppermute | solution.py:72
  23.6 4.3 %collective-permute-start.9 = (bf16[128,2048]{1,0:T(8,128)(2,1)S(1)}, bf16[128,2048]{1,0:T(8,128)(2,1)S(1)}, u32[]{:S(2)}, u32[]{:S(2)}) collective-permute-start(bf16[128,2048]{1,0:T(8,128)(2,1)S(1)} %collective-permute-done.8), channel_id=1, source_target_pairs={{0,2},{1,3},{2,4},{3,5},{4,6},{5,7},{8,10},{9,11},{10,12},{11,13},... | collective-permute-start | bytes 1572872 | tf_op jit(solution)/shard_map/ppermute | solution.py:72
  27.9 1.3 copy.83
  29.2 1.3 copy.81
  30.5 1.3 copy.82
  33.3 4.3 %all-to-all-start = ((bf16[3,8,128,256]{2,3,0,1:T(8,128)(2,1)}), bf16[3,8,128,256]{2,3,0,1:T(8,128)(2,1)}, u32[]{:S(2)}, u32[]{:S(2)}) async-start(bf16[3,8,128,256]{2,3,0,1:T(8,128)(2,1)} %copy.84), calls=%async_computation | async-start | bytes 3145728 | tf_op jit(solution)/shard_map/all_to_all | solution.py:163
  39.3 4.6 %collective-permute-start.10 = (bf16[128,2048]{1,0:T(8,128)(2,1)S(1)}, bf16[128,2048]{1,0:T(8,128)(2,1)S(1)}, u32[]{:S(2)}, u32[]{:S(2)}) collective-permute-start(bf16[128,2048]{1,0:T(8,128)(2,1)S(1)} %collective-permute-done.9), channel_id=1, source_target_pairs={{0,2},{1,3},{2,4},{3,5},{4,6},{5,7},{8,10},{9,11},{10,12},{11,13},... | collective-permute-start | bytes 1572872 | tf_op jit(solution)/shard_map/ppermute | solution.py:72
  44.4 32.8 %collective-permute-done.12 = bf16[128,2048]{1,0:T(8,128)(2,1)S(1)} collective-permute-done((bf16[128,2048]{1,0:T(8,128)(2,1)S(1)}, bf16[128,2048]{1,0:T(8,128)(2,1)S(1)}, u32[]{:S(2)}, u32[]{:S(2)}) %collective-permute-start.12) | collective-permute-done | bytes 524320 | tf_op jit(solution)/shard_map/ppermute | solution.py:73
  78.8 22.0 %collective-permute-done.13 = bf16[128,2048]{1,0:T(8,128)(2,1)S(1)} collective-permute-done((bf16[128,2048]{1,0:T(8,128)(2,1)S(1)}, bf16[128,2048]{1,0:T(8,128)(2,1)S(1)}, u32[]{:S(2)}, u32[]{:S(2)}) %collective-permute-start.13) | collective-permute-done | bytes 524320 | tf_op jit(solution)/shard_map/ppermute | solution.py:73
  101.1 2.7 fusion.29
  103.8 2.5 fusion.72
  107.5 2.2 copy.108
  110.7 1.7 fusion.51
  112.8 2.6 select_reduce_fusion.1
  115.4 2.4 fusion.69
  119.1 2.6 fusion.30
  122.6 2.0 copy.92
  124.6 2.2 select_n.144
  126.8 3.8 %multiply_reduce_fusion.1 = (f32[1024]{0:T(1024)S(1)}, f32[1024]{0:T(1024)S(1)}, bf16[1024,128]{0,1:T(8,128)(2,1)S(1)}) fusion(bf16[1024,256]{0,1:T(8,128)(2,1)} %select_n.144, bf16[1024,128]{0,1:T(8,128)(2,1)S(1)} %fusion.23, f32[1024]{0:T(1024)S(1)} %get-tuple-element.15, bf16[1024,256]{1,0:T(8,128)(2,1)} %bitcast.178, f32[1024]{0:T(1024)S(1)} %get-tuple-element.17, ...), kind=kOutput, calls=%fused_computation.74 | convolution fusion | flops 273938432 | bytes 6569984 | tf_op jit(solution)/shard_map/dot_general | solution.py:35
  130.8 2.0 multiply_convert_fusion.1
  134.1 1.6 convolution_convert_fusion.1
  135.6 2.2 multiply_convert_fusion
  139.1 1.5 convolution_convert_fusion
  140.6 2.2 fusion.17
  142.8 2.2 fusion.20
  145.9 1.4 reshape.59
  147.8 1.5 fusion.73
  156.2 1.4 reshape.60
  157.6 1.7 fusion.74
  161.9 2.9 %fusion = f32[4,128,2048]{2,1,0:T(8,128)S(1)} fusion(bf16[256,2048]{1,0:T(8,128)(2,1)} %collective-permute-done.1, bf16[256,2048]{1,0:T(8,128)(2,1)} %param.11, bf16[4,128,256]{2,1,0:T(8,128)(2,1)S(1)} %select_bitcast_fusion, bf16[4,128,256]{2,1,0:T(8,128)(2,1)S(1)} %select_bitcast_fusion.1), kind=kOutput, calls=%fused_computation.9 | convolution fusion | flops 1078984704 | bytes 6815744 | tf_op jit(solution)/shard_map/dot_general | solution.py:105
  164.8 1.9 copy-done.2
  167.9 4.4 %collective-permute-start.2 = (bf16[128,2048]{1,0:T(8,128)(2,1)}, bf16[128,2048]{1,0:T(8,128)(2,1)}, u32[]{:S(2)}, u32[]{:S(2)}) collective-permute-start(bf16[128,2048]{1,0:T(8,128)(2,1)} %get-tuple-element.23), channel_id=1, source_target_pairs={{0,2},{1,3},{2,4},{3,5},{4,6},{5,7},{8,10},{9,11},{10,12},{11,13},... | collective-permute-start | bytes 1572872 | tf_op jit(solution)/shard_map/ppermute | solution.py:123
  172.3 1.3 pad_maximum_fusion.1
  173.6 4.3 %all-to-all-start.1 = ((bf16[3,8,128,256]{2,3,0,1:T(8,128)(2,1)}), bf16[3,8,128,256]{2,3,0,1:T(8,128)(2,1)}, u32[]{:S(2)}, u32[]{:S(2)}) async-start(bf16[3,8,128,256]{2,3,0,1:T(8,128)(2,1)} %pad_maximum_fusion.1), calls=%async_computation.1 | async-start | bytes 3145728 | tf_op jit(solution)/shard_map/all_to_all | solution.py:218
  179.3 3.0 %convert_reduce_fusion = f32[256,2048]{1,0:T(8,128)S(1)} fusion(bf16[4,128,2048]{2,1,0:T(8,128)(2,1)} %collective-permute-done.14, bf16[4,1,128,256]{3,2,0,1:T(8,128)(2,1)S(1)} %copy.111, bf16[4,1,128,256]{3,2,0,1:T(8,128)(2,1)S(1)} %copy.110, pred[]{:T(512)S(6)} %eq.19), kind=kOutput, calls=%fused_computation | convolution fusion | flops 542769152 | bytes 4718593 | tf_op jit(solution)/shard_map/bnf,bnk->bfk/dot_general | solution.py:191
  184.1 1.5 fusion.35
  185.6 4.4 %collective-permute-start.3 = (bf16[128,2048]{1,0:T(8,128)(2,1)S(1)}, bf16[128,2048]{1,0:T(8,128)(2,1)S(1)}, u32[]{:S(2)}, u32[]{:S(2)}) collective-permute-start(bf16[128,2048]{1,0:T(8,128)(2,1)S(1)} %fusion.35), channel_id=1, source_target_pairs={{0,2},{1,3},{2,4},{3,5},{4,6},{5,7},{8,10},{9,11},{10,12},{11,13},... | collective-permute-start | bytes 1572872 | tf_op jit(solution)/shard_map/ppermute | solution.py:123
  191.3 26.3 %collective-permute-done.5 = bf16[128,2048]{1,0:T(8,128)(2,1)S(1)} collective-permute-done((bf16[128,2048]{1,0:T(8,128)(2,1)S(1)}, bf16[128,2048]{1,0:T(8,128)(2,1)S(1)}, u32[]{:S(2)}, u32[]{:S(2)}) %collective-permute-start.5) | collective-permute-done | bytes 524320 | tf_op jit(solution)/shard_map/ppermute | solution.py:124
  217.6 2.1 collective-permute-done.3
  219.7 1.8 fusion.36
  222.9 11.2 %collective-permute-start.4 = (bf16[128,2048]{1,0:T(8,128)(2,1)S(1)}, bf16[128,2048]{1,0:T(8,128)(2,1)S(1)}, u32[]{:S(2)}, u32[]{:S(2)}) collective-permute-start(bf16[128,2048]{1,0:T(8,128)(2,1)S(1)} %get-tuple-element.21), channel_id=1, source_target_pairs={{0,2},{1,3},{2,4},{3,5},{4,6},{5,7},{8,10},{9,11},{10,12},{11,13},... | collective-permute-start | bytes 1572872 | tf_op jit(solution)/shard_map/ppermute | solution.py:123
  234.1 9.6 %collective-permute-done.6 = bf16[128,2048]{1,0:T(8,128)(2,1)S(1)} collective-permute-done((bf16[128,2048]{1,0:T(8,128)(2,1)S(1)}, bf16[128,2048]{1,0:T(8,128)(2,1)S(1)}, u32[]{:S(2)}, u32[]{:S(2)}) %collective-permute-start.6) | collective-permute-done | bytes 524320 | tf_op jit(solution)/shard_map/ppermute | solution.py:124
  243.7 1.4 fusion.34
  246.4 2.8 %convert_multiply_fusion = f32[256,2048]{1,0:T(8,128)} fusion(bf16[256,2048]{1,0:T(8,128)(2,1)} %all-reduce.2.cloned.1.call-done), kind=kLoop, calls=%fused_computation.12 | loop fusion | flops 1048576 | bytes 3145728 | tf_op jit(solution)/shard_map/div | solution.py:200
  249.2 11.6 %collective-permute-done.7 = bf16[128,2048]{1,0:T(8,128)(2,1)S(1)} collective-permute-done((bf16[128,2048]{1,0:T(8,128)(2,1)S(1)}, bf16[128,2048]{1,0:T(8,128)(2,1)S(1)}, u32[]{:S(2)}, u32[]{:S(2)}) %collective-permute-start.7) | collective-permute-done | bytes 524320 | tf_op jit(solution)/shard_map/ppermute | solution.py:124
  260.8 2.2 fusion.41
  263.0 1.5 fusion.71
  (110 shorter events, 35.7 us)
Async XLA Ops:
  7.2 16.4 %collective-permute-start.8 = (bf16[128,2048]{1,0:T(8,128)(2,1)}, bf16[128,2048]{1,0:T(8,128)(2,1)S(1)}, u32[]{:S(2)}, u32[]{:S(2)}) collective-permute-start(bf16[128,2048]{1,0:T(8,128)(2,1)} %bitcast.176), channel_id=1, source_target_pairs={{0,2},{1,3},{2,4},{3,5},{4,6},{5,7},{8,10},{9,11},{10,12},{11,13},... | collective-permute-start | bytes 1572872 | tf_op jit(solution)/shard_map/ppermute | solution.py:72
  12.1 25.9 %collective-permute-start.11 = (bf16[128,2048]{1,0:T(8,128)(2,1)}, bf16[128,2048]{1,0:T(8,128)(2,1)S(1)}, u32[]{:S(2)}, u32[]{:S(2)}) collective-permute-start(bf16[128,2048]{1,0:T(8,128)(2,1)} %bitcast.177), channel_id=1, source_target_pairs={{2,0},{3,1},{4,2},{5,3},{6,4},{7,5},{10,8},{11,9},{12,10},{13,11},... | collective-permute-start | bytes 1572872 | tf_op jit(solution)/shard_map/ppermute | solution.py:73
  23.6 15.7 %collective-permute-start.9 = (bf16[128,2048]{1,0:T(8,128)(2,1)S(1)}, bf16[128,2048]{1,0:T(8,128)(2,1)S(1)}, u32[]{:S(2)}, u32[]{:S(2)}) collective-permute-start(bf16[128,2048]{1,0:T(8,128)(2,1)S(1)} %collective-permute-done.8), channel_id=1, source_target_pairs={{0,2},{1,3},{2,4},{3,5},{4,6},{5,7},{8,10},{9,11},{10,12},{11,13},... | collective-permute-start | bytes 1572872 | tf_op jit(solution)/shard_map/ppermute | solution.py:72
  31.9 12.0 %copy-start.21 = (s32[1,9]{1,0:T(1,128)S(1)}, s32[1,9]{1,0:T(1,128)}, u32[]{:S(2)}) copy-start(s32[1,9]{1,0:T(1,128)} %param.12) | copy-start | bytes 112
  31.9 12.2 %copy-start.22 = (s32[1,32]{1,0:T(1,128)S(1)}, s32[1,32]{1,0:T(1,128)}, u32[]{:S(2)}) copy-start(s32[1,32]{1,0:T(1,128)} %param.13) | copy-start | bytes 388
  32.1 46.6 %copy-start.12 = (bf16[1,128,2048]{2,1,0:T(8,128)(2,1)S(1)}, bf16[1,128,2048]{2,1,0:T(8,128)(2,1)}, u32[]{:S(2)}) copy-start(bf16[1,128,2048]{2,1,0:T(8,128)(2,1)} %param.10) | copy-start | bytes 1572868
  33.3 70.4 %all-to-all-start = ((bf16[3,8,128,256]{2,3,0,1:T(8,128)(2,1)}), bf16[3,8,128,256]{2,3,0,1:T(8,128)(2,1)}, u32[]{:S(2)}, u32[]{:S(2)}) async-start(bf16[3,8,128,256]{2,3,0,1:T(8,128)(2,1)} %copy.84), calls=%async_computation | async-start | bytes 3145728 | tf_op jit(solution)/shard_map/all_to_all | solution.py:163
  37.6 124.3 %collective-permute-start.1 = (bf16[256,2048]{1,0:T(8,128)(2,1)}, bf16[256,2048]{1,0:T(8,128)(2,1)}, u32[]{:S(2)}, u32[]{:S(2)}) collective-permute-start(bf16[256,2048]{1,0:T(8,128)(2,1)} %param.11), channel_id=1, source_target_pairs={{0,1},{1,0},{2,3},{3,2},{4,5},{5,4},{6,7},{7,6},{8,9},{9,8},{10,11... | collective-permute-start | bytes 3145736 | tf_op jit(solution)/shard_map/ppermute | solution.py:97
  38.0 39.2 %collective-permute-start.12 = (bf16[128,2048]{1,0:T(8,128)(2,1)S(1)}, bf16[128,2048]{1,0:T(8,128)(2,1)S(1)}, u32[]{:S(2)}, u32[]{:S(2)}) collective-permute-start(bf16[128,2048]{1,0:T(8,128)(2,1)S(1)} %collective-permute-done.11), channel_id=1, source_target_pairs={{2,0},{3,1},{4,2},{5,3},{6,4},{7,5},{10,8},{11,9},{12,10},{13,11},... | collective-permute-start | bytes 1572872 | tf_op jit(solution)/shard_map/ppermute | solution.py:73
  39.3 39.2 %collective-permute-start.10 = (bf16[128,2048]{1,0:T(8,128)(2,1)S(1)}, bf16[128,2048]{1,0:T(8,128)(2,1)S(1)}, u32[]{:S(2)}, u32[]{:S(2)}) collective-permute-start(bf16[128,2048]{1,0:T(8,128)(2,1)S(1)} %collective-permute-done.9), channel_id=1, source_target_pairs={{0,2},{1,3},{2,4},{3,5},{4,6},{5,7},{8,10},{9,11},{10,12},{11,13},... | collective-permute-start | bytes 1572872 | tf_op jit(solution)/shard_map/ppermute | solution.py:72
  77.2 23.6 %collective-permute-start.13 = (bf16[128,2048]{1,0:T(8,128)(2,1)S(1)}, bf16[128,2048]{1,0:T(8,128)(2,1)S(1)}, u32[]{:S(2)}, u32[]{:S(2)}) collective-permute-start(bf16[128,2048]{1,0:T(8,128)(2,1)S(1)} %collective-permute-done.12), channel_id=1, source_target_pairs={{2,0},{3,1},{4,2},{5,3},{6,4},{7,5},{10,8},{11,9},{12,10},{13,11},... | collective-permute-start | bytes 1572872 | tf_op jit(solution)/shard_map/ppermute | solution.py:73
  101.0 18.1 %collective-permute-start.14 = (bf16[4,128,2048]{2,1,0:T(8,128)(2,1)S(1)}, bf16[4,128,2048]{2,1,0:T(8,128)(2,1)}, u32[]{:S(2)}, u32[]{:S(2)}) collective-permute-start(bf16[4,128,2048]{2,1,0:T(8,128)(2,1)S(1)} %constant_dynamic-slice_fusion), channel_id=1, source_target_pairs={{0,1},{1,0},{2,3},{3,2},{4,5},{5,4},{6,7},{7,6},{8,9},{9,8},{10,11... | collective-permute-start | bytes 6291464 | tf_op jit(solution)/shard_map/ppermute | solution.py:78
  107.5 3.3 %copy-start.5 = (bf16[1,8,128,256]{3,2,1,0:T(8,128)(2,1)}, bf16[1,8,128,256]{3,2,1,0:T(8,128)(2,1)S(1)}, u32[]{:S(2)}) copy-start(bf16[1,8,128,256]{3,2,1,0:T(8,128)(2,1)S(1)} %copy.107) | copy-start | bytes 1572868
  110.7 2.1 copy-start.10
  112.5 5.4 %copy-start = (f32[1024,1024]{0,1:T(8,128)}, f32[1024,1024]{0,1:T(8,128)S(1)}, u32[]{:S(2)}) copy-start(f32[1024,1024]{0,1:T(8,128)S(1)} %fusion.51) | copy-start | bytes 12582916
  115.4 2.5 copy-start.3
  115.4 2.5 copy-start.13
  117.9 3.9 %copy-start.19 = (bf16[4,1,128,256]{3,2,0,1:T(8,128)(2,1)S(1)}, bf16[4,1,128,256]{3,2,0,1:T(8,128)(2,1)}, u32[]{:S(2)}) copy-start(bf16[4,1,128,256]{3,2,0,1:T(8,128)(2,1)} %fusion.29) | copy-start | bytes 786436
  126.8 3.8 %copy-start.4 = (f32[1024,1024]{0,1:T(8,128)S(1)}, f32[1024,1024]{0,1:T(8,128)}, u32[]{:S(2)}) copy-start(f32[1024,1024]{0,1:T(8,128)} %copy-done.3) | copy-start | bytes 12582916
  126.8 3.8 %copy-start.14 = (bf16[1,8,128,256]{3,2,1,0:T(8,128)(2,1)S(1)}, bf16[1,8,128,256]{3,2,1,0:T(8,128)(2,1)}, u32[]{:S(2)}) copy-start(bf16[1,8,128,256]{3,2,1,0:T(8,128)(2,1)} %copy.109) | copy-start | bytes 1572868
  126.8 4.0 %copy-start.15 = (bf16[1024,256]{0,1:T(8,128)(2,1)S(1)}, bf16[1024,256]{0,1:T(8,128)(2,1)}, u32[]{:S(2)}) copy-start(bf16[1024,256]{0,1:T(8,128)(2,1)} %select_n.144) | copy-start | bytes 1572868
  130.8 2.0 copy-start.11
  130.8 3.3 %copy-start.6 = (bf16[1,8,128,256]{3,2,1,0:T(8,128)(2,1)S(1)}, bf16[1,8,128,256]{3,2,1,0:T(8,128)(2,1)}, u32[]{:S(2)}) copy-start(bf16[1,8,128,256]{3,2,1,0:T(8,128)(2,1)} %copy-done.5) | copy-start | bytes 1572868
  132.8 2.8 %copy-start.1 = (f32[1024,1024]{0,1:T(8,128)S(1)}, f32[1024,1024]{0,1:T(8,128)}, u32[]{:S(2)}) copy-start(f32[1024,1024]{0,1:T(8,128)} %copy-done) | copy-start | bytes 12582916
  145.0 4.3 %copy-start.20 = (bf16[1024,128]{0,1:T(8,128)(2,1)S(1)}, bf16[1024,128]{0,1:T(8,128)(2,1)}, u32[]{:S(2)}) copy-start(bf16[1024,128]{0,1:T(8,128)(2,1)} %convolution_convert_fusion.3) | copy-start | bytes 786436
  147.3 8.9 %collective-permute-start = (bf16[1024,256]{0,1:T(8,128)(2,1)}, bf16[1024,256]{0,1:T(8,128)(2,1)}, u32[]{:S(2)}, u32[]{:S(2)}) collective-permute-start(bf16[1024,256]{0,1:T(8,128)(2,1)} %pad_maximum_fusion.2), channel_id=1, source_target_pairs={{0,1},{1,0},{2,3},{3,2},{4,5},{5,4},{6,7},{7,6},{8,9},{9,8},{10,11... | collective-permute-start | bytes 1572872 | tf_op jit(solution)/shard_map/ppermute | solution.py:96
  150.8 4.3 %copy-start.17 = (bf16[1024,128]{0,1:T(8,128)(2,1)S(1)}, bf16[1024,128]{0,1:T(8,128)(2,1)}, u32[]{:S(2)}) copy-start(bf16[1024,128]{0,1:T(8,128)(2,1)} %fusion.17) | copy-start | bytes 786436
  152.1 3.0 %copy-start.18 = (bf16[1024,128]{0,1:T(8,128)(2,1)S(1)}, bf16[1024,128]{0,1:T(8,128)(2,1)}, u32[]{:S(2)}) copy-start(bf16[1024,128]{0,1:T(8,128)(2,1)} %fusion.20) | copy-start | bytes 786436
  161.9 10.5 %copy-start.7 = (bf16[1,8,128,256]{2,3,0,1:T(8,128)(2,1)S(1)}, bf16[1,8,128,256]{2,3,0,1:T(8,128)(2,1)}, u32[]{:S(2)}) copy-start(bf16[1,8,128,256]{2,3,0,1:T(8,128)(2,1)} %copy.95) | copy-start | bytes 1572868
  161.9 10.4 %copy-start.8 = (bf16[1,8,128,256]{2,3,0,1:T(8,128)(2,1)S(1)}, bf16[1,8,128,256]{2,3,0,1:T(8,128)(2,1)}, u32[]{:S(2)}) copy-start(bf16[1,8,128,256]{2,3,0,1:T(8,128)(2,1)} %copy.96) | copy-start | bytes 1572868
  161.9 10.4 %copy-start.9 = (bf16[1,8,128,256]{2,3,0,1:T(8,128)(2,1)S(1)}, bf16[1,8,128,256]{2,3,0,1:T(8,128)(2,1)}, u32[]{:S(2)}) copy-start(bf16[1,8,128,256]{2,3,0,1:T(8,128)(2,1)} %copy.97) | copy-start | bytes 1572868
  164.8 1.9 copy-start.2
  167.9 16.2 %collective-permute-start.2 = (bf16[128,2048]{1,0:T(8,128)(2,1)}, bf16[128,2048]{1,0:T(8,128)(2,1)}, u32[]{:S(2)}, u32[]{:S(2)}) collective-permute-start(bf16[128,2048]{1,0:T(8,128)(2,1)} %get-tuple-element.23), channel_id=1, source_target_pairs={{0,2},{1,3},{2,4},{3,5},{4,6},{5,7},{8,10},{9,11},{10,12},{11,13},... | collective-permute-start | bytes 1572872 | tf_op jit(solution)/shard_map/ppermute | solution.py:123
  173.6 89.4 %all-to-all-start.1 = ((bf16[3,8,128,256]{2,3,0,1:T(8,128)(2,1)}), bf16[3,8,128,256]{2,3,0,1:T(8,128)(2,1)}, u32[]{:S(2)}, u32[]{:S(2)}) async-start(bf16[3,8,128,256]{2,3,0,1:T(8,128)(2,1)} %pad_maximum_fusion.1), calls=%async_computation.1 | async-start | bytes 3145728 | tf_op jit(solution)/shard_map/all_to_all | solution.py:218
  178.0 4.4 %copy-start.16 = (bf16[128,2048]{1,0:T(8,128)(2,1)S(1)}, bf16[128,2048]{1,0:T(8,128)(2,1)}, u32[]{:S(2)}) copy-start(bf16[128,2048]{1,0:T(8,128)(2,1)} %get-tuple-element.24) | copy-start | bytes 1572868
  178.0 68.4 %all-reduce.2.cloned.1.call-start = ((), (), s32[]{:S(2)}) async-start(), calls=%async_computation.2 | async-start | bytes 2097152 | tf_op jit(solution)/shard_map/psum | solution.py:198
  182.3 35.2 %collective-permute-start.5 = (bf16[128,2048]{1,0:T(8,128)(2,1)S(1)}, bf16[128,2048]{1,0:T(8,128)(2,1)S(1)}, u32[]{:S(2)}, u32[]{:S(2)}) collective-permute-start(bf16[128,2048]{1,0:T(8,128)(2,1)S(1)} %copy-done.16), channel_id=1, source_target_pairs={{2,0},{3,1},{4,2},{5,3},{6,4},{7,5},{10,8},{11,9},{12,10},{13,11},... | collective-permute-start | bytes 1572872 | tf_op jit(solution)/shard_map/ppermute | solution.py:124
  185.6 34.1 %collective-permute-start.3 = (bf16[128,2048]{1,0:T(8,128)(2,1)S(1)}, bf16[128,2048]{1,0:T(8,128)(2,1)S(1)}, u32[]{:S(2)}, u32[]{:S(2)}) collective-permute-start(bf16[128,2048]{1,0:T(8,128)(2,1)S(1)} %fusion.35), channel_id=1, source_target_pairs={{0,2},{1,3},{2,4},{3,5},{4,6},{5,7},{8,10},{9,11},{10,12},{11,13},... | collective-permute-start | bytes 1572872 | tf_op jit(solution)/shard_map/ppermute | solution.py:123
  221.6 22.1 %collective-permute-start.6 = (bf16[128,2048]{1,0:T(8,128)(2,1)S(1)}, bf16[128,2048]{1,0:T(8,128)(2,1)S(1)}, u32[]{:S(2)}, u32[]{:S(2)}) collective-permute-start(bf16[128,2048]{1,0:T(8,128)(2,1)S(1)} %get-tuple-element.22), channel_id=1, source_target_pairs={{2,0},{3,1},{4,2},{5,3},{6,4},{7,5},{10,8},{11,9},{12,10},{13,11},... | collective-permute-start | bytes 1572872 | tf_op jit(solution)/shard_map/ppermute | solution.py:124
  222.9 26.3 %collective-permute-start.4 = (bf16[128,2048]{1,0:T(8,128)(2,1)S(1)}, bf16[128,2048]{1,0:T(8,128)(2,1)S(1)}, u32[]{:S(2)}, u32[]{:S(2)}) collective-permute-start(bf16[128,2048]{1,0:T(8,128)(2,1)S(1)} %get-tuple-element.21), channel_id=1, source_target_pairs={{0,2},{1,3},{2,4},{3,5},{4,6},{5,7},{8,10},{9,11},{10,12},{11,13},... | collective-permute-start | bytes 1572872 | tf_op jit(solution)/shard_map/ppermute | solution.py:123
  245.1 15.7 %collective-permute-start.7 = (bf16[128,2048]{1,0:T(8,128)(2,1)S(1)}, bf16[128,2048]{1,0:T(8,128)(2,1)S(1)}, u32[]{:S(2)}, u32[]{:S(2)}) collective-permute-start(bf16[128,2048]{1,0:T(8,128)(2,1)S(1)} %fusion.34), channel_id=1, source_target_pairs={{2,0},{3,1},{4,2},{5,3},{6,4},{7,5},{10,8},{11,9},{12,10},{13,11},... | collective-permute-start | bytes 1572872 | tf_op jit(solution)/shard_map/ppermute | solution.py:124
Sparse Core Ops, SparseCore 0:
  191.5 52.6 all-reduce.1

commit v10 on v7

--- a/solution.py
+++ b/solution.py
@@ -56,7 +56,7 @@
     )
 
 
-def chip_layer_out(att_flat, w_out):
+def chip_partial_rows(att_flat, w_out):
     n = lax.axis_size("seq")
     rows = att_flat.shape[0] // n
     chips = n // 2
@@ -76,6 +76,13 @@
     chip_partial = lax.dot_general(
         att_chip, w_chip, (((2,), (0,)), ((), ())), preferred_element_type=jnp.float32
     )
+    return chip_partial
+
+
+def chip_exchange(chip_partial):
+    n = lax.axis_size("seq")
+    chips = n // 2
+    z = lax.axis_index("seq") // 2
     total = lax.dynamic_index_in_dim(chip_partial, z, 0, keepdims=False)
     sent = chip_partial.astype(jnp.bfloat16)
     for k in range(1, chips):
@@ -130,7 +137,9 @@
     ]
     att_flat = jnp.concatenate([f[0] for f in fwd], axis=1)
 
-    layer_out = chip_layer_out(att_flat, w_out).astype(jnp.bfloat16)[None]
+    chip_partial = chip_partial_rows(att_flat, w_out)
+    chip_partial, fwd = lax.optimization_barrier((chip_partial, fwd))
+    layer_out = chip_exchange(chip_partial).astype(jnp.bfloat16)[None]
 
     g_flat = lax.dot_general(
         grad_full, w_out, (((1,), (1,)), ((), ())), preferred_element_type=jnp.float32

time: 221 us -> 229 us (1.036)
  waiting for transfers between devices: 128 us -> 142 us
  matrix products: 32 us -> 21.3 us
  local copies, waits for them, and re-layouts: 18.5 us -> 21.6 us
    ppermute x5, waiting for transfers between devices: 20.2 us -> 70.3 us  [the longest x3 70.1 us: chip_exchange(): total = total + lax.ppermute(piece, 'seq', pairs).astype(jnp.float32)]
    psum x1, waiting for transfers between devices: 36.3 us -> 0.01 us  [shards(): w_rows = lax.psum(w_rows.astype(jnp.bfloat16), 'dp').astype(jnp.float32)]
    dot_general x2, matrix products: 4.47 us -> 1.67 us  [attend_back(): v_grad = jnp.dot(prob_low.T, g, preferred_element_type=jnp.float32)]
    convert_element_type x0 -> x1, other arithmetic: none -> 2.66 us  [chip_exchange(): sent = chip_partial.astype(jnp.bfloat16)]
    dot_general x2, matrix products: 4.24 us -> 1.63 us  [attend_back(): prob_grad = jnp.dot(g, v.T, preferred_element_type=jnp.float32)]
    dot_general x1, matrix products: 5.71 us -> 3.35 us  [shards(): jnp.einsum('bnf,bnk->bfk', att_blocks, grad_blocks, preferred_element_typ...]
    unnamed x38 -> x40, local copies, waits for them, and re-layouts: 12 us -> 13.8 us
  transfers between devices with their start and end apart: 9 -> 9, of which waited for: 3 -> 4; matrix products, arithmetic and copies ran while one was open for 27% -> 16% of each run, Pallas kernels for 0% -> 0%
where the time goes in v10:
time: 229 us
  waiting for transfers between devices  142 us (62%)
  local copies, waits for them, and re-layouts  21.6 us (9%)
  matrix products  21.3 us (9%)
  starting transfers between devices  16.1 us (7%)
  between operations  14.6 us (6%)
  other arithmetic  12.9 us (6%)
    all_to_all x1, waiting for transfers between devices, shards(): lax.all_to_all(stacked, 'seq', split_axis=1, concat_axis=1, tiled=True)  71 us
    ppermute x3, waiting for transfers between devices, chip_exchange(): total = total + lax.ppermute(piece, 'seq', pairs).astype(jnp.float32)  70.1 us
    unnamed x40, local copies, waits for them, and re-layouts  13.8 us
    all_to_all x1, starting transfers between devices, shards(): lax.all_to_all(stacked, 'seq', split_axis=1, concat_axis=1, tiled=True)  6.33 us
    dot_general x1, matrix products, chip_partial_rows(): lax.dot_general(att_chip, w_chip, (((2,), (0,)), ((), ())), preferred_ele...  4.8 us
    ppermute x3, starting transfers between devices, chip_exchange(): total = total + lax.ppermute(piece, 'seq', pairs).astype(jnp.float32)  4.72 us
  transfers between devices with their start and end apart: 9, of which 4 were waited for; matrix products, arithmetic and copies ran while one was open for 16% of the time, Pallas kernels for 0%

profile of v10, /device:TPU:0, one launch (start us, length us, event | category | flops | bytes accessed | tf_op | source)
XLA Modules:
  0.0 228.5 jit_solution(11521354522159910261)
XLA Ops:
  7.2 0.7 all-gather.3.cloned.1.call-update
  7.9 1.3 copy.75
  9.2 1.3 copy.74
  10.5 1.3 copy.73
  12.1 1.2 copy.76
  13.3 6.3 %all-to-all-start = ((bf16[3,8,128,256]{2,3,0,1:T(8,128)(2,1)}), bf16[3,8,128,256]{2,3,0,1:T(8,128)(2,1)S(1)}, u32[]{:S(2)}, u32[]{:S(2)}) async-start(bf16[3,8,128,256]{2,3,0,1:T(8,128)(2,1)} %copy.76), calls=%async_computation | async-start | bytes 3145728 | tf_op jit(solution)/shard_map/all_to_all | solution.py:126
  20.1 71.0 %all-to-all-done = bf16[3,8,128,256]{2,3,0,1:T(8,128)(2,1)S(1)} async-done(((bf16[3,8,128,256]{2,3,0,1:T(8,128)(2,1)}), bf16[3,8,128,256]{2,3,0,1:T(8,128)(2,1)S(1)}, u32[]{:S(2)}, u32[]{:S(2)}) %all-to-all-start) | async-done | bytes 1572896 | tf_op jit(solution)/shard_map/all_to_all | solution.py:126
  92.0 0.7 fusion.46
  93.1 1.3 select_reduce_fusion.1
  94.4 2.4 %fusion.65 = (f32[1024]{0:T(1024)S(1)}, f32[1024,1024]{0,1:T(8,128)S(1)}, f32[1024]{0:T(1024)S(1)}, f32[1024,1024]{0,1:T(8,128)S(1)}) fusion(f32[1024]{0:T(1024)S(1)} %get-tuple-element.29, f32[1024,1024]{0,1:T(8,128)S(1)} %get-tuple-element.54, pred[128,8,8,128]{3,2,1,0:T(8,128)(4,1)S(1)} %bitcast.105, f32[1024]{0:T(1024)S(1)} %get-tuple-element.30, ...), kind=kLoop, calls=%fused_computation.86 | loop fusion | flops 8386560 | bytes 17842176 | tf_op jit(solution)/shard_map/reduce_sum | solution.py:34
  96.8 0.5 fusion.28
  97.3 0.5 fusion.31
  97.8 0.9 copy-done
  98.7 1.3 copy-done.2
  100.0 0.9 fusion.64
  100.9 0.5 collective-permute-start.1
  101.8 0.7 fusion.69
  102.6 0.5 copy.98
  103.7 1.4 reshape.56
  105.1 0.7 fusion.70
  106.3 0.7 copy.101
  107.1 4.8 %fusion.2 = f32[4,128,2048]{2,1,0:T(8,128)} fusion(bf16[256,2048]{1,0:T(8,128)(2,1)} %collective-permute-done.1, bf16[256,2048]{1,0:T(8,128)(2,1)} %param.11, bf16[4,128,256]{2,1,0:T(8,128)(2,1)S(1)} %get-tuple-element.55, bf16[4,128,256]{2,1,0:T(8,128)(2,1)S(1)} %get-tuple-element.56), kind=kOutput, calls=%fused_computation.10 | convolution fusion | flops 1078984704 | bytes 6815744 | tf_op jit(solution)/shard_map/dot_general | solution.py:76
  111.9 3.9 %fusion.13 = bf16[1024,256]{0,1:T(8,128)(2,1)S(1)} fusion(bf16[256,2048]{1,0:T(8,128)(2,1)} %param.11, bf16[1,1024,2048]{2,1,0:T(8,128)(2,1)} %all-gather.3.cloned.1.call-done), kind=kOutput, calls=%fused_computation.26 | convolution fusion | flops 1074003968 | bytes 5767168 | tf_op jit(solution)/shard_map/dot_general | solution.py:144
  115.8 0.8 fusion.25
  116.9 0.8 multiply_convert_fusion
  117.7 0.8 convolution_convert_fusion
  118.5 0.5 convolution_convert_fusion.2
  119.0 0.9 copy-done.1
  119.9 0.8 fusion.22
  120.8 0.8 multiply_convert_fusion.1
  121.6 0.8 convolution_convert_fusion.1
  122.4 0.5 convolution_convert_fusion.3
  123.6 1.3 pad_maximum_fusion.1
  124.9 4.4 %all-to-all-start.1 = ((bf16[3,8,128,256]{2,3,0,1:T(8,128)(2,1)}), bf16[3,8,128,256]{2,3,0,1:T(8,128)(2,1)}, u32[]{:S(2)}, u32[]{:S(2)}) async-start(bf16[3,8,128,256]{2,3,0,1:T(8,128)(2,1)} %pad_maximum_fusion.1), calls=%async_computation.1 | async-start | bytes 3145728 | tf_op jit(solution)/shard_map/all_to_all | solution.py:173
  129.5 2.7 %convert_element_type.90 = bf16[4,128,2048]{2,1,0:T(8,128)(2,1)S(1)} convert(f32[4,128,2048]{2,1,0:T(8,128)} %fusion.2) | non-fusion elementwise | flops 1048576 | bytes 6291456 | tf_op jit(solution)/shard_map/convert_element_type | solution.py:87
  132.2 0.8 copy-done.9
  132.9 3.4 %convert_reduce_fusion = bf16[256,2048]{1,0:T(8,128)(2,1)} fusion(bf16[8,128,2048]{2,1,0:T(8,128)(2,1)S(1)} %bitcast.127, bf16[32,8,8,128]{3,2,1,0:T(8,128)(2,1)S(1)} %copy-done.8), kind=kOutput, calls=%fused_computation | convolution fusion | flops 1081606144 | bytes 5767168 | tf_op jit(solution)/shard_map/bnf,bnk->bfk/dot_general | solution.py:149
  136.3 1.0 dynamic-slice_bitcast_fusion.2
  137.3 3.6 %collective-permute-start.4 = (bf16[128,2048]{1,0:T(8,128)(2,1)}, bf16[128,2048]{1,0:T(8,128)(2,1)S(1)}, u32[]{:S(2)}, u32[]{:S(2)}) collective-permute-start(bf16[128,2048]{1,0:T(8,128)(2,1)} %get-tuple-element.38), channel_id=1, source_target_pairs={{0,6},{1,7},{2,0},{3,1},{4,2},{5,3},{6,4},{7,5},{8,14},{9,15},{10,... | collective-permute-start | bytes 1572872 | tf_op jit(solution)/shard_map/ppermute | solution.py:91
  140.9 1.1 collective-permute-start.2
  142.0 27.0 %collective-permute-done.4 = bf16[128,2048]{1,0:T(8,128)(2,1)S(1)} collective-permute-done((bf16[128,2048]{1,0:T(8,128)(2,1)}, bf16[128,2048]{1,0:T(8,128)(2,1)S(1)}, u32[]{:S(2)}, u32[]{:S(2)}) %collective-permute-start.4) | collective-permute-done | bytes 524320 | tf_op jit(solution)/shard_map/ppermute | solution.py:91
  169.0 43.1 %collective-permute-done.3 = bf16[128,2048]{1,0:T(8,128)(2,1)S(1)} collective-permute-done((bf16[128,2048]{1,0:T(8,128)(2,1)S(1)}, bf16[128,2048]{1,0:T(8,128)(2,1)S(1)}, u32[]{:S(2)}, u32[]{:S(2)}) %collective-permute-start.3) | collective-permute-done | bytes 524320 | tf_op jit(solution)/shard_map/ppermute | solution.py:91
  212.1 2.3 %fusion.37 = bf16[1,128,2048]{2,1,0:T(8,128)(2,1)} fusion(bf16[128,2048]{1,0:T(8,128)(2,1)S(1)} %collective-permute-done.4, bf16[128,2048]{1,0:T(8,128)(2,1)S(1)} %collective-permute-done.3, bf16[128,2048]{1,0:T(8,128)(2,1)S(1)} %collective-permute-done.2, f32[4,128,2048]{2,1,0:T(8,128)} %fusion.2, s32[]{:T(128)S(6)} %select_n.79), kind=kLoop, calls=%fused_computation.42 | loop fusion | flops 1835008 | bytes 3145732 | tf_op jit(solution)/shard_map/broadcast_in_dim | solution.py:142
  214.4 2.8 %convert_multiply_fusion = f32[256,2048]{1,0:T(8,128)} fusion(bf16[256,2048]{1,0:T(8,128)(2,1)} %all-reduce.2.cloned.1.call-done), kind=kLoop, calls=%fused_computation.13 | loop fusion | flops 1048576 | bytes 3145728 | tf_op jit(solution)/shard_map/div | solution.py:155
  217.2 1.5 fusion.67
  218.6 1.0 copy.90
  219.7 1.0 copy.91
  220.7 1.0 copy.92
  (55 shorter events, 4.3 us)
Async XLA Ops:
  7.2 104.7 %all-gather.3.cloned.1.call-start = ((), (), s32[]{:S(2)}) async-start(), calls=%async_computation.3 | async-start | bytes 4718592 | tf_op jit(solution)/shard_map/all_gather | solution.py:110
  11.9 7.8 %copy-start.10 = (s32[1,9]{1,0:T(1,128)S(1)}, s32[1,9]{1,0:T(1,128)}, u32[]{:S(2)}) copy-start(s32[1,9]{1,0:T(1,128)} %param.12) | copy-start | bytes 112
  11.9 7.9 %copy-start.11 = (s32[1,32]{1,0:T(1,128)S(1)}, s32[1,32]{1,0:T(1,128)}, u32[]{:S(2)}) copy-start(s32[1,32]{1,0:T(1,128)} %param.13) | copy-start | bytes 388
  13.3 77.9 %all-to-all-start = ((bf16[3,8,128,256]{2,3,0,1:T(8,128)(2,1)}), bf16[3,8,128,256]{2,3,0,1:T(8,128)(2,1)S(1)}, u32[]{:S(2)}, u32[]{:S(2)}) async-start(bf16[3,8,128,256]{2,3,0,1:T(8,128)(2,1)} %copy.76), calls=%async_computation | async-start | bytes 3145728 | tf_op jit(solution)/shard_map/all_to_all | solution.py:126
  91.5 2.9 %copy-start.6 = (bf16[1,8,128,256]{3,2,1,0:T(8,128)(2,1)}, bf16[1,8,128,256]{3,2,1,0:T(8,128)(2,1)S(1)}, u32[]{:S(2)}) copy-start(bf16[1,8,128,256]{3,2,1,0:T(8,128)(2,1)S(1)} %copy.96) | copy-start | bytes 1572868
  92.0 5.3 %copy-start.4 = (bf16[1,8,128,256]{3,2,1,0:T(8,128)(2,1)}, bf16[1,8,128,256]{3,2,1,0:T(8,128)(2,1)S(1)}, u32[]{:S(2)}) copy-start(bf16[1,8,128,256]{3,2,1,0:T(8,128)(2,1)S(1)} %copy.97) | copy-start | bytes 1572868
  96.8 2.0 copy-start
  96.8 3.2 %copy-start.2 = (f32[1024,1024]{0,1:T(8,128)}, f32[1024,1024]{0,1:T(8,128)S(1)}, u32[]{:S(2)}) copy-start(f32[1024,1024]{0,1:T(8,128)S(1)} %get-tuple-element.16) | copy-start | bytes 12582916
  100.9 2.8 %collective-permute-start = (bf16[1024,256]{0,1:T(8,128)(2,1)S(1)}, bf16[1024,256]{0,1:T(8,128)(2,1)}, u32[]{:S(2)}, u32[]{:S(2)}) collective-permute-start(bf16[1024,256]{0,1:T(8,128)(2,1)S(1)} %get-tuple-element.49), channel_id=1, source_target_pairs={{0,1},{1,0},{2,3},{3,2},{4,5},{5,4},{6,7},{7,6},{8,9},{9,8},{10,11... | collective-permute-start | bytes 1572872 | tf_op jit(solution)/shard_map/ppermute | solution.py:67
  100.9 6.1 %collective-permute-start.1 = (bf16[256,2048]{1,0:T(8,128)(2,1)}, bf16[256,2048]{1,0:T(8,128)(2,1)}, u32[]{:S(2)}, u32[]{:S(2)}) collective-permute-start(bf16[256,2048]{1,0:T(8,128)(2,1)} %param.11), channel_id=1, source_target_pairs={{0,1},{1,0},{2,3},{3,2},{4,5},{5,4},{6,7},{7,6},{8,9},{9,8},{10,11... | collective-permute-start | bytes 3145736 | tf_op jit(solution)/shard_map/ppermute | solution.py:68
  111.9 3.9 %copy-start.3 = (f32[1024,1024]{0,1:T(8,128)S(1)}, f32[1024,1024]{0,1:T(8,128)}, u32[]{:S(2)}) copy-start(f32[1024,1024]{0,1:T(8,128)} %copy-done.2) | copy-start | bytes 12582916
  115.8 1.0 copy-start.5
  116.9 1.7 copy-start.7
  117.7 2.2 copy-start.1
  124.9 7.3 %copy-start.8 = (bf16[32,8,8,128]{3,2,1,0:T(8,128)(2,1)S(1)}, bf16[32,8,8,128]{3,2,1,0:T(8,128)(2,1)}, u32[]{:S(2)}) copy-start(bf16[32,8,8,128]{3,2,1,0:T(8,128)(2,1)} %get-tuple-element.48) | copy-start | bytes 1572868
  124.9 92.3 %all-to-all-start.1 = ((bf16[3,8,128,256]{2,3,0,1:T(8,128)(2,1)}), bf16[3,8,128,256]{2,3,0,1:T(8,128)(2,1)}, u32[]{:S(2)}, u32[]{:S(2)}) async-start(bf16[3,8,128,256]{2,3,0,1:T(8,128)(2,1)} %pad_maximum_fusion.1), calls=%async_computation.1 | async-start | bytes 3145728 | tf_op jit(solution)/shard_map/all_to_all | solution.py:173
  129.4 85.0 %all-reduce.2.cloned.1.call-start = ((), (), s32[]{:S(2)}) async-start(), calls=%async_computation.2 | async-start | bytes 2097152 | tf_op jit(solution)/shard_map/psum | solution.py:153
  129.5 3.5 %copy-start.9 = (bf16[1,1024,2048]{2,1,0:T(8,128)(2,1)S(1)}, bf16[1,1024,2048]{2,1,0:T(8,128)(2,1)}, u32[]{:S(2)}) copy-start(bf16[1,1024,2048]{2,1,0:T(8,128)(2,1)} %all-gather.3.cloned.1.call-done) | copy-start | bytes 12582916
  137.3 31.7 %collective-permute-start.4 = (bf16[128,2048]{1,0:T(8,128)(2,1)}, bf16[128,2048]{1,0:T(8,128)(2,1)S(1)}, u32[]{:S(2)}, u32[]{:S(2)}) collective-permute-start(bf16[128,2048]{1,0:T(8,128)(2,1)} %get-tuple-element.38), channel_id=1, source_target_pairs={{0,6},{1,7},{2,0},{3,1},{4,2},{5,3},{6,4},{7,5},{8,14},{9,15},{10,... | collective-permute-start | bytes 1572872 | tf_op jit(solution)/shard_map/ppermute | solution.py:91
  140.9 71.2 %collective-permute-start.3 = (bf16[128,2048]{1,0:T(8,128)(2,1)S(1)}, bf16[128,2048]{1,0:T(8,128)(2,1)S(1)}, u32[]{:S(2)}, u32[]{:S(2)}) collective-permute-start(bf16[128,2048]{1,0:T(8,128)(2,1)S(1)} %get-tuple-element.39), channel_id=1, source_target_pairs={{0,4},{1,5},{2,6},{3,7},{4,0},{5,1},{6,2},{7,3},{8,12},{9,13},{10,... | collective-permute-start | bytes 1572872 | tf_op jit(solution)/shard_map/ppermute | solution.py:91
  140.9 71.2 %collective-permute-start.2 = (bf16[128,2048]{1,0:T(8,128)(2,1)S(1)}, bf16[128,2048]{1,0:T(8,128)(2,1)S(1)}, u32[]{:S(2)}, u32[]{:S(2)}) collective-permute-start(bf16[128,2048]{1,0:T(8,128)(2,1)S(1)} %get-tuple-element.37), channel_id=1, source_target_pairs={{0,2},{1,3},{2,4},{3,5},{4,6},{5,7},{6,0},{7,1},{8,10},{9,11},{10,... | collective-permute-start | bytes 1572872 | tf_op jit(solution)/shard_map/ppermute | solution.py:91
Sparse Core Ops, SparseCore 0:
  9.6 83.0 all-gather.2
  136.4 53.7 all-reduce.1

commit v11 on v7

--- a/solution.py
+++ b/solution.py
@@ -106,18 +106,10 @@
     group_width = width // groups
     local_heads = group_width // HD
 
-    def to_groups(values):
-        return values.reshape(nodes_here, groups, group_width).transpose(1, 0, 2)
-
     stacked = jnp.stack(
-        [
-            to_groups(asking_vectors_matrix[0]),
-            to_groups(matched_keys_matrix[0]),
-            to_groups(carried_vectors_matrix[0]),
-        ]
+        [asking_vectors_matrix[0], matched_keys_matrix[0], carried_vectors_matrix[0]]
     )
-    heads = lax.all_to_all(stacked, "seq", split_axis=1, concat_axis=1, tiled=True)
-    heads = heads.reshape(3, nodes, group_width)
+    heads = lax.all_to_all(stacked, "seq", split_axis=2, concat_axis=1, tiled=True)
 
     allowed = tile_mask(panel_entry_offsets[0], rightward_panel_per_entry[0], nodes)
 
@@ -157,12 +149,9 @@
         )
         for h in range(local_heads)
     ]
-    grads = jnp.stack(
-        [jnp.concatenate([b[i] for b in bwd], axis=1).reshape(groups, nodes_here, group_width)
-         for i in range(3)]
-    )
-    back = lax.all_to_all(grads, "seq", split_axis=1, concat_axis=1, tiled=True)
-    back = back.transpose(0, 2, 1, 3).reshape(3, 1, nodes_here, width)
+    grads = jnp.stack([jnp.concatenate([b[i] for b in bwd], axis=1) for i in range(3)])
+    back = lax.all_to_all(grads, "seq", split_axis=1, concat_axis=2, tiled=True)
+    back = back.reshape(3, 1, nodes_here, width)
     return (layer_out, back[0], back[1], back[2], w_out_grad)
 
 

time: 221 us -> 251 us (1.14)
  local copies, waits for them, and re-layouts: 18.5 us -> 33 us
  waiting for transfers between devices: 128 us -> 139 us
  other arithmetic: 12.6 us -> 15.8 us
    ppermute x3, waiting for transfers between devices: 20.2 us -> 31.3 us  [chip_layer_out(): total = total + lax.ppermute(piece, 'seq', pairs).astype(jnp.float32)]
    slice x1 -> x4, local copies, waits for them, and re-layouts: 0.15 us -> 5.92 us  [shards(): return (layer_out, back[0], back[1], back[2], w_out_grad)]
    all_to_all x2, waiting for transfers between devices: 70.5 us -> 75.8 us  [the longest x1 75.8 us: shards(): lax.all_to_all(stacked, 'seq', split_axis=2, concat_axis=1, tiled=True)]
    psum x1, waiting for transfers between devices: 36.3 us -> 31.6 us  [shards(): w_rows = lax.psum(w_rows.astype(jnp.bfloat16), 'dp').astype(jnp.float32)]
    another operation x2 -> x4, other arithmetic: 1.52 us -> 5.83 us  [the longest x1 4.52 us: shards(): jnp.stack([asking_vectors_matrix[0], matched_keys_matrix[0], carried_vect...]
    squeeze x0 -> x3, local copies, waits for them, and re-layouts: none -> 3.1 us  [shards(): return (layer_out, back[0], back[1], back[2], w_out_grad)]
    unnamed x38 -> x33, local copies, waits for them, and re-layouts: 12 us -> 13.2 us
  transfers between devices with their start and end apart: 9 -> 9, of which waited for: 3 -> 3; matrix products, arithmetic and copies ran while one was open for 27% -> 29% of each run, Pallas kernels for 0% -> 0%
where the time goes in v11:
time: 251 us; the launch traced here: 250 us
  waiting for transfers between devices  139 us (55%)
  local copies, waits for them, and re-layouts  33 us (13%)
  matrix products  31.9 us (13%)
  other arithmetic  15.8 us (6%)
  starting transfers between devices  15.5 us (6%)
  between operations  14.4 us (6%)
    all_to_all x1, waiting for transfers between devices, shards(): lax.all_to_all(stacked, 'seq', split_axis=2, concat_axis=1, tiled=True)  75.8 us
    psum x1, waiting for transfers between devices, shards(): w_rows = lax.psum(w_rows.astype(jnp.bfloat16), 'dp').astype(jnp.float32)  31.6 us
    ppermute x3, waiting for transfers between devices, chip_layer_out(): total = total + lax.ppermute(piece, 'seq', pairs).astype(jnp.float32)  31.3 us
    unnamed x33, local copies, waits for them, and re-layouts  13.2 us
    all_to_all x1, starting transfers between devices, shards(): lax.all_to_all(stacked, 'seq', split_axis=2, concat_axis=1, tiled=True)  6.33 us
    slice x4, local copies, waits for them, and re-layouts, shards(): return (layer_out, back[0], back[1], back[2], w_out_grad)  5.92 us
    dot_general x1, matrix products, shards(): jnp.einsum('bnf,bnk->bfk', att_blocks, grad_blocks, preferred_element_typ...  5.87 us
  transfers between devices with their start and end apart: 9, of which 3 were waited for; matrix products, arithmetic and copies ran while one was open for 29% of the time, Pallas kernels for 0%

profile of v11, /device:TPU:0, one launch (start us, length us, event | category | flops | bytes accessed | tf_op | source)
XLA Modules:
  0.0 250.0 jit_solution(1207090683932097057)
XLA Ops:
  7.9 2.4 copy.71
  10.3 2.4 copy.72
  12.6 2.4 copy.73
  15.0 4.5 %pad_maximum_fusion = bf16[3,128,2048]{1,0,2:T(4,128)(2,1)} fusion(bf16[1,128,2048]{1,0,2:T(2,128)(2,1)S(1)} %copy.73, bf16[1,128,2048]{1,0,2:T(2,128)(2,1)S(1)} %copy.72, bf16[1,128,2048]{1,0,2:T(2,128)(2,1)S(1)} %copy.71), kind=kLoop, calls=%fused_computation.9 | loop fusion | flops 4718592 | bytes 3145728 | tf_op jit(solution)/shard_map/stack | solution.py:109
  19.5 6.3 %all-to-all-start = ((bf16[3,128,2048]{1,0,2:T(4,128)(2,1)}), bf16[3,128,2048]{1,0,2:T(4,128)(2,1)S(1)}, u32[]{:S(2)}, u32[]{:S(2)}) async-start(bf16[3,128,2048]{1,0,2:T(4,128)(2,1)} %pad_maximum_fusion), calls=%async_computation | async-start | bytes 4194304 | tf_op jit(solution)/shard_map/all_to_all | solution.py:112
  26.9 75.8 %all-to-all-done = bf16[3,128,2048]{1,0,2:T(4,128)(2,1)S(1)} async-done(((bf16[3,128,2048]{1,0,2:T(4,128)(2,1)}), bf16[3,128,2048]{1,0,2:T(4,128)(2,1)S(1)}, u32[]{:S(2)}, u32[]{:S(2)}) %all-to-all-start) | async-done | bytes 1572896 | tf_op jit(solution)/shard_map/all_to_all | solution.py:112
  103.0 1.0 copy.77
  104.4 0.7 fusion.46
  105.5 1.3 select_reduce_fusion.1
  106.9 2.2 fusion.65
  109.2 1.2 fusion.28
  110.5 3.6 %fusion.13 = bf16[1024,256]{0,1:T(8,128)(2,1)S(1)} fusion(bf16[256,2048]{1,0:T(8,128)(2,1)S(1)} %copy-done.4, bf16[1,1024,2048]{2,1,0:T(8,128)(2,1)} %all-gather.3.cloned.1.call-done), kind=kOutput, calls=%fused_computation.26 | convolution fusion | flops 1074003968 | bytes 5767168 | tf_op jit(solution)/shard_map/dot_general | solution.py:127
  114.1 2.2 fusion.25
  116.4 2.2 fusion.22
  118.6 1.3 multiply_reduce_fusion.1
  119.9 2.3 multiply_convert_fusion.1
  122.1 0.8 convolution_convert_fusion.1
  123.0 1.2 convolution_convert_fusion.3
  124.2 2.0 multiply_convert_fusion
  126.2 1.2 convolution_convert_fusion.2
  127.4 0.8 convolution_convert_fusion
  128.3 1.0 fusion.64
  129.8 1.1 maximum_bitcast_fusion.2
  131.1 2.6 %copy.84 = bf16[3,1024,256]{2,0,1:T(4,128)(2,1)} copy(bf16[3,1024,256]{1,2,0:T(8,128)(2,1)S(1)} %pad_maximum_fusion.1) | data formatting | bytes 3145728 | tf_op jit(solution)/shard_map/stack | solution.py:152
  133.6 3.6 %all-to-all-start.1 = ((bf16[3,1024,256]{2,0,1:T(4,128)(2,1)}), bf16[3,1024,256]{2,0,1:T(4,128)(2,1)S(1)}, u32[]{:S(2)}, u32[]{:S(2)}) async-start(bf16[3,1024,256]{2,0,1:T(4,128)(2,1)} %copy.84), calls=%async_computation.1 | async-start | bytes 4194304 | tf_op jit(solution)/shard_map/all_to_all | solution.py:153
  137.3 5.9 %convert_reduce_fusion = bf16[256,2048]{1,0:T(8,128)(2,1)} fusion(bf16[8,128,2048]{2,1,0:T(8,128)(2,1)} %bitcast.125, bf16[32,8,8,128]{3,2,1,0:T(8,128)(2,1)} %get-tuple-element.20), kind=kOutput, calls=%fused_computation | convolution fusion | flops 1081606144 | bytes 5767168 | tf_op jit(solution)/shard_map/bnf,bnk->bfk/dot_general | solution.py:132
  143.2 1.7 fusion.69
  144.9 1.2 copy.92
  146.1 1.9 copy.91
  148.0 1.4 reshape.56
  149.4 1.5 fusion.70
  150.9 1.9 copy.94
  152.8 1.1 copy.93
  153.9 1.1 select_bitcast_fusion
  155.0 4.8 %fusion.71 = (bf16[4,128,2048]{2,1,0:T(8,128)(2,1)S(1)}, f32[4,128,2048]{2,1,0:T(8,128)}) fusion(bf16[256,2048]{1,0:T(8,128)(2,1)} %collective-permute-done.1, bf16[256,2048]{1,0:T(8,128)(2,1)} %param.11, bf16[4,128,256]{2,1,0:T(8,128)(2,1)S(1)} %get-tuple-element.30, bf16[4,128,256]{2,1,0:T(8,128)(2,1)S(1)} %get-tuple-element.31), kind=kOutput, calls=%fused_computation.92 | convolution fusion | flops 1080033280 | bytes 8912896 | tf_op jit(solution)/shard_map/dot_general | solution.py:76
  159.8 0.9 dynamic-slice_bitcast_fusion.2
  160.7 1.9 collective-permute-start.2
  162.6 1.9 collective-permute-start.4
  164.6 1.0 collective-permute-start.3
  165.6 31.6 %all-reduce.2.cloned.1.call-done = bf16[256,2048]{1,0:T(8,128)(2,1)} async-done(((bf16[256,2048]{1,0:T(8,128)(2,1)}), bf16[256,2048]{1,0:T(8,128)(2,1)}) %all-reduce.2.cloned.1.call-update) | async-done | bytes 1048592 | tf_op jit(solution)/shard_map/psum | solution.py:136
  197.2 2.8 %convert_multiply_fusion = f32[256,2048]{1,0:T(8,128)} fusion(bf16[256,2048]{1,0:T(8,128)(2,1)} %all-reduce.2.cloned.1.call-done), kind=kLoop, calls=%fused_computation.14 | loop fusion | flops 1048576 | bytes 3145728 | tf_op jit(solution)/shard_map/div | solution.py:138
  200.0 31.3 %collective-permute-done.3 = bf16[128,2048]{1,0:T(8,128)(2,1)} collective-permute-done((bf16[128,2048]{1,0:T(8,128)(2,1)S(1)}, bf16[128,2048]{1,0:T(8,128)(2,1)}, u32[]{:S(2)}, u32[]{:S(2)}) %collective-permute-start.3) | collective-permute-done | bytes 524320 | tf_op jit(solution)/shard_map/ppermute | solution.py:84
  231.3 2.8 %fusion.37 = bf16[1,128,2048]{2,1,0:T(8,128)(2,1)} fusion(bf16[128,2048]{1,0:T(8,128)(2,1)} %collective-permute-done.4, bf16[128,2048]{1,0:T(8,128)(2,1)} %collective-permute-done.3, bf16[128,2048]{1,0:T(8,128)(2,1)} %collective-permute-done.2, f32[4,128,2048]{2,1,0:T(8,128)} %get-tuple-element.28, s32[]{:T(128)S(6)} %select_n.79), kind=kLoop, calls=%fused_computation.42 | loop fusion | flops 1835008 | bytes 3145732 | tf_op jit(solution)/shard_map/broadcast_in_dim | solution.py:125
  234.1 3.0 %fusion.67 = (bf16[1,128,8,256]{3,0,1,2:T(2,128)(2,1)S(1)}, bf16[1,128,8,256]{3,0,1,2:T(2,128)(2,1)}, bf16[1,128,8,256]{3,0,1,2:T(2,128)(2,1)S(1)}) fusion(bf16[3,128,8,256]{3,0,1,2:T(4,128)(2,1)S(1)} %bitcast.103), kind=kLoop, calls=%fused_computation.88 | loop fusion | bytes 3145728 | tf_op jit(solution)/shard_map/slice | solution.py:155
  237.7 1.0 squeeze.59
  238.7 1.8 copy.86
  240.5 1.0 squeeze.58
  242.1 1.0 squeeze.57
  (52 shorter events, 4.8 us)
Async XLA Ops:
  7.2 103.3 %all-gather.3.cloned.1.call-start = ((), (), s32[]{:S(2)}) async-start(), calls=%async_computation.3 | async-start | bytes 4718592 | tf_op jit(solution)/shard_map/all_gather | solution.py:103
  15.0 11.4 %copy-start.11 = (s32[1,9]{1,0:T(1,128)S(1)}, s32[1,9]{1,0:T(1,128)}, u32[]{:S(2)}) copy-start(s32[1,9]{1,0:T(1,128)} %param.12) | copy-start | bytes 112
  15.0 11.5 %copy-start.12 = (s32[1,32]{1,0:T(1,128)S(1)}, s32[1,32]{1,0:T(1,128)}, u32[]{:S(2)}) copy-start(s32[1,32]{1,0:T(1,128)} %param.13) | copy-start | bytes 388
  19.5 83.1 %all-to-all-start = ((bf16[3,128,2048]{1,0,2:T(4,128)(2,1)}), bf16[3,128,2048]{1,0,2:T(4,128)(2,1)S(1)}, u32[]{:S(2)}, u32[]{:S(2)}) async-start(bf16[3,128,2048]{1,0,2:T(4,128)(2,1)} %pad_maximum_fusion), calls=%async_computation | async-start | bytes 4194304 | tf_op jit(solution)/shard_map/all_to_all | solution.py:112
  25.9 129.2 %collective-permute-start.1 = (bf16[256,2048]{1,0:T(8,128)(2,1)}, bf16[256,2048]{1,0:T(8,128)(2,1)}, u32[]{:S(2)}, u32[]{:S(2)}) collective-permute-start(bf16[256,2048]{1,0:T(8,128)(2,1)} %param.11), channel_id=1, source_target_pairs={{0,1},{1,0},{2,3},{3,2},{4,5},{5,4},{6,7},{7,6},{8,9},{9,8},{10,11... | collective-permute-start | bytes 3145736 | tf_op jit(solution)/shard_map/ppermute | solution.py:68
  105.2 4.0 %copy-start = (f32[1024,1024]{0,1:T(8,128)}, f32[1024,1024]{0,1:T(8,128)S(1)}, u32[]{:S(2)}) copy-start(f32[1024,1024]{0,1:T(8,128)S(1)} %fusion.46) | copy-start | bytes 12582916
  106.9 2.3 copy-start.2
  106.9 2.3 copy-start.5
  109.2 1.3 copy-start.4
  110.4 8.2 %copy-start.9 = (bf16[1024,128]{0,1:T(8,128)(2,1)}, bf16[1024,128]{0,1:T(8,128)(2,1)S(1)}, u32[]{:S(2)}) copy-start(bf16[1024,128]{0,1:T(8,128)(2,1)S(1)} %fusion.28) | copy-start | bytes 786436
  110.5 3.6 %copy-start.1 = (f32[1024,1024]{0,1:T(8,128)S(1)}, f32[1024,1024]{0,1:T(8,128)}, u32[]{:S(2)}) copy-start(f32[1024,1024]{0,1:T(8,128)} %copy-done) | copy-start | bytes 12582916
  114.1 2.2 copy-start.3
  116.4 2.2 copy-start.6
  126.2 2.1 copy-start.10
  126.2 3.5 %copy-start.7 = (bf16[1024,128]{0,1:T(8,128)(2,1)S(1)}, bf16[1024,128]{0,1:T(8,128)(2,1)}, u32[]{:S(2)}) copy-start(bf16[1024,128]{0,1:T(8,128)(2,1)} %fusion.25) | copy-start | bytes 786436
  126.2 3.5 %copy-start.8 = (bf16[1024,128]{0,1:T(8,128)(2,1)S(1)}, bf16[1024,128]{0,1:T(8,128)(2,1)}, u32[]{:S(2)}) copy-start(bf16[1024,128]{0,1:T(8,128)(2,1)} %fusion.22) | copy-start | bytes 786436
  129.7 18.4 %collective-permute-start = (bf16[1024,256]{0,1:T(8,128)(2,1)S(1)}, bf16[1024,256]{0,1:T(8,128)(2,1)}, u32[]{:S(2)}, u32[]{:S(2)}) collective-permute-start(bf16[1024,256]{0,1:T(8,128)(2,1)S(1)} %get-tuple-element.21), channel_id=1, source_target_pairs={{0,1},{1,0},{2,3},{3,2},{4,5},{5,4},{6,7},{7,6},{8,9},{9,8},{10,11... | collective-permute-start | bytes 1572872 | tf_op jit(solution)/shard_map/ppermute | solution.py:67
  133.6 100.5 %all-to-all-start.1 = ((bf16[3,1024,256]{2,0,1:T(4,128)(2,1)}), bf16[3,1024,256]{2,0,1:T(4,128)(2,1)S(1)}, u32[]{:S(2)}, u32[]{:S(2)}) async-start(bf16[3,1024,256]{2,0,1:T(4,128)(2,1)} %copy.84), calls=%async_computation.1 | async-start | bytes 4194304 | tf_op jit(solution)/shard_map/all_to_all | solution.py:153
  137.2 60.0 %all-reduce.2.cloned.1.call-start = ((), (), s32[]{:S(2)}) async-start(), calls=%async_computation.2 | async-start | bytes 2097152 | tf_op jit(solution)/shard_map/psum | solution.py:136
  160.7 39.3 %collective-permute-start.2 = (bf16[128,2048]{1,0:T(8,128)(2,1)}, bf16[128,2048]{1,0:T(8,128)(2,1)}, u32[]{:S(2)}, u32[]{:S(2)}) collective-permute-start(bf16[128,2048]{1,0:T(8,128)(2,1)} %get-tuple-element.14), channel_id=1, source_target_pairs={{0,2},{1,3},{2,4},{3,5},{4,6},{5,7},{6,0},{7,1},{8,10},{9,11},{10,... | collective-permute-start | bytes 1572872 | tf_op jit(solution)/shard_map/ppermute | solution.py:84
  162.6 37.3 %collective-permute-start.4 = (bf16[128,2048]{1,0:T(8,128)(2,1)S(1)}, bf16[128,2048]{1,0:T(8,128)(2,1)}, u32[]{:S(2)}, u32[]{:S(2)}) collective-permute-start(bf16[128,2048]{1,0:T(8,128)(2,1)S(1)} %get-tuple-element.15), channel_id=1, source_target_pairs={{0,6},{1,7},{2,0},{3,1},{4,2},{5,3},{6,4},{7,5},{8,14},{9,15},{10,... | collective-permute-start | bytes 1572872 | tf_op jit(solution)/shard_map/ppermute | solution.py:84
  164.6 66.8 %collective-permute-start.3 = (bf16[128,2048]{1,0:T(8,128)(2,1)S(1)}, bf16[128,2048]{1,0:T(8,128)(2,1)}, u32[]{:S(2)}, u32[]{:S(2)}) collective-permute-start(bf16[128,2048]{1,0:T(8,128)(2,1)S(1)} %get-tuple-element.16), channel_id=1, source_target_pairs={{0,4},{1,5},{2,6},{3,7},{4,0},{5,1},{6,2},{7,3},{8,12},{9,13},{10,... | collective-permute-start | bytes 1572872 | tf_op jit(solution)/shard_map/ppermute | solution.py:84
Sparse Core Ops, SparseCore 0:
  9.6 85.9 all-gather.2
  143.3 53.8 all-reduce.1

commit v12 on v7

--- a/solution.py
+++ b/solution.py
@@ -100,7 +100,6 @@
     nodes = nodes_here * n_seq
 
     grad_here = upstream_cotangent[0]
-    grad_full = lax.all_gather(grad_here, "seq", axis=0, tiled=True)
 
     groups = n_seq
     group_width = width // groups
@@ -118,6 +117,8 @@
     )
     heads = lax.all_to_all(stacked, "seq", split_axis=1, concat_axis=1, tiled=True)
     heads = heads.reshape(3, nodes, group_width)
+    heads, grad_here = lax.optimization_barrier((heads, grad_here))
+    grad_full = lax.all_gather(grad_here, "seq", axis=0, tiled=True)
 
     allowed = tile_mask(panel_entry_offsets[0], rightward_panel_per_entry[0], nodes)
 

time: 221 us -> 222 us (level)
  blocking collectives: 0 us -> 44 us
  waiting for transfers between devices: 128 us -> 96 us
  starting transfers between devices: 15.4 us -> 8.91 us
    all_to_all x1 -> x0, waiting for transfers between devices: 70.5 us -> none  [shards(): lax.all_to_all(stacked, 'seq', split_axis=1, concat_axis=1, tiled=True)]
    all_to_all x0 -> x1, blocking collectives: none -> 44 us  [shards(): lax.all_to_all(stacked, 'seq', split_axis=1, concat_axis=1, tiled=True)]
    all_gather x1, waiting for transfers between devices: 0.02 us -> 39.5 us  [shards(): grad_full = lax.all_gather(grad_here, 'seq', axis=0, tiled=True)]
    all_to_all x1 -> x0, starting transfers between devices: 6.33 us -> none  [shards(): lax.all_to_all(stacked, 'seq', split_axis=1, concat_axis=1, tiled=True)]
    unnamed x38 -> x33, local copies, waits for them, and re-layouts: 12 us -> 10.6 us
  transfers between devices with their start and end apart: 9 -> 8, of which waited for: 3 -> 3; matrix products, arithmetic and copies ran while one was open for 27% -> 22% of each run, Pallas kernels for 0% -> 0%
where the time goes in v12:
time: 222 us; the launch traced here: 221 us
  waiting for transfers between devices  96 us (43%)
  blocking collectives  44 us (20%)
  matrix products  30.5 us (14%)
  local copies, waits for them, and re-layouts  16.6 us (7%)
  between operations  14.5 us (7%)
  other arithmetic  10.7 us (5%)
  starting transfers between devices  8.91 us (4%)
    all_to_all x1, blocking collectives, shards(): lax.all_to_all(stacked, 'seq', split_axis=1, concat_axis=1, tiled=True)  44 us
    all_gather x1, waiting for transfers between devices, shards(): grad_full = lax.all_gather(grad_here, 'seq', axis=0, tiled=True)  39.5 us
    psum x1, waiting for transfers between devices, shards(): w_rows = lax.psum(w_rows.astype(jnp.bfloat16), 'dp').astype(jnp.float32)  36.2 us
    ppermute x3, waiting for transfers between devices, chip_layer_out(): total = total + lax.ppermute(piece, 'seq', pairs).astype(jnp.float32)  20.3 us
    unnamed x33, local copies, waits for them, and re-layouts  10.6 us
    dot_general x1, matrix products, shards(): jnp.einsum('bnf,bnk->bfk', att_blocks, grad_blocks, preferred_element_typ...  5.7 us
    ppermute x3, starting transfers between devices, chip_layer_out(): total = total + lax.ppermute(piece, 'seq', pairs).astype(jnp.float32)  4.87 us
    dot_general x1, matrix products, chip_layer_out(): lax.dot_general(att_chip, w_chip, (((2,), (0,)), ((), ())), preferred_ele...  4.74 us
  transfers between devices with their start and end apart: 8, of which 3 were waited for; matrix products, arithmetic and copies ran while one was open for 22% of the time, Pallas kernels for 0%

profile of v12, /device:TPU:0, one launch (start us, length us, event | category | flops | bytes accessed | tf_op | source)
XLA Modules:
  0.0 221.2 jit_solution(7011072904324668440)
XLA Ops:
  7.2 1.3 copy.69
  8.5 1.3 copy.70
  9.8 1.3 copy.71
  11.2 0.2 pad_maximum_fusion
  11.5 44.0 %all_to_all.10 = bf16[3,8,128,256]{2,3,0,1:T(8,128)(2,1)S(1)} all-to-all(bf16[3,8,128,256]{2,3,0,1:T(8,128)(2,1)S(1)} %copy.72), channel_id=1, replica_groups=mesh['dp'=4,'seq'=8] {'seq'}, dimensions={1} | all-to-all | bytes 3145728 | tf_op jit(solution)/shard_map/all_to_all | solution.py:118
  55.5 0.7 copy.73
  56.6 0.3 convolution_compare_fusion
  57.0 0.7 fusion.41
  57.7 0.3 broadcast_in_dim.13
  58.1 1.3 select_reduce_fusion.1
  59.4 2.2 %fusion.60 = (f32[1024]{0:T(1024)S(1)}, f32[1024]{0:T(1024)S(1)}) fusion(f32[1024]{0:T(1024)S(1)} %get-tuple-element.21, f32[1024,1024]{0,1:T(8,128)S(1)} %get-tuple-element.40, pred[128,8,8,128]{3,2,1,0:T(8,128)(4,1)S(1)} %bitcast.126, f32[1024]{0:T(1024)S(1)} %get-tuple-element.22, f32[1024,1024]{0,1:T(8,128)S(1)} %fusion.41), kind=kLoop, calls=%fused_computation.87 | loop fusion | flops 8386560 | bytes 9453568 | tf_op jit(solution)/shard_map/reduce_sum | solution.py:34
  61.7 1.2 fusion.23
  63.0 39.5 %all-gather.2.cloned.1.call-done = bf16[1024,2048]{1,0:T(8,128)(2,1)} async-done(((bf16[128,2048]{1,0:T(8,128)(2,1)}), bf16[1024,2048]{1,0:T(8,128)(2,1)}) %all-gather.2.cloned.1.call-update) | async-done | bytes 4194320 | tf_op jit(solution)/shard_map/all_gather | solution.py:121
  102.4 3.9 %convolution_convert_fusion = bf16[1024,256]{0,1:T(8,128)(2,1)S(1)} fusion(bf16[1024,2048]{1,0:T(8,128)(2,1)} %all-gather.2.cloned.1.call-done, bf16[256,2048]{1,0:T(8,128)(2,1)} %param.11), kind=kOutput, calls=%fused_computation.24 | convolution fusion | flops 1074003968 | bytes 5767168 | tf_op jit(solution)/shard_map/dot_general | solution.py:136
  106.4 2.2 %fusion.20 = bf16[1024,128]{0,1:T(8,128)(2,1)} fusion(f32[1024]{0:T(1024)S(1)} %get-tuple-element.20, bf16[1024,256]{0,1:T(8,128)(2,1)S(1)} %convolution_convert_fusion, f32[1024,1024]{0,1:T(8,128)S(1)} %copy-done.1, f32[1024]{0:T(1024)S(1)} %get-tuple-element.22, pred[128,8,8,128]{3,2,1,0:T(8,128)(4,1)S(1)} %bitcast.128), kind=kOutput, calls=%fused_computation.28 | convolution fusion | flops 273809408 | bytes 5775360 | tf_op jit(solution)/shard_map/dot_general | solution.py:44
  108.6 2.2 %fusion.17 = bf16[1024,128]{0,1:T(8,128)(2,1)} fusion(f32[1024]{0:T(1024)S(1)} %get-tuple-element.19, bf16[1024,256]{0,1:T(8,128)(2,1)S(1)} %convolution_convert_fusion, f32[1024,1024]{0,1:T(8,128)S(1)} %copy-done.3, f32[1024]{0:T(1024)S(1)} %get-tuple-element.21, pred[128,8,8,128]{3,2,1,0:T(8,128)(4,1)S(1)} %bitcast.129), kind=kOutput, calls=%fused_computation.27 | convolution fusion | flops 273809408 | bytes 5775360 | tf_op jit(solution)/shard_map/dot_general | solution.py:44
  110.8 1.3 multiply_reduce_fusion.1
  112.1 2.2 %multiply_convert_fusion.1 = bf16[1024,1024]{0,1:T(8,128)(2,1)S(1)} fusion(f32[1024]{0:T(1024)S(1)} %get-tuple-element.23, f32[1024]{0:T(1024)S(1)} %get-tuple-element.19, bf16[1024,256]{1,0:T(8,128)(2,1)S(1)} %get-tuple-element.31, bf16[1024,256]{0,1:T(8,128)(2,1)S(1)} %convolution_convert_fusion, f32[1024]{0:T(1024)S(1)} %get-tuple-element.21, ...), kind=kOutput, calls=%fused_computation.2 | convolution fusion | flops 276824064 | bytes 7876608 | tf_op jit(solution)/shard_map/dot_general | solution.py:45
  114.3 0.8 convolution_convert_fusion.2
  115.2 0.5 convolution_convert_fusion.4
  115.7 2.0 multiply_convert_fusion
  117.8 0.5 convolution_convert_fusion.3
  118.3 0.8 convolution_convert_fusion.1
  119.1 0.2 fusion.59
  119.3 0.4 reshape.52
  119.7 0.3 collective-permute-start
  120.7 1.3 pad_maximum_fusion.1
  122.0 3.6 %all-to-all-start.1 = ((bf16[3,8,128,256]{2,3,0,1:T(8,128)(2,1)}), bf16[3,8,128,256]{2,3,0,1:T(8,128)(2,1)S(1)}, u32[]{:S(2)}, u32[]{:S(2)}) async-start(bf16[3,8,128,256]{2,3,0,1:T(8,128)(2,1)} %pad_maximum_fusion.1), calls=%async_computation.1 | async-start | bytes 3145728 | tf_op jit(solution)/shard_map/all_to_all | solution.py:165
  125.6 5.7 %convert_reduce_fusion = bf16[256,2048]{1,0:T(8,128)(2,1)} fusion(bf16[8,128,2048]{2,1,0:T(8,128)(2,1)} %bitcast.143, bf16[32,8,8,128]{3,2,1,0:T(8,128)(2,1)S(1)} %get-tuple-element.34), kind=kOutput, calls=%fused_computation | convolution fusion | flops 1081606144 | bytes 5767168 | tf_op jit(solution)/shard_map/bnf,bnk->bfk/dot_general | solution.py:141
  131.4 1.5 fusion.63
  132.9 1.2 copy.90
  134.1 1.1 copy.89
  135.2 1.4 reshape.53
  136.6 0.7 fusion.64
  137.4 0.5 copy.92
  137.9 0.5 copy.91
  138.4 1.0 select_bitcast_fusion
  139.4 4.7 %fusion.65 = (bf16[4,128,2048]{2,1,0:T(8,128)(2,1)S(1)}, f32[4,128,2048]{2,1,0:T(8,128)}) fusion(bf16[256,2048]{1,0:T(8,128)(2,1)} %collective-permute-done.1, bf16[256,2048]{1,0:T(8,128)(2,1)} %param.11, bf16[4,128,256]{2,1,0:T(8,128)(2,1)S(1)} %get-tuple-element.44, bf16[4,128,256]{2,1,0:T(8,128)(2,1)S(1)} %get-tuple-element.45), kind=kOutput, calls=%fused_computation.92 | convolution fusion | flops 1080033280 | bytes 8912896 | tf_op jit(solution)/shard_map/dot_general | solution.py:76
  144.3 1.9 collective-permute-start.2
  146.2 1.9 collective-permute-start.4
  148.2 1.0 collective-permute-start.3
  149.2 36.2 %all-reduce.2.cloned.1.call-done = bf16[256,2048]{1,0:T(8,128)(2,1)} async-done(((bf16[256,2048]{1,0:T(8,128)(2,1)}), bf16[256,2048]{1,0:T(8,128)(2,1)}) %all-reduce.2.cloned.1.call-update) | async-done | bytes 1048592 | tf_op jit(solution)/shard_map/psum | solution.py:145
  185.4 2.8 %convert_multiply_fusion = f32[256,2048]{1,0:T(8,128)} fusion(bf16[256,2048]{1,0:T(8,128)(2,1)} %all-reduce.2.cloned.1.call-done), kind=kLoop, calls=%fused_computation.11 | loop fusion | flops 1048576 | bytes 3145728 | tf_op jit(solution)/shard_map/div | solution.py:147
  188.2 20.3 %collective-permute-done.3 = bf16[128,2048]{1,0:T(8,128)(2,1)} collective-permute-done((bf16[128,2048]{1,0:T(8,128)(2,1)S(1)}, bf16[128,2048]{1,0:T(8,128)(2,1)}, u32[]{:S(2)}, u32[]{:S(2)}) %collective-permute-start.3) | collective-permute-done | bytes 524320 | tf_op jit(solution)/shard_map/ppermute | solution.py:84
  208.4 2.8 %fusion.32 = bf16[1,128,2048]{2,1,0:T(8,128)(2,1)} fusion(bf16[128,2048]{1,0:T(8,128)(2,1)} %collective-permute-done.4, bf16[128,2048]{1,0:T(8,128)(2,1)} %collective-permute-done.3, bf16[128,2048]{1,0:T(8,128)(2,1)} %collective-permute-done.2, f32[4,128,2048]{2,1,0:T(8,128)} %get-tuple-element.42, s32[]{:T(128)S(6)} %select_n.79), kind=kLoop, calls=%fused_computation.40 | loop fusion | flops 1835008 | bytes 3145732 | tf_op jit(solution)/shard_map/broadcast_in_dim | solution.py:134
  211.4 1.0 copy.86
  212.4 1.0 copy.85
  213.4 1.0 copy.84
  (46 shorter events, 1.7 us)
Async XLA Ops:
  7.2 95.3 %all-gather.2.cloned.1.call-start = ((), (), s32[]{:S(2)}) async-start(), calls=%async_computation.2 | async-start | bytes 4718592 | tf_op jit(solution)/shard_map/all_gather | solution.py:121
  11.5 44.9 %copy-start.8 = (s32[1,9]{1,0:T(1,128)S(1)}, s32[1,9]{1,0:T(1,128)}, u32[]{:S(2)}) copy-start(s32[1,9]{1,0:T(1,128)} %param.12) | copy-start | bytes 112
  11.5 45.0 %copy-start.9 = (s32[1,32]{1,0:T(1,128)S(1)}, s32[1,32]{1,0:T(1,128)}, u32[]{:S(2)}) copy-start(s32[1,32]{1,0:T(1,128)} %param.13) | copy-start | bytes 388
  56.2 83.2 %collective-permute-start.1 = (bf16[256,2048]{1,0:T(8,128)(2,1)}, bf16[256,2048]{1,0:T(8,128)(2,1)}, u32[]{:S(2)}, u32[]{:S(2)}) collective-permute-start(bf16[256,2048]{1,0:T(8,128)(2,1)} %param.11), channel_id=1, source_target_pairs={{0,1},{1,0},{2,3},{3,2},{4,5},{5,4},{6,7},{7,6},{8,9},{9,8},{10,11... | collective-permute-start | bytes 3145736 | tf_op jit(solution)/shard_map/ppermute | solution.py:68
  57.7 4.0 %copy-start = (f32[1024,1024]{0,1:T(8,128)}, f32[1024,1024]{0,1:T(8,128)S(1)}, u32[]{:S(2)}) copy-start(f32[1024,1024]{0,1:T(8,128)S(1)} %fusion.41) | copy-start | bytes 12582916
  59.4 2.3 %copy-start.2 = (f32[1024,1024]{0,1:T(8,128)}, f32[1024,1024]{0,1:T(8,128)S(1)}, u32[]{:S(2)}) copy-start(f32[1024,1024]{0,1:T(8,128)S(1)} %get-tuple-element.40) | copy-start | bytes 12582916
  62.9 47.9 %copy-start.6 = (bf16[1024,128]{0,1:T(8,128)(2,1)}, bf16[1024,128]{0,1:T(8,128)(2,1)S(1)}, u32[]{:S(2)}) copy-start(bf16[1024,128]{0,1:T(8,128)(2,1)S(1)} %fusion.23) | copy-start | bytes 786436
  102.4 3.9 %copy-start.1 = (f32[1024,1024]{0,1:T(8,128)S(1)}, f32[1024,1024]{0,1:T(8,128)}, u32[]{:S(2)}) copy-start(f32[1024,1024]{0,1:T(8,128)} %copy-done) | copy-start | bytes 12582916
  106.4 2.2 %copy-start.3 = (f32[1024,1024]{0,1:T(8,128)S(1)}, f32[1024,1024]{0,1:T(8,128)}, u32[]{:S(2)}) copy-start(f32[1024,1024]{0,1:T(8,128)} %copy-done.2) | copy-start | bytes 12582916
  117.7 1.4 copy-start.7
  117.7 2.2 %copy-start.4 = (bf16[1024,128]{0,1:T(8,128)(2,1)S(1)}, bf16[1024,128]{0,1:T(8,128)(2,1)}, u32[]{:S(2)}) copy-start(bf16[1024,128]{0,1:T(8,128)(2,1)} %fusion.20) | copy-start | bytes 786436
  117.8 2.2 %copy-start.5 = (bf16[1024,128]{0,1:T(8,128)(2,1)S(1)}, bf16[1024,128]{0,1:T(8,128)(2,1)}, u32[]{:S(2)}) copy-start(bf16[1024,128]{0,1:T(8,128)(2,1)} %fusion.17) | copy-start | bytes 786436
  119.7 15.6 %collective-permute-start = (bf16[1024,256]{0,1:T(8,128)(2,1)S(1)}, bf16[1024,256]{0,1:T(8,128)(2,1)}, u32[]{:S(2)}, u32[]{:S(2)}) collective-permute-start(bf16[1024,256]{0,1:T(8,128)(2,1)S(1)} %get-tuple-element.35), channel_id=1, source_target_pairs={{0,1},{1,0},{2,3},{3,2},{4,5},{5,4},{6,7},{7,6},{8,9},{9,8},{10,11... | collective-permute-start | bytes 1572872 | tf_op jit(solution)/shard_map/ppermute | solution.py:67
  122.0 89.2 %all-to-all-start.1 = ((bf16[3,8,128,256]{2,3,0,1:T(8,128)(2,1)}), bf16[3,8,128,256]{2,3,0,1:T(8,128)(2,1)S(1)}, u32[]{:S(2)}, u32[]{:S(2)}) async-start(bf16[3,8,128,256]{2,3,0,1:T(8,128)(2,1)} %pad_maximum_fusion.1), calls=%async_computation.1 | async-start | bytes 3145728 | tf_op jit(solution)/shard_map/all_to_all | solution.py:165
  125.6 59.8 %all-reduce.2.cloned.1.call-start = ((), (), s32[]{:S(2)}) async-start(), calls=%async_computation.3 | async-start | bytes 2097152 | tf_op jit(solution)/shard_map/psum | solution.py:145
  144.3 43.9 %collective-permute-start.2 = (bf16[128,2048]{1,0:T(8,128)(2,1)S(1)}, bf16[128,2048]{1,0:T(8,128)(2,1)}, u32[]{:S(2)}, u32[]{:S(2)}) collective-permute-start(bf16[128,2048]{1,0:T(8,128)(2,1)S(1)} %get-tuple-element.25), channel_id=1, source_target_pairs={{0,2},{1,3},{2,4},{3,5},{4,6},{5,7},{6,0},{7,1},{8,10},{9,11},{10,... | collective-permute-start | bytes 1572872 | tf_op jit(solution)/shard_map/ppermute | solution.py:84
  146.2 41.9 %collective-permute-start.4 = (bf16[128,2048]{1,0:T(8,128)(2,1)S(1)}, bf16[128,2048]{1,0:T(8,128)(2,1)}, u32[]{:S(2)}, u32[]{:S(2)}) collective-permute-start(bf16[128,2048]{1,0:T(8,128)(2,1)S(1)} %get-tuple-element.26), channel_id=1, source_target_pairs={{0,6},{1,7},{2,0},{3,1},{4,2},{5,3},{6,4},{7,5},{8,14},{9,15},{10,... | collective-permute-start | bytes 1572872 | tf_op jit(solution)/shard_map/ppermute | solution.py:84
  148.2 60.2 %collective-permute-start.3 = (bf16[128,2048]{1,0:T(8,128)(2,1)S(1)}, bf16[128,2048]{1,0:T(8,128)(2,1)}, u32[]{:S(2)}, u32[]{:S(2)}) collective-permute-start(bf16[128,2048]{1,0:T(8,128)(2,1)S(1)} %get-tuple-element.27), channel_id=1, source_target_pairs={{0,4},{1,5},{2,6},{3,7},{4,0},{5,1},{6,2},{7,3},{8,12},{9,13},{10,... | collective-permute-start | bytes 1572872 | tf_op jit(solution)/shard_map/ppermute | solution.py:84
Sparse Core Ops, SparseCore 0:
  56.3 46.0 all-gather.1
  131.5 53.8 all-reduce.1

commit v13 on v11

--- a/solution.py
+++ b/solution.py
@@ -106,10 +106,21 @@
     group_width = width // groups
     local_heads = group_width // HD
 
-    stacked = jnp.stack(
-        [asking_vectors_matrix[0], matched_keys_matrix[0], carried_vectors_matrix[0]]
-    )
-    heads = lax.all_to_all(stacked, "seq", split_axis=2, concat_axis=1, tiled=True)
+    def head_chunks(values, h):
+        split = values.reshape(nodes_here, groups, local_heads, HD)[:, :, h, :]
+        return split.transpose(1, 0, 2)
+
+    per_head = []
+    for h in range(local_heads):
+        stacked = jnp.stack(
+            [
+                head_chunks(asking_vectors_matrix[0], h),
+                head_chunks(matched_keys_matrix[0], h),
+                head_chunks(carried_vectors_matrix[0], h),
+            ]
+        )
+        moved = lax.all_to_all(stacked, "seq", split_axis=1, concat_axis=1, tiled=True)
+        per_head.append(moved.reshape(3, nodes, HD))
 
     allowed = tile_mask(panel_entry_offsets[0], rightward_panel_per_entry[0], nodes)
 
@@ -117,7 +128,7 @@
         return values[:, h * HD : (h + 1) * HD]
 
     fwd = [
-        attend(head_cols(heads[0], h), head_cols(heads[1], h), head_cols(heads[2], h), allowed)
+        attend(per_head[h][0], per_head[h][1], per_head[h][2], allowed)
         for h in range(local_heads)
     ]
     att_flat = jnp.concatenate([f[0] for f in fwd], axis=1)
@@ -137,21 +148,20 @@
     batch = asking_vectors_matrix.shape[0] * lax.axis_size("dp")
     w_out_grad = w_rows / batch
 
-    bwd = [
-        attend_back(
-            head_cols(heads[0], h),
-            head_cols(heads[1], h),
-            head_cols(heads[2], h),
+    returned = []
+    for h in range(local_heads):
+        q_g, k_g, v_g = attend_back(
+            per_head[h][0],
+            per_head[h][1],
+            per_head[h][2],
             head_cols(g_flat, h),
             fwd[h][0],
             fwd[h][1],
             fwd[h][2],
         )
-        for h in range(local_heads)
-    ]
-    grads = jnp.stack([jnp.concatenate([b[i] for b in bwd], axis=1) for i in range(3)])
-    back = lax.all_to_all(grads, "seq", split_axis=1, concat_axis=2, tiled=True)
-    back = back.reshape(3, 1, nodes_here, width)
+        grads = jnp.stack([q_g, k_g, v_g]).reshape(3, groups, nodes_here, HD)
+        returned.append(lax.all_to_all(grads, "seq", split_axis=1, concat_axis=1, tiled=True))
+    back = jnp.stack(returned, axis=3).transpose(0, 2, 1, 3, 4).reshape(3, 1, nodes_here, width)
     return (layer_out, back[0], back[1], back[2], w_out_grad)
 
 

time: 251 us -> 224 us (0.89)
  the two profiles are of different devices: /device:TPU:0 before, /device:TPU:8 now
where the time goes in v13:
time: 224 us; the launch traced here: 223 us
  waiting for transfers between devices  112 us (50%)
  matrix products  32.8 us (15%)
  starting transfers between devices  29.5 us (13%)
  local copies, waits for them, and re-layouts  22.8 us (10%)
  between operations  14.5 us (6%)
  other arithmetic  11.5 us (5%)
    all_to_all x2, waiting for transfers between devices, shards(): lax.all_to_all(stacked, 'seq', split_axis=1, concat_axis=1, tiled=True)  58.8 us
    psum x1, waiting for transfers between devices, shards(): w_rows = lax.psum(w_rows.astype(jnp.bfloat16), 'dp').astype(jnp.float32)  33.2 us
    ppermute x3, waiting for transfers between devices, chip_layer_out(): total = total + lax.ppermute(piece, 'seq', pairs).astype(jnp.float32)  19.3 us
    unnamed x48, local copies, waits for them, and re-layouts  13.8 us
    all_to_all x2, starting transfers between devices, shards(): lax.all_to_all(stacked, 'seq', split_axis=1, concat_axis=1, tiled=True)  12.5 us
    all_to_all x2, starting transfers between devices, shards(): lax.all_to_all(grads, 'seq', split_axis=1, concat_axis=1, tiled=True)  12.2 us
    dot_general x2, matrix products, attend_back(): prob_grad = jnp.dot(g, v.T, preferred_element_type=jnp.float32)  6.62 us
    dot_general x1, matrix products, shards(): jnp.einsum('bnf,bnk->bfk', att_blocks, grad_blocks, preferred_element_typ...  5.87 us
  transfers between devices with their start and end apart: 11, of which 6 were waited for; matrix products, arithmetic and copies ran while one was open for 28% of the time, Pallas kernels for 0%

profile of v13, /device:TPU:8, one launch (start us, length us, event | category | flops | bytes accessed | tf_op | source)
XLA Modules:
  0.0 223.0 jit_solution(12477292144225878550)
XLA Ops:
  7.9 1.3 copy.141
  9.2 1.3 copy.139
  10.5 1.3 copy.138
  12.1 1.0 copy.151
  13.1 5.3 %all-to-all-start.1 = ((bf16[3,8,128,128]{2,3,0,1:T(8,128)(2,1)}), bf16[3,8,128,128]{2,3,0,1:T(8,128)(2,1)S(1)}, u32[]{:S(2)}, u32[]{:S(2)}) async-start(bf16[3,8,128,128]{2,3,0,1:T(8,128)(2,1)} %copy.151), calls=%async_computation.1 | async-start | bytes 1572864 | tf_op jit(solution)/shard_map/all_to_all | solution.py:122
  18.5 1.0 copy.144
  19.5 37.5 %all-to-all-done.1 = bf16[3,8,128,128]{2,3,0,1:T(8,128)(2,1)S(1)} async-done(((bf16[3,8,128,128]{2,3,0,1:T(8,128)(2,1)}), bf16[3,8,128,128]{2,3,0,1:T(8,128)(2,1)S(1)}, u32[]{:S(2)}, u32[]{:S(2)}) %all-to-all-start.1) | async-done | bytes 786464 | tf_op jit(solution)/shard_map/all_to_all | solution.py:122
  57.0 7.2 %all-to-all-start = ((bf16[3,8,128,128]{2,3,0,1:T(8,128)(2,1)}), bf16[3,8,128,128]{2,3,0,1:T(8,128)(2,1)S(1)}, u32[]{:S(2)}, u32[]{:S(2)}) async-start(bf16[3,8,128,128]{2,3,0,1:T(8,128)(2,1)} %copy.144), calls=%async_computation | async-start | bytes 1572864 | tf_op jit(solution)/shard_map/all_to_all | solution.py:122
  65.3 21.3 %all-to-all-done = bf16[3,8,128,128]{2,3,0,1:T(8,128)(2,1)S(1)} async-done(((bf16[3,8,128,128]{2,3,0,1:T(8,128)(2,1)}), bf16[3,8,128,128]{2,3,0,1:T(8,128)(2,1)S(1)}, u32[]{:S(2)}, u32[]{:S(2)}) %all-to-all-start) | async-done | bytes 786464 | tf_op jit(solution)/shard_map/all_to_all | solution.py:122
  87.4 0.7 fusion.59
  88.5 1.6 select_reduce_fusion.1
  90.1 2.2 %fusion.51 = (f32[1024]{0:T(1024)S(1)}, f32[1024]{0:T(1024)S(1)}) fusion(f32[1024]{0:T(1024)S(1)} %get-tuple-element.17, f32[1024,1024]{0,1:T(8,128)S(1)} %get-tuple-element.45, pred[128,8,8,128]{3,2,1,0:T(8,128)(4,1)S(1)} %bitcast.169, f32[1024]{0:T(1024)S(1)} %get-tuple-element.18, f32[1024,1024]{0,1:T(8,128)S(1)} %fusion.59), kind=kLoop, calls=%fused_computation.78 | loop fusion | flops 8386560 | bytes 9453568 | tf_op jit(solution)/shard_map/reduce_sum | solution.py:34
  92.4 1.2 fusion.28
  93.7 3.9 %fusion.13 = bf16[1024,256]{0,1:T(8,128)(2,1)S(1)} fusion(bf16[256,2048]{1,0:T(8,128)(2,1)} %param.11, bf16[1,1024,2048]{2,1,0:T(8,128)(2,1)} %all-gather.3.cloned.1.call-done), kind=kOutput, calls=%fused_computation.25 | convolution fusion | flops 1074003968 | bytes 5767168 | tf_op jit(solution)/shard_map/dot_general | solution.py:138
  97.6 1.3 multiply_reduce_fusion.1
  98.9 2.2 multiply_convert_fusion.1
  101.1 0.8 convolution_convert_fusion.3
  101.9 0.7 convolution_convert_fusion.2
  102.6 1.4 fusion.22
  104.1 0.7 copy-done.1
  104.8 2.1 fusion.25
  107.0 1.2 fusion.50
  108.1 1.4 reshape.76
  109.7 1.0 pad_maximum_fusion.2
  110.7 7.0 %all-to-all-start.2 = ((bf16[3,8,128,128]{3,2,0,1:T(8,128)(2,1)}), bf16[3,8,128,128]{3,2,0,1:T(8,128)(2,1)S(1)}, u32[]{:S(2)}, u32[]{:S(2)}) async-start(bf16[3,8,128,128]{3,2,0,1:T(8,128)(2,1)} %pad_maximum_fusion.2), calls=%async_computation.2 | async-start | bytes 1572864 | tf_op jit(solution)/shard_map/all_to_all | solution.py:163
  117.8 4.4 %multiply_convert_fusion = bf16[1024,1024]{0,1:T(8,128)(2,1)S(1)} fusion(bf16[1024,128]{1,0:T(8,128)(2,1)} %bitcast.197, f32[1024]{0:T(1024)S(1)} %get-tuple-element.20, f32[1024]{0:T(1024)S(1)} %get-tuple-element.16, bf16[1024,256]{0,1:T(8,128)(2,1)} %copy-done.15, f32[1024]{0:T(1024)S(1)} %get-tuple-element.18, f32[1024,1024]{0,1:T(8,128)} %copy-done, ...), kind=kOutput, calls=%fused_computation.3 | convolution fusion | flops 276824064 | bytes 7876608 | tf_op jit(solution)/shard_map/dot_general | solution.py:45
  122.2 1.7 fusion.56
  123.9 1.9 copy.185
  125.7 1.9 copy.186
  127.6 5.9 %convert_reduce_fusion = bf16[256,2048]{1,0:T(8,128)(2,1)} fusion(bf16[8,128,2048]{2,1,0:T(8,128)(2,1)} %bitcast.202, bf16[32,8,8,128]{3,2,1,0:T(8,128)(2,1)} %get-tuple-element.33), kind=kOutput, calls=%fused_computation | convolution fusion | flops 1081606144 | bytes 5767168 | tf_op jit(solution)/shard_map/bnf,bnk->bfk/dot_general | solution.py:143
  133.6 0.8 convolution_convert_fusion.1
  135.4 1.0 pad_maximum_fusion.3
  136.3 1.4 reshape.77
  137.7 0.7 fusion.57
  139.5 5.1 %all-to-all-start.3 = ((bf16[3,8,128,128]{3,2,0,1:T(8,128)(2,1)}), bf16[3,8,128,128]{3,2,0,1:T(8,128)(2,1)S(1)}, u32[]{:S(2)}, u32[]{:S(2)}) async-start(bf16[3,8,128,128]{3,2,0,1:T(8,128)(2,1)} %pad_maximum_fusion.3), calls=%async_computation.3 | async-start | bytes 1572864 | tf_op jit(solution)/shard_map/all_to_all | solution.py:163
  144.6 4.7 %fusion.58 = (bf16[4,128,2048]{2,1,0:T(8,128)(2,1)S(1)}, f32[4,128,2048]{2,1,0:T(8,128)}) fusion(bf16[256,2048]{1,0:T(8,128)(2,1)} %collective-permute-done.1, bf16[256,2048]{1,0:T(8,128)(2,1)} %param.11, bf16[4,128,256]{2,1,0:T(8,128)(2,1)S(1)} %select_bitcast_fusion, bf16[4,128,256]{2,1,0:T(8,128)(2,1)S(1)} %select_bitcast_fusion.1), kind=kOutput, calls=%fused_computation.85 | convolution fusion | flops 1080033280 | bytes 8912896 | tf_op jit(solution)/shard_map/dot_general | solution.py:76
  149.5 1.5 collective-permute-start.2
  151.1 1.0 collective-permute-start.3
  152.0 1.9 collective-permute-start.4
  154.0 33.2 %all-reduce.2.cloned.1.call-done = bf16[256,2048]{1,0:T(8,128)(2,1)} async-done(((bf16[256,2048]{1,0:T(8,128)(2,1)}), bf16[256,2048]{1,0:T(8,128)(2,1)}) %all-reduce.2.cloned.1.call-update) | async-done | bytes 1048592 | tf_op jit(solution)/shard_map/psum | solution.py:147
  187.2 2.8 %convert_multiply_fusion = f32[256,2048]{1,0:T(8,128)} fusion(bf16[256,2048]{1,0:T(8,128)(2,1)} %all-reduce.2.cloned.1.call-done), kind=kLoop, calls=%fused_computation.13 | loop fusion | flops 1048576 | bytes 3145728 | tf_op jit(solution)/shard_map/div | solution.py:149
  190.0 5.9 %collective-permute-done.2 = bf16[128,2048]{1,0:T(8,128)(2,1)} collective-permute-done((bf16[128,2048]{1,0:T(8,128)(2,1)S(1)}, bf16[128,2048]{1,0:T(8,128)(2,1)}, u32[]{:S(2)}, u32[]{:S(2)}) %collective-permute-start.2) | collective-permute-done | bytes 524320 | tf_op jit(solution)/shard_map/ppermute | solution.py:84
  195.8 11.2 %collective-permute-done.3 = bf16[128,2048]{1,0:T(8,128)(2,1)} collective-permute-done((bf16[128,2048]{1,0:T(8,128)(2,1)S(1)}, bf16[128,2048]{1,0:T(8,128)(2,1)}, u32[]{:S(2)}, u32[]{:S(2)}) %collective-permute-start.3) | collective-permute-done | bytes 524320 | tf_op jit(solution)/shard_map/ppermute | solution.py:84
  207.0 2.2 collective-permute-done.4
  209.2 2.8 %fusion.37 = bf16[1,128,2048]{2,1,0:T(8,128)(2,1)} fusion(bf16[128,2048]{1,0:T(8,128)(2,1)} %collective-permute-done.4, bf16[128,2048]{1,0:T(8,128)(2,1)} %collective-permute-done.3, bf16[128,2048]{1,0:T(8,128)(2,1)} %collective-permute-done.2, f32[4,128,2048]{2,1,0:T(8,128)} %get-tuple-element.47, s32[]{:T(128)S(6)} %select_n.79), kind=kLoop, calls=%fused_computation.45 | loop fusion | flops 1835008 | bytes 3145732 | tf_op jit(solution)/shard_map/broadcast_in_dim | solution.py:136
  213.1 1.0 copy.170
  214.2 1.0 copy.171
  215.2 1.0 copy.172
  (69 shorter events, 6.7 us)
Async XLA Ops:
  7.2 86.5 %all-gather.3.cloned.1.call-start = ((), (), s32[]{:S(2)}) async-start(), calls=%async_computation.5 | async-start | bytes 4718592 | tf_op jit(solution)/shard_map/all_gather | solution.py:103
  12.1 52.2 %copy-start.13 = (s32[1,9]{1,0:T(1,128)S(1)}, s32[1,9]{1,0:T(1,128)}, u32[]{:S(2)}) copy-start(s32[1,9]{1,0:T(1,128)} %param.12) | copy-start | bytes 112
  12.1 52.4 %copy-start.14 = (s32[1,32]{1,0:T(1,128)S(1)}, s32[1,32]{1,0:T(1,128)}, u32[]{:S(2)}) copy-start(s32[1,32]{1,0:T(1,128)} %param.13) | copy-start | bytes 388
  13.1 43.9 %all-to-all-start.1 = ((bf16[3,8,128,128]{2,3,0,1:T(8,128)(2,1)}), bf16[3,8,128,128]{2,3,0,1:T(8,128)(2,1)S(1)}, u32[]{:S(2)}, u32[]{:S(2)}) async-start(bf16[3,8,128,128]{2,3,0,1:T(8,128)(2,1)} %copy.151), calls=%async_computation.1 | async-start | bytes 1572864 | tf_op jit(solution)/shard_map/all_to_all | solution.py:122
  57.0 29.6 %all-to-all-start = ((bf16[3,8,128,128]{2,3,0,1:T(8,128)(2,1)}), bf16[3,8,128,128]{2,3,0,1:T(8,128)(2,1)S(1)}, u32[]{:S(2)}, u32[]{:S(2)}) async-start(bf16[3,8,128,128]{2,3,0,1:T(8,128)(2,1)} %copy.144), calls=%async_computation | async-start | bytes 1572864 | tf_op jit(solution)/shard_map/all_to_all | solution.py:122
  64.2 80.5 %collective-permute-start.1 = (bf16[256,2048]{1,0:T(8,128)(2,1)}, bf16[256,2048]{1,0:T(8,128)(2,1)}, u32[]{:S(2)}, u32[]{:S(2)}) collective-permute-start(bf16[256,2048]{1,0:T(8,128)(2,1)} %param.11), channel_id=1, source_target_pairs={{0,1},{1,0},{2,3},{3,2},{4,5},{5,4},{6,7},{7,6},{8,9},{9,8},{10,11... | collective-permute-start | bytes 3145736 | tf_op jit(solution)/shard_map/ppermute | solution.py:68
  65.1 23.0 %copy-start.5 = (bf16[1,8,128,128]{3,2,1,0:T(8,128)(2,1)}, bf16[1,8,128,128]{3,2,1,0:T(8,128)(2,1)S(1)}, u32[]{:S(2)}) copy-start(bf16[1,8,128,128]{3,2,1,0:T(8,128)(2,1)S(1)} %copy.182) | copy-start | bytes 786436
  65.3 22.9 %copy-start.7 = (bf16[1,8,128,128]{3,2,1,0:T(8,128)(2,1)}, bf16[1,8,128,128]{3,2,1,0:T(8,128)(2,1)S(1)}, u32[]{:S(2)}) copy-start(bf16[1,8,128,128]{3,2,1,0:T(8,128)(2,1)S(1)} %copy.183) | copy-start | bytes 786436
  87.2 5.2 %copy-start.11 = (bf16[1,8,128,128]{3,2,1,0:T(8,128)(2,1)}, bf16[1,8,128,128]{3,2,1,0:T(8,128)(2,1)S(1)}, u32[]{:S(2)}) copy-start(bf16[1,8,128,128]{3,2,1,0:T(8,128)(2,1)S(1)} %copy.184) | copy-start | bytes 786436
  88.1 4.3 %copy-start = (f32[1024,1024]{0,1:T(8,128)}, f32[1024,1024]{0,1:T(8,128)S(1)}, u32[]{:S(2)}) copy-start(f32[1024,1024]{0,1:T(8,128)S(1)} %fusion.59) | copy-start | bytes 12582916
  88.5 15.6 %copy-start.2 = (pred[8,128,8,128]{1,0,3,2:T(8,128)(4,1)}, pred[8,128,8,128]{1,0,3,2:T(8,128)(4,1)S(1)}, u32[]{:S(2)}) copy-start(pred[8,128,8,128]{1,0,3,2:T(8,128)(4,1)S(1)} %broadcast_in_dim.13) | copy-start | bytes 3145732
  90.1 2.3 %copy-start.3 = (f32[1024,1024]{0,1:T(8,128)}, f32[1024,1024]{0,1:T(8,128)S(1)}, u32[]{:S(2)}) copy-start(f32[1024,1024]{0,1:T(8,128)S(1)} %get-tuple-element.45) | copy-start | bytes 12582916
  93.7 3.9 %copy-start.4 = (f32[1024,1024]{0,1:T(8,128)S(1)}, f32[1024,1024]{0,1:T(8,128)}, u32[]{:S(2)}) copy-start(f32[1024,1024]{0,1:T(8,128)} %copy-done.3) | copy-start | bytes 12582916
  97.6 6.5 %copy-start.15 = (bf16[1024,256]{0,1:T(8,128)(2,1)}, bf16[1024,256]{0,1:T(8,128)(2,1)S(1)}, u32[]{:S(2)}) copy-start(bf16[1024,256]{0,1:T(8,128)(2,1)S(1)} %fusion.13) | copy-start | bytes 1572868
  102.6 2.2 copy-start.1
  109.5 26.8 %collective-permute-start = (bf16[1024,256]{0,1:T(8,128)(2,1)}, bf16[1024,256]{0,1:T(8,128)(2,1)}, u32[]{:S(2)}, u32[]{:S(2)}) collective-permute-start(bf16[1024,256]{0,1:T(8,128)(2,1)} %get-tuple-element.34), channel_id=1, source_target_pairs={{0,1},{1,0},{2,3},{3,2},{4,5},{5,4},{6,7},{7,6},{8,9},{9,8},{10,11... | collective-permute-start | bytes 1572872 | tf_op jit(solution)/shard_map/ppermute | solution.py:67
  110.7 28.7 %all-to-all-start.2 = ((bf16[3,8,128,128]{3,2,0,1:T(8,128)(2,1)}), bf16[3,8,128,128]{3,2,0,1:T(8,128)(2,1)S(1)}, u32[]{:S(2)}, u32[]{:S(2)}) async-start(bf16[3,8,128,128]{3,2,0,1:T(8,128)(2,1)} %pad_maximum_fusion.2), calls=%async_computation.2 | async-start | bytes 1572864 | tf_op jit(solution)/shard_map/all_to_all | solution.py:163
  117.8 69.4 %all-reduce.2.cloned.1.call-start = ((), (), s32[]{:S(2)}) async-start(), calls=%async_computation.4 | async-start | bytes 2097152 | tf_op jit(solution)/shard_map/psum | solution.py:147
  127.6 5.9 %copy-start.8 = (bf16[1,8,128,128]{3,2,1,0:T(8,128)(2,1)S(1)}, bf16[1,8,128,128]{3,2,1,0:T(8,128)(2,1)}, u32[]{:S(2)}) copy-start(bf16[1,8,128,128]{3,2,1,0:T(8,128)(2,1)} %copy-done.7) | copy-start | bytes 786436
  133.5 1.1 copy-start.6
  133.5 1.0 copy-start.9
  133.5 1.1 copy-start.10
  133.5 1.8 copy-start.12
  139.5 72.9 %all-to-all-start.3 = ((bf16[3,8,128,128]{3,2,0,1:T(8,128)(2,1)}), bf16[3,8,128,128]{3,2,0,1:T(8,128)(2,1)S(1)}, u32[]{:S(2)}, u32[]{:S(2)}) async-start(bf16[3,8,128,128]{3,2,0,1:T(8,128)(2,1)} %pad_maximum_fusion.3), calls=%async_computation.3 | async-start | bytes 1572864 | tf_op jit(solution)/shard_map/all_to_all | solution.py:163
  149.5 46.3 %collective-permute-start.2 = (bf16[128,2048]{1,0:T(8,128)(2,1)S(1)}, bf16[128,2048]{1,0:T(8,128)(2,1)}, u32[]{:S(2)}, u32[]{:S(2)}) collective-permute-start(bf16[128,2048]{1,0:T(8,128)(2,1)S(1)} %get-tuple-element.21), channel_id=1, source_target_pairs={{0,2},{1,3},{2,4},{3,5},{4,6},{5,7},{6,0},{7,1},{8,10},{9,11},{10,... | collective-permute-start | bytes 1572872 | tf_op jit(solution)/shard_map/ppermute | solution.py:84
  151.1 56.0 %collective-permute-start.3 = (bf16[128,2048]{1,0:T(8,128)(2,1)S(1)}, bf16[128,2048]{1,0:T(8,128)(2,1)}, u32[]{:S(2)}, u32[]{:S(2)}) collective-permute-start(bf16[128,2048]{1,0:T(8,128)(2,1)S(1)} %get-tuple-element.23), channel_id=1, source_target_pairs={{0,4},{1,5},{2,6},{3,7},{4,0},{5,1},{6,2},{7,3},{8,12},{9,13},{10,... | collective-permute-start | bytes 1572872 | tf_op jit(solution)/shard_map/ppermute | solution.py:84
  152.0 57.2 %collective-permute-start.4 = (bf16[128,2048]{1,0:T(8,128)(2,1)S(1)}, bf16[128,2048]{1,0:T(8,128)(2,1)}, u32[]{:S(2)}, u32[]{:S(2)}) collective-permute-start(bf16[128,2048]{1,0:T(8,128)(2,1)S(1)} %get-tuple-element.22), channel_id=1, source_target_pairs={{0,6},{1,7},{2,0},{3,1},{4,2},{5,3},{6,4},{7,5},{8,14},{9,15},{10,... | collective-permute-start | bytes 1572872 | tf_op jit(solution)/shard_map/ppermute | solution.py:84
Sparse Core Ops, SparseCore 0:
  9.6 71.9 all-gather.2
  133.6 53.4 all-reduce.1

commit v14 on v7

--- a/solution.py
+++ b/solution.py
@@ -78,11 +78,14 @@
     )
     total = lax.dynamic_index_in_dim(chip_partial, z, 0, keepdims=False)
     sent = chip_partial.astype(jnp.bfloat16)
+    moved = []
     for k in range(1, chips):
         pairs = [(i, ((i // 2 + k) % chips) * 2 + i % 2) for i in range(n)]
         piece = lax.dynamic_index_in_dim(sent, (z + k) % chips, 0, keepdims=False)
-        total = total + lax.ppermute(piece, "seq", pairs).astype(jnp.float32)
-    return total
+        moved.append(lax.ppermute(piece, "seq", pairs))
+    for piece in moved:
+        total = total + piece.astype(jnp.float32)
+    return total, sent
 
 
 def shards(
@@ -130,13 +133,15 @@
     ]
     att_flat = jnp.concatenate([f[0] for f in fwd], axis=1)
 
-    layer_out = chip_layer_out(att_flat, w_out).astype(jnp.bfloat16)[None]
+    layer_total, sent = chip_layer_out(att_flat, w_out)
+    layer_out = layer_total.astype(jnp.bfloat16)[None]
+    sent, att_later, grad_later = lax.optimization_barrier((sent, att_flat, grad_full))
 
     g_flat = lax.dot_general(
         grad_full, w_out, (((1,), (1,)), ((), ())), preferred_element_type=jnp.float32
     ).astype(jnp.bfloat16)
-    att_blocks = att_flat.reshape(n_seq, nodes_here, local_heads * HD)
-    grad_blocks = grad_full.reshape(n_seq, nodes_here, width)
+    att_blocks = att_later.reshape(n_seq, nodes_here, local_heads * HD)
+    grad_blocks = grad_later.reshape(n_seq, nodes_here, width)
     terms = jnp.einsum(
         "bnf,bnk->bfk", att_blocks, grad_blocks, preferred_element_type=jnp.float32
     ).astype(jnp.bfloat16)

time: 221 us -> 222 us (level)
  waiting for transfers between devices: 128 us -> 136 us
  matrix products: 32 us -> 28.4 us
  other arithmetic: 12.6 us -> 9.12 us
    ppermute x3, waiting for transfers between devices: 20.2 us -> 64.7 us  [chip_layer_out(): moved.append(lax.ppermute(piece, 'seq', pairs))]
    psum x1, waiting for transfers between devices: 36.3 us -> 0.01 us  [shards(): w_rows = lax.psum(w_rows.astype(jnp.bfloat16), 'dp').astype(jnp.float32)]
    dot_general x1, matrix products: 5.71 us -> 3.35 us  [shards(): jnp.einsum('bnf,bnk->bfk', att_blocks, grad_blocks, preferred_element_typ...]
    unnamed x38 -> x36, local copies, waits for them, and re-layouts: 12 us -> 10.6 us
  transfers between devices with their start and end apart: 9 -> 9, of which waited for: 3 -> 4; matrix products, arithmetic and copies ran while one was open for 27% -> 23% of each run, Pallas kernels for 0% -> 0%
where the time goes in v14:
time: 222 us; the launch traced here: 221 us
  waiting for transfers between devices  136 us (61%)
  matrix products  28.4 us (13%)
  local copies, waits for them, and re-layouts  17.4 us (8%)
  starting transfers between devices  16.1 us (7%)
  between operations  14.5 us (7%)
  other arithmetic  9.12 us (4%)
    all_to_all x1, waiting for transfers between devices, shards(): lax.all_to_all(stacked, 'seq', split_axis=1, concat_axis=1, tiled=True)  70.5 us
    ppermute x3, waiting for transfers between devices, chip_layer_out(): moved.append(lax.ppermute(piece, 'seq', pairs))  64.7 us
    unnamed x36, local copies, waits for them, and re-layouts  10.6 us
    all_to_all x1, starting transfers between devices, shards(): lax.all_to_all(stacked, 'seq', split_axis=1, concat_axis=1, tiled=True)  6.33 us
    dot_general x1, matrix products, chip_layer_out(): lax.dot_general(att_chip, w_chip, (((2,), (0,)), ((), ())), preferred_ele...  4.94 us
    ppermute x3, starting transfers between devices, chip_layer_out(): moved.append(lax.ppermute(piece, 'seq', pairs))  4.79 us
    dot_general x2, matrix products, attend_back(): v_grad = jnp.dot(prob_low.T, g, preferred_element_type=jnp.float32)  4.47 us
  transfers between devices with their start and end apart: 9, of which 4 were waited for; matrix products, arithmetic and copies ran while one was open for 23% of the time, Pallas kernels for 0%

profile of v14, /device:TPU:0, one launch (start us, length us, event | category | flops | bytes accessed | tf_op | source)
XLA Modules:
  0.0 221.4 jit_solution(2186708418806702981)
XLA Ops:
  7.2 0.7 all-gather.3.cloned.1.call-update
  7.9 1.3 copy.73
  9.2 1.3 copy.74
  10.5 1.3 copy.75
  12.1 1.2 copy.76
  13.3 6.3 %all-to-all-start = ((bf16[3,8,128,256]{2,3,0,1:T(8,128)(2,1)}), bf16[3,8,128,256]{2,3,0,1:T(8,128)(2,1)S(1)}, u32[]{:S(2)}, u32[]{:S(2)}) async-start(bf16[3,8,128,256]{2,3,0,1:T(8,128)(2,1)} %copy.76), calls=%async_computation | async-start | bytes 3145728 | tf_op jit(solution)/shard_map/all_to_all | solution.py:122
  19.6 0.5 collective-permute-start.1
  20.7 70.5 %all-to-all-done = bf16[3,8,128,256]{2,3,0,1:T(8,128)(2,1)S(1)} async-done(((bf16[3,8,128,256]{2,3,0,1:T(8,128)(2,1)}), bf16[3,8,128,256]{2,3,0,1:T(8,128)(2,1)S(1)}, u32[]{:S(2)}, u32[]{:S(2)}) %all-to-all-start) | async-done | bytes 1572896 | tf_op jit(solution)/shard_map/all_to_all | solution.py:122
  91.3 1.0 copy.97
  92.8 0.7 fusion.41
  93.9 1.3 select_reduce_fusion.1
  95.2 2.2 %fusion.60 = (f32[1024]{0:T(1024)S(1)}, f32[1024]{0:T(1024)S(1)}) fusion(f32[1024]{0:T(1024)S(1)} %get-tuple-element.21, f32[1024,1024]{0,1:T(8,128)S(1)} %get-tuple-element.38, pred[128,8,8,128]{3,2,1,0:T(8,128)(4,1)S(1)} %bitcast.123, f32[1024]{0:T(1024)S(1)} %get-tuple-element.22, f32[1024,1024]{0,1:T(8,128)S(1)} %fusion.41), kind=kLoop, calls=%fused_computation.84 | loop fusion | flops 8386560 | bytes 9453568 | tf_op jit(solution)/shard_map/reduce_sum | solution.py:34
  97.5 1.2 fusion.23
  98.8 3.9 %convolution_convert_fusion = bf16[1024,256]{0,1:T(8,128)(2,1)S(1)} fusion(bf16[256,2048]{1,0:T(8,128)(2,1)} %param.11, bf16[1,1024,2048]{2,1,0:T(8,128)(2,1)} %all-gather.3.cloned.1.call-done), kind=kOutput, calls=%fused_computation.24 | convolution fusion | flops 1074003968 | bytes 5767168 | tf_op jit(solution)/shard_map/dot_general | solution.py:140
  102.7 2.2 %fusion.20 = bf16[1024,128]{0,1:T(8,128)(2,1)} fusion(f32[1024]{0:T(1024)S(1)} %get-tuple-element.20, bf16[1024,256]{0,1:T(8,128)(2,1)S(1)} %convolution_convert_fusion, f32[1024,1024]{0,1:T(8,128)S(1)} %copy-done.1, f32[1024]{0:T(1024)S(1)} %get-tuple-element.22, pred[128,8,8,128]{3,2,1,0:T(8,128)(4,1)S(1)} %bitcast.125), kind=kOutput, calls=%fused_computation.28 | convolution fusion | flops 273809408 | bytes 5775360 | tf_op jit(solution)/shard_map/dot_general | solution.py:44
  105.0 2.2 %fusion.17 = bf16[1024,128]{0,1:T(8,128)(2,1)} fusion(f32[1024]{0:T(1024)S(1)} %get-tuple-element.19, bf16[1024,256]{0,1:T(8,128)(2,1)S(1)} %convolution_convert_fusion, f32[1024,1024]{0,1:T(8,128)S(1)} %copy-done.3, f32[1024]{0:T(1024)S(1)} %get-tuple-element.21, pred[128,8,8,128]{3,2,1,0:T(8,128)(4,1)S(1)} %bitcast.126), kind=kOutput, calls=%fused_computation.27 | convolution fusion | flops 273809408 | bytes 5775360 | tf_op jit(solution)/shard_map/dot_general | solution.py:44
  107.2 1.3 multiply_reduce_fusion.1
  108.5 2.2 %multiply_convert_fusion.1 = bf16[1024,1024]{0,1:T(8,128)(2,1)S(1)} fusion(f32[1024]{0:T(1024)S(1)} %get-tuple-element.23, f32[1024]{0:T(1024)S(1)} %get-tuple-element.19, bf16[1024,256]{1,0:T(8,128)(2,1)S(1)} %bitcast.149, bf16[1024,256]{0,1:T(8,128)(2,1)S(1)} %convolution_convert_fusion, f32[1024]{0:T(1024)S(1)} %get-tuple-element.21, ...), kind=kOutput, calls=%fused_computation.2 | convolution fusion | flops 276824064 | bytes 7876608 | tf_op jit(solution)/shard_map/dot_general | solution.py:45
  110.7 0.8 convolution_convert_fusion.2
  111.6 0.5 convolution_convert_fusion.4
  112.1 2.0 multiply_convert_fusion
  114.2 0.5 convolution_convert_fusion.3
  114.7 0.8 convolution_convert_fusion.1
  115.5 0.4 reshape.55
  116.7 1.3 pad_maximum_fusion.1
  118.0 4.3 %all-to-all-start.1 = ((bf16[3,8,128,256]{2,3,0,1:T(8,128)(2,1)}), bf16[3,8,128,256]{2,3,0,1:T(8,128)(2,1)}, u32[]{:S(2)}, u32[]{:S(2)}) async-start(bf16[3,8,128,256]{2,3,0,1:T(8,128)(2,1)} %pad_maximum_fusion.1), calls=%async_computation.1 | async-start | bytes 3145728 | tf_op jit(solution)/shard_map/all_to_all | solution.py:169
  122.4 0.7 fusion.64
  123.1 0.5 copy.99
  123.6 0.5 copy.98
  124.1 0.4 reshape.56
  124.4 0.7 fusion.65
  125.2 0.5 copy.101
  125.7 0.5 copy.100
  126.2 4.9 %fusion.66 = (bf16[4,128,2048]{2,1,0:T(8,128)(2,1)S(1)}, f32[4,128,2048]{2,1,0:T(8,128)}) fusion(bf16[256,2048]{1,0:T(8,128)(2,1)} %collective-permute-done.1, bf16[256,2048]{1,0:T(8,128)(2,1)} %param.11, bf16[4,128,256]{2,1,0:T(8,128)(2,1)S(1)} %get-tuple-element.42, bf16[4,128,256]{2,1,0:T(8,128)(2,1)S(1)} %get-tuple-element.43), kind=kOutput, calls=%fused_computation.90 | convolution fusion | flops 1080033280 | bytes 8912896 | tf_op jit(solution)/shard_map/dot_general | solution.py:76
  131.2 3.4 %convert_reduce_fusion = bf16[256,2048]{1,0:T(8,128)(2,1)} fusion(bf16[8,128,2048]{2,1,0:T(8,128)(2,1)S(1)} %bitcast.151, bf16[1024,256]{0,1:T(8,128)(2,1)S(1)} %pad_maximum_fusion.2), kind=kOutput, calls=%fused_computation | convolution fusion | flops 1081606144 | bytes 5767168 | tf_op jit(solution)/shard_map/bnf,bnk->bfk/dot_general | solution.py:145
  134.5 1.0 dynamic-slice_bitcast_fusion.2
  135.5 1.8 collective-permute-start.2
  137.4 2.0 collective-permute-start.4
  139.3 1.0 collective-permute-start.3
  140.3 24.0 %collective-permute-done.2 = bf16[128,2048]{1,0:T(8,128)(2,1)S(1)} collective-permute-done((bf16[128,2048]{1,0:T(8,128)(2,1)}, bf16[128,2048]{1,0:T(8,128)(2,1)S(1)}, u32[]{:S(2)}, u32[]{:S(2)}) %collective-permute-start.2) | collective-permute-done | bytes 524320 | tf_op jit(solution)/shard_map/ppermute | solution.py:85
  164.3 8.8 %collective-permute-done.4 = bf16[128,2048]{1,0:T(8,128)(2,1)S(1)} collective-permute-done((bf16[128,2048]{1,0:T(8,128)(2,1)S(1)}, bf16[128,2048]{1,0:T(8,128)(2,1)S(1)}, u32[]{:S(2)}, u32[]{:S(2)}) %collective-permute-start.4) | collective-permute-done | bytes 524320 | tf_op jit(solution)/shard_map/ppermute | solution.py:85
  173.2 31.9 %collective-permute-done.3 = bf16[128,2048]{1,0:T(8,128)(2,1)S(1)} collective-permute-done((bf16[128,2048]{1,0:T(8,128)(2,1)S(1)}, bf16[128,2048]{1,0:T(8,128)(2,1)S(1)}, u32[]{:S(2)}, u32[]{:S(2)}) %collective-permute-start.3) | collective-permute-done | bytes 524320 | tf_op jit(solution)/shard_map/ppermute | solution.py:85
  205.0 2.3 %fusion.32 = bf16[1,128,2048]{2,1,0:T(8,128)(2,1)} fusion(bf16[128,2048]{1,0:T(8,128)(2,1)S(1)} %collective-permute-done.4, bf16[128,2048]{1,0:T(8,128)(2,1)S(1)} %collective-permute-done.3, bf16[128,2048]{1,0:T(8,128)(2,1)S(1)} %collective-permute-done.2, f32[4,128,2048]{2,1,0:T(8,128)} %get-tuple-element.40, s32[]{:T(128)S(6)} %select_n.79), kind=kLoop, calls=%fused_computation.40 | loop fusion | flops 1835008 | bytes 3145732 | tf_op jit(solution)/shard_map/broadcast_in_dim | solution.py:137
  207.3 2.8 %convert_multiply_fusion = f32[256,2048]{1,0:T(8,128)} fusion(bf16[256,2048]{1,0:T(8,128)(2,1)} %all-reduce.2.cloned.1.call-done), kind=kLoop, calls=%fused_computation.11 | loop fusion | flops 1048576 | bytes 3145728 | tf_op jit(solution)/shard_map/div | solution.py:151
  210.1 1.5 fusion.62
  211.6 1.0 copy.92
  212.6 1.0 copy.91
  213.6 1.0 copy.90
  (49 shorter events, 2.5 us)
Async XLA Ops:
  7.2 91.6 %all-gather.3.cloned.1.call-start = ((), (), s32[]{:S(2)}) async-start(), calls=%async_computation.3 | async-start | bytes 4718592 | tf_op jit(solution)/shard_map/all_gather | solution.py:106
  11.9 8.3 %copy-start.8 = (s32[1,9]{1,0:T(1,128)S(1)}, s32[1,9]{1,0:T(1,128)}, u32[]{:S(2)}) copy-start(s32[1,9]{1,0:T(1,128)} %param.12) | copy-start | bytes 112
  11.9 8.4 %copy-start.9 = (s32[1,32]{1,0:T(1,128)S(1)}, s32[1,32]{1,0:T(1,128)}, u32[]{:S(2)}) copy-start(s32[1,32]{1,0:T(1,128)} %param.13) | copy-start | bytes 388
  13.3 77.9 %all-to-all-start = ((bf16[3,8,128,256]{2,3,0,1:T(8,128)(2,1)}), bf16[3,8,128,256]{2,3,0,1:T(8,128)(2,1)S(1)}, u32[]{:S(2)}, u32[]{:S(2)}) async-start(bf16[3,8,128,256]{2,3,0,1:T(8,128)(2,1)} %copy.76), calls=%async_computation | async-start | bytes 3145728 | tf_op jit(solution)/shard_map/all_to_all | solution.py:122
  19.6 106.6 %collective-permute-start.1 = (bf16[256,2048]{1,0:T(8,128)(2,1)}, bf16[256,2048]{1,0:T(8,128)(2,1)}, u32[]{:S(2)}, u32[]{:S(2)}) collective-permute-start(bf16[256,2048]{1,0:T(8,128)(2,1)} %param.11), channel_id=1, source_target_pairs={{0,1},{1,0},{2,3},{3,2},{4,5},{5,4},{6,7},{7,6},{8,9},{9,8},{10,11... | collective-permute-start | bytes 3145736 | tf_op jit(solution)/shard_map/ppermute | solution.py:68
  93.5 4.0 %copy-start = (f32[1024,1024]{0,1:T(8,128)}, f32[1024,1024]{0,1:T(8,128)S(1)}, u32[]{:S(2)}) copy-start(f32[1024,1024]{0,1:T(8,128)S(1)} %fusion.41) | copy-start | bytes 12582916
  95.2 2.3 %copy-start.2 = (f32[1024,1024]{0,1:T(8,128)}, f32[1024,1024]{0,1:T(8,128)S(1)}, u32[]{:S(2)}) copy-start(f32[1024,1024]{0,1:T(8,128)S(1)} %get-tuple-element.38) | copy-start | bytes 12582916
  95.2 2.3 %copy-start.4 = (bf16[1,8,128,256]{3,2,1,0:T(8,128)(2,1)S(1)}, bf16[1,8,128,256]{3,2,1,0:T(8,128)(2,1)}, u32[]{:S(2)}) copy-start(bf16[1,8,128,256]{3,2,1,0:T(8,128)(2,1)} %copy.97) | copy-start | bytes 1572868
  98.8 3.9 %copy-start.1 = (f32[1024,1024]{0,1:T(8,128)S(1)}, f32[1024,1024]{0,1:T(8,128)}, u32[]{:S(2)}) copy-start(f32[1024,1024]{0,1:T(8,128)} %copy-done) | copy-start | bytes 12582916
  102.7 2.2 %copy-start.3 = (f32[1024,1024]{0,1:T(8,128)S(1)}, f32[1024,1024]{0,1:T(8,128)}, u32[]{:S(2)}) copy-start(f32[1024,1024]{0,1:T(8,128)} %copy-done.2) | copy-start | bytes 12582916
  114.1 1.9 copy-start.5
  114.1 1.9 copy-start.6
  115.9 8.1 %collective-permute-start = (bf16[1024,256]{0,1:T(8,128)(2,1)S(1)}, bf16[1024,256]{0,1:T(8,128)(2,1)S(1)}, u32[]{:S(2)}, u32[]{:S(2)}) collective-permute-start(bf16[1024,256]{0,1:T(8,128)(2,1)S(1)} %pad_maximum_fusion.2), channel_id=1, source_target_pairs={{0,1},{1,0},{2,3},{3,2},{4,5},{5,4},{6,7},{7,6},{8,9},{9,8},{10,11... | collective-permute-start | bytes 1572872 | tf_op jit(solution)/shard_map/ppermute | solution.py:67
  118.0 92.1 %all-to-all-start.1 = ((bf16[3,8,128,256]{2,3,0,1:T(8,128)(2,1)}), bf16[3,8,128,256]{2,3,0,1:T(8,128)(2,1)}, u32[]{:S(2)}, u32[]{:S(2)}) async-start(bf16[3,8,128,256]{2,3,0,1:T(8,128)(2,1)} %pad_maximum_fusion.1), calls=%async_computation.1 | async-start | bytes 3145728 | tf_op jit(solution)/shard_map/all_to_all | solution.py:169
  122.3 85.0 %all-reduce.2.cloned.1.call-start = ((), (), s32[]{:S(2)}) async-start(), calls=%async_computation.2 | async-start | bytes 2097152 | tf_op jit(solution)/shard_map/psum | solution.py:149
  126.2 5.0 %copy-start.7 = (bf16[1,1024,2048]{2,1,0:T(8,128)(2,1)S(1)}, bf16[1,1024,2048]{2,1,0:T(8,128)(2,1)}, u32[]{:S(2)}) copy-start(bf16[1,1024,2048]{2,1,0:T(8,128)(2,1)} %all-gather.3.cloned.1.call-done) | copy-start | bytes 12582916
  135.5 28.8 %collective-permute-start.2 = (bf16[128,2048]{1,0:T(8,128)(2,1)}, bf16[128,2048]{1,0:T(8,128)(2,1)S(1)}, u32[]{:S(2)}, u32[]{:S(2)}) collective-permute-start(bf16[128,2048]{1,0:T(8,128)(2,1)} %get-tuple-element.25), channel_id=1, source_target_pairs={{0,2},{1,3},{2,4},{3,5},{4,6},{5,7},{6,0},{7,1},{8,10},{9,11},{10,... | collective-permute-start | bytes 1572872 | tf_op jit(solution)/shard_map/ppermute | solution.py:85
  137.4 35.8 %collective-permute-start.4 = (bf16[128,2048]{1,0:T(8,128)(2,1)S(1)}, bf16[128,2048]{1,0:T(8,128)(2,1)S(1)}, u32[]{:S(2)}, u32[]{:S(2)}) collective-permute-start(bf16[128,2048]{1,0:T(8,128)(2,1)S(1)} %get-tuple-element.26), channel_id=1, source_target_pairs={{0,6},{1,7},{2,0},{3,1},{4,2},{5,3},{6,4},{7,5},{8,14},{9,15},{10,... | collective-permute-start | bytes 1572872 | tf_op jit(solution)/shard_map/ppermute | solution.py:85
  139.3 65.7 %collective-permute-start.3 = (bf16[128,2048]{1,0:T(8,128)(2,1)S(1)}, bf16[128,2048]{1,0:T(8,128)(2,1)S(1)}, u32[]{:S(2)}, u32[]{:S(2)}) collective-permute-start(bf16[128,2048]{1,0:T(8,128)(2,1)S(1)} %get-tuple-element.27), channel_id=1, source_target_pairs={{0,4},{1,5},{2,6},{3,7},{4,0},{5,1},{6,2},{7,3},{8,12},{9,13},{10,... | collective-permute-start | bytes 1572872 | tf_op jit(solution)/shard_map/ppermute | solution.py:85
Sparse Core Ops, SparseCore 0:
  9.6 83.0 all-gather.2
  134.7 53.8 all-reduce.1

commit v15 on v7

--- a/solution.py
+++ b/solution.py
@@ -106,15 +106,10 @@
     group_width = width // groups
     local_heads = group_width // HD
 
-    def to_groups(values):
-        return values.reshape(nodes_here, groups, group_width).transpose(1, 0, 2)
-
-    stacked = jnp.stack(
-        [
-            to_groups(asking_vectors_matrix[0]),
-            to_groups(matched_keys_matrix[0]),
-            to_groups(carried_vectors_matrix[0]),
-        ]
+    stacked = (
+        jnp.stack([asking_vectors_matrix[0], matched_keys_matrix[0], carried_vectors_matrix[0]])
+        .reshape(3, nodes_here, groups, group_width)
+        .transpose(0, 2, 1, 3)
     )
     heads = lax.all_to_all(stacked, "seq", split_axis=1, concat_axis=1, tiled=True)
     heads = heads.reshape(3, nodes, group_width)

time: 221 us -> 221 us (level)
  no operation moved by 1% of the time
where the time goes in v15:
time: 221 us
  waiting for transfers between devices  128 us (58%)
  matrix products  32 us (14%)
  local copies, waits for them, and re-layouts  18.5 us (8%)
  starting transfers between devices  15.4 us (7%)
  between operations  14.5 us (7%)
  other arithmetic  12.6 us (6%)
    all_to_all x1, waiting for transfers between devices, shards(): lax.all_to_all(stacked, 'seq', split_axis=1, concat_axis=1, tiled=True)  70.5 us
    psum x1, waiting for transfers between devices, shards(): w_rows = lax.psum(w_rows.astype(jnp.bfloat16), 'dp').astype(jnp.float32)  36.3 us
    ppermute x3, waiting for transfers between devices, chip_layer_out(): total = total + lax.ppermute(piece, 'seq', pairs).astype(jnp.float32)  20.2 us
    unnamed x38, local copies, waits for them, and re-layouts  12 us
    all_to_all x1, starting transfers between devices, shards(): lax.all_to_all(stacked, 'seq', split_axis=1, concat_axis=1, tiled=True)  6.33 us
    dot_general x1, matrix products, shards(): jnp.einsum('bnf,bnk->bfk', att_blocks, grad_blocks, preferred_element_typ...  5.71 us
    ppermute x3, starting transfers between devices, chip_layer_out(): total = total + lax.ppermute(piece, 'seq', pairs).astype(jnp.float32)  4.87 us
    dot_general x1, matrix products, chip_layer_out(): lax.dot_general(att_chip, w_chip, (((2,), (0,)), ((), ())), preferred_ele...  4.75 us
  transfers between devices with their start and end apart: 9, of which 3 were waited for; matrix products, arithmetic and copies ran while one was open for 27% of the time, Pallas kernels for 0%

profile of v15, /device:TPU:0, one launch (start us, length us, event | category | flops | bytes accessed | tf_op | source)
XLA Modules:
  0.0 220.7 jit_solution(16444093942752190734)
XLA Ops:
  7.2 0.7 all-gather.3.cloned.1.call-update
  7.9 1.3 copy.73
  9.2 1.3 copy.74
  10.5 1.3 copy.75
  12.1 1.2 copy.76
  13.3 6.3 %all-to-all-start = ((bf16[3,8,128,256]{2,3,0,1:T(8,128)(2,1)}), bf16[3,8,128,256]{2,3,0,1:T(8,128)(2,1)S(1)}, u32[]{:S(2)}, u32[]{:S(2)}) async-start(bf16[3,8,128,256]{2,3,0,1:T(8,128)(2,1)} %copy.76), calls=%async_computation | async-start | bytes 3145728 | tf_op jit(solution)/shard_map/all_to_all | solution.py:114
  19.6 0.5 collective-permute-start.1
  20.7 70.5 %all-to-all-done = bf16[3,8,128,256]{2,3,0,1:T(8,128)(2,1)S(1)} async-done(((bf16[3,8,128,256]{2,3,0,1:T(8,128)(2,1)}), bf16[3,8,128,256]{2,3,0,1:T(8,128)(2,1)S(1)}, u32[]{:S(2)}, u32[]{:S(2)}) %all-to-all-start) | async-done | bytes 1572896 | tf_op jit(solution)/shard_map/all_to_all | solution.py:114
  91.3 1.0 copy.97
  92.8 0.7 fusion.46
  93.8 1.3 select_reduce_fusion.1
  95.2 2.2 %fusion.65 = (f32[1024]{0:T(1024)S(1)}, f32[1024]{0:T(1024)S(1)}) fusion(f32[1024]{0:T(1024)S(1)} %get-tuple-element.17, f32[1024,1024]{0,1:T(8,128)S(1)} %get-tuple-element.36, pred[128,8,8,128]{3,2,1,0:T(8,128)(4,1)S(1)} %bitcast.113, f32[1024]{0:T(1024)S(1)} %get-tuple-element.18, f32[1024,1024]{0,1:T(8,128)S(1)} %fusion.46), kind=kLoop, calls=%fused_computation.86 | loop fusion | flops 8386560 | bytes 9453568 | tf_op jit(solution)/shard_map/reduce_sum | solution.py:34
  97.5 1.2 fusion.28
  98.8 3.9 %fusion.13 = bf16[1024,256]{0,1:T(8,128)(2,1)S(1)} fusion(bf16[256,2048]{1,0:T(8,128)(2,1)} %param.11, bf16[1,1024,2048]{2,1,0:T(8,128)(2,1)} %all-gather.3.cloned.1.call-done), kind=kOutput, calls=%fused_computation.26 | convolution fusion | flops 1074003968 | bytes 5767168 | tf_op jit(solution)/shard_map/dot_general | solution.py:130
  102.7 2.2 %fusion.25 = bf16[1024,128]{0,1:T(8,128)(2,1)} fusion(f32[1024]{0:T(1024)S(1)} %get-tuple-element.16, bf16[1024,256]{0,1:T(8,128)(2,1)S(1)} %fusion.13, f32[1024,1024]{0,1:T(8,128)S(1)} %copy-done.1, f32[1024]{0:T(1024)S(1)} %get-tuple-element.18, pred[128,8,8,128]{3,2,1,0:T(8,128)(4,1)S(1)} %bitcast.115), kind=kOutput, calls=%fused_computation.30 | convolution fusion | flops 273809408 | bytes 5775360 | tf_op jit(solution)/shard_map/dot_general | solution.py:44
  105.0 2.2 %fusion.22 = bf16[1024,128]{0,1:T(8,128)(2,1)} fusion(f32[1024]{0:T(1024)S(1)} %get-tuple-element.15, bf16[1024,256]{0,1:T(8,128)(2,1)S(1)} %fusion.13, f32[1024,1024]{0,1:T(8,128)S(1)} %copy-done.3, f32[1024]{0:T(1024)S(1)} %get-tuple-element.17, pred[128,8,8,128]{3,2,1,0:T(8,128)(4,1)S(1)} %bitcast.116), kind=kOutput, calls=%fused_computation.29 | convolution fusion | flops 273809408 | bytes 5775360 | tf_op jit(solution)/shard_map/dot_general | solution.py:44
  107.2 1.3 multiply_reduce_fusion.1
  108.5 2.2 %multiply_convert_fusion.1 = bf16[1024,1024]{0,1:T(8,128)(2,1)S(1)} fusion(f32[1024]{0:T(1024)S(1)} %get-tuple-element.19, f32[1024]{0:T(1024)S(1)} %get-tuple-element.15, bf16[1024,256]{1,0:T(8,128)(2,1)S(1)} %bitcast.136, bf16[1024,256]{0,1:T(8,128)(2,1)S(1)} %fusion.13, f32[1024]{0:T(1024)S(1)} %get-tuple-element.17, f32[1024,1024]{0,1:T(8,128)S(1)} %copy-done.3, ...), kind=kOutput, calls=%fused_computation.4 | convolution fusion | flops 276824064 | bytes 7876608 | tf_op jit(solution)/shard_map/dot_general | solution.py:45
  110.7 0.8 convolution_convert_fusion.1
  111.6 1.2 convolution_convert_fusion.3
  112.8 2.0 multiply_convert_fusion
  114.8 1.2 convolution_convert_fusion.2
  116.0 0.8 convolution_convert_fusion
  117.1 0.4 reshape.59
  117.5 1.0 maximum_bitcast_fusion.4
  118.9 1.0 maximum_bitcast_fusion.2
  120.1 1.3 pad_maximum_fusion.1
  121.4 3.6 %all-to-all-start.1 = ((bf16[3,8,128,256]{2,3,0,1:T(8,128)(2,1)}), bf16[3,8,128,256]{2,3,0,1:T(8,128)(2,1)S(1)}, u32[]{:S(2)}, u32[]{:S(2)}) async-start(bf16[3,8,128,256]{2,3,0,1:T(8,128)(2,1)} %pad_maximum_fusion.1), calls=%async_computation.1 | async-start | bytes 3145728 | tf_op jit(solution)/shard_map/all_to_all | solution.py:159
  125.1 5.7 %convert_reduce_fusion = bf16[256,2048]{1,0:T(8,128)(2,1)} fusion(bf16[8,128,2048]{2,1,0:T(8,128)(2,1)} %bitcast.138, bf16[32,8,8,128]{3,2,1,0:T(8,128)(2,1)S(1)} %get-tuple-element.30), kind=kOutput, calls=%fused_computation | convolution fusion | flops 1081606144 | bytes 5767168 | tf_op jit(solution)/shard_map/bnf,bnk->bfk/dot_general | solution.py:135
  130.8 1.5 fusion.69
  132.3 1.2 copy.99
  133.6 1.1 copy.98
  134.7 1.4 reshape.60
  136.1 0.7 fusion.70
  136.8 0.5 copy.101
  137.3 0.5 copy.100
  137.8 1.0 select_bitcast_fusion
  138.8 4.8 %fusion.71 = (bf16[4,128,2048]{2,1,0:T(8,128)(2,1)S(1)}, f32[4,128,2048]{2,1,0:T(8,128)}) fusion(bf16[256,2048]{1,0:T(8,128)(2,1)} %collective-permute-done.1, bf16[256,2048]{1,0:T(8,128)(2,1)} %param.11, bf16[4,128,256]{2,1,0:T(8,128)(2,1)S(1)} %get-tuple-element.40, bf16[4,128,256]{2,1,0:T(8,128)(2,1)S(1)} %get-tuple-element.41), kind=kOutput, calls=%fused_computation.92 | convolution fusion | flops 1080033280 | bytes 8912896 | tf_op jit(solution)/shard_map/dot_general | solution.py:76
  143.8 1.9 collective-permute-start.2
  145.7 1.9 collective-permute-start.4
  147.6 1.0 collective-permute-start.3
  148.6 36.3 %all-reduce.2.cloned.1.call-done = bf16[256,2048]{1,0:T(8,128)(2,1)} async-done(((bf16[256,2048]{1,0:T(8,128)(2,1)}), bf16[256,2048]{1,0:T(8,128)(2,1)}) %all-reduce.2.cloned.1.call-update) | async-done | bytes 1048592 | tf_op jit(solution)/shard_map/psum | solution.py:139
  184.9 2.8 %convert_multiply_fusion = f32[256,2048]{1,0:T(8,128)} fusion(bf16[256,2048]{1,0:T(8,128)(2,1)} %all-reduce.2.cloned.1.call-done), kind=kLoop, calls=%fused_computation.13 | loop fusion | flops 1048576 | bytes 3145728 | tf_op jit(solution)/shard_map/div | solution.py:141
  187.7 20.2 %collective-permute-done.3 = bf16[128,2048]{1,0:T(8,128)(2,1)} collective-permute-done((bf16[128,2048]{1,0:T(8,128)(2,1)S(1)}, bf16[128,2048]{1,0:T(8,128)(2,1)}, u32[]{:S(2)}, u32[]{:S(2)}) %collective-permute-start.3) | collective-permute-done | bytes 524320 | tf_op jit(solution)/shard_map/ppermute | solution.py:84
  207.9 2.8 %fusion.37 = bf16[1,128,2048]{2,1,0:T(8,128)(2,1)} fusion(bf16[128,2048]{1,0:T(8,128)(2,1)} %collective-permute-done.4, bf16[128,2048]{1,0:T(8,128)(2,1)} %collective-permute-done.3, bf16[128,2048]{1,0:T(8,128)(2,1)} %collective-permute-done.2, f32[4,128,2048]{2,1,0:T(8,128)} %get-tuple-element.38, s32[]{:T(128)S(6)} %select_n.79), kind=kLoop, calls=%fused_computation.42 | loop fusion | flops 1835008 | bytes 3145732 | tf_op jit(solution)/shard_map/broadcast_in_dim | solution.py:128
  210.8 1.0 copy.92
  211.8 1.0 copy.91
  212.8 1.0 copy.90
  (51 shorter events, 2.9 us)
Async XLA Ops:
  7.2 91.6 %all-gather.3.cloned.1.call-start = ((), (), s32[]{:S(2)}) async-start(), calls=%async_computation.3 | async-start | bytes 4718592 | tf_op jit(solution)/shard_map/all_gather | solution.py:103
  11.9 8.3 %copy-start.9 = (s32[1,9]{1,0:T(1,128)S(1)}, s32[1,9]{1,0:T(1,128)}, u32[]{:S(2)}) copy-start(s32[1,9]{1,0:T(1,128)} %param.12) | copy-start | bytes 112
  11.9 8.4 %copy-start.10 = (s32[1,32]{1,0:T(1,128)S(1)}, s32[1,32]{1,0:T(1,128)}, u32[]{:S(2)}) copy-start(s32[1,32]{1,0:T(1,128)} %param.13) | copy-start | bytes 388
  13.3 77.9 %all-to-all-start = ((bf16[3,8,128,256]{2,3,0,1:T(8,128)(2,1)}), bf16[3,8,128,256]{2,3,0,1:T(8,128)(2,1)S(1)}, u32[]{:S(2)}, u32[]{:S(2)}) async-start(bf16[3,8,128,256]{2,3,0,1:T(8,128)(2,1)} %copy.76), calls=%async_computation | async-start | bytes 3145728 | tf_op jit(solution)/shard_map/all_to_all | solution.py:114
  19.6 119.2 %collective-permute-start.1 = (bf16[256,2048]{1,0:T(8,128)(2,1)}, bf16[256,2048]{1,0:T(8,128)(2,1)}, u32[]{:S(2)}, u32[]{:S(2)}) collective-permute-start(bf16[256,2048]{1,0:T(8,128)(2,1)} %param.11), channel_id=1, source_target_pairs={{0,1},{1,0},{2,3},{3,2},{4,5},{5,4},{6,7},{7,6},{8,9},{9,8},{10,11... | collective-permute-start | bytes 3145736 | tf_op jit(solution)/shard_map/ppermute | solution.py:68
  93.5 4.0 %copy-start = (f32[1024,1024]{0,1:T(8,128)}, f32[1024,1024]{0,1:T(8,128)S(1)}, u32[]{:S(2)}) copy-start(f32[1024,1024]{0,1:T(8,128)S(1)} %fusion.46) | copy-start | bytes 12582916
  95.2 2.3 %copy-start.2 = (f32[1024,1024]{0,1:T(8,128)}, f32[1024,1024]{0,1:T(8,128)S(1)}, u32[]{:S(2)}) copy-start(f32[1024,1024]{0,1:T(8,128)S(1)} %get-tuple-element.36) | copy-start | bytes 12582916
  95.2 2.3 %copy-start.4 = (bf16[1,8,128,256]{3,2,1,0:T(8,128)(2,1)S(1)}, bf16[1,8,128,256]{3,2,1,0:T(8,128)(2,1)}, u32[]{:S(2)}) copy-start(bf16[1,8,128,256]{3,2,1,0:T(8,128)(2,1)} %copy.97) | copy-start | bytes 1572868
  98.7 8.5 %copy-start.7 = (bf16[1024,128]{0,1:T(8,128)(2,1)}, bf16[1024,128]{0,1:T(8,128)(2,1)S(1)}, u32[]{:S(2)}) copy-start(bf16[1024,128]{0,1:T(8,128)(2,1)S(1)} %fusion.28) | copy-start | bytes 786436
  98.8 3.9 %copy-start.1 = (f32[1024,1024]{0,1:T(8,128)S(1)}, f32[1024,1024]{0,1:T(8,128)}, u32[]{:S(2)}) copy-start(f32[1024,1024]{0,1:T(8,128)} %copy-done) | copy-start | bytes 12582916
  102.7 2.2 %copy-start.3 = (f32[1024,1024]{0,1:T(8,128)S(1)}, f32[1024,1024]{0,1:T(8,128)}, u32[]{:S(2)}) copy-start(f32[1024,1024]{0,1:T(8,128)} %copy-done.2) | copy-start | bytes 12582916
  114.8 2.1 copy-start.8
  114.8 2.7 %copy-start.6 = (bf16[1024,128]{0,1:T(8,128)(2,1)S(1)}, bf16[1024,128]{0,1:T(8,128)(2,1)}, u32[]{:S(2)}) copy-start(bf16[1024,128]{0,1:T(8,128)(2,1)} %fusion.25) | copy-start | bytes 786436
  116.9 2.1 copy-start.5
  117.4 17.3 %collective-permute-start = (bf16[1024,256]{0,1:T(8,128)(2,1)S(1)}, bf16[1024,256]{0,1:T(8,128)(2,1)}, u32[]{:S(2)}, u32[]{:S(2)}) collective-permute-start(bf16[1024,256]{0,1:T(8,128)(2,1)S(1)} %get-tuple-element.31), channel_id=1, source_target_pairs={{0,1},{1,0},{2,3},{3,2},{4,5},{5,4},{6,7},{7,6},{8,9},{9,8},{10,11... | collective-permute-start | bytes 1572872 | tf_op jit(solution)/shard_map/ppermute | solution.py:67
  121.4 89.2 %all-to-all-start.1 = ((bf16[3,8,128,256]{2,3,0,1:T(8,128)(2,1)}), bf16[3,8,128,256]{2,3,0,1:T(8,128)(2,1)S(1)}, u32[]{:S(2)}, u32[]{:S(2)}) async-start(bf16[3,8,128,256]{2,3,0,1:T(8,128)(2,1)} %pad_maximum_fusion.1), calls=%async_computation.1 | async-start | bytes 3145728 | tf_op jit(solution)/shard_map/all_to_all | solution.py:159
  125.0 59.8 %all-reduce.2.cloned.1.call-start = ((), (), s32[]{:S(2)}) async-start(), calls=%async_computation.2 | async-start | bytes 2097152 | tf_op jit(solution)/shard_map/psum | solution.py:139
  143.8 43.9 %collective-permute-start.2 = (bf16[128,2048]{1,0:T(8,128)(2,1)S(1)}, bf16[128,2048]{1,0:T(8,128)(2,1)}, u32[]{:S(2)}, u32[]{:S(2)}) collective-permute-start(bf16[128,2048]{1,0:T(8,128)(2,1)S(1)} %get-tuple-element.21), channel_id=1, source_target_pairs={{0,2},{1,3},{2,4},{3,5},{4,6},{5,7},{6,0},{7,1},{8,10},{9,11},{10,... | collective-permute-start | bytes 1572872 | tf_op jit(solution)/shard_map/ppermute | solution.py:84
  145.7 42.0 %collective-permute-start.4 = (bf16[128,2048]{1,0:T(8,128)(2,1)S(1)}, bf16[128,2048]{1,0:T(8,128)(2,1)}, u32[]{:S(2)}, u32[]{:S(2)}) collective-permute-start(bf16[128,2048]{1,0:T(8,128)(2,1)S(1)} %get-tuple-element.22), channel_id=1, source_target_pairs={{0,6},{1,7},{2,0},{3,1},{4,2},{5,3},{6,4},{7,5},{8,14},{9,15},{10,... | collective-permute-start | bytes 1572872 | tf_op jit(solution)/shard_map/ppermute | solution.py:84
  147.6 60.2 %collective-permute-start.3 = (bf16[128,2048]{1,0:T(8,128)(2,1)S(1)}, bf16[128,2048]{1,0:T(8,128)(2,1)}, u32[]{:S(2)}, u32[]{:S(2)}) collective-permute-start(bf16[128,2048]{1,0:T(8,128)(2,1)S(1)} %get-tuple-element.23), channel_id=1, source_target_pairs={{0,4},{1,5},{2,6},{3,7},{4,0},{5,1},{6,2},{7,3},{8,12},{9,13},{10,... | collective-permute-start | bytes 1572872 | tf_op jit(solution)/shard_map/ppermute | solution.py:84
Sparse Core Ops, SparseCore 0:
  9.6 83.0 all-gather.2
  130.9 53.8 all-reduce.1

commit v16 on v7

--- a/solution.py
+++ b/solution.py
@@ -30,7 +30,7 @@
     scores = jnp.dot(q, k.T, preferred_element_type=jnp.float32) * factor
     masked = jnp.where(allowed, scores, -jnp.inf)
     row_max = jnp.max(masked, axis=1, keepdims=True)
-    expd = jnp.where(allowed, jnp.exp(scores - row_max), 0.0)
+    expd = jnp.exp(masked - row_max)
     row_total = jnp.sum(expd, axis=1, keepdims=True)
     weighted = jnp.dot(expd.astype(jnp.bfloat16), v, preferred_element_type=jnp.float32)
     attended = (weighted / row_total).astype(jnp.bfloat16)

time: 221 us -> 218 us (0.986)
  matrix products: 32 us -> 27.5 us
  local copies, waits for them, and re-layouts: 18.5 us -> 21 us
    unnamed x38 -> x32, local copies, waits for them, and re-layouts: 12 us -> 14.6 us
  transfers between devices with their start and end apart: 9 -> 9, of which waited for: 3 -> 3; matrix products, arithmetic and copies ran while one was open for 27% -> 25% of each run, Pallas kernels for 0% -> 0%
where the time goes in v16:
time: 218 us; the launch traced here: 217 us
  waiting for transfers between devices  128 us (59%)
  matrix products  27.5 us (13%)
  local copies, waits for them, and re-layouts  21 us (10%)
  starting transfers between devices  15.4 us (7%)
  between operations  14.4 us (7%)
  other arithmetic  10.8 us (5%)
    all_to_all x1, waiting for transfers between devices, shards(): lax.all_to_all(stacked, 'seq', split_axis=1, concat_axis=1, tiled=True)  70.5 us
    psum x1, waiting for transfers between devices, shards(): w_rows = lax.psum(w_rows.astype(jnp.bfloat16), 'dp').astype(jnp.float32)  36.3 us
    ppermute x3, waiting for transfers between devices, chip_layer_out(): total = total + lax.ppermute(piece, 'seq', pairs).astype(jnp.float32)  20.2 us
    unnamed x32, local copies, waits for them, and re-layouts  14.6 us
    all_to_all x1, starting transfers between devices, shards(): lax.all_to_all(stacked, 'seq', split_axis=1, concat_axis=1, tiled=True)  6.33 us
    dot_general x1, matrix products, shards(): jnp.einsum('bnf,bnk->bfk', att_blocks, grad_blocks, preferred_element_typ...  5.7 us
    ppermute x3, starting transfers between devices, chip_layer_out(): total = total + lax.ppermute(piece, 'seq', pairs).astype(jnp.float32)  4.87 us
    dot_general x1, matrix products, chip_layer_out(): lax.dot_general(att_chip, w_chip, (((2,), (0,)), ((), ())), preferred_ele...  4.74 us
  transfers between devices with their start and end apart: 9, of which 3 were waited for; matrix products, arithmetic and copies ran while one was open for 25% of the time, Pallas kernels for 0%

profile of v16, /device:TPU:0, one launch (start us, length us, event | category | flops | bytes accessed | tf_op | source)
XLA Modules:
  0.0 216.9 jit_solution(426929152881993361)
XLA Ops:
  7.2 0.7 all-gather.3.cloned.1.call-update
  7.9 1.3 copy.73
  9.2 1.3 copy.74
  10.5 1.3 copy.75
  12.1 1.2 copy.76
  13.3 6.3 %all-to-all-start = ((bf16[3,8,128,256]{2,3,0,1:T(8,128)(2,1)}), bf16[3,8,128,256]{2,3,0,1:T(8,128)(2,1)S(1)}, u32[]{:S(2)}, u32[]{:S(2)}) async-start(bf16[3,8,128,256]{2,3,0,1:T(8,128)(2,1)} %copy.76), calls=%async_computation | async-start | bytes 3145728 | tf_op jit(solution)/shard_map/all_to_all | solution.py:119
  19.6 0.5 collective-permute-start.1
  20.7 70.5 %all-to-all-done = bf16[3,8,128,256]{2,3,0,1:T(8,128)(2,1)S(1)} async-done(((bf16[3,8,128,256]{2,3,0,1:T(8,128)(2,1)}), bf16[3,8,128,256]{2,3,0,1:T(8,128)(2,1)S(1)}, u32[]{:S(2)}, u32[]{:S(2)}) %all-to-all-start) | async-done | bytes 1572896 | tf_op jit(solution)/shard_map/all_to_all | solution.py:119
  91.3 1.0 copy.97
  93.1 1.0 fusion.77
  94.1 0.6 fusion.6
  94.7 1.0 fusion.78
  95.7 2.0 copy-done.2
  97.7 0.6 fusion.3
  98.3 0.8 fusion.32
  99.2 3.9 %fusion.21 = bf16[1024,256]{0,1:T(8,128)(2,1)S(1)} fusion(bf16[256,2048]{1,0:T(8,128)(2,1)} %param.11, bf16[1,1024,2048]{2,1,0:T(8,128)(2,1)} %all-gather.3.cloned.1.call-done), kind=kOutput, calls=%fused_computation.30 | convolution fusion | flops 1074003968 | bytes 5767168 | tf_op jit(solution)/shard_map/dot_general | solution.py:135
  103.1 1.6 fusion.41
  104.8 0.6 copy-done.3
  105.4 1.6 fusion.38
  107.1 0.8 multiply_reduce_fusion.1
  107.9 1.2 multiply_convert_fusion.1
  109.1 0.8 convolution_convert_fusion.1
  110.0 0.5 convolution_convert_fusion.3
  110.5 1.2 multiply_convert_fusion
  111.7 1.4 convolution_convert_fusion.2
  113.1 0.8 convolution_convert_fusion
  114.6 1.1 maximum_bitcast_fusion.4
  116.3 1.3 pad_maximum_fusion.1
  117.6 3.6 %all-to-all-start.1 = ((bf16[3,8,128,256]{2,3,0,1:T(8,128)(2,1)}), bf16[3,8,128,256]{2,3,0,1:T(8,128)(2,1)S(1)}, u32[]{:S(2)}, u32[]{:S(2)}) async-start(bf16[3,8,128,256]{2,3,0,1:T(8,128)(2,1)} %pad_maximum_fusion.1), calls=%async_computation.1 | async-start | bytes 3145728 | tf_op jit(solution)/shard_map/all_to_all | solution.py:164
  121.3 5.7 %convert_reduce_fusion = bf16[256,2048]{1,0:T(8,128)(2,1)} fusion(bf16[8,128,2048]{2,1,0:T(8,128)(2,1)} %bitcast.122, bf16[32,8,8,128]{3,2,1,0:T(8,128)(2,1)S(1)} %get-tuple-element.26), kind=kOutput, calls=%fused_computation | convolution fusion | flops 1081606144 | bytes 5767168 | tf_op jit(solution)/shard_map/bnf,bnk->bfk/dot_general | solution.py:140
  127.0 1.5 fusion.75
  128.5 1.2 copy.99
  129.7 1.1 copy.98
  130.9 1.4 reshape.56
  132.3 0.7 fusion.76
  133.0 0.5 copy.101
  134.0 1.0 select_bitcast_fusion
  135.0 4.7 %fusion.79 = (bf16[4,128,2048]{2,1,0:T(8,128)(2,1)S(1)}, f32[4,128,2048]{2,1,0:T(8,128)}) fusion(bf16[256,2048]{1,0:T(8,128)(2,1)} %collective-permute-done.1, bf16[256,2048]{1,0:T(8,128)(2,1)} %param.11, bf16[4,128,256]{2,1,0:T(8,128)(2,1)S(1)} %get-tuple-element.39, bf16[4,128,256]{2,1,0:T(8,128)(2,1)S(1)} %get-tuple-element.40), kind=kOutput, calls=%fused_computation.94 | convolution fusion | flops 1080033280 | bytes 8912896 | tf_op jit(solution)/shard_map/dot_general | solution.py:76
  139.9 1.9 collective-permute-start.2
  141.9 1.9 collective-permute-start.4
  143.8 1.0 collective-permute-start.3
  144.8 36.3 %all-reduce.2.cloned.1.call-done = bf16[256,2048]{1,0:T(8,128)(2,1)} async-done(((bf16[256,2048]{1,0:T(8,128)(2,1)}), bf16[256,2048]{1,0:T(8,128)(2,1)}) %all-reduce.2.cloned.1.call-update) | async-done | bytes 1048592 | tf_op jit(solution)/shard_map/psum | solution.py:144
  181.1 2.8 %convert_multiply_fusion = f32[256,2048]{1,0:T(8,128)} fusion(bf16[256,2048]{1,0:T(8,128)(2,1)} %all-reduce.2.cloned.1.call-done), kind=kLoop, calls=%fused_computation.21 | loop fusion | flops 1048576 | bytes 3145728 | tf_op jit(solution)/shard_map/div | solution.py:146
  183.9 20.2 %collective-permute-done.3 = bf16[128,2048]{1,0:T(8,128)(2,1)} collective-permute-done((bf16[128,2048]{1,0:T(8,128)(2,1)S(1)}, bf16[128,2048]{1,0:T(8,128)(2,1)}, u32[]{:S(2)}, u32[]{:S(2)}) %collective-permute-start.3) | collective-permute-done | bytes 524320 | tf_op jit(solution)/shard_map/ppermute | solution.py:84
  204.0 2.8 %fusion.47 = bf16[1,128,2048]{2,1,0:T(8,128)(2,1)} fusion(bf16[128,2048]{1,0:T(8,128)(2,1)} %collective-permute-done.4, bf16[128,2048]{1,0:T(8,128)(2,1)} %collective-permute-done.3, bf16[128,2048]{1,0:T(8,128)(2,1)} %collective-permute-done.2, f32[4,128,2048]{2,1,0:T(8,128)} %get-tuple-element.37, s32[]{:T(128)S(6)} %select_n.71), kind=kLoop, calls=%fused_computation.46 | loop fusion | flops 1835008 | bytes 3145732 | tf_op jit(solution)/shard_map/broadcast_in_dim | solution.py:133
  207.0 1.0 copy.92
  208.0 1.0 copy.91
  209.0 1.0 copy.90
  (46 shorter events, 3.7 us)
Async XLA Ops:
  7.2 92.0 %all-gather.3.cloned.1.call-start = ((), (), s32[]{:S(2)}) async-start(), calls=%async_computation.3 | async-start | bytes 4718592 | tf_op jit(solution)/shard_map/all_gather | solution.py:103
  11.9 8.3 %copy-start.6 = (s32[1,9]{1,0:T(1,128)S(1)}, s32[1,9]{1,0:T(1,128)}, u32[]{:S(2)}) copy-start(s32[1,9]{1,0:T(1,128)} %param.12) | copy-start | bytes 112
  11.9 8.4 %copy-start.7 = (s32[1,32]{1,0:T(1,128)S(1)}, s32[1,32]{1,0:T(1,128)}, u32[]{:S(2)}) copy-start(s32[1,32]{1,0:T(1,128)} %param.13) | copy-start | bytes 388
  13.3 77.9 %all-to-all-start = ((bf16[3,8,128,256]{2,3,0,1:T(8,128)(2,1)}), bf16[3,8,128,256]{2,3,0,1:T(8,128)(2,1)S(1)}, u32[]{:S(2)}, u32[]{:S(2)}) async-start(bf16[3,8,128,256]{2,3,0,1:T(8,128)(2,1)} %copy.76), calls=%async_computation | async-start | bytes 3145728 | tf_op jit(solution)/shard_map/all_to_all | solution.py:119
  19.6 115.4 %collective-permute-start.1 = (bf16[256,2048]{1,0:T(8,128)(2,1)}, bf16[256,2048]{1,0:T(8,128)(2,1)}, u32[]{:S(2)}, u32[]{:S(2)}) collective-permute-start(bf16[256,2048]{1,0:T(8,128)(2,1)} %param.11), channel_id=1, source_target_pairs={{0,1},{1,0},{2,3},{3,2},{4,5},{5,4},{6,7},{7,6},{8,9},{9,8},{10,11... | collective-permute-start | bytes 3145736 | tf_op jit(solution)/shard_map/ppermute | solution.py:68
  94.1 4.2 %copy-start = (f32[1024,1024]{0,1:T(8,128)}, f32[1024,1024]{0,1:T(8,128)S(1)}, u32[]{:S(2)}) copy-start(f32[1024,1024]{0,1:T(8,128)S(1)} %get-tuple-element.33) | copy-start | bytes 12582916
  95.7 2.0 copy-start.2
  95.7 2.6 %copy-start.4 = (bf16[1,8,128,256]{3,2,1,0:T(8,128)(2,1)S(1)}, bf16[1,8,128,256]{3,2,1,0:T(8,128)(2,1)}, u32[]{:S(2)}) copy-start(bf16[1,8,128,256]{3,2,1,0:T(8,128)(2,1)} %copy.97) | copy-start | bytes 1572868
  99.2 3.9 %copy-start.1 = (f32[1024,1024]{0,1:T(8,128)S(1)}, f32[1024,1024]{0,1:T(8,128)}, u32[]{:S(2)}) copy-start(f32[1024,1024]{0,1:T(8,128)} %copy-done) | copy-start | bytes 12582916
  103.1 2.3 %copy-start.3 = (f32[1024,1024]{0,1:T(8,128)S(1)}, f32[1024,1024]{0,1:T(8,128)}, u32[]{:S(2)}) copy-start(f32[1024,1024]{0,1:T(8,128)} %copy-done.2) | copy-start | bytes 12582916
  113.9 2.1 copy-start.5
  114.5 16.4 %collective-permute-start = (bf16[1024,256]{0,1:T(8,128)(2,1)S(1)}, bf16[1024,256]{0,1:T(8,128)(2,1)}, u32[]{:S(2)}, u32[]{:S(2)}) collective-permute-start(bf16[1024,256]{0,1:T(8,128)(2,1)S(1)} %get-tuple-element.27), channel_id=1, source_target_pairs={{0,1},{1,0},{2,3},{3,2},{4,5},{5,4},{6,7},{7,6},{8,9},{9,8},{10,11... | collective-permute-start | bytes 1572872 | tf_op jit(solution)/shard_map/ppermute | solution.py:67
  117.6 89.2 %all-to-all-start.1 = ((bf16[3,8,128,256]{2,3,0,1:T(8,128)(2,1)}), bf16[3,8,128,256]{2,3,0,1:T(8,128)(2,1)S(1)}, u32[]{:S(2)}, u32[]{:S(2)}) async-start(bf16[3,8,128,256]{2,3,0,1:T(8,128)(2,1)} %pad_maximum_fusion.1), calls=%async_computation.1 | async-start | bytes 3145728 | tf_op jit(solution)/shard_map/all_to_all | solution.py:164
  121.2 59.9 %all-reduce.2.cloned.1.call-start = ((), (), s32[]{:S(2)}) async-start(), calls=%async_computation.2 | async-start | bytes 2097152 | tf_op jit(solution)/shard_map/psum | solution.py:144
  139.9 43.9 %collective-permute-start.2 = (bf16[128,2048]{1,0:T(8,128)(2,1)S(1)}, bf16[128,2048]{1,0:T(8,128)(2,1)}, u32[]{:S(2)}, u32[]{:S(2)}) collective-permute-start(bf16[128,2048]{1,0:T(8,128)(2,1)S(1)} %get-tuple-element.17), channel_id=1, source_target_pairs={{0,2},{1,3},{2,4},{3,5},{4,6},{5,7},{6,0},{7,1},{8,10},{9,11},{10,... | collective-permute-start | bytes 1572872 | tf_op jit(solution)/shard_map/ppermute | solution.py:84
  141.9 42.0 %collective-permute-start.4 = (bf16[128,2048]{1,0:T(8,128)(2,1)S(1)}, bf16[128,2048]{1,0:T(8,128)(2,1)}, u32[]{:S(2)}, u32[]{:S(2)}) collective-permute-start(bf16[128,2048]{1,0:T(8,128)(2,1)S(1)} %get-tuple-element.18), channel_id=1, source_target_pairs={{0,6},{1,7},{2,0},{3,1},{4,2},{5,3},{6,4},{7,5},{8,14},{9,15},{10,... | collective-permute-start | bytes 1572872 | tf_op jit(solution)/shard_map/ppermute | solution.py:84
  143.8 60.2 %collective-permute-start.3 = (bf16[128,2048]{1,0:T(8,128)(2,1)S(1)}, bf16[128,2048]{1,0:T(8,128)(2,1)}, u32[]{:S(2)}, u32[]{:S(2)}) collective-permute-start(bf16[128,2048]{1,0:T(8,128)(2,1)S(1)} %get-tuple-element.19), channel_id=1, source_target_pairs={{0,4},{1,5},{2,6},{3,7},{4,0},{5,1},{6,2},{7,3},{8,12},{9,13},{10,... | collective-permute-start | bytes 1572872 | tf_op jit(solution)/shard_map/ppermute | solution.py:84
Sparse Core Ops, SparseCore 0:
  9.6 83.0 all-gather.2
  127.1 53.9 all-reduce.1

commit v17 on v16

--- a/solution.py
+++ b/solution.py
@@ -22,13 +22,13 @@
     full = jnp.broadcast_to(
         pairs[:, None, :, None], (tile_count, tile_size, tile_count, tile_size)
     )
-    return full.reshape(nodes, nodes)
+    return jnp.where(full.reshape(nodes, nodes), 0.0, -jnp.inf)
 
 
 def attend(q, k, v, allowed):
     factor = 1.0 / math.sqrt(q.shape[-1])
     scores = jnp.dot(q, k.T, preferred_element_type=jnp.float32) * factor
-    masked = jnp.where(allowed, scores, -jnp.inf)
+    masked = scores + allowed
     row_max = jnp.max(masked, axis=1, keepdims=True)
     expd = jnp.exp(masked - row_max)
     row_total = jnp.sum(expd, axis=1, keepdims=True)

time: 218 us -> 212 us (0.972)
  the two profiles are of different devices: /device:TPU:0 before, /device:TPU:14 now
where the time goes in v17:
time: 212 us
  waiting for transfers between devices  124 us (58%)
  matrix products  26 us (12%)
  local copies, waits for them, and re-layouts  20.4 us (10%)
  starting transfers between devices  17 us (8%)
  between operations  14.4 us (7%)
  other arithmetic  9.59 us (5%)
    all_to_all x1, waiting for transfers between devices, shards(): lax.all_to_all(stacked, 'seq', split_axis=1, concat_axis=1, tiled=True)  67.4 us
    psum x1, waiting for transfers between devices, shards(): w_rows = lax.psum(w_rows.astype(jnp.bfloat16), 'dp').astype(jnp.float32)  40.1 us
    ppermute x3, waiting for transfers between devices, chip_layer_out(): total = total + lax.ppermute(piece, 'seq', pairs).astype(jnp.float32)  16.2 us
    unnamed x28, local copies, waits for them, and re-layouts  14 us
    all_to_all x1, starting transfers between devices, shards(): back = lax.all_to_all(grads, 'seq', split_axis=1, concat_axis=1, tiled=True)  6.91 us
    dot_general x1, matrix products, shards(): jnp.einsum('bnf,bnk->bfk', att_blocks, grad_blocks, preferred_element_typ...  5.87 us
    all_to_all x1, starting transfers between devices, shards(): lax.all_to_all(stacked, 'seq', split_axis=1, concat_axis=1, tiled=True)  5.32 us
    dot_general x1, matrix products, chip_layer_out(): lax.dot_general(att_chip, w_chip, (((2,), (0,)), ((), ())), preferred_ele...  4.73 us
  transfers between devices with their start and end apart: 9, of which 5 were waited for; matrix products, arithmetic and copies ran while one was open for 24% of the time, Pallas kernels for 0%

profile of v17, /device:TPU:14, one launch (start us, length us, event | category | flops | bytes accessed | tf_op | source)
XLA Modules:
  0.0 211.8 jit_solution(7407488027923959950)
XLA Ops:
  7.2 0.7 all-gather.3.cloned.1.call-update
  7.9 1.3 copy.72
  9.2 1.3 copy.73
  10.5 1.3 copy.74
  12.1 1.2 copy.75
  13.3 5.3 %all-to-all-start = ((bf16[3,8,128,256]{2,3,0,1:T(8,128)(2,1)}), bf16[3,8,128,256]{2,3,0,1:T(8,128)(2,1)S(1)}, u32[]{:S(2)}, u32[]{:S(2)}) async-start(bf16[3,8,128,256]{2,3,0,1:T(8,128)(2,1)} %copy.75), calls=%async_computation | async-start | bytes 3145728 | tf_op jit(solution)/shard_map/all_to_all | solution.py:119
  19.3 67.4 %all-to-all-done = bf16[3,8,128,256]{2,3,0,1:T(8,128)(2,1)S(1)} async-done(((bf16[3,8,128,256]{2,3,0,1:T(8,128)(2,1)}), bf16[3,8,128,256]{2,3,0,1:T(8,128)(2,1)S(1)}, u32[]{:S(2)}, u32[]{:S(2)}) %all-to-all-start) | async-done | bytes 1572896 | tf_op jit(solution)/shard_map/all_to_all | solution.py:119
  87.9 1.2 fusion.78
  89.1 0.6 fusion.6
  89.7 1.3 fusion.79
  91.0 1.9 copy-done.2
  92.9 0.6 fusion.3
  93.5 0.8 fusion.32
  94.4 3.9 %fusion.21 = bf16[1024,256]{0,1:T(8,128)(2,1)S(1)} fusion(bf16[256,2048]{1,0:T(8,128)(2,1)} %param.11, bf16[1,1024,2048]{2,1,0:T(8,128)(2,1)} %all-gather.3.cloned.1.call-done), kind=kOutput, calls=%fused_computation.30 | convolution fusion | flops 1074003968 | bytes 5767168 | tf_op jit(solution)/shard_map/dot_general | solution.py:135
  98.3 0.9 multiply_reduce_fusion.1
  99.2 1.2 multiply_convert_fusion.1
  100.4 0.5 convolution_convert_fusion.3
  100.9 0.8 convolution_convert_fusion.1
  101.8 0.8 copy-done.1
  102.6 1.2 multiply_convert_fusion
  103.8 0.5 convolution_convert_fusion.2
  104.3 0.8 convolution_convert_fusion
  105.1 1.1 fusion.38
  106.3 0.9 fusion.41
  107.2 1.0 fusion.73
  109.3 1.4 pad_maximum_fusion.1
  110.6 6.9 %all-to-all-start.1 = ((bf16[3,8,128,256]{2,3,0,1:T(8,128)(2,1)}), bf16[3,8,128,256]{2,3,0,1:T(8,128)(2,1)S(1)}, u32[]{:S(2)}, u32[]{:S(2)}) async-start(bf16[3,8,128,256]{2,3,0,1:T(8,128)(2,1)} %pad_maximum_fusion.1), calls=%async_computation.1 | async-start | bytes 3145728 | tf_op jit(solution)/shard_map/all_to_all | solution.py:164
  117.5 1.5 fusion.76
  119.1 1.2 copy.98
  120.3 1.1 copy.99
  121.4 5.9 %convert_reduce_fusion = bf16[256,2048]{1,0:T(8,128)(2,1)} fusion(bf16[8,128,2048]{2,1,0:T(8,128)(2,1)} %bitcast.122, bf16[32,8,8,128]{3,2,1,0:T(8,128)(2,1)} %get-tuple-element.26), kind=kOutput, calls=%fused_computation | convolution fusion | flops 1081606144 | bytes 5767168 | tf_op jit(solution)/shard_map/bnf,bnk->bfk/dot_general | solution.py:140
  127.3 1.4 reshape.56
  128.7 0.7 fusion.77
  129.5 0.5 copy.100
  130.0 0.5 copy.101
  130.5 4.7 %fusion.80 = (bf16[4,128,2048]{2,1,0:T(8,128)(2,1)S(1)}, f32[4,128,2048]{2,1,0:T(8,128)}) fusion(bf16[256,2048]{1,0:T(8,128)(2,1)} %collective-permute-done.1, bf16[256,2048]{1,0:T(8,128)(2,1)} %param.11, bf16[4,128,256]{2,1,0:T(8,128)(2,1)S(1)} %get-tuple-element.39, bf16[4,128,256]{2,1,0:T(8,128)(2,1)S(1)} %get-tuple-element.40), kind=kOutput, calls=%fused_computation.95 | convolution fusion | flops 1080033280 | bytes 8912896 | tf_op jit(solution)/shard_map/dot_general | solution.py:76
  135.4 1.5 collective-permute-start.2
  137.0 1.0 collective-permute-start.3
  138.0 1.9 collective-permute-start.4
  139.9 40.1 %all-reduce.2.cloned.1.call-done = bf16[256,2048]{1,0:T(8,128)(2,1)} async-done(((bf16[256,2048]{1,0:T(8,128)(2,1)}), bf16[256,2048]{1,0:T(8,128)(2,1)}) %all-reduce.2.cloned.1.call-update) | async-done | bytes 1048592 | tf_op jit(solution)/shard_map/psum | solution.py:144
  180.0 2.8 %convert_multiply_fusion = f32[256,2048]{1,0:T(8,128)} fusion(bf16[256,2048]{1,0:T(8,128)(2,1)} %all-reduce.2.cloned.1.call-done), kind=kLoop, calls=%fused_computation.21 | loop fusion | flops 1048576 | bytes 3145728 | tf_op jit(solution)/shard_map/div | solution.py:146
  182.8 2.8 %collective-permute-done.2 = bf16[128,2048]{1,0:T(8,128)(2,1)} collective-permute-done((bf16[128,2048]{1,0:T(8,128)(2,1)S(1)}, bf16[128,2048]{1,0:T(8,128)(2,1)}, u32[]{:S(2)}, u32[]{:S(2)}) %collective-permute-start.2) | collective-permute-done | bytes 524320 | tf_op jit(solution)/shard_map/ppermute | solution.py:84
  185.6 11.2 %collective-permute-done.3 = bf16[128,2048]{1,0:T(8,128)(2,1)} collective-permute-done((bf16[128,2048]{1,0:T(8,128)(2,1)S(1)}, bf16[128,2048]{1,0:T(8,128)(2,1)}, u32[]{:S(2)}, u32[]{:S(2)}) %collective-permute-start.3) | collective-permute-done | bytes 524320 | tf_op jit(solution)/shard_map/ppermute | solution.py:84
  196.8 2.2 %collective-permute-done.4 = bf16[128,2048]{1,0:T(8,128)(2,1)} collective-permute-done((bf16[128,2048]{1,0:T(8,128)(2,1)S(1)}, bf16[128,2048]{1,0:T(8,128)(2,1)}, u32[]{:S(2)}, u32[]{:S(2)}) %collective-permute-start.4) | collective-permute-done | bytes 524320 | tf_op jit(solution)/shard_map/ppermute | solution.py:84
  199.0 2.8 %fusion.48 = bf16[1,128,2048]{2,1,0:T(8,128)(2,1)} fusion(bf16[128,2048]{1,0:T(8,128)(2,1)} %collective-permute-done.4, bf16[128,2048]{1,0:T(8,128)(2,1)} %collective-permute-done.3, bf16[128,2048]{1,0:T(8,128)(2,1)} %collective-permute-done.2, f32[4,128,2048]{2,1,0:T(8,128)} %get-tuple-element.37, s32[]{:T(128)S(6)} %select_n.72), kind=kLoop, calls=%fused_computation.47 | loop fusion | flops 1835008 | bytes 3145732 | tf_op jit(solution)/shard_map/broadcast_in_dim | solution.py:133
  202.0 1.0 copy.90
  203.0 1.0 copy.91
  204.0 1.0 copy.92
  (42 shorter events, 3.4 us)
Async XLA Ops:
  7.2 87.2 %all-gather.3.cloned.1.call-start = ((), (), s32[]{:S(2)}) async-start(), calls=%async_computation.3 | async-start | bytes 4718592 | tf_op jit(solution)/shard_map/all_gather | solution.py:103
  11.9 6.9 %copy-start.4 = (s32[1,9]{1,0:T(1,128)S(1)}, s32[1,9]{1,0:T(1,128)}, u32[]{:S(2)}) copy-start(s32[1,9]{1,0:T(1,128)} %param.12) | copy-start | bytes 112
  11.9 7.1 %copy-start.5 = (s32[1,32]{1,0:T(1,128)S(1)}, s32[1,32]{1,0:T(1,128)}, u32[]{:S(2)}) copy-start(s32[1,32]{1,0:T(1,128)} %param.13) | copy-start | bytes 388
  13.3 73.4 %all-to-all-start = ((bf16[3,8,128,256]{2,3,0,1:T(8,128)(2,1)}), bf16[3,8,128,256]{2,3,0,1:T(8,128)(2,1)S(1)}, u32[]{:S(2)}, u32[]{:S(2)}) async-start(bf16[3,8,128,256]{2,3,0,1:T(8,128)(2,1)} %copy.75), calls=%async_computation | async-start | bytes 3145728 | tf_op jit(solution)/shard_map/all_to_all | solution.py:119
  18.6 111.9 %collective-permute-start.1 = (bf16[256,2048]{1,0:T(8,128)(2,1)}, bf16[256,2048]{1,0:T(8,128)(2,1)}, u32[]{:S(2)}, u32[]{:S(2)}) collective-permute-start(bf16[256,2048]{1,0:T(8,128)(2,1)} %param.11), channel_id=1, source_target_pairs={{0,1},{1,0},{2,3},{3,2},{4,5},{5,4},{6,7},{7,6},{8,9},{9,8},{10,11... | collective-permute-start | bytes 3145736 | tf_op jit(solution)/shard_map/ppermute | solution.py:68
  89.1 4.5 %copy-start = (f32[1024,1024]{0,1:T(8,128)}, f32[1024,1024]{0,1:T(8,128)S(1)}, u32[]{:S(2)}) copy-start(f32[1024,1024]{0,1:T(8,128)S(1)} %get-tuple-element.33) | copy-start | bytes 12582916
  91.0 2.0 copy-start.2
  94.4 3.9 %copy-start.3 = (f32[1024,1024]{0,1:T(8,128)S(1)}, f32[1024,1024]{0,1:T(8,128)}, u32[]{:S(2)}) copy-start(f32[1024,1024]{0,1:T(8,128)} %copy-done.2) | copy-start | bytes 12582916
  100.4 2.2 %copy-start.1 = (f32[1024,1024]{0,1:T(8,128)S(1)}, f32[1024,1024]{0,1:T(8,128)}, u32[]{:S(2)}) copy-start(f32[1024,1024]{0,1:T(8,128)} %copy-done) | copy-start | bytes 12582916
  108.2 19.1 %collective-permute-start = (bf16[1024,256]{0,1:T(8,128)(2,1)S(1)}, bf16[1024,256]{0,1:T(8,128)(2,1)}, u32[]{:S(2)}, u32[]{:S(2)}) collective-permute-start(bf16[1024,256]{0,1:T(8,128)(2,1)S(1)} %get-tuple-element.27), channel_id=1, source_target_pairs={{0,1},{1,0},{2,3},{3,2},{4,5},{5,4},{6,7},{7,6},{8,9},{9,8},{10,11... | collective-permute-start | bytes 1572872 | tf_op jit(solution)/shard_map/ppermute | solution.py:67
  110.6 91.2 %all-to-all-start.1 = ((bf16[3,8,128,256]{2,3,0,1:T(8,128)(2,1)}), bf16[3,8,128,256]{2,3,0,1:T(8,128)(2,1)S(1)}, u32[]{:S(2)}, u32[]{:S(2)}) async-start(bf16[3,8,128,256]{2,3,0,1:T(8,128)(2,1)} %pad_maximum_fusion.1), calls=%async_computation.1 | async-start | bytes 3145728 | tf_op jit(solution)/shard_map/all_to_all | solution.py:164
  117.5 62.5 %all-reduce.2.cloned.1.call-start = ((), (), s32[]{:S(2)}) async-start(), calls=%async_computation.2 | async-start | bytes 2097152 | tf_op jit(solution)/shard_map/psum | solution.py:144
  135.4 50.2 %collective-permute-start.2 = (bf16[128,2048]{1,0:T(8,128)(2,1)S(1)}, bf16[128,2048]{1,0:T(8,128)(2,1)}, u32[]{:S(2)}, u32[]{:S(2)}) collective-permute-start(bf16[128,2048]{1,0:T(8,128)(2,1)S(1)} %get-tuple-element.17), channel_id=1, source_target_pairs={{0,2},{1,3},{2,4},{3,5},{4,6},{5,7},{6,0},{7,1},{8,10},{9,11},{10,... | collective-permute-start | bytes 1572872 | tf_op jit(solution)/shard_map/ppermute | solution.py:84
  137.0 59.8 %collective-permute-start.3 = (bf16[128,2048]{1,0:T(8,128)(2,1)S(1)}, bf16[128,2048]{1,0:T(8,128)(2,1)}, u32[]{:S(2)}, u32[]{:S(2)}) collective-permute-start(bf16[128,2048]{1,0:T(8,128)(2,1)S(1)} %get-tuple-element.19), channel_id=1, source_target_pairs={{0,4},{1,5},{2,6},{3,7},{4,0},{5,1},{6,2},{7,3},{8,12},{9,13},{10,... | collective-permute-start | bytes 1572872 | tf_op jit(solution)/shard_map/ppermute | solution.py:84
  138.0 61.0 %collective-permute-start.4 = (bf16[128,2048]{1,0:T(8,128)(2,1)S(1)}, bf16[128,2048]{1,0:T(8,128)(2,1)}, u32[]{:S(2)}, u32[]{:S(2)}) collective-permute-start(bf16[128,2048]{1,0:T(8,128)(2,1)S(1)} %get-tuple-element.18), channel_id=1, source_target_pairs={{0,6},{1,7},{2,0},{3,1},{4,2},{5,3},{6,4},{7,5},{8,14},{9,15},{10,... | collective-permute-start | bytes 1572872 | tf_op jit(solution)/shard_map/ppermute | solution.py:84
Sparse Core Ops, SparseCore 0:
  9.6 77.0 all-gather.2
  127.4 52.5 all-reduce.1

commit v18 on v17

--- a/solution.py
+++ b/solution.py
@@ -39,7 +39,7 @@
 
 def attend_back(q, k, v, g, attended, expd, row_total):
     factor = 1.0 / math.sqrt(q.shape[-1])
-    prob = expd / row_total
+    prob = expd * (1.0 / row_total)
     prob_low = prob.astype(jnp.bfloat16)
     v_grad = jnp.dot(prob_low.T, g, preferred_element_type=jnp.float32)
     prob_grad = jnp.dot(g, v.T, preferred_element_type=jnp.float32)

time: 212 us -> 212 us (level)
  the two profiles are of different devices: /device:TPU:14 before, /device:TPU:10 now
where the time goes in v18:
time: 212 us; the launch traced here: 211 us
  waiting for transfers between devices  124 us (58%)
  matrix products  25.9 us (12%)
  local copies, waits for them, and re-layouts  19.9 us (9%)
  starting transfers between devices  17 us (8%)
  between operations  14.4 us (7%)
  other arithmetic  9.61 us (5%)
    all_to_all x1, waiting for transfers between devices, shards(): lax.all_to_all(stacked, 'seq', split_axis=1, concat_axis=1, tiled=True)  67.4 us
    psum x1, waiting for transfers between devices, shards(): w_rows = lax.psum(w_rows.astype(jnp.bfloat16), 'dp').astype(jnp.float32)  41.1 us
    ppermute x3, waiting for transfers between devices, chip_layer_out(): total = total + lax.ppermute(piece, 'seq', pairs).astype(jnp.float32)  15.3 us
    unnamed x28, local copies, waits for them, and re-layouts  13.5 us
    all_to_all x1, starting transfers between devices, shards(): back = lax.all_to_all(grads, 'seq', split_axis=1, concat_axis=1, tiled=True)  6.9 us
    dot_general x1, matrix products, shards(): jnp.einsum('bnf,bnk->bfk', att_blocks, grad_blocks, preferred_element_typ...  5.87 us
    all_to_all x1, starting transfers between devices, shards(): lax.all_to_all(stacked, 'seq', split_axis=1, concat_axis=1, tiled=True)  5.32 us
    dot_general x1, matrix products, chip_layer_out(): lax.dot_general(att_chip, w_chip, (((2,), (0,)), ((), ())), preferred_ele...  4.73 us
  transfers between devices with their start and end apart: 9, of which 5 were waited for; matrix products, arithmetic and copies ran while one was open for 24% of the time, Pallas kernels for 0%

profile of v18, /device:TPU:10, one launch (start us, length us, event | category | flops | bytes accessed | tf_op | source)
XLA Modules:
  0.0 211.3 jit_solution(6985377320653367382)
XLA Ops:
  7.2 0.7 all-gather.3.cloned.1.call-update
  7.9 1.3 copy.72
  9.2 1.3 copy.73
  10.5 1.3 copy.74
  12.1 1.2 copy.75
  13.3 5.3 %all-to-all-start = ((bf16[3,8,128,256]{2,3,0,1:T(8,128)(2,1)}), bf16[3,8,128,256]{2,3,0,1:T(8,128)(2,1)S(1)}, u32[]{:S(2)}, u32[]{:S(2)}) async-start(bf16[3,8,128,256]{2,3,0,1:T(8,128)(2,1)} %copy.75), calls=%async_computation | async-start | bytes 3145728 | tf_op jit(solution)/shard_map/all_to_all | solution.py:119
  19.3 67.4 %all-to-all-done = bf16[3,8,128,256]{2,3,0,1:T(8,128)(2,1)S(1)} async-done(((bf16[3,8,128,256]{2,3,0,1:T(8,128)(2,1)}), bf16[3,8,128,256]{2,3,0,1:T(8,128)(2,1)S(1)}, u32[]{:S(2)}, u32[]{:S(2)}) %all-to-all-start) | async-done | bytes 1572896 | tf_op jit(solution)/shard_map/all_to_all | solution.py:119
  87.9 1.2 fusion.73
  89.1 0.6 fusion.2
  89.7 1.2 fusion.72
  91.1 0.6 fusion.4
  91.7 1.3 copy-done.2
  93.0 0.8 fusion.32
  93.9 3.9 %fusion.21 = bf16[1024,256]{0,1:T(8,128)(2,1)S(1)} fusion(bf16[256,2048]{1,0:T(8,128)(2,1)} %param.11, bf16[1,1024,2048]{2,1,0:T(8,128)(2,1)} %all-gather.3.cloned.1.call-done), kind=kOutput, calls=%fused_computation.32 | convolution fusion | flops 1074003968 | bytes 5767168 | tf_op jit(solution)/shard_map/dot_general | solution.py:135
  97.8 0.9 multiply_reduce_fusion.1
  98.7 1.2 multiply_convert_fusion.1
  99.9 0.5 convolution_convert_fusion.3
  100.4 0.8 convolution_convert_fusion.1
  101.2 0.8 copy-done.3
  102.1 1.2 multiply_convert_fusion
  103.3 0.5 convolution_convert_fusion.2
  103.8 0.8 convolution_convert_fusion
  104.6 1.1 fusion.31
  105.7 0.9 fusion.30
  106.7 1.0 fusion.67
  108.8 1.4 pad_maximum_fusion.1
  110.1 6.9 %all-to-all-start.1 = ((bf16[3,8,128,256]{2,3,0,1:T(8,128)(2,1)}), bf16[3,8,128,256]{2,3,0,1:T(8,128)(2,1)S(1)}, u32[]{:S(2)}, u32[]{:S(2)}) async-start(bf16[3,8,128,256]{2,3,0,1:T(8,128)(2,1)} %pad_maximum_fusion.1), calls=%async_computation.1 | async-start | bytes 3145728 | tf_op jit(solution)/shard_map/all_to_all | solution.py:164
  117.0 1.5 fusion.70
  118.5 1.2 copy.98
  119.8 1.1 copy.99
  120.9 5.9 %convert_reduce_fusion = bf16[256,2048]{1,0:T(8,128)(2,1)} fusion(bf16[8,128,2048]{2,1,0:T(8,128)(2,1)} %bitcast.122, bf16[32,8,8,128]{3,2,1,0:T(8,128)(2,1)} %get-tuple-element.26), kind=kOutput, calls=%fused_computation | convolution fusion | flops 1081606144 | bytes 5767168 | tf_op jit(solution)/shard_map/bnf,bnk->bfk/dot_general | solution.py:140
  126.8 1.4 reshape.64
  128.2 0.7 fusion.71
  128.9 0.5 copy.100
  129.4 0.5 copy.101
  130.0 4.7 %fusion.74 = (bf16[4,128,2048]{2,1,0:T(8,128)(2,1)S(1)}, f32[4,128,2048]{2,1,0:T(8,128)}) fusion(bf16[256,2048]{1,0:T(8,128)(2,1)} %collective-permute-done.1, bf16[256,2048]{1,0:T(8,128)(2,1)} %param.11, bf16[4,128,256]{2,1,0:T(8,128)(2,1)S(1)} %get-tuple-element.39, bf16[4,128,256]{2,1,0:T(8,128)(2,1)S(1)} %get-tuple-element.40), kind=kOutput, calls=%fused_computation.99 | convolution fusion | flops 1080033280 | bytes 8912896 | tf_op jit(solution)/shard_map/dot_general | solution.py:76
  134.9 1.5 collective-permute-start.2
  136.4 1.0 collective-permute-start.3
  137.5 1.9 collective-permute-start.4
  139.4 41.1 %all-reduce.2.cloned.1.call-done = bf16[256,2048]{1,0:T(8,128)(2,1)} async-done(((bf16[256,2048]{1,0:T(8,128)(2,1)}), bf16[256,2048]{1,0:T(8,128)(2,1)}) %all-reduce.2.cloned.1.call-update) | async-done | bytes 1048592 | tf_op jit(solution)/shard_map/psum | solution.py:144
  180.4 2.8 %convert_multiply_fusion = f32[256,2048]{1,0:T(8,128)} fusion(bf16[256,2048]{1,0:T(8,128)(2,1)} %all-reduce.2.cloned.1.call-done), kind=kLoop, calls=%fused_computation.23 | loop fusion | flops 1048576 | bytes 3145728 | tf_op jit(solution)/shard_map/div | solution.py:146
  183.2 1.9 collective-permute-done.2
  185.1 11.2 %collective-permute-done.3 = bf16[128,2048]{1,0:T(8,128)(2,1)} collective-permute-done((bf16[128,2048]{1,0:T(8,128)(2,1)S(1)}, bf16[128,2048]{1,0:T(8,128)(2,1)}, u32[]{:S(2)}, u32[]{:S(2)}) %collective-permute-start.3) | collective-permute-done | bytes 524320 | tf_op jit(solution)/shard_map/ppermute | solution.py:84
  196.3 2.2 %collective-permute-done.4 = bf16[128,2048]{1,0:T(8,128)(2,1)} collective-permute-done((bf16[128,2048]{1,0:T(8,128)(2,1)S(1)}, bf16[128,2048]{1,0:T(8,128)(2,1)}, u32[]{:S(2)}, u32[]{:S(2)}) %collective-permute-start.4) | collective-permute-done | bytes 524320 | tf_op jit(solution)/shard_map/ppermute | solution.py:84
  198.5 2.8 %fusion.42 = bf16[1,128,2048]{2,1,0:T(8,128)(2,1)} fusion(bf16[128,2048]{1,0:T(8,128)(2,1)} %collective-permute-done.4, bf16[128,2048]{1,0:T(8,128)(2,1)} %collective-permute-done.3, bf16[128,2048]{1,0:T(8,128)(2,1)} %collective-permute-done.2, f32[4,128,2048]{2,1,0:T(8,128)} %get-tuple-element.37, s32[]{:T(128)S(6)} %select_n.72), kind=kLoop, calls=%fused_computation.49 | loop fusion | flops 1835008 | bytes 3145732 | tf_op jit(solution)/shard_map/broadcast_in_dim | solution.py:133
  201.4 1.0 copy.90
  202.4 1.0 copy.91
  203.4 1.0 copy.92
  (44 shorter events, 3.6 us)
Async XLA Ops:
  7.2 86.7 %all-gather.3.cloned.1.call-start = ((), (), s32[]{:S(2)}) async-start(), calls=%async_computation.3 | async-start | bytes 4718592 | tf_op jit(solution)/shard_map/all_gather | solution.py:103
  11.9 6.9 %copy-start.4 = (s32[1,9]{1,0:T(1,128)S(1)}, s32[1,9]{1,0:T(1,128)}, u32[]{:S(2)}) copy-start(s32[1,9]{1,0:T(1,128)} %param.12) | copy-start | bytes 112
  11.9 7.1 %copy-start.5 = (s32[1,32]{1,0:T(1,128)S(1)}, s32[1,32]{1,0:T(1,128)}, u32[]{:S(2)}) copy-start(s32[1,32]{1,0:T(1,128)} %param.13) | copy-start | bytes 388
  13.3 73.4 %all-to-all-start = ((bf16[3,8,128,256]{2,3,0,1:T(8,128)(2,1)}), bf16[3,8,128,256]{2,3,0,1:T(8,128)(2,1)S(1)}, u32[]{:S(2)}, u32[]{:S(2)}) async-start(bf16[3,8,128,256]{2,3,0,1:T(8,128)(2,1)} %copy.75), calls=%async_computation | async-start | bytes 3145728 | tf_op jit(solution)/shard_map/all_to_all | solution.py:119
  18.6 111.3 %collective-permute-start.1 = (bf16[256,2048]{1,0:T(8,128)(2,1)}, bf16[256,2048]{1,0:T(8,128)(2,1)}, u32[]{:S(2)}, u32[]{:S(2)}) collective-permute-start(bf16[256,2048]{1,0:T(8,128)(2,1)} %param.11), channel_id=1, source_target_pairs={{0,1},{1,0},{2,3},{3,2},{4,5},{5,4},{6,7},{7,6},{8,9},{9,8},{10,11... | collective-permute-start | bytes 3145736 | tf_op jit(solution)/shard_map/ppermute | solution.py:68
  89.1 2.0 copy-start
  91.1 2.0 copy-start.2
  93.9 3.9 %copy-start.1 = (f32[1024,1024]{0,1:T(8,128)S(1)}, f32[1024,1024]{0,1:T(8,128)}, u32[]{:S(2)}) copy-start(f32[1024,1024]{0,1:T(8,128)} %copy-done) | copy-start | bytes 12582916
  99.9 2.2 %copy-start.3 = (f32[1024,1024]{0,1:T(8,128)S(1)}, f32[1024,1024]{0,1:T(8,128)}, u32[]{:S(2)}) copy-start(f32[1024,1024]{0,1:T(8,128)} %copy-done.2) | copy-start | bytes 12582916
  107.6 19.1 %collective-permute-start = (bf16[1024,256]{0,1:T(8,128)(2,1)S(1)}, bf16[1024,256]{0,1:T(8,128)(2,1)}, u32[]{:S(2)}, u32[]{:S(2)}) collective-permute-start(bf16[1024,256]{0,1:T(8,128)(2,1)S(1)} %get-tuple-element.27), channel_id=1, source_target_pairs={{0,1},{1,0},{2,3},{3,2},{4,5},{5,4},{6,7},{7,6},{8,9},{9,8},{10,11... | collective-permute-start | bytes 1572872 | tf_op jit(solution)/shard_map/ppermute | solution.py:67
  110.1 91.2 %all-to-all-start.1 = ((bf16[3,8,128,256]{2,3,0,1:T(8,128)(2,1)}), bf16[3,8,128,256]{2,3,0,1:T(8,128)(2,1)S(1)}, u32[]{:S(2)}, u32[]{:S(2)}) async-start(bf16[3,8,128,256]{2,3,0,1:T(8,128)(2,1)} %pad_maximum_fusion.1), calls=%async_computation.1 | async-start | bytes 3145728 | tf_op jit(solution)/shard_map/all_to_all | solution.py:164
  117.0 63.4 %all-reduce.2.cloned.1.call-start = ((), (), s32[]{:S(2)}) async-start(), calls=%async_computation.2 | async-start | bytes 2097152 | tf_op jit(solution)/shard_map/psum | solution.py:144
  134.9 50.2 %collective-permute-start.2 = (bf16[128,2048]{1,0:T(8,128)(2,1)S(1)}, bf16[128,2048]{1,0:T(8,128)(2,1)}, u32[]{:S(2)}, u32[]{:S(2)}) collective-permute-start(bf16[128,2048]{1,0:T(8,128)(2,1)S(1)} %get-tuple-element.17), channel_id=1, source_target_pairs={{0,2},{1,3},{2,4},{3,5},{4,6},{5,7},{6,0},{7,1},{8,10},{9,11},{10,... | collective-permute-start | bytes 1572872 | tf_op jit(solution)/shard_map/ppermute | solution.py:84
  136.4 59.8 %collective-permute-start.3 = (bf16[128,2048]{1,0:T(8,128)(2,1)S(1)}, bf16[128,2048]{1,0:T(8,128)(2,1)}, u32[]{:S(2)}, u32[]{:S(2)}) collective-permute-start(bf16[128,2048]{1,0:T(8,128)(2,1)S(1)} %get-tuple-element.19), channel_id=1, source_target_pairs={{0,4},{1,5},{2,6},{3,7},{4,0},{5,1},{6,2},{7,3},{8,12},{9,13},{10,... | collective-permute-start | bytes 1572872 | tf_op jit(solution)/shard_map/ppermute | solution.py:84
  137.5 61.0 %collective-permute-start.4 = (bf16[128,2048]{1,0:T(8,128)(2,1)S(1)}, bf16[128,2048]{1,0:T(8,128)(2,1)}, u32[]{:S(2)}, u32[]{:S(2)}) collective-permute-start(bf16[128,2048]{1,0:T(8,128)(2,1)S(1)} %get-tuple-element.18), channel_id=1, source_target_pairs={{0,6},{1,7},{2,0},{3,1},{4,2},{5,3},{6,4},{7,5},{8,14},{9,15},{10,... | collective-permute-start | bytes 1572872 | tf_op jit(solution)/shard_map/ppermute | solution.py:84
Sparse Core Ops, SparseCore 0:
  9.6 77.0 all-gather.2
  126.9 53.4 all-reduce.1
